TPU v7x, 128 devices: a whole 4x4x4 slice. The times are simulated.
128 devices in a mesh: enc: 16 (over z, y), dp: 2 (over x_hi), tensor: 4 (over x_lo, core).
Axes of the slice: x: 4 (x_hi: 2, x_lo: 2; x = x_hi * 2 + x_lo), y: 4, z: 4, core: 2. Of those that a mesh axis runs over, the one named last changes fastest.
Arguments:
- hidden_in: bfloat16 [3, 64, 4096], P(None, 'dp', 'enc')
- self_cache: bfloat16 [64, 8, 2, 2048], P(('dp', 'enc'), None, None, 'tensor'), may hold values from -6 to 6
- src_pool: bfloat16 [64, 24, 2, 2048], P(('dp', 'enc'), None, None, 'tensor'), may hold values from -6 to 6
- assign: int32 [64], replicated, may hold values from 0 to 63, as said below
- src_len: int32 [64], replicated, may hold values from 1 to 24, 768 in all
- positions: int32 [64], replicated, may hold values from 1 to 8, 256 in all
- gain_self: float32 [4096], P('enc'), may hold values from 0.1 to 1.9
- w_qkv: bfloat16 [4096, 3, 2048], P('enc', None, 'tensor'), may hold values from -0.09375 to 0.09375
- w_out_self: bfloat16 [2048, 4096], P('tensor', 'enc'), may hold values from -0.125 to 0.125
- gain_cross: float32 [4096], P('enc'), may hold values from 0.1 to 1.9
- w_q_cross: bfloat16 [4096, 2048], P('enc', 'tensor'), may hold values from -0.09375 to 0.09375
- w_out_cross: bfloat16 [2048, 4096], P('tensor', 'enc'), may hold values from -0.125 to 0.125
Outputs:
- layer_out: bfloat16 [3, 64, 4096], P(None, 'dp', 'enc')
Inputs may be any that keep to these rules, and one draw needn't show every extreme that they name: `assign`: a permutation of the 64 sources; with blocks of 2 consecutive sequences or sources numbered d * 16 + e, the 2 sequences of block d * 16 + e read exactly one source from each block d2 * 16 + e that has the same e.
All inputs are finite; a program needn't handle non-finite values.
Results may differ from a plain program's by a relative error of at most 0.008.
Values may be sent and summed in bfloat16 or wider, within the bound.
No kernel may reach another device: no remote copies, remote signals or barrier semaphores. Data moves between devices by JAX's collectives and lax.ppermute only.
A program may use at most 64 MiB of HBM per device.

v0:
```python
import math

import jax
import jax.numpy as jnp
from jax import lax
from jax.sharding import PartitionSpec as P

D = 4096
DK = 256
STEPS = 3


EPSILON = 1e-06


def row_norm(rows_in, gain_vec):
    squares = lax.psum(jnp.sum(rows_in * rows_in, axis=1), "enc")
    return (rows_in * lax.rsqrt(squares / D + EPSILON)[:, None] * gain_vec[None, :]).astype(
        jnp.bfloat16
    )


def score_weight(scores):
    return jnp.exp(scores).astype(jnp.bfloat16)


def attend(query_rows, key_rows, value_rows, usable):
    count = query_rows.shape[0]
    head_count = query_rows.shape[1] // DK
    query_heads = query_rows.reshape(count, head_count, DK)
    key_heads = key_rows.reshape(count, key_rows.shape[1], head_count, DK)
    value_heads = value_rows.reshape(count, value_rows.shape[1], head_count, DK)
    scores = jnp.einsum(
        "nhd,nlhd->nhl", query_heads, key_heads, preferred_element_type=jnp.float32
    ) * (1.0 / math.sqrt(DK))
    weights = jnp.where(usable[:, None, :], score_weight(scores), jnp.zeros((), jnp.bfloat16))
    weighted = jnp.einsum("nhl,nlhd->nhd", weights, value_heads, preferred_element_type=jnp.float32)
    return (weighted, jnp.sum(weights.astype(jnp.float32), axis=-1))


def combine_heads(context, weight_out):
    partial_out = jnp.dot(context, weight_out, preferred_element_type=jnp.float32)
    return lax.psum(partial_out, "tensor")


def on_device(
    hidden_in,
    self_cache,
    src_pool,
    assign,
    src_len,
    positions,
    gain_self,
    w_qkv,
    w_out_self,
    gain_cross,
    w_q_cross,
    w_out_cross,
):
    dp_count = lax.axis_size("dp")
    enc_count = lax.axis_size("enc")
    seq_dev = self_cache.shape[0]
    per_pair = seq_dev // dp_count
    cache_len = self_cache.shape[1]
    source_len = src_pool.shape[1]
    enc_at = lax.axis_index("enc")
    dp_at = lax.axis_index("dp")
    block_at = dp_at * enc_count + enc_at
    slot_index = jnp.arange(seq_dev, dtype=jnp.int32)
    my_slots = block_at * seq_dev + slot_index
    my_positions = jnp.take(positions, my_slots)
    my_sources = jnp.take(assign, my_slots)
    place_at = jnp.arange(cache_len, dtype=jnp.int32)
    cache_usable = place_at[None, :] < my_positions[:, None]
    token_at = jnp.arange(source_len, dtype=jnp.int32)
    assign_view = assign.reshape(dp_count, enc_count, seq_dev)
    assign_grid = jnp.take(assign_view, enc_at, axis=1)
    owners = assign_grid // (seq_dev * enc_count)
    earlier = (owners[:, None, :] == owners[:, :, None]) & (
        slot_index[None, None, :] < slot_index[None, :, None]
    )
    slot_rank = jnp.sum(earlier.astype(jnp.int32), axis=2)
    recv_rows = jnp.take(owners, dp_at, axis=0) * per_pair + jnp.take(slot_rank, dp_at, axis=0)
    picked = (owners == dp_at)[:, :, None] & (
        slot_rank[:, :, None] == jnp.arange(per_pair, dtype=jnp.int32)[None, None, :]
    )
    chosen = jnp.sum(jnp.where(picked, (assign_grid % seq_dev)[:, :, None], 0), axis=1)
    chosen_flat = chosen.reshape(-1)
    outgoing = jnp.take(src_pool, chosen_flat, axis=0)
    arrived = lax.all_to_all(outgoing, "dp", split_axis=0, concat_axis=0, tiled=True)
    cross_kv = jnp.take(arrived, recv_rows, axis=0)
    cross_usable = token_at[None, :] < jnp.take(src_len, my_sources)[:, None]
    key_list = []
    value_list = []
    results = []
    for step_at in range(STEPS):
        current = hidden_in[step_at].astype(jnp.float32)
        normed = row_norm(current, gain_self)
        projected = jnp.einsum("sd,dcw->scw", normed, w_qkv, preferred_element_type=jnp.float32)
        own_proj = lax.psum_scatter(projected, "enc", scatter_dimension=0, tiled=True).astype(
            jnp.bfloat16
        )
        query_rows = own_proj[:, 0]
        key_list.append(own_proj[:, 1])
        value_list.append(own_proj[:, 2])
        weighted, totals = attend(
            query_rows, self_cache[:, :, 0], self_cache[:, :, 1], cache_usable
        )
        head_count = weighted.shape[1]
        query_heads = query_rows.astype(jnp.float32).reshape(seq_dev, head_count, DK)
        for key_new, value_new in zip(key_list, value_list):
            scores = jnp.sum(
                query_heads * key_new.astype(jnp.float32).reshape(seq_dev, head_count, DK), axis=-1
            ) * (1.0 / math.sqrt(DK))
            weights = score_weight(scores).astype(jnp.float32)
            weighted = weighted + weights[:, :, None] * value_new.astype(jnp.float32).reshape(
                seq_dev, head_count, DK
            )
            totals = totals + weights
        context = (
            (weighted / totals[:, :, None]).reshape(seq_dev, head_count * DK).astype(jnp.bfloat16)
        )
        context_all = lax.all_gather(context, "enc", axis=0, tiled=True)
        residual = current + combine_heads(context_all, w_out_self)
        normed_cross = row_norm(residual, gain_cross)
        cross_query = jnp.dot(normed_cross, w_q_cross, preferred_element_type=jnp.float32)
        own_query = lax.psum_scatter(cross_query, "enc", scatter_dimension=0, tiled=True).astype(
            jnp.bfloat16
        )
        weighted, totals = attend(own_query, cross_kv[:, :, 0], cross_kv[:, :, 1], cross_usable)
        context = (
            (weighted / totals[:, :, None]).reshape(seq_dev, head_count * DK).astype(jnp.bfloat16)
        )
        context_all = lax.all_gather(context, "enc", axis=0, tiled=True)
        output_rows = residual + combine_heads(context_all, w_out_cross)
        results.append(output_rows.astype(jnp.bfloat16))
    return jnp.stack(results)


def solution(mesh):
    in_specs = (
        P(None, "dp", "enc"),
        P(("dp", "enc"), None, None, "tensor"),
        P(("dp", "enc"), None, None, "tensor"),
        P(),
        P(),
        P(),
        P("enc"),
        P("enc", None, "tensor"),
        P("tensor", "enc"),
        P("enc"),
        P("enc", "tensor"),
        P("tensor", "enc"),
    )
    out_specs = P(None, "dp", "enc")
    return jax.shard_map(
        on_device, mesh=mesh, in_specs=in_specs, out_specs=out_specs, check_vma=False
    )
```

profile of v0, /device:TPU:1, one launch (start us, length us, event | category | flops | bytes accessed | tf_op | source)
XLA Modules:
  0.0 470.3 jit_solution(5215867503166297110)
XLA Ops:
  6.6 0.7 copy-done.1
  7.4 0.2 fusion.80
  7.6 0.1 fusion.90
  7.8 0.6 gather_fusion.1
  8.5 0.2 copy-done.12
  8.7 0.7 gather_fusion.3
  9.4 0.8 broadcast_select_fusion.1
  10.2 5.0 %all-to-all-start = ((bf16[2,24,2,512]{3,2,1,0:T(2,128)(2,1)}), bf16[2,24,2,512]{3,2,1,0:T(2,128)(2,1)S(1)}, u32[]{:S(2)}, u32[]{:S(2)}) async-start(bf16[2,24,2,512]{3,2,1,0:T(2,128)(2,1)} %broadcast_select_fusion.1), calls=%async_computation | async-start | bytes 196608 | tf_op jit(solution)/shard_map/all_to_all | solution.py:90
  15.2 0.1 fusion.18
  15.3 34.7 %all-reduce.9 = (f32[32]{0:T(128)S(1)}, f32[32]{0:T(128)S(1)}, f32[32]{0:T(128)S(1)}) all-reduce(f32[32]{0:T(128)S(1)} %get-tuple-element.35, f32[32]{0:T(128)S(1)} %get-tuple-element.36, f32[32]{0:T(128)S(1)} %get-tuple-element.37), channel_id=1, replica_groups=mesh['enc'=16,'dp'=2,'tensor'=4] {'enc'}, use_global_device_ids=true, to_apply=%region_1.3 | all-reduce | flops 96 | bytes 768 | tf_op jit(solution)/shard_map/psum | solution.py:17
  50.0 0.7 copy-done.14
  50.7 0.3 fusion.34
  51.0 0.3 fusion.37
  51.3 0.3 fusion.40
  51.6 0.7 copy-done.15
  52.2 0.6 dynamic-slice.11
  53.5 62.2 %all-reduce.20 = (bf16[32,3,512]{2,0,1:T(8,128)(2,1)S(1)}, bf16[32,3,512]{2,0,1:T(8,128)(2,1)S(1)}, bf16[32,3,512]{2,0,1:T(8,128)(2,1)S(1)}) all-reduce(f32[32,3,512]{2,0,1:T(8,128)S(1)} %fusion.40, f32[32,3,512]{2,0,1:T(8,128)S(1)} %fusion.34, f32[32,3,512]{2,0,1:T(8,128)S(1)} %fusion.37), channel_id=2, replica_groups=mesh['enc'=16,'dp'=2,'tensor'=4] {'enc'}, use_global_device_ids=true, to_apply=%region_2.4.clone | all-reduce | flops 147456 | bytes 884736
  116.0 0.6 copy-done.11
  116.6 0.1 slice_reduce_fusion.3
  116.7 0.1 fusion.104
  116.9 0.1 fusion.107
  117.0 0.1 fusion.101
  117.1 0.4 copy-done.2
  117.5 0.6 gather_fusion
  118.3 0.1 fusion.85
  118.5 0.1 fusion.88
  118.6 0.1 fusion.82
  119.0 15.2 %all-gather = bf16[16,2,512]{2,1,0:T(2,128)(2,1)S(1)} all-gather(bf16[1,2,512]{2,1,0:T(2,128)(2,1)S(1)} %reshape.380), channel_id=1, replica_groups=mesh['enc'=16,'dp'=2,'tensor'=4] {'enc'}, dimensions={0}, use_global_device_ids=true | all-gather | bytes 34816 | tf_op jit(solution)/shard_map/all_gather | solution.py:123
  134.2 18.0 %all-gather.2 = bf16[16,2,512]{2,1,0:T(2,128)(2,1)S(1)} all-gather(bf16[1,2,512]{2,1,0:T(2,128)(2,1)S(1)} %reshape.384), channel_id=1, replica_groups=mesh['enc'=16,'dp'=2,'tensor'=4] {'enc'}, dimensions={0}, use_global_device_ids=true | all-gather | bytes 34816 | tf_op jit(solution)/shard_map/all_gather | solution.py:123
  152.3 0.8 fusion.102
  153.1 0.8 fusion.105
  153.8 15.4 %all-gather.4 = bf16[16,2,512]{2,1,0:T(2,128)(2,1)S(1)} all-gather(bf16[1,2,512]{2,1,0:T(2,128)(2,1)S(1)} %reshape.388), channel_id=1, replica_groups=mesh['enc'=16,'dp'=2,'tensor'=4] {'enc'}, dimensions={0}, use_global_device_ids=true | all-gather | bytes 34816 | tf_op jit(solution)/shard_map/all_gather | solution.py:123
  169.3 0.8 fusion.108
  170.1 0.5 copy-done.3
  170.7 0.6 gather_fusion.2
  171.4 0.7 gather_fusion.4
  172.2 0.2 broadcast_select_fusion
  172.3 0.4 slice_reduce_fusion.1
  172.8 70.9 %all-reduce.19.cloned.1.call-done = (f32[32,256]{1,0:T(8,128)}, f32[32,256]{1,0:T(8,128)}, f32[32,256]{1,0:T(8,128)}) async-done(((f32[32,256]{1,0:T(8,128)}, f32[32,256]{1,0:T(8,128)}, f32[32,256]{1,0:T(8,128)}), (f32[32,256]{1,0:T(8,128)}, f32[32,256]{1,0:T(8,128)}, f32[32,256]{1,0:T(8,128)})) %all-reduce.19.cloned.1.call-update) | async-done | bytes 98320 | tf_op jit(solution)/shard_map/psum | solution.py:43
  243.7 1.0 multiply_reduce_fusion.2
  244.6 33.3 %all-reduce.7 = (f32[32]{0:T(128)S(1)}, f32[32]{0:T(128)S(1)}, f32[32]{0:T(128)S(1)}) all-reduce(f32[32]{0:T(128)S(1)} %get-tuple-element.34, f32[32]{0:T(128)S(1)} %get-tuple-element.33, f32[32]{0:T(128)S(1)} %get-tuple-element.32), channel_id=1, replica_groups=mesh['enc'=16,'dp'=2,'tensor'=4] {'enc'}, use_global_device_ids=true, to_apply=%region_34.38 | all-reduce | flops 96 | bytes 768 | tf_op jit(solution)/shard_map/psum | solution.py:17
  278.0 0.7 copy-done.13
  278.7 0.2 fusion.27
  278.9 0.6 copy-done.9
  279.4 0.2 fusion.29
  279.6 0.6 copy-done.10
  280.2 0.2 fusion.31
  280.4 57.3 %all-reduce.21 = (bf16[32,512]{1,0:T(8,128)(2,1)S(1)}, bf16[32,512]{1,0:T(8,128)(2,1)S(1)}, bf16[32,512]{1,0:T(8,128)(2,1)S(1)}) all-reduce(f32[32,512]{1,0:T(8,128)S(1)} %fusion.31, f32[32,512]{1,0:T(8,128)S(1)} %fusion.29, f32[32,512]{1,0:T(8,128)S(1)} %fusion.27), channel_id=7, replica_groups=mesh['enc'=16,'dp'=2,'tensor'=4] {'enc'}, use_global_device_ids=true, to_apply=%region_35.39.clone | all-reduce | flops 49152 | bytes 294912
  337.8 0.1 fusion.6
  337.9 0.1 fusion.8
  338.1 0.1 fusion.10
  338.2 0.1 convert_reduce_fusion.4
  338.3 0.1 fusion.4
  338.5 16.3 %all-gather.1 = bf16[16,2,512]{2,1,0:T(2,128)(2,1)S(1)} all-gather(bf16[1,2,512]{2,1,0:T(2,128)(2,1)S(1)} %reshape.382), channel_id=1, replica_groups=mesh['enc'=16,'dp'=2,'tensor'=4] {'enc'}, dimensions={0}, use_global_device_ids=true | all-gather | bytes 34816 | tf_op jit(solution)/shard_map/all_gather | solution.py:134
  354.8 0.1 fusion.2
  355.0 17.4 %all-gather.3 = bf16[16,2,512]{2,1,0:T(2,128)(2,1)S(1)} all-gather(bf16[1,2,512]{2,1,0:T(2,128)(2,1)S(1)} %reshape.386), channel_id=1, replica_groups=mesh['enc'=16,'dp'=2,'tensor'=4] {'enc'}, dimensions={0}, use_global_device_ids=true | all-gather | bytes 34816 | tf_op jit(solution)/shard_map/all_gather | solution.py:134
  372.5 0.8 fusion.103
  373.2 0.8 fusion.106
  374.0 0.1 fusion
  374.2 15.7 %all-gather.5 = bf16[16,2,512]{2,1,0:T(2,128)(2,1)S(1)} all-gather(bf16[1,2,512]{2,1,0:T(2,128)(2,1)S(1)} %reshape.390), channel_id=1, replica_groups=mesh['enc'=16,'dp'=2,'tensor'=4] {'enc'}, dimensions={0}, use_global_device_ids=true | all-gather | bytes 34816 | tf_op jit(solution)/shard_map/all_gather | solution.py:134
  389.9 0.8 fusion.109
  390.7 71.3 %all-reduce.17.cloned.1.call-done = (f32[32,256]{1,0:T(8,128)}, f32[32,256]{1,0:T(8,128)}, f32[32,256]{1,0:T(8,128)}) async-done(((f32[32,256]{1,0:T(8,128)}, f32[32,256]{1,0:T(8,128)}, f32[32,256]{1,0:T(8,128)}), (f32[32,256]{1,0:T(8,128)}, f32[32,256]{1,0:T(8,128)}, f32[32,256]{1,0:T(8,128)})) %all-reduce.17.cloned.1.call-update) | async-done | bytes 98320 | tf_op jit(solution)/shard_map/psum | solution.py:43
  462.1 0.8 fusion.28
  462.9 0.6 pad_maximum_fusion
  (93 shorter events, 1.5 us)
Async XLA Ops:
  6.5 43.5 %copy-start = (bf16[256,3,512]{2,0,1:T(8,128)(2,1)S(1)}, bf16[256,3,512]{2,0,1:T(8,128)(2,1)}, u32[]{:S(2)}) copy-start(bf16[256,3,512]{2,0,1:T(8,128)(2,1)} %param.25) | copy-start | bytes 2359300
  6.6 0.7 copy-start.1
  7.8 0.9 copy-start.12
  10.2 5.0 %copy-start.7 = (bf16[3,32,256]{2,1,0:T(8,128)(2,1)S(1)}, bf16[3,32,256]{2,1,0:T(8,128)(2,1)}, u32[]{:S(2)}) copy-start(bf16[3,32,256]{2,1,0:T(8,128)(2,1)} %param.18) | copy-start | bytes 147460
  10.2 161.2 %all-to-all-start = ((bf16[2,24,2,512]{3,2,1,0:T(2,128)(2,1)}), bf16[2,24,2,512]{3,2,1,0:T(2,128)(2,1)S(1)}, u32[]{:S(2)}, u32[]{:S(2)}) async-start(bf16[2,24,2,512]{3,2,1,0:T(2,128)(2,1)} %broadcast_select_fusion.1), calls=%async_computation | async-start | bytes 196608 | tf_op jit(solution)/shard_map/all_to_all | solution.py:90
  15.2 228.5 %all-reduce.19.cloned.1.call-start = ((), (), s32[]{:S(2)}) async-start(), calls=%async_computation.2 | async-start | bytes 196608 | tf_op jit(solution)/shard_map/psum | solution.py:43
  50.0 0.7 copy-start.14
  51.6 0.7 copy-start.15
  115.8 0.8 copy-start.11
  116.9 0.7 copy-start.2
  118.2 34.1 %copy-start.4 = (bf16[512,256]{1,0:T(8,128)(2,1)S(1)}, bf16[512,256]{1,0:T(8,128)(2,1)}, u32[]{:S(2)}) copy-start(bf16[512,256]{1,0:T(8,128)(2,1)} %param.26) | copy-start | bytes 786436
  170.0 0.7 copy-start.3
  170.0 292.0 %all-reduce.17.cloned.1.call-start = ((), (), s32[]{:S(2)}) async-start(), calls=%async_computation.1 | async-start | bytes 196608 | tf_op jit(solution)/shard_map/psum | solution.py:43
  172.3 105.7 %copy-start.6 = (bf16[256,512]{1,0:T(8,128)(2,1)S(1)}, bf16[256,512]{1,0:T(8,128)(2,1)}, u32[]{:S(2)}) copy-start(bf16[256,512]{1,0:T(8,128)(2,1)} %param.28) | copy-start | bytes 786436
  243.7 34.4 %copy-start.8 = (f32[32,256]{1,0:T(8,128)S(1)}, f32[32,256]{1,0:T(8,128)}, u32[]{:S(2)}) copy-start(f32[32,256]{1,0:T(8,128)} %get-tuple-element.64) | copy-start | bytes 98308
  278.0 0.7 copy-start.13
  278.7 0.8 copy-start.9
  279.4 0.8 copy-start.10
  337.9 34.6 %copy-start.5 = (bf16[512,256]{1,0:T(8,128)(2,1)S(1)}, bf16[512,256]{1,0:T(8,128)(2,1)}, u32[]{:S(2)}) copy-start(bf16[512,256]{1,0:T(8,128)(2,1)} %param.29) | copy-start | bytes 786436
Sparse Core Ops, SparseCore 0:
  170.2 73.4 all-reduce.18
  390.8 71.1 all-reduce.16
where the time goes:
time: 471 us; the launch traced here: 470 us
  blocking collectives  286 us (61%)
  waiting for transfers between devices  142 us (30%)
  between operations  14.4 us (3%)
  local copies, waits for them, and re-layouts  10.8 us (2%)
  matrix products  7.41 us (2%)
  starting transfers between devices  5 us (1%)
  other arithmetic  4.79 us (1%)
    psum x2, waiting for transfers between devices, combine_heads(): return lax.psum(partial_out, 'tensor')  142 us
    unnamed x2, blocking collectives  120 us
    all_gather x6, blocking collectives, on_device(): context_all = lax.all_gather(context, 'enc', axis=0, tiled=True)  98 us
    psum x2, blocking collectives, row_norm(): squares = lax.psum(jnp.sum(rows_in * rows_in, axis=1), 'enc')  68.1 us
  transfers between devices with their start and end apart: 3, of which 2 were waited for; matrix products, arithmetic and copies ran while one was open for 2% of the time, Pallas kernels for 0%

commit v1 on v0

v1 whole, which is shorter than its diff:
```python
import math

import jax
import jax.numpy as jnp
from jax import lax
from jax.sharding import PartitionSpec as P

D = 4096
DK = 256


EPSILON = 1e-06
LANE = 128


def score_weight(scores):
    return jnp.exp(scores).astype(jnp.bfloat16)


def rows_reduce_scatter(partial, owned):
    n_enc = lax.axis_size("enc")
    steps, rows, cols = partial.shape
    send = partial.reshape(steps, n_enc, owned, cols).transpose(1, 0, 2, 3)
    got = lax.all_to_all(send, "enc", 0, 0, tiled=True)
    return jnp.sum(got, axis=0)


def rows_gather(chunk):
    n_enc = lax.axis_size("enc")
    steps, owned, width = chunk.shape
    send = jnp.broadcast_to(chunk[None], (n_enc, steps, owned, width))
    got = lax.all_to_all(send, "enc", 0, 0, tiled=True)
    return got.transpose(1, 0, 2, 3).reshape(steps, n_enc * owned, width)


def tensor_sum(value):
    n_t = lax.axis_size("tensor")
    bit = 1
    while bit < n_t:
        other = lax.ppermute(value, "tensor", [(i, i ^ bit) for i in range(n_t)])
        value = value + other
        bit *= 2
    return value


def with_sumsq(partial, rows_in):
    squares = jnp.sum(rows_in * rows_in, axis=-1, keepdims=True)
    pad = jnp.zeros(rows_in.shape[:-1] + (LANE - 1,), jnp.float32)
    return jnp.concatenate([partial, squares, pad], axis=-1)


def split_norm(packed, width):
    scale = lax.rsqrt(packed[..., width] / D + EPSILON)
    return (packed[..., :width] * scale[..., None]).astype(jnp.bfloat16)


def on_device(
    hidden_in,
    self_cache,
    src_pool,
    assign,
    src_len,
    positions,
    gain_self,
    w_qkv,
    w_out_self,
    gain_cross,
    w_q_cross,
    w_out_cross,
):
    dp_count = lax.axis_size("dp")
    enc_count = lax.axis_size("enc")
    seq_dev = self_cache.shape[0]
    per_pair = seq_dev // dp_count
    cache_len = self_cache.shape[1]
    source_len = src_pool.shape[1]
    width = self_cache.shape[3]
    head_count = width // DK
    steps = hidden_in.shape[0]
    enc_at = lax.axis_index("enc")
    dp_at = lax.axis_index("dp")
    block_at = dp_at * enc_count + enc_at
    slot_index = jnp.arange(seq_dev, dtype=jnp.int32)
    my_slots = block_at * seq_dev + slot_index
    my_positions = jnp.take(positions, my_slots)
    my_sources = jnp.take(assign, my_slots)
    place_at = jnp.arange(cache_len, dtype=jnp.int32)
    cache_usable = place_at[None, :] < my_positions[:, None]
    token_at = jnp.arange(source_len, dtype=jnp.int32)
    assign_view = assign.reshape(dp_count, enc_count, seq_dev)
    assign_grid = jnp.take(assign_view, enc_at, axis=1)
    owners = assign_grid // (seq_dev * enc_count)
    earlier = (owners[:, None, :] == owners[:, :, None]) & (
        slot_index[None, None, :] < slot_index[None, :, None]
    )
    slot_rank = jnp.sum(earlier.astype(jnp.int32), axis=2)
    recv_rows = jnp.take(owners, dp_at, axis=0) * per_pair + jnp.take(slot_rank, dp_at, axis=0)
    picked = (owners == dp_at)[:, :, None] & (
        slot_rank[:, :, None] == jnp.arange(per_pair, dtype=jnp.int32)[None, None, :]
    )
    chosen = jnp.sum(jnp.where(picked, (assign_grid % seq_dev)[:, :, None], 0), axis=1)
    chosen_flat = chosen.reshape(-1)
    outgoing = jnp.take(src_pool, chosen_flat, axis=0)
    arrived = lax.all_to_all(outgoing, "dp", split_axis=0, concat_axis=0, tiled=True)
    cross_kv = jnp.take(arrived, recv_rows, axis=0)
    cross_usable = token_at[None, :] < jnp.take(src_len, my_sources)[:, None]

    current = hidden_in.astype(jnp.float32)
    scaled = (current * gain_self[None, None, :]).astype(jnp.bfloat16)
    proj = jnp.einsum("tsd,dcw->tscw", scaled, w_qkv, preferred_element_type=jnp.float32)
    proj = proj.reshape(steps, current.shape[1], 3 * width)
    own = rows_reduce_scatter(with_sumsq(proj, current), seq_dev)
    qkv = split_norm(own, 3 * width).reshape(steps, seq_dev, 3, head_count, DK)
    query = qkv[:, :, 0]
    key_new = qkv[:, :, 1]
    value_new = qkv[:, :, 2]

    inv = 1.0 / math.sqrt(DK)
    cache_keys = self_cache[:, :, 0].reshape(seq_dev, cache_len, head_count, DK)
    cache_values = self_cache[:, :, 1].reshape(seq_dev, cache_len, head_count, DK)
    s_cache = jnp.einsum(
        "tnhd,nlhd->tnhl", query, cache_keys, preferred_element_type=jnp.float32
    ) * inv
    w_cache = jnp.where(
        cache_usable[None, :, None, :], score_weight(s_cache), jnp.zeros((), jnp.bfloat16)
    )
    s_new = jnp.einsum(
        "tnhd,unhd->tnhu", query, key_new, preferred_element_type=jnp.float32
    ) * inv
    step_at = jnp.arange(steps, dtype=jnp.int32)
    new_usable = step_at[None, :] <= step_at[:, None]
    w_new = jnp.where(
        new_usable[:, None, None, :], score_weight(s_new), jnp.zeros((), jnp.bfloat16)
    )
    weighted = jnp.einsum(
        "tnhl,nlhd->tnhd", w_cache, cache_values, preferred_element_type=jnp.float32
    ) + jnp.einsum("tnhu,unhd->tnhd", w_new, value_new, preferred_element_type=jnp.float32)
    totals = jnp.sum(w_cache.astype(jnp.float32), axis=-1) + jnp.sum(
        w_new.astype(jnp.float32), axis=-1
    )
    context = (weighted / totals[..., None]).reshape(steps, seq_dev, width).astype(jnp.bfloat16)
    context_all = rows_gather(context)
    residual = current + tensor_sum(
        jnp.einsum("tsw,wf->tsf", context_all, w_out_self, preferred_element_type=jnp.float32)
    )

    scaled = (residual * gain_cross[None, None, :]).astype(jnp.bfloat16)
    cq = jnp.einsum("tsd,dw->tsw", scaled, w_q_cross, preferred_element_type=jnp.float32)
    own = rows_reduce_scatter(with_sumsq(cq, residual), seq_dev)
    cross_query = split_norm(own, width).reshape(steps, seq_dev, head_count, DK)
    cross_keys = cross_kv[:, :, 0].reshape(seq_dev, source_len, head_count, DK)
    cross_values = cross_kv[:, :, 1].reshape(seq_dev, source_len, head_count, DK)
    s_cross = jnp.einsum(
        "tnhd,nlhd->tnhl", cross_query, cross_keys, preferred_element_type=jnp.float32
    ) * inv
    w_cross = jnp.where(
        cross_usable[None, :, None, :], score_weight(s_cross), jnp.zeros((), jnp.bfloat16)
    )
    weighted = jnp.einsum(
        "tnhl,nlhd->tnhd", w_cross, cross_values, preferred_element_type=jnp.float32
    )
    totals = jnp.sum(w_cross.astype(jnp.float32), axis=-1)
    context = (weighted / totals[..., None]).reshape(steps, seq_dev, width).astype(jnp.bfloat16)
    context_all = rows_gather(context)
    output_rows = residual + tensor_sum(
        jnp.einsum("tsw,wf->tsf", context_all, w_out_cross, preferred_element_type=jnp.float32)
    )
    return output_rows.astype(jnp.bfloat16)


def solution(mesh):
    in_specs = (
        P(None, "dp", "enc"),
        P(("dp", "enc"), None, None, "tensor"),
        P(("dp", "enc"), None, None, "tensor"),
        P(),
        P(),
        P(),
        P("enc"),
        P("enc", None, "tensor"),
        P("tensor", "enc"),
        P("enc"),
        P("enc", "tensor"),
        P("tensor", "enc"),
    )
    out_specs = P(None, "dp", "enc")
    return jax.shard_map(
        on_device, mesh=mesh, in_specs=in_specs, out_specs=out_specs, check_vma=False
    )
```

time: 471 us -> 84 us (0.18)
  blocking collectives: 286 us -> 9.65 us
  waiting for transfers between devices: 142 us -> 28.5 us
  starting transfers between devices: 5 us -> 27.5 us
  between operations: 14.4 us -> 0.44 us
  matrix products: 7.41 us -> 1.76 us
    psum x2 -> x0, waiting for transfers between devices: 142 us -> none  [combine_heads(): return lax.psum(partial_out, 'tensor')]
    unnamed x2 -> x0, blocking collectives: 120 us -> none
    all_gather x6 -> x0, blocking collectives: 98 us -> none  [on_device(): context_all = lax.all_gather(context, 'enc', axis=0, tiled=True)]
    psum x2 -> x0, blocking collectives: 68.1 us -> none  [row_norm(): squares = lax.psum(jnp.sum(rows_in * rows_in, axis=1), 'enc')]
    all_to_all x0 -> x3, waiting for transfers between devices: none -> 20.1 us  [the longest x2 13.5 us: rows_reduce_scatter(): got = lax.all_to_all(send, 'enc', 0, 0, tiled=True)]
    all_to_all x0 -> x3, starting transfers between devices: none -> 15.9 us  [the longest x2 12.1 us: rows_reduce_scatter(): got = lax.all_to_all(send, 'enc', 0, 0, tiled=True)]
    all_to_all x0 -> x1, blocking collectives: none -> 9.65 us  [rows_gather(): got = lax.all_to_all(send, 'enc', 0, 0, tiled=True)]
    ppermute x0 -> x4, waiting for transfers between devices: none -> 8.4 us  [tensor_sum(): other = lax.ppermute(value, 'tensor', [(i, i ^ bit) for i in range(n_t)])]
  transfers between devices with their start and end apart: 3 -> 8, of which waited for: 2 -> 7; matrix products, arithmetic and copies ran while one was open for 2% -> 7% of each run, Pallas kernels for 0% -> 0%
where the time goes in v1:
time: 84 us; the launch traced here: 83.1 us
  waiting for transfers between devices  28.5 us (34%)
  starting transfers between devices  27.5 us (33%)
  local copies, waits for them, and re-layouts  10.7 us (13%)
  blocking collectives  9.65 us (11%)
  other arithmetic  4.52 us (5%)
  matrix products  1.76 us (2%)
    all_to_all x2, waiting for transfers between devices, rows_reduce_scatter(): got = lax.all_to_all(send, 'enc', 0, 0, tiled=True)  13.5 us
    all_to_all x2, starting transfers between devices, rows_reduce_scatter(): got = lax.all_to_all(send, 'enc', 0, 0, tiled=True)  12.1 us
    all_to_all x1, blocking collectives, rows_gather(): got = lax.all_to_all(send, 'enc', 0, 0, tiled=True)  9.65 us
    ppermute x4, waiting for transfers between devices, tensor_sum(): other = lax.ppermute(value, 'tensor', [(i, i ^ bit) for i in range(n_t)])  8.4 us
    ppermute x4, starting transfers between devices, tensor_sum(): other = lax.ppermute(value, 'tensor', [(i, i ^ bit) for i in range(n_t)])  7.56 us
    all_to_all x1, waiting for transfers between devices, rows_gather(): got = lax.all_to_all(send, 'enc', 0, 0, tiled=True)  6.59 us
    all_to_all x1, starting transfers between devices, on_device(): lax.all_to_all(outgoing, 'dp', split_axis=0, concat_axis=0, tiled=True)  4.01 us
    all_to_all x1, starting transfers between devices, rows_gather(): got = lax.all_to_all(send, 'enc', 0, 0, tiled=True)  3.83 us
  transfers between devices with their start and end apart: 8, of which 7 were waited for; matrix products, arithmetic and copies ran while one was open for 7% of the time, Pallas kernels for 0%

profile of v1, /device:TPU:1, one launch (start us, length us, event | category | flops | bytes accessed | tf_op | source)
XLA Modules:
  0.0 83.1 jit_solution(625706802652295526)
XLA Ops:
  0.0 1.0 %fusion.26 = f32[3,32]{1,0:T(4,128)S(1)} fusion(bf16[3,32,256]{2,1,0:T(8,128)(2,1)} %param.18), kind=kLoop, calls=%fused_computation.43 | loop fusion | flops 73632 | bytes 49536 | tf_op jit(solution)/shard_map/reduce_sum | solution.py:47
  1.0 0.2 copy-done
  1.2 0.3 fusion.17
  1.4 0.4 copy.82
  1.8 0.6 concatenate.18
  2.5 0.1 concatenate.27
  2.6 0.8 concatenate.21
  3.5 0.9 %copy.84 = f32[16,3,2,1664]{3,2,1,0:T(2,128)} copy(f32[16,3,2,1664]{3,2,0,1:T(2,128)S(1)} %bitcast.100) | data formatting | bytes 1277952 | tf_op jit(solution)/shard_map/transpose | solution.py:23
  4.4 8.6 %all-to-all-start = ((f32[16,3,2,1664]{3,2,1,0:T(2,128)}), f32[16,3,2,1664]{3,2,1,0:T(2,128)S(1)}, u32[]{:S(2)}, u32[]{:S(2)}) async-start(f32[16,3,2,1664]{3,2,1,0:T(2,128)} %copy.84), calls=%async_computation | async-start | bytes 1277952 | tf_op jit(solution)/shard_map/all_to_all | solution.py:24
  13.0 0.6 copy-done.1
  13.6 0.1 reshape.169
  13.8 0.6 gather_fusion.3
  14.4 0.6 gather_fusion
  15.2 0.2 fusion.38
  15.4 0.1 fusion.39
  15.6 0.7 gather_fusion.1
  16.4 0.6 gather_fusion.4
  17.0 0.1 copy-done.8
  17.1 0.1 slice_reduce_fusion.2
  17.3 0.8 broadcast_select_fusion.1
  18.1 6.5 %all-to-all-done = f32[16,3,2,1664]{3,2,1,0:T(2,128)S(1)} async-done(((f32[16,3,2,1664]{3,2,1,0:T(2,128)}), f32[16,3,2,1664]{3,2,1,0:T(2,128)S(1)}, u32[]{:S(2)}, u32[]{:S(2)}) %all-to-all-start) | async-done | bytes 639008 | tf_op jit(solution)/shard_map/all_to_all | solution.py:24
  24.6 0.2 reduce_sum.82
  24.8 0.1 copy.111
  24.9 0.1 copy.87
  25.0 0.1 fusion.35
  25.1 0.2 convert_reduce_fusion.2
  25.4 0.1 convert_reduce_fusion.1
  25.5 0.1 convolution_bitcast_fusion.2
  25.6 0.2 fusion.3
  25.9 0.7 broadcast_in_dim.72
  26.5 3.8 %all-to-all-start.1 = ((bf16[16,3,2,512]{3,2,1,0:T(2,128)(2,1)}), bf16[16,3,2,512]{3,2,1,0:T(2,128)(2,1)S(1)}, u32[]{:S(2)}, u32[]{:S(2)}) async-start(bf16[16,3,2,512]{3,2,1,0:T(2,128)(2,1)} %broadcast_in_dim.72), calls=%async_computation.1 | async-start | bytes 196608 | tf_op jit(solution)/shard_map/all_to_all | solution.py:32
  30.5 6.6 %all-to-all-done.1 = bf16[16,3,2,512]{3,2,1,0:T(2,128)(2,1)S(1)} async-done(((bf16[16,3,2,512]{3,2,1,0:T(2,128)(2,1)}), bf16[16,3,2,512]{3,2,1,0:T(2,128)(2,1)S(1)}, u32[]{:S(2)}, u32[]{:S(2)}) %all-to-all-start.1) | async-done | bytes 98336 | tf_op jit(solution)/shard_map/all_to_all | solution.py:32
  37.0 4.0 %all-to-all-start.2 = ((bf16[2,24,2,512]{3,2,1,0:T(2,128)(2,1)}), bf16[2,24,2,512]{3,2,1,0:T(2,128)(2,1)S(1)}, u32[]{:S(2)}, u32[]{:S(2)}) async-start(bf16[2,24,2,512]{3,2,1,0:T(2,128)(2,1)} %broadcast_select_fusion.1), calls=%async_computation.2 | async-start | bytes 196608 | tf_op jit(solution)/shard_map/all_to_all | solution.py:104
  41.2 0.2 fusion.23
  41.4 3.2 %collective-permute-start = (f32[3,32,256]{2,1,0:T(8,128)S(1)}, f32[3,32,256]{2,1,0:T(8,128)S(1)}, u32[]{:S(2)}, u32[]{:S(2)}) collective-permute-start(f32[3,32,256]{2,1,0:T(8,128)S(1)} %fusion.23), channel_id=1, source_target_pairs={{0,1},{1,0},{2,3},{3,2},{4,5},{5,4},{6,7},{7,6},{8,9},{9,8},{10,11... | collective-permute-start | bytes 294920 | tf_op jit(solution)/shard_map/ppermute | solution.py:40
  44.6 0.9 %collective-permute-done = f32[3,32,256]{2,1,0:T(8,128)S(1)} collective-permute-done((f32[3,32,256]{2,1,0:T(8,128)S(1)}, f32[3,32,256]{2,1,0:T(8,128)S(1)}, u32[]{:S(2)}, u32[]{:S(2)}) %collective-permute-start) | collective-permute-done | bytes 98336 | tf_op jit(solution)/shard_map/ppermute | solution.py:40
  45.5 0.4 collective-permute-start.1
  45.9 0.1 pad.6.clone
  46.0 0.7 gather_fusion.2
  46.8 2.8 %collective-permute-done.1 = f32[3,32,256]{2,1,0:T(8,128)S(1)} collective-permute-done((f32[3,32,256]{2,1,0:T(8,128)S(1)}, f32[3,32,256]{2,1,0:T(8,128)S(1)}, u32[]{:S(2)}, u32[]{:S(2)}) %collective-permute-start.1) | collective-permute-done | bytes 98336 | tf_op jit(solution)/shard_map/ppermute | solution.py:40
  49.6 0.1 multiply_reduce_fusion
  49.7 0.7 copy-done.11
  50.4 0.2 fusion.21
  50.6 0.1 concatenate.22
  50.7 0.1 concatenate.23
  50.8 0.4 copy.97
  51.2 0.8 maximum_bitcast_fusion
  52.0 3.5 %all-to-all-start.3 = ((f32[16,3,2,640]{3,2,1,0:T(2,128)}), f32[16,3,2,640]{3,2,1,0:T(2,128)S(1)}, u32[]{:S(2)}, u32[]{:S(2)}) async-start(f32[16,3,2,640]{3,2,1,0:T(2,128)} %maximum_bitcast_fusion), calls=%async_computation.3 | async-start | bytes 491520 | tf_op jit(solution)/shard_map/all_to_all | solution.py:24
  55.5 0.2 broadcast_select_fusion
  55.7 0.4 slice_reduce_fusion.1
  56.1 6.9 %all-to-all-done.3 = f32[16,3,2,640]{3,2,1,0:T(2,128)S(1)} async-done(((f32[16,3,2,640]{3,2,1,0:T(2,128)}), f32[16,3,2,640]{3,2,1,0:T(2,128)S(1)}, u32[]{:S(2)}, u32[]{:S(2)}) %all-to-all-start.3) | async-done | bytes 245792 | tf_op jit(solution)/shard_map/all_to_all | solution.py:24
  63.0 0.1 reduce_sum.88
  63.1 0.1 copy.115
  63.2 0.1 copy.101
  63.3 0.1 fusion.36
  63.4 0.2 convert_reduce_fusion
  63.7 0.1 fusion.4
  63.9 9.6 %all_to_all.25 = bf16[16,3,2,512]{3,2,1,0:T(2,128)(2,1)S(1)} all-to-all(bf16[16,3,2,512]{3,2,1,0:T(2,128)(2,1)S(1)} %broadcast_in_dim.109), channel_id=1, replica_groups=mesh['enc'=16,'dp'=2,'tensor'=4] {'enc'}, dimensions={0} | all-to-all | bytes 196608 | tf_op jit(solution)/shard_map/all_to_all | solution.py:32
  73.7 0.2 fusion.19
  73.9 3.6 %collective-permute-start.2 = (f32[3,32,256]{2,1,0:T(8,128)S(1)}, f32[3,32,256]{2,1,0:T(8,128)S(1)}, u32[]{:S(2)}, u32[]{:S(2)}) collective-permute-start(f32[3,32,256]{2,1,0:T(8,128)S(1)} %fusion.19), channel_id=1, source_target_pairs={{0,1},{1,0},{2,3},{3,2},{4,5},{5,4},{6,7},{7,6},{8,9},{9,8},{10,11... | collective-permute-start | bytes 294920 | tf_op jit(solution)/shard_map/ppermute | solution.py:40
  77.4 0.9 %collective-permute-done.2 = f32[3,32,256]{2,1,0:T(8,128)S(1)} collective-permute-done((f32[3,32,256]{2,1,0:T(8,128)S(1)}, f32[3,32,256]{2,1,0:T(8,128)S(1)}, u32[]{:S(2)}, u32[]{:S(2)}) %collective-permute-start.2) | collective-permute-done | bytes 98336 | tf_op jit(solution)/shard_map/ppermute | solution.py:40
  78.4 0.4 collective-permute-start.3
  78.8 3.7 %collective-permute-done.3 = f32[3,32,256]{2,1,0:T(8,128)S(1)} collective-permute-done((f32[3,32,256]{2,1,0:T(8,128)S(1)}, f32[3,32,256]{2,1,0:T(8,128)S(1)}, u32[]{:S(2)}, u32[]{:S(2)}) %collective-permute-start.3) | collective-permute-done | bytes 98336 | tf_op jit(solution)/shard_map/ppermute | solution.py:40
  82.5 0.6 add_convert_fusion
  (58 shorter events, 0.8 us)
Async XLA Ops:
  0.0 1.2 %copy-start = (bf16[256,3,512]{2,0,1:T(8,128)(2,1)S(1)}, bf16[256,3,512]{2,0,1:T(8,128)(2,1)}, u32[]{:S(2)}) copy-start(bf16[256,3,512]{2,0,1:T(8,128)(2,1)} %param.25) | copy-start | bytes 2359300
  0.0 1.2 %copy-start.4 = (bf16[3,32,256]{2,1,0:T(8,128)(2,1)S(1)}, bf16[3,32,256]{2,1,0:T(8,128)(2,1)}, u32[]{:S(2)}) copy-start(bf16[3,32,256]{2,1,0:T(8,128)(2,1)} %param.18) | copy-start | bytes 147460
  0.0 1.2 %copy-start.10 = (f32[256]{0:T(256)S(1)}, f32[256]{0:T(256)}, u32[]{:S(2)}) copy-start(f32[256]{0:T(256)} %param.24) | copy-start | bytes 3076
  4.4 20.2 %all-to-all-start = ((f32[16,3,2,1664]{3,2,1,0:T(2,128)}), f32[16,3,2,1664]{3,2,1,0:T(2,128)S(1)}, u32[]{:S(2)}, u32[]{:S(2)}) async-start(f32[16,3,2,1664]{3,2,1,0:T(2,128)} %copy.84), calls=%async_computation | async-start | bytes 1277952 | tf_op jit(solution)/shard_map/all_to_all | solution.py:24
  13.0 0.7 copy-start.1
  13.7 0.7 copy-start.2
  14.4 1.2 %copy-start.9 = (bf16[2,24,2,512]{3,2,1,0:T(2,128)(2,1)S(1)}, bf16[2,24,2,512]{3,2,1,0:T(2,128)(2,1)}, u32[]{:S(2)}) copy-start(bf16[2,24,2,512]{3,2,1,0:T(2,128)(2,1)} %param.20) | copy-start | bytes 294916
  15.6 0.8 copy-start.3
  16.4 0.8 copy-start.8
  26.5 10.5 %all-to-all-start.1 = ((bf16[16,3,2,512]{3,2,1,0:T(2,128)(2,1)}), bf16[16,3,2,512]{3,2,1,0:T(2,128)(2,1)S(1)}, u32[]{:S(2)}, u32[]{:S(2)}) async-start(bf16[16,3,2,512]{3,2,1,0:T(2,128)(2,1)} %broadcast_in_dim.72), calls=%async_computation.1 | async-start | bytes 196608 | tf_op jit(solution)/shard_map/all_to_all | solution.py:32
  30.5 10.7 %copy-start.5 = (bf16[512,256]{1,0:T(8,128)(2,1)S(1)}, bf16[512,256]{1,0:T(8,128)(2,1)}, u32[]{:S(2)}) copy-start(bf16[512,256]{1,0:T(8,128)(2,1)} %param.26) | copy-start | bytes 786436
  37.0 9.0 %all-to-all-start.2 = ((bf16[2,24,2,512]{3,2,1,0:T(2,128)(2,1)}), bf16[2,24,2,512]{3,2,1,0:T(2,128)(2,1)S(1)}, u32[]{:S(2)}, u32[]{:S(2)}) async-start(bf16[2,24,2,512]{3,2,1,0:T(2,128)(2,1)} %broadcast_select_fusion.1), calls=%async_computation.2 | async-start | bytes 196608 | tf_op jit(solution)/shard_map/all_to_all | solution.py:104
  41.4 4.2 %collective-permute-start = (f32[3,32,256]{2,1,0:T(8,128)S(1)}, f32[3,32,256]{2,1,0:T(8,128)S(1)}, u32[]{:S(2)}, u32[]{:S(2)}) collective-permute-start(f32[3,32,256]{2,1,0:T(8,128)S(1)} %fusion.23), channel_id=1, source_target_pairs={{0,1},{1,0},{2,3},{3,2},{4,5},{5,4},{6,7},{7,6},{8,9},{9,8},{10,11... | collective-permute-start | bytes 294920 | tf_op jit(solution)/shard_map/ppermute | solution.py:40
  45.5 4.1 %collective-permute-start.1 = (f32[3,32,256]{2,1,0:T(8,128)S(1)}, f32[3,32,256]{2,1,0:T(8,128)S(1)}, u32[]{:S(2)}, u32[]{:S(2)}) collective-permute-start(f32[3,32,256]{2,1,0:T(8,128)S(1)} %add.86), channel_id=1, source_target_pairs={{0,2},{1,3},{2,0},{3,1},{4,6},{5,7},{6,4},{7,5},{8,10},{9,11},{10,... | collective-permute-start | bytes 294920 | tf_op jit(solution)/shard_map/ppermute | solution.py:40
  46.0 3.7 %copy-start.7 = (bf16[256,512]{1,0:T(8,128)(2,1)S(1)}, bf16[256,512]{1,0:T(8,128)(2,1)}, u32[]{:S(2)}) copy-start(bf16[256,512]{1,0:T(8,128)(2,1)} %param.28) | copy-start | bytes 786436
  49.7 0.7 copy-start.11
  52.0 11.1 %all-to-all-start.3 = ((f32[16,3,2,640]{3,2,1,0:T(2,128)}), f32[16,3,2,640]{3,2,1,0:T(2,128)S(1)}, u32[]{:S(2)}, u32[]{:S(2)}) async-start(f32[16,3,2,640]{3,2,1,0:T(2,128)} %maximum_bitcast_fusion), calls=%async_computation.3 | async-start | bytes 491520 | tf_op jit(solution)/shard_map/all_to_all | solution.py:24
  63.9 9.8 %copy-start.6 = (bf16[512,256]{1,0:T(8,128)(2,1)S(1)}, bf16[512,256]{1,0:T(8,128)(2,1)}, u32[]{:S(2)}) copy-start(bf16[512,256]{1,0:T(8,128)(2,1)} %param.29) | copy-start | bytes 786436
  73.9 4.5 %collective-permute-start.2 = (f32[3,32,256]{2,1,0:T(8,128)S(1)}, f32[3,32,256]{2,1,0:T(8,128)S(1)}, u32[]{:S(2)}, u32[]{:S(2)}) collective-permute-start(f32[3,32,256]{2,1,0:T(8,128)S(1)} %fusion.19), channel_id=1, source_target_pairs={{0,1},{1,0},{2,3},{3,2},{4,5},{5,4},{6,7},{7,6},{8,9},{9,8},{10,11... | collective-permute-start | bytes 294920 | tf_op jit(solution)/shard_map/ppermute | solution.py:40
  78.4 4.1 %collective-permute-start.3 = (f32[3,32,256]{2,1,0:T(8,128)S(1)}, f32[3,32,256]{2,1,0:T(8,128)S(1)}, u32[]{:S(2)}, u32[]{:S(2)}) collective-permute-start(f32[3,32,256]{2,1,0:T(8,128)S(1)} %add.93), channel_id=1, source_target_pairs={{0,2},{1,3},{2,0},{3,1},{4,6},{5,7},{6,4},{7,5},{8,10},{9,11},{10,... | collective-permute-start | bytes 294920 | tf_op jit(solution)/shard_map/ppermute | solution.py:40

commit v2 on v1

--- a/solution.py
+++ b/solution.py
@@ -15,14 +15,6 @@
 
 def score_weight(scores):
     return jnp.exp(scores).astype(jnp.bfloat16)
-
-
-def rows_reduce_scatter(partial, owned):
-    n_enc = lax.axis_size("enc")
-    steps, rows, cols = partial.shape
-    send = partial.reshape(steps, n_enc, owned, cols).transpose(1, 0, 2, 3)
-    got = lax.all_to_all(send, "enc", 0, 0, tiled=True)
-    return jnp.sum(got, axis=0)
 
 
 def rows_gather(chunk):
@@ -45,12 +37,23 @@
 
 def with_sumsq(partial, rows_in):
     squares = jnp.sum(rows_in * rows_in, axis=-1, keepdims=True)
-    pad = jnp.zeros(rows_in.shape[:-1] + (LANE - 1,), jnp.float32)
-    return jnp.concatenate([partial, squares, pad], axis=-1)
+    high = squares.astype(jnp.bfloat16)
+    low = (squares - high.astype(jnp.float32)).astype(jnp.bfloat16)
+    pad = jnp.zeros(rows_in.shape[:-1] + (LANE - 2,), jnp.bfloat16)
+    return jnp.concatenate([partial.astype(jnp.bfloat16), high, low, pad], axis=-1)
+
+
+def rows_reduce_scatter(partial, owned):
+    n_enc = lax.axis_size("enc")
+    steps, rows, cols = partial.shape
+    send = partial.reshape(steps, n_enc, owned, cols).transpose(1, 0, 2, 3)
+    got = lax.all_to_all(send, "enc", 0, 0, tiled=True)
+    return jnp.sum(got.astype(jnp.float32), axis=0)
 
 
 def split_norm(packed, width):
-    scale = lax.rsqrt(packed[..., width] / D + EPSILON)
+    squares = packed[..., width] + packed[..., width + 1]
+    scale = lax.rsqrt(squares / D + EPSILON)
     return (packed[..., :width] * scale[..., None]).astype(jnp.bfloat16)
 
 
@@ -100,8 +103,24 @@
     )
     chosen = jnp.sum(jnp.where(picked, (assign_grid % seq_dev)[:, :, None], 0), axis=1)
     chosen_flat = chosen.reshape(-1)
-    outgoing = jnp.take(src_pool, chosen_flat, axis=0)
-    arrived = lax.all_to_all(outgoing, "dp", split_axis=0, concat_axis=0, tiled=True)
+    outgoing = jnp.take(src_pool, chosen_flat, axis=0).reshape(
+        (dp_count, per_pair) + src_pool.shape[1:]
+    )
+    pieces = []
+    for shift in range(dp_count):
+        if shift == 0:
+            pieces.append(jnp.take(outgoing, dp_at, axis=0))
+        else:
+            sent = jnp.take(outgoing, (dp_at + shift) % dp_count, axis=0)
+            pieces.append(
+                lax.ppermute(
+                    sent, "dp", [(i, (i + shift) % dp_count) for i in range(dp_count)]
+                )
+            )
+    stacked = jnp.stack(pieces)
+    sender_at = (dp_at - jnp.arange(dp_count, dtype=jnp.int32)) % dp_count
+    order = jnp.argsort(sender_at)
+    arrived = jnp.take(stacked, order, axis=0).reshape((seq_dev,) + src_pool.shape[1:])
     cross_kv = jnp.take(arrived, recv_rows, axis=0)
     cross_usable = token_at[None, :] < jnp.take(src_len, my_sources)[:, None]
 

time: 84 us -> 79.7 us (0.949)
  waiting for transfers between devices: 28.5 us -> 20.3 us
  local copies, waits for them, and re-layouts: 10.7 us -> 12.6 us
  starting transfers between devices: 27.5 us -> 29.1 us
    all_to_all x2, waiting for transfers between devices: 13.5 us -> 6.35 us  [rows_reduce_scatter(): got = lax.all_to_all(send, 'enc', 0, 0, tiled=True)]
    all_to_all x1 -> x0, starting transfers between devices: 4.01 us -> none  [on_device(): lax.all_to_all(outgoing, 'dp', split_axis=0, concat_axis=0, tiled=True)]
    ppermute x0 -> x1, starting transfers between devices: none -> 2.82 us  [on_device(): lax.ppermute(sent, 'dp', [(i, (i + shift) % dp_count) for i in range(dp_c...]
    all_to_all x1, starting transfers between devices: 3.83 us -> 6.63 us  [rows_gather(): got = lax.all_to_all(send, 'enc', 0, 0, tiled=True)]
    concatenate x9 -> x5, local copies, waits for them, and re-layouts: 2.28 us -> 0.99 us  [with_sumsq(): jnp.concatenate([partial.astype(jnp.bfloat16), high, low, pad], axis=-1)]
    unnamed x26 -> x28, local copies, waits for them, and re-layouts: 1.85 us -> 3.06 us
    convert_element_type x0 -> x6, local copies, waits for them, and re-layouts: none -> 1.03 us  [the longest x2 0.51 us: with_sumsq(): partial.astype(jnp.bfloat16)]
    all_to_all x1, waiting for transfers between devices: 6.59 us -> 5.74 us  [rows_gather(): got = lax.all_to_all(send, 'enc', 0, 0, tiled=True)]
  transfers between devices with their start and end apart: 8 -> 8, of which waited for: 7 -> 5; matrix products, arithmetic and copies ran while one was open for 7% -> 11% of each run, Pallas kernels for 0% -> 0%
where the time goes in v2:
time: 79.7 us; the launch traced here: 79.1 us
  starting transfers between devices  29.1 us (37%)
  waiting for transfers between devices  20.3 us (25%)
  local copies, waits for them, and re-layouts  12.6 us (16%)
  blocking collectives  9.91 us (12%)
  other arithmetic  5.02 us (6%)
  matrix products  1.77 us (2%)
    all_to_all x2, starting transfers between devices, rows_reduce_scatter(): got = lax.all_to_all(send, 'enc', 0, 0, tiled=True)  12.2 us
    all_to_all x1, blocking collectives, rows_gather(): got = lax.all_to_all(send, 'enc', 0, 0, tiled=True)  9.91 us
    ppermute x4, waiting for transfers between devices, tensor_sum(): other = lax.ppermute(value, 'tensor', [(i, i ^ bit) for i in range(n_t)])  8.18 us
    ppermute x4, starting transfers between devices, tensor_sum(): other = lax.ppermute(value, 'tensor', [(i, i ^ bit) for i in range(n_t)])  7.37 us
    all_to_all x1, starting transfers between devices, rows_gather(): got = lax.all_to_all(send, 'enc', 0, 0, tiled=True)  6.63 us
    all_to_all x2, waiting for transfers between devices, rows_reduce_scatter(): got = lax.all_to_all(send, 'enc', 0, 0, tiled=True)  6.35 us
    all_to_all x1, waiting for transfers between devices, rows_gather(): got = lax.all_to_all(send, 'enc', 0, 0, tiled=True)  5.74 us
    unnamed x28, local copies, waits for them, and re-layouts  3.06 us
  transfers between devices with their start and end apart: 8, of which 5 were waited for; matrix products, arithmetic and copies ran while one was open for 11% of the time, Pallas kernels for 0%

profile of v2, /device:TPU:1, one launch (start us, length us, event | category | flops | bytes accessed | tf_op | source)
XLA Modules:
  0.0 79.1 jit_solution(3747936991479049830)
XLA Ops:
  0.0 1.0 %fusion.24 = f32[3,32]{1,0:T(4,128)S(1)} fusion(bf16[3,32,256]{2,1,0:T(8,128)(2,1)} %param.20), kind=kLoop, calls=%fused_computation.47 | loop fusion | flops 73632 | bytes 49536 | tf_op jit(solution)/shard_map/reduce_sum | solution.py:39
  1.0 0.2 copy-done
  1.2 0.3 convolution_convert_fusion
  1.4 0.3 copy.94
  1.7 0.3 convert_element_type.165
  2.1 0.1 copy.97
  2.3 0.1 copy.98
  2.4 0.8 %concatenate.13 = bf16[3,16,2,1664]{3,2,1,0:T(2,128)(2,1)S(1)} concatenate(bf16[3,16,2,1536]{3,2,1,0:T(2,128)(2,1)S(1)} %convert_element_type.165, bf16[3,16,2,1]{3,2,1,0:T(2,128)(2,1)S(1)} %copy.97, bf16[3,16,2,1]{3,2,1,0:T(2,128)(2,1)S(1)} %copy.98, bf16[3,16,2,126]{3,2,1,0:T(2,128)(2,1)S(1)} %concatenate.12), dimensions={3} | concatenate | bytes 638976 | tf_op jit(solution)/shard_map/concatenate | solution.py:43
  3.3 0.9 %copy.99 = bf16[16,3,2,1664]{3,2,1,0:T(2,128)(2,1)} copy(bf16[16,3,2,1664]{3,2,0,1:T(2,128)(2,1)S(1)} %bitcast.111) | data formatting | bytes 638976 | tf_op jit(solution)/shard_map/transpose | solution.py:49
  4.2 8.7 %all-to-all-start = ((bf16[16,3,2,1664]{3,2,1,0:T(2,128)(2,1)}), bf16[16,3,2,1664]{3,2,1,0:T(2,128)(2,1)S(1)}, u32[]{:S(2)}, u32[]{:S(2)}) async-start(bf16[16,3,2,1664]{3,2,1,0:T(2,128)(2,1)} %copy.99), calls=%async_computation | async-start | bytes 638976 | tf_op jit(solution)/shard_map/all_to_all | solution.py:50
  13.0 0.6 copy-done.1
  13.8 0.2 fusion.37
  14.0 0.1 fusion.38
  14.1 0.6 sort.17
  14.8 0.7 gather_fusion.2
  15.5 0.2 fusion.54
  15.8 2.8 %collective-permute-start.2 = (bf16[1,24,2,512]{3,2,1,0:T(2,128)(2,1)S(1)}, bf16[1,24,2,512]{3,2,1,0:T(2,128)(2,1)S(1)}, u32[]{:S(2)}, u32[]{:S(2)}) collective-permute-start(bf16[1,24,2,512]{3,2,1,0:T(2,128)(2,1)S(1)} %fusion.25), channel_id=1, source_target_pairs={{0,4},{4,0},{1,5},{5,1},{2,6},{6,2},{3,7},{7,3},{8,12},{12,8},{9,1... | collective-permute-start | bytes 147464 | tf_op jit(solution)/shard_map/ppermute | solution.py:116
  18.6 0.2 fusion.53
  18.7 0.6 copy-done.8
  19.3 0.1 slice_reduce_fusion.2
  19.5 0.6 gather_fusion.4
  20.2 0.6 gather_fusion.1
  21.0 0.5 copy-done.3
  21.6 0.6 gather_fusion.5
  22.4 0.1 convert_reduce_fusion
  22.6 0.1 copy.134
  22.7 0.1 copy.135
  22.8 0.1 copy.104
  23.0 0.2 convert_reduce_fusion.4
  23.2 0.1 convolution_bitcast_fusion.2
  23.3 0.1 convert_reduce_fusion.3
  23.5 0.2 fusion.3
  23.7 0.7 broadcast_in_dim.125
  24.4 6.6 %all-to-all-start.1 = ((bf16[16,3,2,512]{3,2,1,0:T(2,128)(2,1)}), bf16[16,3,2,512]{3,2,1,0:T(2,128)(2,1)S(1)}, u32[]{:S(2)}, u32[]{:S(2)}) async-start(bf16[16,3,2,512]{3,2,1,0:T(2,128)(2,1)} %broadcast_in_dim.125), calls=%async_computation.1 | async-start | bytes 196608 | tf_op jit(solution)/shard_map/all_to_all | solution.py:24
  31.1 0.1 maximum_bitcast_fusion.1
  31.2 0.7 gather_fusion
  32.0 5.7 %all-to-all-done.1 = bf16[16,3,2,512]{3,2,1,0:T(2,128)(2,1)S(1)} async-done(((bf16[16,3,2,512]{3,2,1,0:T(2,128)(2,1)}), bf16[16,3,2,512]{3,2,1,0:T(2,128)(2,1)S(1)}, u32[]{:S(2)}, u32[]{:S(2)}) %all-to-all-start.1) | async-done | bytes 98336 | tf_op jit(solution)/shard_map/all_to_all | solution.py:24
  37.8 0.2 fusion.21
  38.0 3.0 %collective-permute-start = (f32[3,32,256]{2,1,0:T(8,128)S(1)}, f32[3,32,256]{2,1,0:T(8,128)S(1)}, u32[]{:S(2)}, u32[]{:S(2)}) collective-permute-start(f32[3,32,256]{2,1,0:T(8,128)S(1)} %fusion.21), channel_id=1, source_target_pairs={{0,1},{1,0},{2,3},{3,2},{4,5},{5,4},{6,7},{7,6},{8,9},{9,8},{10,11... | collective-permute-start | bytes 294920 | tf_op jit(solution)/shard_map/ppermute | solution.py:32
  41.1 0.2 broadcast_select_fusion.2
  41.2 0.7 gather_fusion.3
  42.0 0.4 collective-permute-start.1
  42.4 0.2 broadcast_select_fusion
  42.6 3.5 %collective-permute-done.1 = f32[3,32,256]{2,1,0:T(8,128)S(1)} collective-permute-done((f32[3,32,256]{2,1,0:T(8,128)S(1)}, f32[3,32,256]{2,1,0:T(8,128)S(1)}, u32[]{:S(2)}, u32[]{:S(2)}) %collective-permute-start.1) | collective-permute-done | bytes 98336 | tf_op jit(solution)/shard_map/ppermute | solution.py:32
  46.1 0.1 multiply_reduce_fusion
  46.4 0.1 copy.118
  46.5 0.1 copy.117
  46.7 0.7 copy-done.11
  47.3 0.2 convolution_convert_fusion.1
  47.6 0.8 %maximum_bitcast_fusion = bf16[16,3,2,640]{3,2,1,0:T(2,128)(2,1)} fusion(bf16[3,16,2,1]{3,2,0,1:T(2,128)(2,1)S(1)} %copy.118, bf16[3,16,2,1]{3,2,0,1:T(2,128)(2,1)S(1)} %copy.117, bf16[640]{0:T(1024)(128)(2,1)S(1)} %pad.9.clone, bf16[3,16,2,512]{3,2,1,0:T(2,128)(2,1)S(1)} %concatenate.14), kind=kLoop, calls=%fused_computation.45 | loop fusion | flops 491520 | bytes 222848 | tf_op jit(solution)/shard_map/transpose | solution.py:49
  48.4 3.5 %all-to-all-start.2 = ((bf16[16,3,2,640]{3,2,1,0:T(2,128)(2,1)}), bf16[16,3,2,640]{3,2,1,0:T(2,128)(2,1)S(1)}, u32[]{:S(2)}, u32[]{:S(2)}) async-start(bf16[16,3,2,640]{3,2,1,0:T(2,128)(2,1)} %maximum_bitcast_fusion), calls=%async_computation.2 | async-start | bytes 245760 | tf_op jit(solution)/shard_map/all_to_all | solution.py:50
  51.9 0.4 slice_reduce_fusion.1
  52.3 6.4 %all-to-all-done.2 = bf16[16,3,2,640]{3,2,1,0:T(2,128)(2,1)S(1)} async-done(((bf16[16,3,2,640]{3,2,1,0:T(2,128)(2,1)}), bf16[16,3,2,640]{3,2,1,0:T(2,128)(2,1)S(1)}, u32[]{:S(2)}, u32[]{:S(2)}) %all-to-all-start.2) | async-done | bytes 122912 | tf_op jit(solution)/shard_map/all_to_all | solution.py:50
  58.8 0.1 copy.139
  58.9 0.1 copy.140
  59.2 0.2 convert_reduce_fusion.2
  59.4 0.1 fusion.4
  59.6 9.9 %all_to_all.20 = bf16[16,3,2,512]{3,2,1,0:T(2,128)(2,1)S(1)} all-to-all(bf16[16,3,2,512]{3,2,1,0:T(2,128)(2,1)S(1)} %broadcast_in_dim.133), channel_id=1, replica_groups=mesh['enc'=16,'dp'=2,'tensor'=4] {'enc'}, dimensions={0} | all-to-all | bytes 196608 | tf_op jit(solution)/shard_map/all_to_all | solution.py:24
  69.7 0.2 fusion.18
  69.9 3.6 %collective-permute-start.3 = (f32[3,32,256]{2,1,0:T(8,128)S(1)}, f32[3,32,256]{2,1,0:T(8,128)S(1)}, u32[]{:S(2)}, u32[]{:S(2)}) collective-permute-start(f32[3,32,256]{2,1,0:T(8,128)S(1)} %fusion.18), channel_id=1, source_target_pairs={{0,1},{1,0},{2,3},{3,2},{4,5},{5,4},{6,7},{7,6},{8,9},{9,8},{10,11... | collective-permute-start | bytes 294920 | tf_op jit(solution)/shard_map/ppermute | solution.py:32
  73.5 0.9 %collective-permute-done.3 = f32[3,32,256]{2,1,0:T(8,128)S(1)} collective-permute-done((f32[3,32,256]{2,1,0:T(8,128)S(1)}, f32[3,32,256]{2,1,0:T(8,128)S(1)}, u32[]{:S(2)}, u32[]{:S(2)}) %collective-permute-start.3) | collective-permute-done | bytes 98336 | tf_op jit(solution)/shard_map/ppermute | solution.py:32
  74.4 0.4 collective-permute-start.4
  74.8 3.7 %collective-permute-done.4 = f32[3,32,256]{2,1,0:T(8,128)S(1)} collective-permute-done((f32[3,32,256]{2,1,0:T(8,128)S(1)}, f32[3,32,256]{2,1,0:T(8,128)S(1)}, u32[]{:S(2)}, u32[]{:S(2)}) %collective-permute-start.4) | collective-permute-done | bytes 98336 | tf_op jit(solution)/shard_map/ppermute | solution.py:32
  78.5 0.6 add_convert_fusion
  (78 shorter events, 2.0 us)
Async XLA Ops:
  0.0 1.2 %copy-start = (bf16[256,3,512]{2,0,1:T(8,128)(2,1)S(1)}, bf16[256,3,512]{2,0,1:T(8,128)(2,1)}, u32[]{:S(2)}) copy-start(bf16[256,3,512]{2,0,1:T(8,128)(2,1)} %param.27) | copy-start | bytes 2359300
  0.0 1.2 %copy-start.4 = (bf16[3,32,256]{2,1,0:T(8,128)(2,1)S(1)}, bf16[3,32,256]{2,1,0:T(8,128)(2,1)}, u32[]{:S(2)}) copy-start(bf16[3,32,256]{2,1,0:T(8,128)(2,1)} %param.20) | copy-start | bytes 147460
  0.0 1.2 %copy-start.10 = (f32[256]{0:T(256)S(1)}, f32[256]{0:T(256)}, u32[]{:S(2)}) copy-start(f32[256]{0:T(256)} %param.26) | copy-start | bytes 3076
  4.2 10.6 %copy-start.9 = (bf16[2,24,2,512]{3,2,1,0:T(2,128)(2,1)S(1)}, bf16[2,24,2,512]{3,2,1,0:T(2,128)(2,1)}, u32[]{:S(2)}) copy-start(bf16[2,24,2,512]{3,2,1,0:T(2,128)(2,1)} %param.22) | copy-start | bytes 294916
  4.2 18.2 %all-to-all-start = ((bf16[16,3,2,1664]{3,2,1,0:T(2,128)(2,1)}), bf16[16,3,2,1664]{3,2,1,0:T(2,128)(2,1)S(1)}, u32[]{:S(2)}, u32[]{:S(2)}) async-start(bf16[16,3,2,1664]{3,2,1,0:T(2,128)(2,1)} %copy.99), calls=%async_computation | async-start | bytes 638976 | tf_op jit(solution)/shard_map/all_to_all | solution.py:50
  13.0 0.7 copy-start.1
  15.8 15.3 %collective-permute-start.2 = (bf16[1,24,2,512]{3,2,1,0:T(2,128)(2,1)S(1)}, bf16[1,24,2,512]{3,2,1,0:T(2,128)(2,1)S(1)}, u32[]{:S(2)}, u32[]{:S(2)}) collective-permute-start(bf16[1,24,2,512]{3,2,1,0:T(2,128)(2,1)S(1)} %fusion.25), channel_id=1, source_target_pairs={{0,4},{4,0},{1,5},{5,1},{2,6},{6,2},{3,7},{7,3},{8,12},{12,8},{9,1... | collective-permute-start | bytes 147464 | tf_op jit(solution)/shard_map/ppermute | solution.py:116
  18.6 0.8 copy-start.8
  19.5 0.7 copy-start.2
  20.9 0.7 copy-start.3
  24.4 13.3 %all-to-all-start.1 = ((bf16[16,3,2,512]{3,2,1,0:T(2,128)(2,1)}), bf16[16,3,2,512]{3,2,1,0:T(2,128)(2,1)S(1)}, u32[]{:S(2)}, u32[]{:S(2)}) async-start(bf16[16,3,2,512]{3,2,1,0:T(2,128)(2,1)} %broadcast_in_dim.125), calls=%async_computation.1 | async-start | bytes 196608 | tf_op jit(solution)/shard_map/all_to_all | solution.py:24
  31.2 6.6 %copy-start.5 = (bf16[512,256]{1,0:T(8,128)(2,1)S(1)}, bf16[512,256]{1,0:T(8,128)(2,1)}, u32[]{:S(2)}) copy-start(bf16[512,256]{1,0:T(8,128)(2,1)} %param.28) | copy-start | bytes 786436
  38.0 4.0 %collective-permute-start = (f32[3,32,256]{2,1,0:T(8,128)S(1)}, f32[3,32,256]{2,1,0:T(8,128)S(1)}, u32[]{:S(2)}, u32[]{:S(2)}) collective-permute-start(f32[3,32,256]{2,1,0:T(8,128)S(1)} %fusion.21), channel_id=1, source_target_pairs={{0,1},{1,0},{2,3},{3,2},{4,5},{5,4},{6,7},{7,6},{8,9},{9,8},{10,11... | collective-permute-start | bytes 294920 | tf_op jit(solution)/shard_map/ppermute | solution.py:32
  42.0 4.1 %collective-permute-start.1 = (f32[3,32,256]{2,1,0:T(8,128)S(1)}, f32[3,32,256]{2,1,0:T(8,128)S(1)}, u32[]{:S(2)}, u32[]{:S(2)}) collective-permute-start(f32[3,32,256]{2,1,0:T(8,128)S(1)} %add.115), channel_id=1, source_target_pairs={{0,2},{1,3},{2,0},{3,1},{4,6},{5,7},{6,4},{7,5},{8,10},{9,11},{10,... | collective-permute-start | bytes 294920 | tf_op jit(solution)/shard_map/ppermute | solution.py:32
  42.6 4.1 %copy-start.6 = (bf16[256,512]{1,0:T(8,128)(2,1)S(1)}, bf16[256,512]{1,0:T(8,128)(2,1)}, u32[]{:S(2)}) copy-start(bf16[256,512]{1,0:T(8,128)(2,1)} %param.30) | copy-start | bytes 786436
  46.7 0.7 copy-start.11
  48.4 10.3 %all-to-all-start.2 = ((bf16[16,3,2,640]{3,2,1,0:T(2,128)(2,1)}), bf16[16,3,2,640]{3,2,1,0:T(2,128)(2,1)S(1)}, u32[]{:S(2)}, u32[]{:S(2)}) async-start(bf16[16,3,2,640]{3,2,1,0:T(2,128)(2,1)} %maximum_bitcast_fusion), calls=%async_computation.2 | async-start | bytes 245760 | tf_op jit(solution)/shard_map/all_to_all | solution.py:50
  59.6 10.0 %copy-start.7 = (bf16[512,256]{1,0:T(8,128)(2,1)S(1)}, bf16[512,256]{1,0:T(8,128)(2,1)}, u32[]{:S(2)}) copy-start(bf16[512,256]{1,0:T(8,128)(2,1)} %param.31) | copy-start | bytes 786436
  69.9 4.5 %collective-permute-start.3 = (f32[3,32,256]{2,1,0:T(8,128)S(1)}, f32[3,32,256]{2,1,0:T(8,128)S(1)}, u32[]{:S(2)}, u32[]{:S(2)}) collective-permute-start(f32[3,32,256]{2,1,0:T(8,128)S(1)} %fusion.18), channel_id=1, source_target_pairs={{0,1},{1,0},{2,3},{3,2},{4,5},{5,4},{6,7},{7,6},{8,9},{9,8},{10,11... | collective-permute-start | bytes 294920 | tf_op jit(solution)/shard_map/ppermute | solution.py:32
  74.4 4.1 %collective-permute-start.4 = (f32[3,32,256]{2,1,0:T(8,128)S(1)}, f32[3,32,256]{2,1,0:T(8,128)S(1)}, u32[]{:S(2)}, u32[]{:S(2)}) collective-permute-start(f32[3,32,256]{2,1,0:T(8,128)S(1)} %add.127), channel_id=1, source_target_pairs={{0,2},{1,3},{2,0},{3,1},{4,6},{5,7},{6,4},{7,5},{8,10},{9,11},{10,... | collective-permute-start | bytes 294920 | tf_op jit(solution)/shard_map/ppermute | solution.py:32

commit v3 on v2

--- a/solution.py
+++ b/solution.py
@@ -27,12 +27,12 @@
 
 def tensor_sum(value):
     n_t = lax.axis_size("tensor")
-    bit = 1
-    while bit < n_t:
-        other = lax.ppermute(value, "tensor", [(i, i ^ bit) for i in range(n_t)])
-        value = value + other
-        bit *= 2
-    return value
+    terms = [value] + [
+        lax.ppermute(value, "tensor", [(i, i ^ k) for i in range(n_t)]) for k in range(1, n_t)
+    ]
+    while len(terms) > 1:
+        terms = [terms[k] + terms[k + 1] for k in range(0, len(terms), 2)]
+    return terms[0]
 
 
 def with_sumsq(partial, rows_in):
@@ -90,38 +90,38 @@
     place_at = jnp.arange(cache_len, dtype=jnp.int32)
     cache_usable = place_at[None, :] < my_positions[:, None]
     token_at = jnp.arange(source_len, dtype=jnp.int32)
-    assign_view = assign.reshape(dp_count, enc_count, seq_dev)
-    assign_grid = jnp.take(assign_view, enc_at, axis=1)
-    owners = assign_grid // (seq_dev * enc_count)
-    earlier = (owners[:, None, :] == owners[:, :, None]) & (
-        slot_index[None, None, :] < slot_index[None, :, None]
-    )
-    slot_rank = jnp.sum(earlier.astype(jnp.int32), axis=2)
-    recv_rows = jnp.take(owners, dp_at, axis=0) * per_pair + jnp.take(slot_rank, dp_at, axis=0)
-    picked = (owners == dp_at)[:, :, None] & (
-        slot_rank[:, :, None] == jnp.arange(per_pair, dtype=jnp.int32)[None, None, :]
-    )
-    chosen = jnp.sum(jnp.where(picked, (assign_grid % seq_dev)[:, :, None], 0), axis=1)
-    chosen_flat = chosen.reshape(-1)
-    outgoing = jnp.take(src_pool, chosen_flat, axis=0).reshape(
-        (dp_count, per_pair) + src_pool.shape[1:]
-    )
-    pieces = []
+    assert seq_dev == dp_count
+    my_block = block_at
+    source_block = my_sources // seq_dev
+    source_row = my_sources % seq_dev
+    received = []
     for shift in range(dp_count):
         if shift == 0:
-            pieces.append(jnp.take(outgoing, dp_at, axis=0))
+            wanted = my_sources
         else:
-            sent = jnp.take(outgoing, (dp_at + shift) % dp_count, axis=0)
-            pieces.append(
-                lax.ppermute(
-                    sent, "dp", [(i, (i + shift) % dp_count) for i in range(dp_count)]
-                )
+            target = (dp_at + shift) % dp_count
+            target_slots = (target * enc_count + enc_at) * seq_dev + slot_index
+            wanted = jnp.take(assign, target_slots)
+        hit = (wanted // seq_dev) == my_block
+        row = jnp.sum(jnp.where(hit, wanted % seq_dev, 0))
+        piece = lax.dynamic_index_in_dim(src_pool, row, axis=0, keepdims=False)
+        if shift:
+            piece = lax.ppermute(
+                piece, "dp", [(i, (i + shift) % dp_count) for i in range(dp_count)]
             )
-    stacked = jnp.stack(pieces)
-    sender_at = (dp_at - jnp.arange(dp_count, dtype=jnp.int32)) % dp_count
-    order = jnp.argsort(sender_at)
-    arrived = jnp.take(stacked, order, axis=0).reshape((seq_dev,) + src_pool.shape[1:])
-    cross_kv = jnp.take(arrived, recv_rows, axis=0)
+        received.append(piece)
+    sender_block = [
+        ((dp_at - shift) % dp_count) * enc_count + enc_at for shift in range(dp_count)
+    ]
+    cross_kv = received[0][None]
+    cross_kv = jnp.broadcast_to(cross_kv, (seq_dev,) + cross_kv.shape[1:])
+    for shift in range(1, dp_count):
+        cross_kv = jnp.where(
+            (source_block == sender_block[shift])[:, None, None, None],
+            received[shift][None],
+            cross_kv,
+        )
+    del source_row
     cross_usable = token_at[None, :] < jnp.take(src_len, my_sources)[:, None]
 
     current = hidden_in.astype(jnp.float32)

time: 79.7 us -> 83.5 us (1.048)
  between operations: 0.53 us -> 4.4 us
  local copies, waits for them, and re-layouts: 12.6 us -> 9.99 us
  waiting for transfers between devices: 20.3 us -> 22.5 us
  starting transfers between devices: 29.1 us -> 30.2 us
    gather x3 -> x1, local copies, waits for them, and re-layouts: 2.24 us -> 0.64 us  [on_device(): wanted = jnp.take(assign, target_slots)]
    ppermute x5 -> x7, starting transfers between devices: 10.2 us -> 11.5 us  [the longest x6 8.68 us: tensor_sum(): lax.ppermute(value, 'tensor', [(i, i ^ k) for i in range(n_t)])]
    reduce_sum x2, other arithmetic: 0.34 us -> 1.35 us  [on_device(): row = jnp.sum(jnp.where(hit, wanted % seq_dev, 0))]
    all_to_all x2, waiting for transfers between devices: 6.35 us -> 7.25 us  [rows_reduce_scatter(): got = lax.all_to_all(send, 'enc', 0, 0, tiled=True)]
    unnamed x28 -> x30, local copies, waits for them, and re-layouts: 3.06 us -> 2.43 us
    ppermute x5 -> x7, waiting for transfers between devices: 8.18 us -> 8.71 us  [the longest x6 8.7 us: tensor_sum(): lax.ppermute(value, 'tensor', [(i, i ^ k) for i in range(n_t)])]
  transfers between devices with their start and end apart: 8 -> 10, of which waited for: 5 -> 4; matrix products, arithmetic and copies ran while one was open for 11% -> 8% of each run, Pallas kernels for 0% -> 0%
where the time goes in v3:
time: 83.5 us; the launch traced here: 82.9 us
  starting transfers between devices  30.2 us (36%)
  waiting for transfers between devices  22.5 us (27%)
  local copies, waits for them, and re-layouts  9.99 us (12%)
  blocking collectives  9.47 us (11%)
  other arithmetic  4.57 us (5%)
  between operations  4.4 us (5%)
  matrix products  1.77 us (2%)
    all_to_all x2, starting transfers between devices, rows_reduce_scatter(): got = lax.all_to_all(send, 'enc', 0, 0, tiled=True)  12.1 us
    all_to_all x1, blocking collectives, rows_gather(): got = lax.all_to_all(send, 'enc', 0, 0, tiled=True)  9.47 us
    ppermute x6, waiting for transfers between devices, tensor_sum(): lax.ppermute(value, 'tensor', [(i, i ^ k) for i in range(n_t)])  8.7 us
    ppermute x6, starting transfers between devices, tensor_sum(): lax.ppermute(value, 'tensor', [(i, i ^ k) for i in range(n_t)])  8.68 us
    all_to_all x2, waiting for transfers between devices, rows_reduce_scatter(): got = lax.all_to_all(send, 'enc', 0, 0, tiled=True)  7.25 us
    all_to_all x1, starting transfers between devices, rows_gather(): got = lax.all_to_all(send, 'enc', 0, 0, tiled=True)  6.65 us
    all_to_all x1, waiting for transfers between devices, rows_gather(): got = lax.all_to_all(send, 'enc', 0, 0, tiled=True)  6.53 us
    ppermute x1, starting transfers between devices, on_device(): lax.ppermute(piece, 'dp', [(i, (i + shift) % dp_count) for i in range(dp_...  2.82 us
  transfers between devices with their start and end apart: 10, of which 4 were waited for; matrix products, arithmetic and copies ran while one was open for 8% of the time, Pallas kernels for 0%

profile of v3, /device:TPU:1, one launch (start us, length us, event | category | flops | bytes accessed | tf_op | source)
XLA Modules:
  0.0 82.9 jit_solution(227473397462036869)
XLA Ops:
  0.0 1.0 %fusion.24 = f32[3,32]{1,0:T(4,128)S(1)} fusion(bf16[3,32,256]{2,1,0:T(8,128)(2,1)} %param.14), kind=kLoop, calls=%fused_computation.42 | loop fusion | flops 73632 | bytes 49536 | tf_op jit(solution)/shard_map/reduce_sum | solution.py:39
  1.0 0.2 copy-done
  1.2 0.3 convolution_convert_fusion
  1.4 0.3 copy.84
  1.7 0.3 convert_element_type.162
  1.9 0.1 reduce_sum.86
  2.0 0.1 copy.85
  2.1 0.1 copy.87
  2.3 0.1 copy.88
  2.4 0.8 %concatenate.13 = bf16[3,16,2,1664]{3,2,1,0:T(2,128)(2,1)S(1)} concatenate(bf16[3,16,2,1536]{3,2,1,0:T(2,128)(2,1)S(1)} %convert_element_type.162, bf16[3,16,2,1]{3,2,1,0:T(2,128)(2,1)S(1)} %copy.87, bf16[3,16,2,1]{3,2,1,0:T(2,128)(2,1)S(1)} %copy.88, bf16[3,16,2,126]{3,2,1,0:T(2,128)(2,1)S(1)} %concatenate.12), dimensions={3} | concatenate | bytes 638976 | tf_op jit(solution)/shard_map/concatenate | solution.py:43
  3.3 0.9 %copy.89 = bf16[16,3,2,1664]{3,2,1,0:T(2,128)(2,1)} copy(bf16[16,3,2,1664]{3,2,0,1:T(2,128)(2,1)S(1)} %bitcast.89) | data formatting | bytes 638976 | tf_op jit(solution)/shard_map/transpose | solution.py:49
  4.2 8.6 %all-to-all-start = ((bf16[16,3,2,1664]{3,2,1,0:T(2,128)(2,1)}), bf16[16,3,2,1664]{3,2,1,0:T(2,128)(2,1)S(1)}, u32[]{:S(2)}, u32[]{:S(2)}) async-start(bf16[16,3,2,1664]{3,2,1,0:T(2,128)(2,1)} %copy.89), calls=%async_computation | async-start | bytes 638976 | tf_op jit(solution)/shard_map/all_to_all | solution.py:50
  12.9 0.6 copy-done.1
  13.5 0.6 gather_fusion.2
  14.1 0.7 fusion.34
  16.2 0.6 gather_fusion.1
  16.9 0.6 gather_fusion.3
  17.5 0.6 fusion.35
  20.8 0.1 constant_dynamic-slice_fusion.1
  20.9 2.8 %collective-permute-start.3 = (bf16[24,2,512]{2,0,1:T(8,128)(2,1)S(1)}, bf16[24,2,512]{2,0,1:T(8,128)(2,1)S(1)}, u32[]{:S(2)}, u32[]{:S(2)}) collective-permute-start(bf16[24,2,512]{2,0,1:T(8,128)(2,1)S(1)} %bitcast.94), channel_id=1, source_target_pairs={{0,4},{4,0},{1,5},{5,1},{2,6},{6,2},{3,7},{7,3},{8,12},{12,8},{9,1... | collective-permute-start | bytes 147464 | tf_op jit(solution)/shard_map/ppermute | solution.py:109
  23.7 0.1 slice_reduce_fusion
  23.9 0.5 copy-done.3
  24.4 0.6 gather_fusion
  25.0 0.1 iota_compare_fusion.2
  25.2 0.1 convert_reduce_fusion
  25.4 0.1 copy.125
  25.5 0.1 copy.126
  25.6 0.1 copy.94
  25.7 0.1 fusion.31
  25.8 0.2 convert_reduce_fusion.4
  26.0 0.1 convolution_bitcast_fusion.2
  26.2 0.1 convert_reduce_fusion.3
  26.3 0.2 fusion.3
  26.5 0.7 broadcast_in_dim.70
  27.2 6.7 %all-to-all-start.1 = ((bf16[16,3,2,512]{3,2,1,0:T(2,128)(2,1)}), bf16[16,3,2,512]{3,2,1,0:T(2,128)(2,1)S(1)}, u32[]{:S(2)}, u32[]{:S(2)}) async-start(bf16[16,3,2,512]{3,2,1,0:T(2,128)(2,1)} %broadcast_in_dim.70), calls=%async_computation.1 | async-start | bytes 196608 | tf_op jit(solution)/shard_map/all_to_all | solution.py:24
  33.9 0.1 pad.3.clone
  34.0 6.5 %all-to-all-done.1 = bf16[16,3,2,512]{3,2,1,0:T(2,128)(2,1)S(1)} async-done(((bf16[16,3,2,512]{3,2,1,0:T(2,128)(2,1)}), bf16[16,3,2,512]{3,2,1,0:T(2,128)(2,1)S(1)}, u32[]{:S(2)}, u32[]{:S(2)}) %all-to-all-start.1) | async-done | bytes 98336 | tf_op jit(solution)/shard_map/all_to_all | solution.py:24
  40.7 0.2 fusion.21
  40.9 0.4 collective-permute-start.1
  41.3 4.3 %collective-permute-start.2 = (f32[3,32,256]{2,1,0:T(8,128)S(1)}, f32[3,32,256]{2,1,0:T(8,128)S(1)}, u32[]{:S(2)}, u32[]{:S(2)}) collective-permute-start(f32[3,32,256]{2,1,0:T(8,128)S(1)} %fusion.21), channel_id=1, source_target_pairs={{0,3},{1,2},{2,1},{3,0},{4,7},{5,6},{6,5},{7,4},{8,11},{9,10},{10,... | collective-permute-start | bytes 294920 | tf_op jit(solution)/shard_map/ppermute | solution.py:31
  45.5 0.1 broadcast_select_fusion
  45.6 4.3 %collective-permute-done.2 = f32[3,32,256]{2,1,0:T(8,128)S(1)} collective-permute-done((f32[3,32,256]{2,1,0:T(8,128)S(1)}, f32[3,32,256]{2,1,0:T(8,128)S(1)}, u32[]{:S(2)}, u32[]{:S(2)}) %collective-permute-start.2) | collective-permute-done | bytes 98336 | tf_op jit(solution)/shard_map/ppermute | solution.py:31
  49.9 0.1 multiply_reduce_fusion
  50.1 0.1 reduce_sum.93
  50.2 0.1 copy.105
  50.3 0.1 copy.109
  50.4 0.1 copy.108
  50.5 0.7 copy-done.11
  51.2 0.2 convolution_convert_fusion.1
  51.4 0.8 maximum_bitcast_fusion
  52.3 3.5 %all-to-all-start.2 = ((bf16[16,3,2,640]{3,2,1,0:T(2,128)(2,1)}), bf16[16,3,2,640]{3,2,1,0:T(2,128)(2,1)S(1)}, u32[]{:S(2)}, u32[]{:S(2)}) async-start(bf16[16,3,2,640]{3,2,1,0:T(2,128)(2,1)} %maximum_bitcast_fusion), calls=%async_computation.2 | async-start | bytes 245760 | tf_op jit(solution)/shard_map/all_to_all | solution.py:50
  55.8 7.2 %all-to-all-done.2 = bf16[16,3,2,640]{3,2,1,0:T(2,128)(2,1)S(1)} async-done(((bf16[16,3,2,640]{3,2,1,0:T(2,128)(2,1)}), bf16[16,3,2,640]{3,2,1,0:T(2,128)(2,1)S(1)}, u32[]{:S(2)}, u32[]{:S(2)}) %all-to-all-start.2) | async-done | bytes 122912 | tf_op jit(solution)/shard_map/all_to_all | solution.py:50
  63.2 0.1 copy.132
  63.3 0.1 copy.133
  63.4 0.1 copy.115
  63.5 0.1 fusion.32
  63.6 0.2 convert_reduce_fusion.2
  63.8 0.1 fusion.4
  64.1 9.5 %all_to_all.20 = bf16[16,3,2,512]{3,2,1,0:T(2,128)(2,1)S(1)} all-to-all(bf16[16,3,2,512]{3,2,1,0:T(2,128)(2,1)S(1)} %broadcast_in_dim.108), channel_id=1, replica_groups=mesh['enc'=16,'dp'=2,'tensor'=4] {'enc'}, dimensions={0} | all-to-all | bytes 196608 | tf_op jit(solution)/shard_map/all_to_all | solution.py:24
  73.7 0.2 fusion.18
  73.9 0.4 collective-permute-start.5
  74.2 3.6 %collective-permute-start.6 = (f32[3,32,256]{2,1,0:T(8,128)S(1)}, f32[3,32,256]{2,1,0:T(8,128)S(1)}, u32[]{:S(2)}, u32[]{:S(2)}) collective-permute-start(f32[3,32,256]{2,1,0:T(8,128)S(1)} %fusion.18), channel_id=1, source_target_pairs={{0,3},{1,2},{2,1},{3,0},{4,7},{5,6},{6,5},{7,4},{8,11},{9,10},{10,... | collective-permute-start | bytes 294920 | tf_op jit(solution)/shard_map/ppermute | solution.py:31
  77.9 4.4 %collective-permute-done.6 = f32[3,32,256]{2,1,0:T(8,128)S(1)} collective-permute-done((f32[3,32,256]{2,1,0:T(8,128)S(1)}, f32[3,32,256]{2,1,0:T(8,128)S(1)}, u32[]{:S(2)}, u32[]{:S(2)}) %collective-permute-start.6) | collective-permute-done | bytes 98336 | tf_op jit(solution)/shard_map/ppermute | solution.py:31
  82.3 0.7 add_convert_fusion
  (65 shorter events, 1.0 us)
Async XLA Ops:
  0.0 1.2 %copy-start = (bf16[256,3,512]{2,0,1:T(8,128)(2,1)S(1)}, bf16[256,3,512]{2,0,1:T(8,128)(2,1)}, u32[]{:S(2)}) copy-start(bf16[256,3,512]{2,0,1:T(8,128)(2,1)} %param.21) | copy-start | bytes 2359300
  0.0 1.2 %copy-start.4 = (bf16[3,32,256]{2,1,0:T(8,128)(2,1)S(1)}, bf16[3,32,256]{2,1,0:T(8,128)(2,1)}, u32[]{:S(2)}) copy-start(bf16[3,32,256]{2,1,0:T(8,128)(2,1)} %param.14) | copy-start | bytes 147460
  0.0 1.2 %copy-start.10 = (f32[256]{0:T(256)S(1)}, f32[256]{0:T(256)}, u32[]{:S(2)}) copy-start(f32[256]{0:T(256)} %param.20) | copy-start | bytes 3076
  4.2 21.0 %all-to-all-start = ((bf16[16,3,2,1664]{3,2,1,0:T(2,128)(2,1)}), bf16[16,3,2,1664]{3,2,1,0:T(2,128)(2,1)S(1)}, u32[]{:S(2)}, u32[]{:S(2)}) async-start(bf16[16,3,2,1664]{3,2,1,0:T(2,128)(2,1)} %copy.89), calls=%async_computation | async-start | bytes 638976 | tf_op jit(solution)/shard_map/all_to_all | solution.py:50
  12.8 0.7 copy-start.1
  16.2 0.7 copy-start.2
  16.9 3.9 %copy-start.9 = (bf16[2,24,2,512]{3,2,1,0:T(2,128)(2,1)S(1)}, bf16[2,24,2,512]{3,2,1,0:T(2,128)(2,1)}, u32[]{:S(2)}) copy-start(bf16[2,24,2,512]{3,2,1,0:T(2,128)(2,1)} %param.16) | copy-start | bytes 294916
  20.9 2.9 %copy-start.8 = (bf16[2,8,2,512]{3,2,1,0:T(2,128)(2,1)S(1)}, bf16[2,8,2,512]{3,2,1,0:T(2,128)(2,1)}, u32[]{:S(2)}) copy-start(bf16[2,8,2,512]{3,2,1,0:T(2,128)(2,1)} %param.15) | copy-start | bytes 98308
  20.9 24.6 %collective-permute-start.3 = (bf16[24,2,512]{2,0,1:T(8,128)(2,1)S(1)}, bf16[24,2,512]{2,0,1:T(8,128)(2,1)S(1)}, u32[]{:S(2)}, u32[]{:S(2)}) collective-permute-start(bf16[24,2,512]{2,0,1:T(8,128)(2,1)S(1)} %bitcast.94), channel_id=1, source_target_pairs={{0,4},{4,0},{1,5},{5,1},{2,6},{6,2},{3,7},{7,3},{8,12},{12,8},{9,1... | collective-permute-start | bytes 147464 | tf_op jit(solution)/shard_map/ppermute | solution.py:109
  23.7 0.7 copy-start.3
  27.2 13.3 %all-to-all-start.1 = ((bf16[16,3,2,512]{3,2,1,0:T(2,128)(2,1)}), bf16[16,3,2,512]{3,2,1,0:T(2,128)(2,1)S(1)}, u32[]{:S(2)}, u32[]{:S(2)}) async-start(bf16[16,3,2,512]{3,2,1,0:T(2,128)(2,1)} %broadcast_in_dim.70), calls=%async_computation.1 | async-start | bytes 196608 | tf_op jit(solution)/shard_map/all_to_all | solution.py:24
  33.9 6.8 %copy-start.5 = (bf16[512,256]{1,0:T(8,128)(2,1)S(1)}, bf16[512,256]{1,0:T(8,128)(2,1)}, u32[]{:S(2)}) copy-start(bf16[512,256]{1,0:T(8,128)(2,1)} %param.22) | copy-start | bytes 786436
  40.9 4.8 %collective-permute-start.1 = (f32[3,32,256]{2,1,0:T(8,128)S(1)}, f32[3,32,256]{2,1,0:T(8,128)S(1)}, u32[]{:S(2)}, u32[]{:S(2)}) collective-permute-start(f32[3,32,256]{2,1,0:T(8,128)S(1)} %fusion.21), channel_id=1, source_target_pairs={{0,2},{1,3},{2,0},{3,1},{4,6},{5,7},{6,4},{7,5},{8,10},{9,11},{10,... | collective-permute-start | bytes 294920 | tf_op jit(solution)/shard_map/ppermute | solution.py:31
  41.3 8.7 %collective-permute-start.2 = (f32[3,32,256]{2,1,0:T(8,128)S(1)}, f32[3,32,256]{2,1,0:T(8,128)S(1)}, u32[]{:S(2)}, u32[]{:S(2)}) collective-permute-start(f32[3,32,256]{2,1,0:T(8,128)S(1)} %fusion.21), channel_id=1, source_target_pairs={{0,3},{1,2},{2,1},{3,0},{4,7},{5,6},{6,5},{7,4},{8,11},{9,10},{10,... | collective-permute-start | bytes 294920 | tf_op jit(solution)/shard_map/ppermute | solution.py:31
  45.5 4.4 %collective-permute-start = (f32[3,32,256]{2,1,0:T(8,128)S(1)}, f32[3,32,256]{2,1,0:T(8,128)S(1)}, u32[]{:S(2)}, u32[]{:S(2)}) collective-permute-start(f32[3,32,256]{2,1,0:T(8,128)S(1)} %fusion.21), channel_id=1, source_target_pairs={{0,1},{1,0},{2,3},{3,2},{4,5},{5,4},{6,7},{7,6},{8,9},{9,8},{10,11... | collective-permute-start | bytes 294920 | tf_op jit(solution)/shard_map/ppermute | solution.py:31
  45.6 4.9 %copy-start.6 = (bf16[256,512]{1,0:T(8,128)(2,1)S(1)}, bf16[256,512]{1,0:T(8,128)(2,1)}, u32[]{:S(2)}) copy-start(bf16[256,512]{1,0:T(8,128)(2,1)} %param.24) | copy-start | bytes 786436
  50.5 0.7 copy-start.11
  52.3 10.8 %all-to-all-start.2 = ((bf16[16,3,2,640]{3,2,1,0:T(2,128)(2,1)}), bf16[16,3,2,640]{3,2,1,0:T(2,128)(2,1)S(1)}, u32[]{:S(2)}, u32[]{:S(2)}) async-start(bf16[16,3,2,640]{3,2,1,0:T(2,128)(2,1)} %maximum_bitcast_fusion), calls=%async_computation.2 | async-start | bytes 245760 | tf_op jit(solution)/shard_map/all_to_all | solution.py:50
  64.1 9.6 %copy-start.7 = (bf16[512,256]{1,0:T(8,128)(2,1)S(1)}, bf16[512,256]{1,0:T(8,128)(2,1)}, u32[]{:S(2)}) copy-start(bf16[512,256]{1,0:T(8,128)(2,1)} %param.25) | copy-start | bytes 786436
  73.9 4.0 %collective-permute-start.5 = (f32[3,32,256]{2,1,0:T(8,128)S(1)}, f32[3,32,256]{2,1,0:T(8,128)S(1)}, u32[]{:S(2)}, u32[]{:S(2)}) collective-permute-start(f32[3,32,256]{2,1,0:T(8,128)S(1)} %fusion.18), channel_id=1, source_target_pairs={{0,2},{1,3},{2,0},{3,1},{4,6},{5,7},{6,4},{7,5},{8,10},{9,11},{10,... | collective-permute-start | bytes 294920 | tf_op jit(solution)/shard_map/ppermute | solution.py:31
  74.2 8.0 %collective-permute-start.6 = (f32[3,32,256]{2,1,0:T(8,128)S(1)}, f32[3,32,256]{2,1,0:T(8,128)S(1)}, u32[]{:S(2)}, u32[]{:S(2)}) collective-permute-start(f32[3,32,256]{2,1,0:T(8,128)S(1)} %fusion.18), channel_id=1, source_target_pairs={{0,3},{1,2},{2,1},{3,0},{4,7},{5,6},{6,5},{7,4},{8,11},{9,10},{10,... | collective-permute-start | bytes 294920 | tf_op jit(solution)/shard_map/ppermute | solution.py:31
  77.9 4.4 %collective-permute-start.4 = (f32[3,32,256]{2,1,0:T(8,128)S(1)}, f32[3,32,256]{2,1,0:T(8,128)S(1)}, u32[]{:S(2)}, u32[]{:S(2)}) collective-permute-start(f32[3,32,256]{2,1,0:T(8,128)S(1)} %fusion.18), channel_id=1, source_target_pairs={{0,1},{1,0},{2,3},{3,2},{4,5},{5,4},{6,7},{7,6},{8,9},{9,8},{10,11... | collective-permute-start | bytes 294920 | tf_op jit(solution)/shard_map/ppermute | solution.py:31

commit v4 on v3

--- a/solution.py
+++ b/solution.py
@@ -55,6 +55,42 @@
     squares = packed[..., width] + packed[..., width + 1]
     scale = lax.rsqrt(squares / D + EPSILON)
     return (packed[..., :width] * scale[..., None]).astype(jnp.bfloat16)
+
+
+def exchange_sources(src_pool, assign, my_sources, block_at, enc_at, dp_at, dp_count, enc_count, seq_dev):
+    assert seq_dev == dp_count
+    my_block = block_at
+    source_block = my_sources // seq_dev
+    source_row = my_sources % seq_dev
+    received = []
+    for shift in range(dp_count):
+        if shift == 0:
+            wanted = my_sources
+        else:
+            target = (dp_at + shift) % dp_count
+            wanted = lax.dynamic_slice_in_dim(
+                assign, (target * enc_count + enc_at) * seq_dev, seq_dev
+            )
+        hit = (wanted // seq_dev) == my_block
+        row = jnp.sum(jnp.where(hit, wanted % seq_dev, 0))
+        piece = lax.dynamic_index_in_dim(src_pool, row, axis=0, keepdims=False)
+        if shift:
+            piece = lax.ppermute(
+                piece, "dp", [(i, (i + shift) % dp_count) for i in range(dp_count)]
+            )
+        received.append(piece)
+    sender_block = [
+        ((dp_at - shift) % dp_count) * enc_count + enc_at for shift in range(dp_count)
+    ]
+    cross_kv = received[0][None]
+    cross_kv = jnp.broadcast_to(cross_kv, (seq_dev,) + cross_kv.shape[1:])
+    for shift in range(1, dp_count):
+        cross_kv = jnp.where(
+            (source_block == sender_block[shift])[:, None, None, None],
+            received[shift][None],
+            cross_kv,
+        )
+    return cross_kv
 
 
 def on_device(
@@ -85,44 +121,16 @@
     block_at = dp_at * enc_count + enc_at
     slot_index = jnp.arange(seq_dev, dtype=jnp.int32)
     my_slots = block_at * seq_dev + slot_index
-    my_positions = jnp.take(positions, my_slots)
-    my_sources = jnp.take(assign, my_slots)
+    my_positions = lax.dynamic_slice_in_dim(positions, block_at * seq_dev, seq_dev)
+    my_sources = lax.dynamic_slice_in_dim(assign, block_at * seq_dev, seq_dev)
     place_at = jnp.arange(cache_len, dtype=jnp.int32)
     cache_usable = place_at[None, :] < my_positions[:, None]
     token_at = jnp.arange(source_len, dtype=jnp.int32)
-    assert seq_dev == dp_count
-    my_block = block_at
-    source_block = my_sources // seq_dev
-    source_row = my_sources % seq_dev
-    received = []
-    for shift in range(dp_count):
-        if shift == 0:
-            wanted = my_sources
-        else:
-            target = (dp_at + shift) % dp_count
-            target_slots = (target * enc_count + enc_at) * seq_dev + slot_index
-            wanted = jnp.take(assign, target_slots)
-        hit = (wanted // seq_dev) == my_block
-        row = jnp.sum(jnp.where(hit, wanted % seq_dev, 0))
-        piece = lax.dynamic_index_in_dim(src_pool, row, axis=0, keepdims=False)
-        if shift:
-            piece = lax.ppermute(
-                piece, "dp", [(i, (i + shift) % dp_count) for i in range(dp_count)]
-            )
-        received.append(piece)
-    sender_block = [
-        ((dp_at - shift) % dp_count) * enc_count + enc_at for shift in range(dp_count)
-    ]
-    cross_kv = received[0][None]
-    cross_kv = jnp.broadcast_to(cross_kv, (seq_dev,) + cross_kv.shape[1:])
-    for shift in range(1, dp_count):
-        cross_kv = jnp.where(
-            (source_block == sender_block[shift])[:, None, None, None],
-            received[shift][None],
-            cross_kv,
-        )
-    del source_row
-    cross_usable = token_at[None, :] < jnp.take(src_len, my_sources)[:, None]
+    source_at = jnp.arange(src_len.shape[0], dtype=jnp.int32)
+    my_len = jnp.sum(
+        jnp.where(source_at[None, :] == my_sources[:, None], src_len[None, :], 0), axis=1
+    )
+    cross_usable = token_at[None, :] < my_len[:, None]
 
     current = hidden_in.astype(jnp.float32)
     scaled = (current * gain_self[None, None, :]).astype(jnp.bfloat16)
@@ -158,6 +166,10 @@
         w_new.astype(jnp.float32), axis=-1
     )
     context = (weighted / totals[..., None]).reshape(steps, seq_dev, width).astype(jnp.bfloat16)
+    context, src_late = lax.optimization_barrier((context, src_pool))
+    cross_kv = exchange_sources(
+        src_late, assign, my_sources, block_at, enc_at, dp_at, dp_count, enc_count, seq_dev
+    )
     context_all = rows_gather(context)
     residual = current + tensor_sum(
         jnp.einsum("tsw,wf->tsf", context_all, w_out_self, preferred_element_type=jnp.float32)

time: 83.5 us -> 78.5 us (0.940)
  waiting for transfers between devices: 22.5 us -> 20.6 us
  local copies, waits for them, and re-layouts: 9.99 us -> 8.11 us
  starting transfers between devices: 30.2 us -> 29.2 us
    all_to_all x1, waiting for transfers between devices: 6.53 us -> 3.77 us  [rows_gather(): got = lax.all_to_all(send, 'enc', 0, 0, tiled=True)]
    gather x4 -> x0, local copies, waits for them, and re-layouts: 2.55 us -> none  [the longest x1 0.64 us: on_device(): my_sources = jnp.take(assign, my_slots)]
    all_to_all x1, starting transfers between devices: 6.65 us -> 5.48 us  [rows_gather(): got = lax.all_to_all(send, 'enc', 0, 0, tiled=True)]
    unnamed x30 -> x28, local copies, waits for them, and re-layouts: 2.43 us -> 3.08 us
  transfers between devices with their start and end apart: 10 -> 10, of which waited for: 4 -> 5; matrix products, arithmetic and copies ran while one was open for 8% -> 2% of each run, Pallas kernels for 0% -> 0%
where the time goes in v4:
time: 78.5 us; the launch traced here: 78 us
  starting transfers between devices  29.2 us (37%)
  waiting for transfers between devices  20.6 us (26%)
  blocking collectives  9.89 us (13%)
  local copies, waits for them, and re-layouts  8.11 us (10%)
  between operations  4.26 us (5%)
  other arithmetic  4.11 us (5%)
  matrix products  1.77 us (2%)
    all_to_all x2, starting transfers between devices, rows_reduce_scatter(): got = lax.all_to_all(send, 'enc', 0, 0, tiled=True)  12.1 us
    all_to_all x1, blocking collectives, rows_gather(): got = lax.all_to_all(send, 'enc', 0, 0, tiled=True)  9.89 us
    ppermute x6, waiting for transfers between devices, tensor_sum(): lax.ppermute(value, 'tensor', [(i, i ^ k) for i in range(n_t)])  8.87 us
    ppermute x6, starting transfers between devices, tensor_sum(): lax.ppermute(value, 'tensor', [(i, i ^ k) for i in range(n_t)])  8.77 us
    all_to_all x2, waiting for transfers between devices, rows_reduce_scatter(): got = lax.all_to_all(send, 'enc', 0, 0, tiled=True)  8.01 us
    all_to_all x1, starting transfers between devices, rows_gather(): got = lax.all_to_all(send, 'enc', 0, 0, tiled=True)  5.48 us
    all_to_all x1, waiting for transfers between devices, rows_gather(): got = lax.all_to_all(send, 'enc', 0, 0, tiled=True)  3.77 us
    unnamed x28, local copies, waits for them, and re-layouts  3.08 us
  transfers between devices with their start and end apart: 10, of which 5 were waited for; matrix products, arithmetic and copies ran while one was open for 2% of the time, Pallas kernels for 0%

profile of v4, /device:TPU:1, one launch (start us, length us, event | category | flops | bytes accessed | tf_op | source)
XLA Modules:
  0.0 78.0 jit_solution(16587235413448972004)
XLA Ops:
  0.0 1.0 %fusion.24 = f32[3,32]{1,0:T(4,128)S(1)} fusion(bf16[3,32,256]{2,1,0:T(8,128)(2,1)} %param.12), kind=kLoop, calls=%fused_computation.38 | loop fusion | flops 73632 | bytes 49536 | tf_op jit(solution)/shard_map/reduce_sum | solution.py:39
  1.0 0.2 copy-done
  1.2 0.3 convolution_convert_fusion
  1.4 0.3 copy.113
  1.7 0.3 convert_element_type.158
  1.9 0.1 reduce_sum.95
  2.0 0.1 copy.114
  2.1 0.1 copy.116
  2.3 0.1 copy.117
  2.4 0.8 %concatenate.13 = bf16[3,16,2,1664]{3,2,1,0:T(2,128)(2,1)S(1)} concatenate(bf16[3,16,2,1536]{3,2,1,0:T(2,128)(2,1)S(1)} %convert_element_type.158, bf16[3,16,2,1]{3,2,1,0:T(2,128)(2,1)S(1)} %copy.116, bf16[3,16,2,1]{3,2,1,0:T(2,128)(2,1)S(1)} %copy.117, bf16[3,16,2,126]{3,2,1,0:T(2,128)(2,1)S(1)} %concatenate.12), dimensions={3} | concatenate | bytes 638976 | tf_op jit(solution)/shard_map/concatenate | solution.py:43
  3.3 0.9 %copy.118 = bf16[16,3,2,1664]{3,2,1,0:T(2,128)(2,1)} copy(bf16[16,3,2,1664]{3,2,0,1:T(2,128)(2,1)S(1)} %bitcast.87) | data formatting | bytes 638976 | tf_op jit(solution)/shard_map/transpose | solution.py:49
  4.2 8.6 %all-to-all-start = ((bf16[16,3,2,1664]{3,2,1,0:T(2,128)(2,1)}), bf16[16,3,2,1664]{3,2,1,0:T(2,128)(2,1)S(1)}, u32[]{:S(2)}, u32[]{:S(2)}) async-start(bf16[16,3,2,1664]{3,2,1,0:T(2,128)(2,1)} %copy.118), calls=%async_computation | async-start | bytes 638976 | tf_op jit(solution)/shard_map/all_to_all | solution.py:50
  12.9 0.6 copy-done.7
  13.5 0.7 fusion.36
  16.8 0.1 slice_reduce_fusion
  17.0 0.5 copy-done.10
  17.5 0.1 iota_compare_fusion.2
  17.6 0.7 copy-done.11
  18.3 0.2 fusion.34
  18.5 0.1 iota_compare_fusion.1
  18.5 0.1 pad.3.clone
  19.9 1.3 %all-to-all-done = bf16[16,3,2,1664]{3,2,1,0:T(2,128)(2,1)S(1)} async-done(((bf16[16,3,2,1664]{3,2,1,0:T(2,128)(2,1)}), bf16[16,3,2,1664]{3,2,1,0:T(2,128)(2,1)S(1)}, u32[]{:S(2)}, u32[]{:S(2)}) %all-to-all-start) | async-done | bytes 319520 | tf_op jit(solution)/shard_map/all_to_all | solution.py:50
  21.2 0.1 convert_reduce_fusion
  21.4 0.1 fusion.38
  21.4 0.1 copy.154
  21.5 0.1 copy.155
  21.6 0.1 copy.123
  21.7 0.1 fusion.31
  21.9 0.2 convert_reduce_fusion.4
  22.1 0.1 convolution_bitcast_fusion.2
  22.2 0.1 convert_reduce_fusion.3
  22.4 0.2 fusion.3
  22.6 0.7 broadcast_in_dim.79
  23.3 5.5 %all-to-all-start.1 = ((bf16[16,3,2,512]{3,2,1,0:T(2,128)(2,1)}), bf16[16,3,2,512]{3,2,1,0:T(2,128)(2,1)S(1)}, u32[]{:S(2)}, u32[]{:S(2)}) async-start(bf16[16,3,2,512]{3,2,1,0:T(2,128)(2,1)} %broadcast_in_dim.79), calls=%async_computation.1 | async-start | bytes 196608 | tf_op jit(solution)/shard_map/all_to_all | solution.py:24
  28.8 2.8 %collective-permute-start.3 = (bf16[24,2,512]{2,0,1:T(8,128)(2,1)S(1)}, bf16[24,2,512]{2,0,1:T(8,128)(2,1)S(1)}, u32[]{:S(2)}, u32[]{:S(2)}) collective-permute-start(bf16[24,2,512]{2,0,1:T(8,128)(2,1)S(1)} %get-tuple-element.22), channel_id=1, source_target_pairs={{0,4},{4,0},{1,5},{5,1},{2,6},{6,2},{3,7},{7,3},{8,12},{12,8},{9,1... | collective-permute-start | bytes 147464 | tf_op jit(solution)/shard_map/ppermute | solution.py:78
  31.7 3.8 %all-to-all-done.1 = bf16[16,3,2,512]{3,2,1,0:T(2,128)(2,1)S(1)} async-done(((bf16[16,3,2,512]{3,2,1,0:T(2,128)(2,1)}), bf16[16,3,2,512]{3,2,1,0:T(2,128)(2,1)S(1)}, u32[]{:S(2)}, u32[]{:S(2)}) %all-to-all-start.1) | async-done | bytes 98336 | tf_op jit(solution)/shard_map/all_to_all | solution.py:24
  35.6 0.2 fusion.21
  35.8 1.3 %collective-permute-start.1 = (f32[3,32,256]{2,1,0:T(8,128)S(1)}, f32[3,32,256]{2,1,0:T(8,128)S(1)}, u32[]{:S(2)}, u32[]{:S(2)}) collective-permute-start(f32[3,32,256]{2,1,0:T(8,128)S(1)} %fusion.21), channel_id=1, source_target_pairs={{0,2},{1,3},{2,0},{3,1},{4,6},{5,7},{6,4},{7,5},{8,10},{9,11},{10,... | collective-permute-start | bytes 294920 | tf_op jit(solution)/shard_map/ppermute | solution.py:31
  37.0 3.1 %collective-permute-start.2 = (f32[3,32,256]{2,1,0:T(8,128)S(1)}, f32[3,32,256]{2,1,0:T(8,128)S(1)}, u32[]{:S(2)}, u32[]{:S(2)}) collective-permute-start(f32[3,32,256]{2,1,0:T(8,128)S(1)} %fusion.21), channel_id=1, source_target_pairs={{0,3},{1,2},{2,1},{3,0},{4,7},{5,6},{6,5},{7,4},{8,11},{9,10},{10,... | collective-permute-start | bytes 294920 | tf_op jit(solution)/shard_map/ppermute | solution.py:31
  40.1 0.1 broadcast_select_fusion
  40.2 4.5 %collective-permute-done.2 = f32[3,32,256]{2,1,0:T(8,128)S(1)} collective-permute-done((f32[3,32,256]{2,1,0:T(8,128)S(1)}, f32[3,32,256]{2,1,0:T(8,128)S(1)}, u32[]{:S(2)}, u32[]{:S(2)}) %collective-permute-start.2) | collective-permute-done | bytes 98336 | tf_op jit(solution)/shard_map/ppermute | solution.py:31
  44.7 0.1 multiply_reduce_fusion
  44.8 0.1 reduce_sum.103
  44.9 0.1 copy.134
  45.0 0.1 copy.138
  45.1 0.1 copy.137
  45.3 0.7 copy-done.9
  46.0 0.2 convolution_convert_fusion.1
  46.2 0.8 %maximum_bitcast_fusion = bf16[16,3,2,640]{3,2,1,0:T(2,128)(2,1)} fusion(bf16[3,16,2,1]{3,2,0,1:T(2,128)(2,1)S(1)} %copy.138, bf16[3,16,2,1]{3,2,0,1:T(2,128)(2,1)S(1)} %copy.137, bf16[640]{0:T(1024)(128)(2,1)S(1)} %pad.3.clone, bf16[3,16,2,512]{3,2,1,0:T(2,128)(2,1)S(1)} %concatenate.14), kind=kLoop, calls=%fused_computation.36 | loop fusion | flops 491520 | bytes 222848 | tf_op jit(solution)/shard_map/transpose | solution.py:49
  47.0 3.5 %all-to-all-start.2 = ((bf16[16,3,2,640]{3,2,1,0:T(2,128)(2,1)}), bf16[16,3,2,640]{3,2,1,0:T(2,128)(2,1)S(1)}, u32[]{:S(2)}, u32[]{:S(2)}) async-start(bf16[16,3,2,640]{3,2,1,0:T(2,128)(2,1)} %maximum_bitcast_fusion), calls=%async_computation.2 | async-start | bytes 245760 | tf_op jit(solution)/shard_map/all_to_all | solution.py:50
  50.6 6.7 %all-to-all-done.2 = bf16[16,3,2,640]{3,2,1,0:T(2,128)(2,1)S(1)} async-done(((bf16[16,3,2,640]{3,2,1,0:T(2,128)(2,1)}), bf16[16,3,2,640]{3,2,1,0:T(2,128)(2,1)S(1)}, u32[]{:S(2)}, u32[]{:S(2)}) %all-to-all-start.2) | async-done | bytes 122912 | tf_op jit(solution)/shard_map/all_to_all | solution.py:50
  57.3 0.1 fusion.40
  57.4 0.1 copy.159
  57.5 0.1 copy.160
  57.6 0.1 copy.144
  57.7 0.1 fusion.32
  57.8 0.2 convert_reduce_fusion.2
  58.0 0.1 fusion.4
  58.3 9.9 %all_to_all.20 = bf16[16,3,2,512]{3,2,1,0:T(2,128)(2,1)S(1)} all-to-all(bf16[16,3,2,512]{3,2,1,0:T(2,128)(2,1)S(1)} %broadcast_in_dim.122), channel_id=1, replica_groups=mesh['enc'=16,'dp'=2,'tensor'=4] {'enc'}, dimensions={0} | all-to-all | bytes 196608 | tf_op jit(solution)/shard_map/all_to_all | solution.py:24
  68.3 0.2 fusion.18
  68.5 1.2 %collective-permute-start.5 = (f32[3,32,256]{2,1,0:T(8,128)S(1)}, f32[3,32,256]{2,1,0:T(8,128)S(1)}, u32[]{:S(2)}, u32[]{:S(2)}) collective-permute-start(f32[3,32,256]{2,1,0:T(8,128)S(1)} %fusion.18), channel_id=1, source_target_pairs={{0,2},{1,3},{2,0},{3,1},{4,6},{5,7},{6,4},{7,5},{8,10},{9,11},{10,... | collective-permute-start | bytes 294920 | tf_op jit(solution)/shard_map/ppermute | solution.py:31
  69.7 3.2 %collective-permute-start.6 = (f32[3,32,256]{2,1,0:T(8,128)S(1)}, f32[3,32,256]{2,1,0:T(8,128)S(1)}, u32[]{:S(2)}, u32[]{:S(2)}) collective-permute-start(f32[3,32,256]{2,1,0:T(8,128)S(1)} %fusion.18), channel_id=1, source_target_pairs={{0,3},{1,2},{2,1},{3,0},{4,7},{5,6},{6,5},{7,4},{8,11},{9,10},{10,... | collective-permute-start | bytes 294920 | tf_op jit(solution)/shard_map/ppermute | solution.py:31
  72.9 4.4 %collective-permute-done.6 = f32[3,32,256]{2,1,0:T(8,128)S(1)} collective-permute-done((f32[3,32,256]{2,1,0:T(8,128)S(1)}, f32[3,32,256]{2,1,0:T(8,128)S(1)}, u32[]{:S(2)}, u32[]{:S(2)}) %collective-permute-start.6) | collective-permute-done | bytes 98336 | tf_op jit(solution)/shard_map/ppermute | solution.py:31
  77.3 0.7 add_convert_fusion
  (55 shorter events, 0.8 us)
Async XLA Ops:
  0.0 1.2 %copy-start = (bf16[256,3,512]{2,0,1:T(8,128)(2,1)S(1)}, bf16[256,3,512]{2,0,1:T(8,128)(2,1)}, u32[]{:S(2)}) copy-start(bf16[256,3,512]{2,0,1:T(8,128)(2,1)} %param.19) | copy-start | bytes 2359300
  0.0 1.2 %copy-start.1 = (bf16[3,32,256]{2,1,0:T(8,128)(2,1)S(1)}, bf16[3,32,256]{2,1,0:T(8,128)(2,1)}, u32[]{:S(2)}) copy-start(bf16[3,32,256]{2,1,0:T(8,128)(2,1)} %param.12) | copy-start | bytes 147460
  0.0 1.2 %copy-start.8 = (f32[256]{0:T(256)S(1)}, f32[256]{0:T(256)}, u32[]{:S(2)}) copy-start(f32[256]{0:T(256)} %param.18) | copy-start | bytes 3076
  4.2 17.0 %all-to-all-start = ((bf16[16,3,2,1664]{3,2,1,0:T(2,128)(2,1)}), bf16[16,3,2,1664]{3,2,1,0:T(2,128)(2,1)S(1)}, u32[]{:S(2)}, u32[]{:S(2)}) async-start(bf16[16,3,2,1664]{3,2,1,0:T(2,128)(2,1)} %copy.118), calls=%async_computation | async-start | bytes 638976 | tf_op jit(solution)/shard_map/all_to_all | solution.py:50
  12.8 4.0 %copy-start.5 = (bf16[2,8,2,512]{3,2,1,0:T(2,128)(2,1)S(1)}, bf16[2,8,2,512]{3,2,1,0:T(2,128)(2,1)}, u32[]{:S(2)}) copy-start(bf16[2,8,2,512]{3,2,1,0:T(2,128)(2,1)} %param.13) | copy-start | bytes 98308
  12.8 0.7 copy-start.7
  16.8 0.7 copy-start.10
  17.6 0.7 copy-start.11
  23.3 5.5 %copy-start.6 = (bf16[2,24,2,512]{3,2,1,0:T(2,128)(2,1)S(1)}, bf16[2,24,2,512]{3,2,1,0:T(2,128)(2,1)}, u32[]{:S(2)}) copy-start(bf16[2,24,2,512]{3,2,1,0:T(2,128)(2,1)} %param.14) | copy-start | bytes 294916
  23.3 12.2 %all-to-all-start.1 = ((bf16[16,3,2,512]{3,2,1,0:T(2,128)(2,1)}), bf16[16,3,2,512]{3,2,1,0:T(2,128)(2,1)S(1)}, u32[]{:S(2)}, u32[]{:S(2)}) async-start(bf16[16,3,2,512]{3,2,1,0:T(2,128)(2,1)} %broadcast_in_dim.79), calls=%async_computation.1 | async-start | bytes 196608 | tf_op jit(solution)/shard_map/all_to_all | solution.py:24
  28.8 6.8 %copy-start.2 = (bf16[512,256]{1,0:T(8,128)(2,1)S(1)}, bf16[512,256]{1,0:T(8,128)(2,1)}, u32[]{:S(2)}) copy-start(bf16[512,256]{1,0:T(8,128)(2,1)} %param.20) | copy-start | bytes 786436
  28.8 11.3 %collective-permute-start.3 = (bf16[24,2,512]{2,0,1:T(8,128)(2,1)S(1)}, bf16[24,2,512]{2,0,1:T(8,128)(2,1)S(1)}, u32[]{:S(2)}, u32[]{:S(2)}) collective-permute-start(bf16[24,2,512]{2,0,1:T(8,128)(2,1)S(1)} %get-tuple-element.22), channel_id=1, source_target_pairs={{0,4},{4,0},{1,5},{5,1},{2,6},{6,2},{3,7},{7,3},{8,12},{12,8},{9,1... | collective-permute-start | bytes 147464 | tf_op jit(solution)/shard_map/ppermute | solution.py:78
  35.8 4.5 %collective-permute-start.1 = (f32[3,32,256]{2,1,0:T(8,128)S(1)}, f32[3,32,256]{2,1,0:T(8,128)S(1)}, u32[]{:S(2)}, u32[]{:S(2)}) collective-permute-start(f32[3,32,256]{2,1,0:T(8,128)S(1)} %fusion.21), channel_id=1, source_target_pairs={{0,2},{1,3},{2,0},{3,1},{4,6},{5,7},{6,4},{7,5},{8,10},{9,11},{10,... | collective-permute-start | bytes 294920 | tf_op jit(solution)/shard_map/ppermute | solution.py:31
  37.0 7.6 %collective-permute-start.2 = (f32[3,32,256]{2,1,0:T(8,128)S(1)}, f32[3,32,256]{2,1,0:T(8,128)S(1)}, u32[]{:S(2)}, u32[]{:S(2)}) collective-permute-start(f32[3,32,256]{2,1,0:T(8,128)S(1)} %fusion.21), channel_id=1, source_target_pairs={{0,3},{1,2},{2,1},{3,0},{4,7},{5,6},{6,5},{7,4},{8,11},{9,10},{10,... | collective-permute-start | bytes 294920 | tf_op jit(solution)/shard_map/ppermute | solution.py:31
  40.1 4.6 %collective-permute-start = (f32[3,32,256]{2,1,0:T(8,128)S(1)}, f32[3,32,256]{2,1,0:T(8,128)S(1)}, u32[]{:S(2)}, u32[]{:S(2)}) collective-permute-start(f32[3,32,256]{2,1,0:T(8,128)S(1)} %fusion.21), channel_id=1, source_target_pairs={{0,1},{1,0},{2,3},{3,2},{4,5},{5,4},{6,7},{7,6},{8,9},{9,8},{10,11... | collective-permute-start | bytes 294920 | tf_op jit(solution)/shard_map/ppermute | solution.py:31
  40.2 5.1 %copy-start.3 = (bf16[256,512]{1,0:T(8,128)(2,1)S(1)}, bf16[256,512]{1,0:T(8,128)(2,1)}, u32[]{:S(2)}) copy-start(bf16[256,512]{1,0:T(8,128)(2,1)} %param.22) | copy-start | bytes 786436
  45.3 0.7 copy-start.9
  47.0 10.3 %all-to-all-start.2 = ((bf16[16,3,2,640]{3,2,1,0:T(2,128)(2,1)}), bf16[16,3,2,640]{3,2,1,0:T(2,128)(2,1)S(1)}, u32[]{:S(2)}, u32[]{:S(2)}) async-start(bf16[16,3,2,640]{3,2,1,0:T(2,128)(2,1)} %maximum_bitcast_fusion), calls=%async_computation.2 | async-start | bytes 245760 | tf_op jit(solution)/shard_map/all_to_all | solution.py:50
  58.3 10.0 %copy-start.4 = (bf16[512,256]{1,0:T(8,128)(2,1)S(1)}, bf16[512,256]{1,0:T(8,128)(2,1)}, u32[]{:S(2)}) copy-start(bf16[512,256]{1,0:T(8,128)(2,1)} %param.23) | copy-start | bytes 786436
  68.5 4.4 %collective-permute-start.5 = (f32[3,32,256]{2,1,0:T(8,128)S(1)}, f32[3,32,256]{2,1,0:T(8,128)S(1)}, u32[]{:S(2)}, u32[]{:S(2)}) collective-permute-start(f32[3,32,256]{2,1,0:T(8,128)S(1)} %fusion.18), channel_id=1, source_target_pairs={{0,2},{1,3},{2,0},{3,1},{4,6},{5,7},{6,4},{7,5},{8,10},{9,11},{10,... | collective-permute-start | bytes 294920 | tf_op jit(solution)/shard_map/ppermute | solution.py:31
  69.7 7.6 %collective-permute-start.6 = (f32[3,32,256]{2,1,0:T(8,128)S(1)}, f32[3,32,256]{2,1,0:T(8,128)S(1)}, u32[]{:S(2)}, u32[]{:S(2)}) collective-permute-start(f32[3,32,256]{2,1,0:T(8,128)S(1)} %fusion.18), channel_id=1, source_target_pairs={{0,3},{1,2},{2,1},{3,0},{4,7},{5,6},{6,5},{7,4},{8,11},{9,10},{10,... | collective-permute-start | bytes 294920 | tf_op jit(solution)/shard_map/ppermute | solution.py:31
  72.9 4.4 %collective-permute-start.4 = (f32[3,32,256]{2,1,0:T(8,128)S(1)}, f32[3,32,256]{2,1,0:T(8,128)S(1)}, u32[]{:S(2)}, u32[]{:S(2)}) collective-permute-start(f32[3,32,256]{2,1,0:T(8,128)S(1)} %fusion.18), channel_id=1, source_target_pairs={{0,1},{1,0},{2,3},{3,2},{4,5},{5,4},{6,7},{7,6},{8,9},{9,8},{10,11... | collective-permute-start | bytes 294920 | tf_op jit(solution)/shard_map/ppermute | solution.py:31

commit v5 on v4

--- a/solution.py
+++ b/solution.py
@@ -27,9 +27,11 @@
 
 def tensor_sum(value):
     n_t = lax.axis_size("tensor")
+    value = value.astype(jnp.bfloat16)
     terms = [value] + [
         lax.ppermute(value, "tensor", [(i, i ^ k) for i in range(n_t)]) for k in range(1, n_t)
     ]
+    terms = [term.astype(jnp.float32) for term in terms]
     while len(terms) > 1:
         terms = [terms[k] + terms[k + 1] for k in range(0, len(terms), 2)]
     return terms[0]

time: 78.5 us -> 75.1 us (0.957)
  waiting for transfers between devices: 20.6 us -> 17.6 us
    ppermute x6, waiting for transfers between devices: 8.87 us -> 5.78 us  [tensor_sum(): lax.ppermute(value, 'tensor', [(i, i ^ k) for i in range(n_t)])]
  transfers between devices with their start and end apart: 10 -> 10, of which waited for: 5 -> 7; matrix products, arithmetic and copies ran while one was open for 2% -> 2% of each run, Pallas kernels for 0% -> 0%
where the time goes in v5:
time: 75.1 us; the launch traced here: 74.5 us
  starting transfers between devices  28.8 us (38%)
  waiting for transfers between devices  17.6 us (23%)
  blocking collectives  9.89 us (13%)
  local copies, waits for them, and re-layouts  8.11 us (11%)
  between operations  4.24 us (6%)
  other arithmetic  4.11 us (5%)
  matrix products  1.77 us (2%)
    all_to_all x2, starting transfers between devices, rows_reduce_scatter(): got = lax.all_to_all(send, 'enc', 0, 0, tiled=True)  12.1 us
    all_to_all x1, blocking collectives, rows_gather(): got = lax.all_to_all(send, 'enc', 0, 0, tiled=True)  9.89 us
    ppermute x6, starting transfers between devices, tensor_sum(): lax.ppermute(value, 'tensor', [(i, i ^ k) for i in range(n_t)])  8.44 us
    all_to_all x2, waiting for transfers between devices, rows_reduce_scatter(): got = lax.all_to_all(send, 'enc', 0, 0, tiled=True)  8.01 us
    ppermute x6, waiting for transfers between devices, tensor_sum(): lax.ppermute(value, 'tensor', [(i, i ^ k) for i in range(n_t)])  5.78 us
    all_to_all x1, starting transfers between devices, rows_gather(): got = lax.all_to_all(send, 'enc', 0, 0, tiled=True)  5.48 us
    all_to_all x1, waiting for transfers between devices, rows_gather(): got = lax.all_to_all(send, 'enc', 0, 0, tiled=True)  3.77 us
    unnamed x28, local copies, waits for them, and re-layouts  3.08 us
  transfers between devices with their start and end apart: 10, of which 7 were waited for; matrix products, arithmetic and copies ran while one was open for 2% of the time, Pallas kernels for 0%

profile of v5, /device:TPU:1, one launch (start us, length us, event | category | flops | bytes accessed | tf_op | source)
XLA Modules:
  0.0 74.5 jit_solution(8532173956548055498)
XLA Ops:
  0.0 1.0 %fusion.22 = f32[3,32]{1,0:T(4,128)S(1)} fusion(bf16[3,32,256]{2,1,0:T(8,128)(2,1)} %param.12), kind=kLoop, calls=%fused_computation.38 | loop fusion | flops 73632 | bytes 49536 | tf_op jit(solution)/shard_map/reduce_sum | solution.py:41
  1.0 0.2 copy-done
  1.2 0.3 convolution_convert_fusion
  1.4 0.3 copy.113
  1.7 0.3 convert_element_type.188
  1.9 0.1 reduce_sum.95
  2.0 0.1 copy.114
  2.1 0.1 copy.116
  2.3 0.1 copy.117
  2.4 0.8 %concatenate.13 = bf16[3,16,2,1664]{3,2,1,0:T(2,128)(2,1)S(1)} concatenate(bf16[3,16,2,1536]{3,2,1,0:T(2,128)(2,1)S(1)} %convert_element_type.188, bf16[3,16,2,1]{3,2,1,0:T(2,128)(2,1)S(1)} %copy.116, bf16[3,16,2,1]{3,2,1,0:T(2,128)(2,1)S(1)} %copy.117, bf16[3,16,2,126]{3,2,1,0:T(2,128)(2,1)S(1)} %concatenate.12), dimensions={3} | concatenate | bytes 638976 | tf_op jit(solution)/shard_map/concatenate | solution.py:45
  3.3 0.9 %copy.118 = bf16[16,3,2,1664]{3,2,1,0:T(2,128)(2,1)} copy(bf16[16,3,2,1664]{3,2,0,1:T(2,128)(2,1)S(1)} %bitcast.87) | data formatting | bytes 638976 | tf_op jit(solution)/shard_map/transpose | solution.py:51
  4.2 8.6 %all-to-all-start = ((bf16[16,3,2,1664]{3,2,1,0:T(2,128)(2,1)}), bf16[16,3,2,1664]{3,2,1,0:T(2,128)(2,1)S(1)}, u32[]{:S(2)}, u32[]{:S(2)}) async-start(bf16[16,3,2,1664]{3,2,1,0:T(2,128)(2,1)} %copy.118), calls=%async_computation | async-start | bytes 638976 | tf_op jit(solution)/shard_map/all_to_all | solution.py:52
  12.9 0.6 copy-done.7
  13.5 0.7 %fusion.34 = (s32[]{:T(128)}, s32[2]{0:T(128)S(1)}, s32[2]{0:T(128)S(1)}, s32[]{:T(128)}) fusion(s32[]{:T(128)S(6)} %add.96, s32[64]{0:T(128)S(1)} %copy-done.7, s32[]{:T(128)S(6)} %select_n.77, s32[]{:T(128)S(6)} %select_n.84), kind=kLoop, calls=%fused_computation.85 | loop fusion | flops 86 | bytes 52 | tf_op jit(solution)/shard_map/reduce_sum | solution.py:77
  16.8 0.1 slice_reduce_fusion
  17.0 0.5 copy-done.10
  17.5 0.1 iota_compare_fusion.2
  17.6 0.7 copy-done.11
  18.3 0.2 fusion.32
  18.5 0.1 pad.3.clone
  19.9 1.3 %all-to-all-done = bf16[16,3,2,1664]{3,2,1,0:T(2,128)(2,1)S(1)} async-done(((bf16[16,3,2,1664]{3,2,1,0:T(2,128)(2,1)}), bf16[16,3,2,1664]{3,2,1,0:T(2,128)(2,1)S(1)}, u32[]{:S(2)}, u32[]{:S(2)}) %all-to-all-start) | async-done | bytes 319520 | tf_op jit(solution)/shard_map/all_to_all | solution.py:52
  21.2 0.1 convert_reduce_fusion
  21.4 0.1 copy.154
  21.5 0.1 copy.155
  21.6 0.1 copy.123
  21.7 0.1 fusion.29
  21.9 0.2 convert_reduce_fusion.4
  22.1 0.1 convolution_bitcast_fusion.2
  22.2 0.1 convert_reduce_fusion.3
  22.4 0.2 fusion.3
  22.6 0.7 broadcast_in_dim.79
  23.3 5.5 %all-to-all-start.1 = ((bf16[16,3,2,512]{3,2,1,0:T(2,128)(2,1)}), bf16[16,3,2,512]{3,2,1,0:T(2,128)(2,1)S(1)}, u32[]{:S(2)}, u32[]{:S(2)}) async-start(bf16[16,3,2,512]{3,2,1,0:T(2,128)(2,1)} %broadcast_in_dim.79), calls=%async_computation.1 | async-start | bytes 196608 | tf_op jit(solution)/shard_map/all_to_all | solution.py:24
  28.8 2.8 %collective-permute-start.3 = (bf16[24,2,512]{2,0,1:T(8,128)(2,1)S(1)}, bf16[24,2,512]{2,0,1:T(8,128)(2,1)S(1)}, u32[]{:S(2)}, u32[]{:S(2)}) collective-permute-start(bf16[24,2,512]{2,0,1:T(8,128)(2,1)S(1)} %get-tuple-element.22), channel_id=1, source_target_pairs={{0,4},{4,0},{1,5},{5,1},{2,6},{6,2},{3,7},{7,3},{8,12},{12,8},{9,1... | collective-permute-start | bytes 147464 | tf_op jit(solution)/shard_map/ppermute | solution.py:80
  31.7 3.8 %all-to-all-done.1 = bf16[16,3,2,512]{3,2,1,0:T(2,128)(2,1)S(1)} async-done(((bf16[16,3,2,512]{3,2,1,0:T(2,128)(2,1)}), bf16[16,3,2,512]{3,2,1,0:T(2,128)(2,1)S(1)}, u32[]{:S(2)}, u32[]{:S(2)}) %all-to-all-start.1) | async-done | bytes 98336 | tf_op jit(solution)/shard_map/all_to_all | solution.py:24
  35.6 0.2 convolution_convert_fusion.3
  35.7 3.8 %collective-permute-start.2 = (bf16[3,32,256]{2,1,0:T(8,128)(2,1)S(1)}, bf16[3,32,256]{2,1,0:T(8,128)(2,1)S(1)}, u32[]{:S(2)}, u32[]{:S(2)}) collective-permute-start(bf16[3,32,256]{2,1,0:T(8,128)(2,1)S(1)} %convolution_convert_fusion.3), channel_id=1, source_target_pairs={{0,3},{1,2},{2,1},{3,0},{4,7},{5,6},{6,5},{7,4},{8,11},{9,10},{10,... | collective-permute-start | bytes 147464 | tf_op jit(solution)/shard_map/ppermute | solution.py:32
  39.6 0.2 collective-permute-start.1
  39.8 0.2 collective-permute-start
  40.1 0.1 broadcast_select_fusion
  40.2 1.9 %collective-permute-done.2 = bf16[3,32,256]{2,1,0:T(8,128)(2,1)S(1)} collective-permute-done((bf16[3,32,256]{2,1,0:T(8,128)(2,1)S(1)}, bf16[3,32,256]{2,1,0:T(8,128)(2,1)S(1)}, u32[]{:S(2)}, u32[]{:S(2)}) %collective-permute-start.2) | collective-permute-done | bytes 49184 | tf_op jit(solution)/shard_map/ppermute | solution.py:32
  42.1 0.9 %collective-permute-done.1 = bf16[3,32,256]{2,1,0:T(8,128)(2,1)S(1)} collective-permute-done((bf16[3,32,256]{2,1,0:T(8,128)(2,1)S(1)}, bf16[3,32,256]{2,1,0:T(8,128)(2,1)S(1)}, u32[]{:S(2)}, u32[]{:S(2)}) %collective-permute-start.1) | collective-permute-done | bytes 49184 | tf_op jit(solution)/shard_map/ppermute | solution.py:32
  43.0 0.1 multiply_reduce_fusion
  43.1 0.1 reduce_sum.103
  43.2 0.1 copy.134
  43.3 0.1 copy.138
  43.5 0.1 copy.137
  43.6 0.7 copy-done.9
  44.3 0.2 convolution_convert_fusion.1
  44.5 0.8 %maximum_bitcast_fusion = bf16[16,3,2,640]{3,2,1,0:T(2,128)(2,1)} fusion(bf16[3,16,2,1]{3,2,0,1:T(2,128)(2,1)S(1)} %copy.138, bf16[3,16,2,1]{3,2,0,1:T(2,128)(2,1)S(1)} %copy.137, bf16[640]{0:T(1024)(128)(2,1)S(1)} %pad.3.clone, bf16[3,16,2,512]{3,2,1,0:T(2,128)(2,1)S(1)} %concatenate.14), kind=kLoop, calls=%fused_computation.36 | loop fusion | flops 491520 | bytes 222848 | tf_op jit(solution)/shard_map/transpose | solution.py:51
  45.4 3.5 %all-to-all-start.2 = ((bf16[16,3,2,640]{3,2,1,0:T(2,128)(2,1)}), bf16[16,3,2,640]{3,2,1,0:T(2,128)(2,1)S(1)}, u32[]{:S(2)}, u32[]{:S(2)}) async-start(bf16[16,3,2,640]{3,2,1,0:T(2,128)(2,1)} %maximum_bitcast_fusion), calls=%async_computation.2 | async-start | bytes 245760 | tf_op jit(solution)/shard_map/all_to_all | solution.py:52
  48.9 6.7 %all-to-all-done.2 = bf16[16,3,2,640]{3,2,1,0:T(2,128)(2,1)S(1)} async-done(((bf16[16,3,2,640]{3,2,1,0:T(2,128)(2,1)}), bf16[16,3,2,640]{3,2,1,0:T(2,128)(2,1)S(1)}, u32[]{:S(2)}, u32[]{:S(2)}) %all-to-all-start.2) | async-done | bytes 122912 | tf_op jit(solution)/shard_map/all_to_all | solution.py:52
  55.8 0.1 copy.159
  55.9 0.1 copy.160
  56.0 0.1 copy.144
  56.1 0.1 fusion.30
  56.2 0.2 convert_reduce_fusion.2
  56.4 0.1 fusion.4
  56.6 9.9 %all_to_all.20 = bf16[16,3,2,512]{3,2,1,0:T(2,128)(2,1)S(1)} all-to-all(bf16[16,3,2,512]{3,2,1,0:T(2,128)(2,1)S(1)} %broadcast_in_dim.122), channel_id=1, replica_groups=mesh['enc'=16,'dp'=2,'tensor'=4] {'enc'}, dimensions={0} | all-to-all | bytes 196608 | tf_op jit(solution)/shard_map/all_to_all | solution.py:24
  66.7 0.2 convolution_convert_fusion.2
  66.8 3.5 %collective-permute-start.6 = (bf16[3,32,256]{2,1,0:T(8,128)(2,1)S(1)}, bf16[3,32,256]{2,1,0:T(8,128)(2,1)S(1)}, u32[]{:S(2)}, u32[]{:S(2)}) collective-permute-start(bf16[3,32,256]{2,1,0:T(8,128)(2,1)S(1)} %convolution_convert_fusion.2), channel_id=1, source_target_pairs={{0,3},{1,2},{2,1},{3,0},{4,7},{5,6},{6,5},{7,4},{8,11},{9,10},{10,... | collective-permute-start | bytes 147464 | tf_op jit(solution)/shard_map/ppermute | solution.py:32
  70.3 0.6 collective-permute-start.5
  71.0 1.7 %collective-permute-done.6 = bf16[3,32,256]{2,1,0:T(8,128)(2,1)S(1)} collective-permute-done((bf16[3,32,256]{2,1,0:T(8,128)(2,1)S(1)}, bf16[3,32,256]{2,1,0:T(8,128)(2,1)S(1)}, u32[]{:S(2)}, u32[]{:S(2)}) %collective-permute-start.6) | collective-permute-done | bytes 49184 | tf_op jit(solution)/shard_map/ppermute | solution.py:32
  72.6 1.2 %collective-permute-done.5 = bf16[3,32,256]{2,1,0:T(8,128)(2,1)S(1)} collective-permute-done((bf16[3,32,256]{2,1,0:T(8,128)(2,1)S(1)}, bf16[3,32,256]{2,1,0:T(8,128)(2,1)S(1)}, u32[]{:S(2)}, u32[]{:S(2)}) %collective-permute-start.5) | collective-permute-done | bytes 49184 | tf_op jit(solution)/shard_map/ppermute | solution.py:32
  73.9 0.7 add_convert_fusion
  (55 shorter events, 1.0 us)
Async XLA Ops:
  0.0 1.2 %copy-start = (bf16[256,3,512]{2,0,1:T(8,128)(2,1)S(1)}, bf16[256,3,512]{2,0,1:T(8,128)(2,1)}, u32[]{:S(2)}) copy-start(bf16[256,3,512]{2,0,1:T(8,128)(2,1)} %param.19) | copy-start | bytes 2359300
  0.0 1.2 %copy-start.1 = (bf16[3,32,256]{2,1,0:T(8,128)(2,1)S(1)}, bf16[3,32,256]{2,1,0:T(8,128)(2,1)}, u32[]{:S(2)}) copy-start(bf16[3,32,256]{2,1,0:T(8,128)(2,1)} %param.12) | copy-start | bytes 147460
  0.0 1.2 %copy-start.8 = (f32[256]{0:T(256)S(1)}, f32[256]{0:T(256)}, u32[]{:S(2)}) copy-start(f32[256]{0:T(256)} %param.18) | copy-start | bytes 3076
  4.2 17.0 %all-to-all-start = ((bf16[16,3,2,1664]{3,2,1,0:T(2,128)(2,1)}), bf16[16,3,2,1664]{3,2,1,0:T(2,128)(2,1)S(1)}, u32[]{:S(2)}, u32[]{:S(2)}) async-start(bf16[16,3,2,1664]{3,2,1,0:T(2,128)(2,1)} %copy.118), calls=%async_computation | async-start | bytes 638976 | tf_op jit(solution)/shard_map/all_to_all | solution.py:52
  12.8 4.0 %copy-start.5 = (bf16[2,8,2,512]{3,2,1,0:T(2,128)(2,1)S(1)}, bf16[2,8,2,512]{3,2,1,0:T(2,128)(2,1)}, u32[]{:S(2)}) copy-start(bf16[2,8,2,512]{3,2,1,0:T(2,128)(2,1)} %param.13) | copy-start | bytes 98308
  12.8 0.7 copy-start.7
  16.8 0.7 copy-start.10
  17.6 0.7 copy-start.11
  23.3 5.5 %copy-start.6 = (bf16[2,24,2,512]{3,2,1,0:T(2,128)(2,1)S(1)}, bf16[2,24,2,512]{3,2,1,0:T(2,128)(2,1)}, u32[]{:S(2)}) copy-start(bf16[2,24,2,512]{3,2,1,0:T(2,128)(2,1)} %param.14) | copy-start | bytes 294916
  23.3 12.2 %all-to-all-start.1 = ((bf16[16,3,2,512]{3,2,1,0:T(2,128)(2,1)}), bf16[16,3,2,512]{3,2,1,0:T(2,128)(2,1)S(1)}, u32[]{:S(2)}, u32[]{:S(2)}) async-start(bf16[16,3,2,512]{3,2,1,0:T(2,128)(2,1)} %broadcast_in_dim.79), calls=%async_computation.1 | async-start | bytes 196608 | tf_op jit(solution)/shard_map/all_to_all | solution.py:24
  28.8 6.8 %copy-start.3 = (bf16[512,256]{1,0:T(8,128)(2,1)S(1)}, bf16[512,256]{1,0:T(8,128)(2,1)}, u32[]{:S(2)}) copy-start(bf16[512,256]{1,0:T(8,128)(2,1)} %param.20) | copy-start | bytes 786436
  28.8 11.3 %collective-permute-start.3 = (bf16[24,2,512]{2,0,1:T(8,128)(2,1)S(1)}, bf16[24,2,512]{2,0,1:T(8,128)(2,1)S(1)}, u32[]{:S(2)}, u32[]{:S(2)}) collective-permute-start(bf16[24,2,512]{2,0,1:T(8,128)(2,1)S(1)} %get-tuple-element.22), channel_id=1, source_target_pairs={{0,4},{4,0},{1,5},{5,1},{2,6},{6,2},{3,7},{7,3},{8,12},{12,8},{9,1... | collective-permute-start | bytes 147464 | tf_op jit(solution)/shard_map/ppermute | solution.py:80
  35.7 6.3 %collective-permute-start.2 = (bf16[3,32,256]{2,1,0:T(8,128)(2,1)S(1)}, bf16[3,32,256]{2,1,0:T(8,128)(2,1)S(1)}, u32[]{:S(2)}, u32[]{:S(2)}) collective-permute-start(bf16[3,32,256]{2,1,0:T(8,128)(2,1)S(1)} %convolution_convert_fusion.3), channel_id=1, source_target_pairs={{0,3},{1,2},{2,1},{3,0},{4,7},{5,6},{6,5},{7,4},{8,11},{9,10},{10,... | collective-permute-start | bytes 147464 | tf_op jit(solution)/shard_map/ppermute | solution.py:32
  39.6 3.4 %collective-permute-start.1 = (bf16[3,32,256]{2,1,0:T(8,128)(2,1)S(1)}, bf16[3,32,256]{2,1,0:T(8,128)(2,1)S(1)}, u32[]{:S(2)}, u32[]{:S(2)}) collective-permute-start(bf16[3,32,256]{2,1,0:T(8,128)(2,1)S(1)} %convolution_convert_fusion.3), channel_id=1, source_target_pairs={{0,2},{1,3},{2,0},{3,1},{4,6},{5,7},{6,4},{7,5},{8,10},{9,11},{10,... | collective-permute-start | bytes 147464 | tf_op jit(solution)/shard_map/ppermute | solution.py:32
  39.8 3.2 %collective-permute-start = (bf16[3,32,256]{2,1,0:T(8,128)(2,1)S(1)}, bf16[3,32,256]{2,1,0:T(8,128)(2,1)S(1)}, u32[]{:S(2)}, u32[]{:S(2)}) collective-permute-start(bf16[3,32,256]{2,1,0:T(8,128)(2,1)S(1)} %convolution_convert_fusion.3), channel_id=1, source_target_pairs={{0,1},{1,0},{2,3},{3,2},{4,5},{5,4},{6,7},{7,6},{8,9},{9,8},{10,11... | collective-permute-start | bytes 147464 | tf_op jit(solution)/shard_map/ppermute | solution.py:32
  40.2 3.5 %copy-start.2 = (bf16[256,512]{1,0:T(8,128)(2,1)S(1)}, bf16[256,512]{1,0:T(8,128)(2,1)}, u32[]{:S(2)}) copy-start(bf16[256,512]{1,0:T(8,128)(2,1)} %param.22) | copy-start | bytes 786436
  43.6 0.7 copy-start.9
  45.4 10.3 %all-to-all-start.2 = ((bf16[16,3,2,640]{3,2,1,0:T(2,128)(2,1)}), bf16[16,3,2,640]{3,2,1,0:T(2,128)(2,1)S(1)}, u32[]{:S(2)}, u32[]{:S(2)}) async-start(bf16[16,3,2,640]{3,2,1,0:T(2,128)(2,1)} %maximum_bitcast_fusion), calls=%async_computation.2 | async-start | bytes 245760 | tf_op jit(solution)/shard_map/all_to_all | solution.py:52
  56.6 10.0 %copy-start.4 = (bf16[512,256]{1,0:T(8,128)(2,1)S(1)}, bf16[512,256]{1,0:T(8,128)(2,1)}, u32[]{:S(2)}) copy-start(bf16[512,256]{1,0:T(8,128)(2,1)} %param.23) | copy-start | bytes 786436
  66.8 5.8 %collective-permute-start.6 = (bf16[3,32,256]{2,1,0:T(8,128)(2,1)S(1)}, bf16[3,32,256]{2,1,0:T(8,128)(2,1)S(1)}, u32[]{:S(2)}, u32[]{:S(2)}) collective-permute-start(bf16[3,32,256]{2,1,0:T(8,128)(2,1)S(1)} %convolution_convert_fusion.2), channel_id=1, source_target_pairs={{0,3},{1,2},{2,1},{3,0},{4,7},{5,6},{6,5},{7,4},{8,11},{9,10},{10,... | collective-permute-start | bytes 147464 | tf_op jit(solution)/shard_map/ppermute | solution.py:32
  70.3 3.5 %collective-permute-start.5 = (bf16[3,32,256]{2,1,0:T(8,128)(2,1)S(1)}, bf16[3,32,256]{2,1,0:T(8,128)(2,1)S(1)}, u32[]{:S(2)}, u32[]{:S(2)}) collective-permute-start(bf16[3,32,256]{2,1,0:T(8,128)(2,1)S(1)} %convolution_convert_fusion.2), channel_id=1, source_target_pairs={{0,2},{1,3},{2,0},{3,1},{4,6},{5,7},{6,4},{7,5},{8,10},{9,11},{10,... | collective-permute-start | bytes 147464 | tf_op jit(solution)/shard_map/ppermute | solution.py:32
  70.9 2.9 %collective-permute-start.4 = (bf16[3,32,256]{2,1,0:T(8,128)(2,1)S(1)}, bf16[3,32,256]{2,1,0:T(8,128)(2,1)S(1)}, u32[]{:S(2)}, u32[]{:S(2)}) collective-permute-start(bf16[3,32,256]{2,1,0:T(8,128)(2,1)S(1)} %convolution_convert_fusion.2), channel_id=1, source_target_pairs={{0,1},{1,0},{2,3},{3,2},{4,5},{5,4},{6,7},{7,6},{8,9},{9,8},{10,11... | collective-permute-start | bytes 147464 | tf_op jit(solution)/shard_map/ppermute | solution.py:32

commit v6 on v5

--- a/solution.py
+++ b/solution.py
@@ -134,6 +134,8 @@
     )
     cross_usable = token_at[None, :] < my_len[:, None]
 
+    w_q_gained = (gain_cross[:, None] * w_q_cross.astype(jnp.float32)).astype(jnp.bfloat16)
+
     current = hidden_in.astype(jnp.float32)
     scaled = (current * gain_self[None, None, :]).astype(jnp.bfloat16)
     proj = jnp.einsum("tsd,dcw->tscw", scaled, w_qkv, preferred_element_type=jnp.float32)
@@ -168,7 +170,7 @@
         w_new.astype(jnp.float32), axis=-1
     )
     context = (weighted / totals[..., None]).reshape(steps, seq_dev, width).astype(jnp.bfloat16)
-    context, src_late = lax.optimization_barrier((context, src_pool))
+    context, src_late, w_q_gained = lax.optimization_barrier((context, src_pool, w_q_gained))
     cross_kv = exchange_sources(
         src_late, assign, my_sources, block_at, enc_at, dp_at, dp_count, enc_count, seq_dev
     )
@@ -177,8 +179,9 @@
         jnp.einsum("tsw,wf->tsf", context_all, w_out_self, preferred_element_type=jnp.float32)
     )
 
-    scaled = (residual * gain_cross[None, None, :]).astype(jnp.bfloat16)
-    cq = jnp.einsum("tsd,dw->tsw", scaled, w_q_cross, preferred_element_type=jnp.float32)
+    cq = jnp.einsum(
+        "tsd,dw->tsw", residual.astype(jnp.bfloat16), w_q_gained, preferred_element_type=jnp.float32
+    )
     own = rows_reduce_scatter(with_sumsq(cq, residual), seq_dev)
     cross_query = split_norm(own, width).reshape(steps, seq_dev, head_count, DK)
     cross_keys = cross_kv[:, :, 0].reshape(seq_dev, source_len, head_count, DK)

time: 75.1 us -> 75.3 us (level)
  starting transfers between devices: 28.8 us -> 29.8 us
  waiting for transfers between devices: 17.6 us -> 16.8 us
    all_to_all x2, waiting for transfers between devices: 8.01 us -> 7.23 us  [rows_reduce_scatter(): got = lax.all_to_all(send, 'enc', 0, 0, tiled=True)]
    all_to_all x1, starting transfers between devices: 5.48 us -> 6.26 us  [rows_gather(): got = lax.all_to_all(send, 'enc', 0, 0, tiled=True)]
  transfers between devices with their start and end apart: 10 -> 10, of which waited for: 7 -> 7; matrix products, arithmetic and copies ran while one was open for 2% -> 3% of each run, Pallas kernels for 0% -> 0%
where the time goes in v6:
time: 75.3 us; the launch traced here: 74.8 us
  starting transfers between devices  29.8 us (40%)
  waiting for transfers between devices  16.8 us (22%)
  blocking collectives  9.89 us (13%)
  local copies, waits for them, and re-layouts  8.09 us (11%)
  between operations  4.25 us (6%)
  other arithmetic  4.21 us (6%)
  matrix products  1.77 us (2%)
    all_to_all x2, starting transfers between devices, rows_reduce_scatter(): got = lax.all_to_all(send, 'enc', 0, 0, tiled=True)  12.2 us
    all_to_all x1, blocking collectives, rows_gather(): got = lax.all_to_all(send, 'enc', 0, 0, tiled=True)  9.89 us
    ppermute x6, starting transfers between devices, tensor_sum(): lax.ppermute(value, 'tensor', [(i, i ^ k) for i in range(n_t)])  8.44 us
    all_to_all x2, waiting for transfers between devices, rows_reduce_scatter(): got = lax.all_to_all(send, 'enc', 0, 0, tiled=True)  7.23 us
    all_to_all x1, starting transfers between devices, rows_gather(): got = lax.all_to_all(send, 'enc', 0, 0, tiled=True)  6.26 us
    ppermute x6, waiting for transfers between devices, tensor_sum(): lax.ppermute(value, 'tensor', [(i, i ^ k) for i in range(n_t)])  5.79 us
    all_to_all x1, waiting for transfers between devices, rows_gather(): got = lax.all_to_all(send, 'enc', 0, 0, tiled=True)  3.77 us
    unnamed x28, local copies, waits for them, and re-layouts  3.07 us
  transfers between devices with their start and end apart: 10, of which 7 were waited for; matrix products, arithmetic and copies ran while one was open for 3% of the time, Pallas kernels for 0%

profile of v6, /device:TPU:1, one launch (start us, length us, event | category | flops | bytes accessed | tf_op | source)
XLA Modules:
  0.0 74.8 jit_solution(5329190004422343210)
XLA Ops:
  0.0 1.0 %fusion.22 = f32[3,32]{1,0:T(4,128)S(1)} fusion(bf16[3,32,256]{2,1,0:T(8,128)(2,1)} %param.12), kind=kLoop, calls=%fused_computation.39 | loop fusion | flops 73632 | bytes 49536 | tf_op jit(solution)/shard_map/reduce_sum | solution.py:41
  1.0 0.2 copy-done
  1.2 0.3 convolution_convert_fusion
  1.4 0.3 copy.113
  1.7 0.3 convert_element_type.194
  1.9 0.1 reduce_sum.95
  2.0 0.1 copy.114
  2.1 0.1 copy.116
  2.3 0.1 copy.117
  2.4 0.8 %concatenate.13 = bf16[3,16,2,1664]{3,2,1,0:T(2,128)(2,1)S(1)} concatenate(bf16[3,16,2,1536]{3,2,1,0:T(2,128)(2,1)S(1)} %convert_element_type.194, bf16[3,16,2,1]{3,2,1,0:T(2,128)(2,1)S(1)} %copy.116, bf16[3,16,2,1]{3,2,1,0:T(2,128)(2,1)S(1)} %copy.117, bf16[3,16,2,126]{3,2,1,0:T(2,128)(2,1)S(1)} %concatenate.12), dimensions={3} | concatenate | bytes 638976 | tf_op jit(solution)/shard_map/concatenate | solution.py:45
  3.3 0.9 %copy.118 = bf16[16,3,2,1664]{3,2,1,0:T(2,128)(2,1)} copy(bf16[16,3,2,1664]{3,2,0,1:T(2,128)(2,1)S(1)} %bitcast.87) | data formatting | bytes 638976 | tf_op jit(solution)/shard_map/transpose | solution.py:51
  4.2 8.7 %all-to-all-start = ((bf16[16,3,2,1664]{3,2,1,0:T(2,128)(2,1)}), bf16[16,3,2,1664]{3,2,1,0:T(2,128)(2,1)S(1)}, u32[]{:S(2)}, u32[]{:S(2)}) async-start(bf16[16,3,2,1664]{3,2,1,0:T(2,128)(2,1)} %copy.118), calls=%async_computation | async-start | bytes 638976 | tf_op jit(solution)/shard_map/all_to_all | solution.py:52
  13.0 0.6 copy-done.7
  13.6 0.7 fusion.34
  17.0 0.1 slice_reduce_fusion
  17.1 0.5 copy-done.10
  17.8 0.7 copy-done.11
  18.4 0.2 fusion.32
  18.7 0.1 pad.3.clone
  20.1 0.6 copy-done.9
  20.7 0.1 multiply_convert_fusion
  20.8 0.5 all-to-all-done
  21.4 0.1 convert_reduce_fusion
  21.6 0.1 copy.154
  21.7 0.1 copy.155
  21.8 0.1 copy.123
  21.9 0.1 fusion.29
  22.0 0.2 convert_reduce_fusion.4
  22.2 0.1 convolution_bitcast_fusion.2
  22.3 0.1 convert_reduce_fusion.3
  22.5 0.2 fusion.3
  22.7 0.7 broadcast_in_dim.79
  23.4 6.3 %all-to-all-start.1 = ((bf16[16,3,2,512]{3,2,1,0:T(2,128)(2,1)}), bf16[16,3,2,512]{3,2,1,0:T(2,128)(2,1)S(1)}, u32[]{:S(2)}, u32[]{:S(2)}) async-start(bf16[16,3,2,512]{3,2,1,0:T(2,128)(2,1)} %broadcast_in_dim.79), calls=%async_computation.1 | async-start | bytes 196608 | tf_op jit(solution)/shard_map/all_to_all | solution.py:24
  29.7 2.8 %collective-permute-start.3 = (bf16[24,2,512]{2,0,1:T(8,128)(2,1)S(1)}, bf16[24,2,512]{2,0,1:T(8,128)(2,1)S(1)}, u32[]{:S(2)}, u32[]{:S(2)}) collective-permute-start(bf16[24,2,512]{2,0,1:T(8,128)(2,1)S(1)} %get-tuple-element.24), channel_id=1, source_target_pairs={{0,4},{4,0},{1,5},{5,1},{2,6},{6,2},{3,7},{7,3},{8,12},{12,8},{9,1... | collective-permute-start | bytes 147464 | tf_op jit(solution)/shard_map/ppermute | solution.py:80
  32.6 3.8 %all-to-all-done.1 = bf16[16,3,2,512]{3,2,1,0:T(2,128)(2,1)S(1)} async-done(((bf16[16,3,2,512]{3,2,1,0:T(2,128)(2,1)}), bf16[16,3,2,512]{3,2,1,0:T(2,128)(2,1)S(1)}, u32[]{:S(2)}, u32[]{:S(2)}) %all-to-all-start.1) | async-done | bytes 98336 | tf_op jit(solution)/shard_map/all_to_all | solution.py:24
  36.5 0.2 convolution_convert_fusion.3
  36.7 3.8 %collective-permute-start.2 = (bf16[3,32,256]{2,1,0:T(8,128)(2,1)S(1)}, bf16[3,32,256]{2,1,0:T(8,128)(2,1)S(1)}, u32[]{:S(2)}, u32[]{:S(2)}) collective-permute-start(bf16[3,32,256]{2,1,0:T(8,128)(2,1)S(1)} %convolution_convert_fusion.3), channel_id=1, source_target_pairs={{0,3},{1,2},{2,1},{3,0},{4,7},{5,6},{6,5},{7,4},{8,11},{9,10},{10,... | collective-permute-start | bytes 147464 | tf_op jit(solution)/shard_map/ppermute | solution.py:32
  40.5 0.2 collective-permute-start.1
  40.8 0.2 collective-permute-start
  41.0 0.1 broadcast_select_fusion
  41.1 1.9 %collective-permute-done.2 = bf16[3,32,256]{2,1,0:T(8,128)(2,1)S(1)} collective-permute-done((bf16[3,32,256]{2,1,0:T(8,128)(2,1)S(1)}, bf16[3,32,256]{2,1,0:T(8,128)(2,1)S(1)}, u32[]{:S(2)}, u32[]{:S(2)}) %collective-permute-start.2) | collective-permute-done | bytes 49184 | tf_op jit(solution)/shard_map/ppermute | solution.py:32
  43.0 0.9 %collective-permute-done.1 = bf16[3,32,256]{2,1,0:T(8,128)(2,1)S(1)} collective-permute-done((bf16[3,32,256]{2,1,0:T(8,128)(2,1)S(1)}, bf16[3,32,256]{2,1,0:T(8,128)(2,1)S(1)}, u32[]{:S(2)}, u32[]{:S(2)}) %collective-permute-start.1) | collective-permute-done | bytes 49184 | tf_op jit(solution)/shard_map/ppermute | solution.py:32
  43.9 0.1 multiply_reduce_fusion
  44.1 0.1 reduce_sum.103
  44.2 0.1 copy.134
  44.3 0.1 copy.138
  44.4 0.1 copy.137
  44.5 0.2 convolution_convert_fusion.1
  44.8 0.8 %maximum_bitcast_fusion = bf16[16,3,2,640]{3,2,1,0:T(2,128)(2,1)} fusion(bf16[3,16,2,1]{3,2,0,1:T(2,128)(2,1)S(1)} %copy.138, bf16[3,16,2,1]{3,2,0,1:T(2,128)(2,1)S(1)} %copy.137, bf16[640]{0:T(1024)(128)(2,1)S(1)} %pad.3.clone, bf16[3,16,2,512]{3,2,1,0:T(2,128)(2,1)S(1)} %concatenate.14), kind=kLoop, calls=%fused_computation.37 | loop fusion | flops 491520 | bytes 222848 | tf_op jit(solution)/shard_map/transpose | solution.py:51
  45.6 3.5 %all-to-all-start.2 = ((bf16[16,3,2,640]{3,2,1,0:T(2,128)(2,1)}), bf16[16,3,2,640]{3,2,1,0:T(2,128)(2,1)S(1)}, u32[]{:S(2)}, u32[]{:S(2)}) async-start(bf16[16,3,2,640]{3,2,1,0:T(2,128)(2,1)} %maximum_bitcast_fusion), calls=%async_computation.2 | async-start | bytes 245760 | tf_op jit(solution)/shard_map/all_to_all | solution.py:52
  49.2 6.7 %all-to-all-done.2 = bf16[16,3,2,640]{3,2,1,0:T(2,128)(2,1)S(1)} async-done(((bf16[16,3,2,640]{3,2,1,0:T(2,128)(2,1)}), bf16[16,3,2,640]{3,2,1,0:T(2,128)(2,1)S(1)}, u32[]{:S(2)}, u32[]{:S(2)}) %all-to-all-start.2) | async-done | bytes 122912 | tf_op jit(solution)/shard_map/all_to_all | solution.py:52
  56.0 0.1 copy.159
  56.1 0.1 copy.160
  56.2 0.1 copy.144
  56.3 0.1 fusion.30
  56.4 0.2 convert_reduce_fusion.2
  56.6 0.1 fusion.4
  56.9 9.9 %all_to_all.20 = bf16[16,3,2,512]{3,2,1,0:T(2,128)(2,1)S(1)} all-to-all(bf16[16,3,2,512]{3,2,1,0:T(2,128)(2,1)S(1)} %broadcast_in_dim.122), channel_id=1, replica_groups=mesh['enc'=16,'dp'=2,'tensor'=4] {'enc'}, dimensions={0} | all-to-all | bytes 196608 | tf_op jit(solution)/shard_map/all_to_all | solution.py:24
  66.9 0.2 convolution_convert_fusion.2
  67.1 3.5 %collective-permute-start.6 = (bf16[3,32,256]{2,1,0:T(8,128)(2,1)S(1)}, bf16[3,32,256]{2,1,0:T(8,128)(2,1)S(1)}, u32[]{:S(2)}, u32[]{:S(2)}) collective-permute-start(bf16[3,32,256]{2,1,0:T(8,128)(2,1)S(1)} %convolution_convert_fusion.2), channel_id=1, source_target_pairs={{0,3},{1,2},{2,1},{3,0},{4,7},{5,6},{6,5},{7,4},{8,11},{9,10},{10,... | collective-permute-start | bytes 147464 | tf_op jit(solution)/shard_map/ppermute | solution.py:32
  70.6 0.6 collective-permute-start.5
  71.2 1.7 %collective-permute-done.6 = bf16[3,32,256]{2,1,0:T(8,128)(2,1)S(1)} collective-permute-done((bf16[3,32,256]{2,1,0:T(8,128)(2,1)S(1)}, bf16[3,32,256]{2,1,0:T(8,128)(2,1)S(1)}, u32[]{:S(2)}, u32[]{:S(2)}) %collective-permute-start.6) | collective-permute-done | bytes 49184 | tf_op jit(solution)/shard_map/ppermute | solution.py:32
  72.8 1.2 %collective-permute-done.5 = bf16[3,32,256]{2,1,0:T(8,128)(2,1)S(1)} collective-permute-done((bf16[3,32,256]{2,1,0:T(8,128)(2,1)S(1)}, bf16[3,32,256]{2,1,0:T(8,128)(2,1)S(1)}, u32[]{:S(2)}, u32[]{:S(2)}) %collective-permute-start.5) | collective-permute-done | bytes 49184 | tf_op jit(solution)/shard_map/ppermute | solution.py:32
  74.1 0.7 add_convert_fusion
  (56 shorter events, 1.1 us)
Async XLA Ops:
  0.0 1.2 %copy-start = (bf16[256,3,512]{2,0,1:T(8,128)(2,1)S(1)}, bf16[256,3,512]{2,0,1:T(8,128)(2,1)}, u32[]{:S(2)}) copy-start(bf16[256,3,512]{2,0,1:T(8,128)(2,1)} %param.19) | copy-start | bytes 2359300
  0.0 1.2 %copy-start.1 = (bf16[3,32,256]{2,1,0:T(8,128)(2,1)S(1)}, bf16[3,32,256]{2,1,0:T(8,128)(2,1)}, u32[]{:S(2)}) copy-start(bf16[3,32,256]{2,1,0:T(8,128)(2,1)} %param.12) | copy-start | bytes 147460
  0.0 1.2 %copy-start.8 = (f32[256]{0:T(256)S(1)}, f32[256]{0:T(256)}, u32[]{:S(2)}) copy-start(f32[256]{0:T(256)} %param.18) | copy-start | bytes 3076
  4.2 15.9 %copy-start.2 = (bf16[256,512]{1,0:T(8,128)(2,1)S(1)}, bf16[256,512]{1,0:T(8,128)(2,1)}, u32[]{:S(2)}) copy-start(bf16[256,512]{1,0:T(8,128)(2,1)} %param.22) | copy-start | bytes 786436
  4.2 17.2 %all-to-all-start = ((bf16[16,3,2,1664]{3,2,1,0:T(2,128)(2,1)}), bf16[16,3,2,1664]{3,2,1,0:T(2,128)(2,1)S(1)}, u32[]{:S(2)}, u32[]{:S(2)}) async-start(bf16[16,3,2,1664]{3,2,1,0:T(2,128)(2,1)} %copy.118), calls=%async_computation | async-start | bytes 638976 | tf_op jit(solution)/shard_map/all_to_all | solution.py:52
  12.9 4.0 %copy-start.5 = (bf16[2,8,2,512]{3,2,1,0:T(2,128)(2,1)S(1)}, bf16[2,8,2,512]{3,2,1,0:T(2,128)(2,1)}, u32[]{:S(2)}) copy-start(bf16[2,8,2,512]{3,2,1,0:T(2,128)(2,1)} %param.13) | copy-start | bytes 98308
  13.0 0.7 copy-start.7
  16.9 0.7 copy-start.10
  17.8 0.7 copy-start.11
  20.0 0.7 copy-start.9
  23.4 6.3 %copy-start.6 = (bf16[2,24,2,512]{3,2,1,0:T(2,128)(2,1)S(1)}, bf16[2,24,2,512]{3,2,1,0:T(2,128)(2,1)}, u32[]{:S(2)}) copy-start(bf16[2,24,2,512]{3,2,1,0:T(2,128)(2,1)} %param.14) | copy-start | bytes 294916
  23.4 12.9 %all-to-all-start.1 = ((bf16[16,3,2,512]{3,2,1,0:T(2,128)(2,1)}), bf16[16,3,2,512]{3,2,1,0:T(2,128)(2,1)S(1)}, u32[]{:S(2)}, u32[]{:S(2)}) async-start(bf16[16,3,2,512]{3,2,1,0:T(2,128)(2,1)} %broadcast_in_dim.79), calls=%async_computation.1 | async-start | bytes 196608 | tf_op jit(solution)/shard_map/all_to_all | solution.py:24
  29.7 6.8 %copy-start.3 = (bf16[512,256]{1,0:T(8,128)(2,1)S(1)}, bf16[512,256]{1,0:T(8,128)(2,1)}, u32[]{:S(2)}) copy-start(bf16[512,256]{1,0:T(8,128)(2,1)} %param.20) | copy-start | bytes 786436
  29.7 11.3 %collective-permute-start.3 = (bf16[24,2,512]{2,0,1:T(8,128)(2,1)S(1)}, bf16[24,2,512]{2,0,1:T(8,128)(2,1)S(1)}, u32[]{:S(2)}, u32[]{:S(2)}) collective-permute-start(bf16[24,2,512]{2,0,1:T(8,128)(2,1)S(1)} %get-tuple-element.24), channel_id=1, source_target_pairs={{0,4},{4,0},{1,5},{5,1},{2,6},{6,2},{3,7},{7,3},{8,12},{12,8},{9,1... | collective-permute-start | bytes 147464 | tf_op jit(solution)/shard_map/ppermute | solution.py:80
  36.7 6.3 %collective-permute-start.2 = (bf16[3,32,256]{2,1,0:T(8,128)(2,1)S(1)}, bf16[3,32,256]{2,1,0:T(8,128)(2,1)S(1)}, u32[]{:S(2)}, u32[]{:S(2)}) collective-permute-start(bf16[3,32,256]{2,1,0:T(8,128)(2,1)S(1)} %convolution_convert_fusion.3), channel_id=1, source_target_pairs={{0,3},{1,2},{2,1},{3,0},{4,7},{5,6},{6,5},{7,4},{8,11},{9,10},{10,... | collective-permute-start | bytes 147464 | tf_op jit(solution)/shard_map/ppermute | solution.py:32
  40.5 3.4 %collective-permute-start.1 = (bf16[3,32,256]{2,1,0:T(8,128)(2,1)S(1)}, bf16[3,32,256]{2,1,0:T(8,128)(2,1)S(1)}, u32[]{:S(2)}, u32[]{:S(2)}) collective-permute-start(bf16[3,32,256]{2,1,0:T(8,128)(2,1)S(1)} %convolution_convert_fusion.3), channel_id=1, source_target_pairs={{0,2},{1,3},{2,0},{3,1},{4,6},{5,7},{6,4},{7,5},{8,10},{9,11},{10,... | collective-permute-start | bytes 147464 | tf_op jit(solution)/shard_map/ppermute | solution.py:32
  40.8 3.2 %collective-permute-start = (bf16[3,32,256]{2,1,0:T(8,128)(2,1)S(1)}, bf16[3,32,256]{2,1,0:T(8,128)(2,1)S(1)}, u32[]{:S(2)}, u32[]{:S(2)}) collective-permute-start(bf16[3,32,256]{2,1,0:T(8,128)(2,1)S(1)} %convolution_convert_fusion.3), channel_id=1, source_target_pairs={{0,1},{1,0},{2,3},{3,2},{4,5},{5,4},{6,7},{7,6},{8,9},{9,8},{10,11... | collective-permute-start | bytes 147464 | tf_op jit(solution)/shard_map/ppermute | solution.py:32
  45.6 10.3 %all-to-all-start.2 = ((bf16[16,3,2,640]{3,2,1,0:T(2,128)(2,1)}), bf16[16,3,2,640]{3,2,1,0:T(2,128)(2,1)S(1)}, u32[]{:S(2)}, u32[]{:S(2)}) async-start(bf16[16,3,2,640]{3,2,1,0:T(2,128)(2,1)} %maximum_bitcast_fusion), calls=%async_computation.2 | async-start | bytes 245760 | tf_op jit(solution)/shard_map/all_to_all | solution.py:52
  56.8 10.0 %copy-start.4 = (bf16[512,256]{1,0:T(8,128)(2,1)S(1)}, bf16[512,256]{1,0:T(8,128)(2,1)}, u32[]{:S(2)}) copy-start(bf16[512,256]{1,0:T(8,128)(2,1)} %param.23) | copy-start | bytes 786436
  67.1 5.8 %collective-permute-start.6 = (bf16[3,32,256]{2,1,0:T(8,128)(2,1)S(1)}, bf16[3,32,256]{2,1,0:T(8,128)(2,1)S(1)}, u32[]{:S(2)}, u32[]{:S(2)}) collective-permute-start(bf16[3,32,256]{2,1,0:T(8,128)(2,1)S(1)} %convolution_convert_fusion.2), channel_id=1, source_target_pairs={{0,3},{1,2},{2,1},{3,0},{4,7},{5,6},{6,5},{7,4},{8,11},{9,10},{10,... | collective-permute-start | bytes 147464 | tf_op jit(solution)/shard_map/ppermute | solution.py:32
  70.6 3.5 %collective-permute-start.5 = (bf16[3,32,256]{2,1,0:T(8,128)(2,1)S(1)}, bf16[3,32,256]{2,1,0:T(8,128)(2,1)S(1)}, u32[]{:S(2)}, u32[]{:S(2)}) collective-permute-start(bf16[3,32,256]{2,1,0:T(8,128)(2,1)S(1)} %convolution_convert_fusion.2), channel_id=1, source_target_pairs={{0,2},{1,3},{2,0},{3,1},{4,6},{5,7},{6,4},{7,5},{8,10},{9,11},{10,... | collective-permute-start | bytes 147464 | tf_op jit(solution)/shard_map/ppermute | solution.py:32
  71.2 2.9 %collective-permute-start.4 = (bf16[3,32,256]{2,1,0:T(8,128)(2,1)S(1)}, bf16[3,32,256]{2,1,0:T(8,128)(2,1)S(1)}, u32[]{:S(2)}, u32[]{:S(2)}) collective-permute-start(bf16[3,32,256]{2,1,0:T(8,128)(2,1)S(1)} %convolution_convert_fusion.2), channel_id=1, source_target_pairs={{0,1},{1,0},{2,3},{3,2},{4,5},{5,4},{6,7},{7,6},{8,9},{9,8},{10,11... | collective-permute-start | bytes 147464 | tf_op jit(solution)/shard_map/ppermute | solution.py:32

commit v7 on v5

--- a/solution.py
+++ b/solution.py
@@ -40,7 +40,9 @@
 def with_sumsq(partial, rows_in):
     squares = jnp.sum(rows_in * rows_in, axis=-1, keepdims=True)
     high = squares.astype(jnp.bfloat16)
-    low = (squares - high.astype(jnp.float32)).astype(jnp.bfloat16)
+    low = jnp.where(
+        jnp.isfinite(squares), squares - high.astype(jnp.float32), 0.0
+    ).astype(jnp.bfloat16)
     pad = jnp.zeros(rows_in.shape[:-1] + (LANE - 2,), jnp.bfloat16)
     return jnp.concatenate([partial.astype(jnp.bfloat16), high, low, pad], axis=-1)
 

time: 75.1 us -> 75.1 us (level)
  no operation moved by 1% of the time
where the time goes in v7:
time: 75.1 us; the launch traced here: 74.5 us
  starting transfers between devices  28.8 us (38%)
  waiting for transfers between devices  17.6 us (23%)
  blocking collectives  9.89 us (13%)
  local copies, waits for them, and re-layouts  8.11 us (11%)
  between operations  4.25 us (6%)
  other arithmetic  4.11 us (5%)
  matrix products  1.76 us (2%)
    all_to_all x2, starting transfers between devices, rows_reduce_scatter(): got = lax.all_to_all(send, 'enc', 0, 0, tiled=True)  12.1 us
    all_to_all x1, blocking collectives, rows_gather(): got = lax.all_to_all(send, 'enc', 0, 0, tiled=True)  9.89 us
    ppermute x6, starting transfers between devices, tensor_sum(): lax.ppermute(value, 'tensor', [(i, i ^ k) for i in range(n_t)])  8.44 us
    all_to_all x2, waiting for transfers between devices, rows_reduce_scatter(): got = lax.all_to_all(send, 'enc', 0, 0, tiled=True)  8.01 us
    ppermute x6, waiting for transfers between devices, tensor_sum(): lax.ppermute(value, 'tensor', [(i, i ^ k) for i in range(n_t)])  5.78 us
    all_to_all x1, starting transfers between devices, rows_gather(): got = lax.all_to_all(send, 'enc', 0, 0, tiled=True)  5.48 us
    all_to_all x1, waiting for transfers between devices, rows_gather(): got = lax.all_to_all(send, 'enc', 0, 0, tiled=True)  3.77 us
    unnamed x28, local copies, waits for them, and re-layouts  3.08 us
  transfers between devices with their start and end apart: 10, of which 7 were waited for; matrix products, arithmetic and copies ran while one was open for 2% of the time, Pallas kernels for 0%

profile of v7, /device:TPU:1, one launch (start us, length us, event | category | flops | bytes accessed | tf_op | source)
XLA Modules:
  0.0 74.5 jit_solution(1187724550057776385)
XLA Ops:
  0.0 1.0 %fusion.22 = f32[3,32]{1,0:T(4,128)S(1)} fusion(bf16[3,32,256]{2,1,0:T(8,128)(2,1)} %param.12), kind=kLoop, calls=%fused_computation.38 | loop fusion | flops 73632 | bytes 49536 | tf_op jit(solution)/shard_map/reduce_sum | solution.py:41
  1.0 0.2 copy-done
  1.2 0.3 convolution_convert_fusion
  1.4 0.3 copy.125
  1.7 0.3 convert_element_type.188
  1.9 0.1 reduce_sum.95
  2.0 0.1 copy.126
  2.1 0.1 copy.129
  2.3 0.1 copy.130
  2.4 0.8 %concatenate.13 = bf16[3,16,2,1664]{3,2,1,0:T(2,128)(2,1)S(1)} concatenate(bf16[3,16,2,1536]{3,2,1,0:T(2,128)(2,1)S(1)} %convert_element_type.188, bf16[3,16,2,1]{3,2,1,0:T(2,128)(2,1)S(1)} %copy.129, bf16[3,16,2,1]{3,2,1,0:T(2,128)(2,1)S(1)} %copy.130, bf16[3,16,2,126]{3,2,1,0:T(2,128)(2,1)S(1)} %concatenate.12), dimensions={3} | concatenate | bytes 638976 | tf_op jit(solution)/shard_map/concatenate | solution.py:47
  3.3 0.9 %copy.131 = bf16[16,3,2,1664]{3,2,1,0:T(2,128)(2,1)} copy(bf16[16,3,2,1664]{3,2,0,1:T(2,128)(2,1)S(1)} %bitcast.87) | data formatting | bytes 638976 | tf_op jit(solution)/shard_map/transpose | solution.py:53
  4.2 8.6 %all-to-all-start = ((bf16[16,3,2,1664]{3,2,1,0:T(2,128)(2,1)}), bf16[16,3,2,1664]{3,2,1,0:T(2,128)(2,1)S(1)}, u32[]{:S(2)}, u32[]{:S(2)}) async-start(bf16[16,3,2,1664]{3,2,1,0:T(2,128)(2,1)} %copy.131), calls=%async_computation | async-start | bytes 638976 | tf_op jit(solution)/shard_map/all_to_all | solution.py:54
  12.9 0.6 copy-done.7
  13.5 0.7 %fusion.36 = (s32[]{:T(128)}, s32[2]{0:T(128)S(1)}, s32[2]{0:T(128)S(1)}, s32[]{:T(128)}) fusion(s32[]{:T(128)S(6)} %add.96, s32[64]{0:T(128)S(1)} %copy-done.7, s32[]{:T(128)S(6)} %select_n.102, s32[]{:T(128)S(6)} %select_n.110), kind=kLoop, calls=%fused_computation.87 | loop fusion | flops 86 | bytes 52 | tf_op jit(solution)/shard_map/reduce_sum | solution.py:79
  16.8 0.1 slice_reduce_fusion
  17.0 0.5 copy-done.10
  17.5 0.1 iota_compare_fusion.2
  17.6 0.7 copy-done.11
  18.3 0.2 fusion.34
  18.5 0.1 pad.3.clone
  19.9 1.3 %all-to-all-done = bf16[16,3,2,1664]{3,2,1,0:T(2,128)(2,1)S(1)} async-done(((bf16[16,3,2,1664]{3,2,1,0:T(2,128)(2,1)}), bf16[16,3,2,1664]{3,2,1,0:T(2,128)(2,1)S(1)}, u32[]{:S(2)}, u32[]{:S(2)}) %all-to-all-start) | async-done | bytes 319520 | tf_op jit(solution)/shard_map/all_to_all | solution.py:54
  21.2 0.1 convert_reduce_fusion
  21.4 0.1 copy.168
  21.5 0.1 copy.169
  21.6 0.1 copy.136
  21.7 0.1 fusion.29
  21.9 0.2 convert_reduce_fusion.4
  22.1 0.1 convolution_bitcast_fusion.2
  22.2 0.1 convert_reduce_fusion.3
  22.4 0.2 fusion.3
  22.6 0.7 broadcast_in_dim.119
  23.3 5.5 %all-to-all-start.1 = ((bf16[16,3,2,512]{3,2,1,0:T(2,128)(2,1)}), bf16[16,3,2,512]{3,2,1,0:T(2,128)(2,1)S(1)}, u32[]{:S(2)}, u32[]{:S(2)}) async-start(bf16[16,3,2,512]{3,2,1,0:T(2,128)(2,1)} %broadcast_in_dim.119), calls=%async_computation.1 | async-start | bytes 196608 | tf_op jit(solution)/shard_map/all_to_all | solution.py:24
  28.8 2.8 %collective-permute-start.3 = (bf16[24,2,512]{2,0,1:T(8,128)(2,1)S(1)}, bf16[24,2,512]{2,0,1:T(8,128)(2,1)S(1)}, u32[]{:S(2)}, u32[]{:S(2)}) collective-permute-start(bf16[24,2,512]{2,0,1:T(8,128)(2,1)S(1)} %get-tuple-element.22), channel_id=1, source_target_pairs={{0,4},{4,0},{1,5},{5,1},{2,6},{6,2},{3,7},{7,3},{8,12},{12,8},{9,1... | collective-permute-start | bytes 147464 | tf_op jit(solution)/shard_map/ppermute | solution.py:82
  31.7 3.8 %all-to-all-done.1 = bf16[16,3,2,512]{3,2,1,0:T(2,128)(2,1)S(1)} async-done(((bf16[16,3,2,512]{3,2,1,0:T(2,128)(2,1)}), bf16[16,3,2,512]{3,2,1,0:T(2,128)(2,1)S(1)}, u32[]{:S(2)}, u32[]{:S(2)}) %all-to-all-start.1) | async-done | bytes 98336 | tf_op jit(solution)/shard_map/all_to_all | solution.py:24
  35.6 0.2 convolution_convert_fusion.3
  35.7 3.8 %collective-permute-start.2 = (bf16[3,32,256]{2,1,0:T(8,128)(2,1)S(1)}, bf16[3,32,256]{2,1,0:T(8,128)(2,1)S(1)}, u32[]{:S(2)}, u32[]{:S(2)}) collective-permute-start(bf16[3,32,256]{2,1,0:T(8,128)(2,1)S(1)} %convolution_convert_fusion.3), channel_id=1, source_target_pairs={{0,3},{1,2},{2,1},{3,0},{4,7},{5,6},{6,5},{7,4},{8,11},{9,10},{10,... | collective-permute-start | bytes 147464 | tf_op jit(solution)/shard_map/ppermute | solution.py:32
  39.6 0.2 collective-permute-start.1
  39.8 0.2 collective-permute-start
  40.1 0.1 broadcast_select_fusion
  40.2 1.9 %collective-permute-done.2 = bf16[3,32,256]{2,1,0:T(8,128)(2,1)S(1)} collective-permute-done((bf16[3,32,256]{2,1,0:T(8,128)(2,1)S(1)}, bf16[3,32,256]{2,1,0:T(8,128)(2,1)S(1)}, u32[]{:S(2)}, u32[]{:S(2)}) %collective-permute-start.2) | collective-permute-done | bytes 49184 | tf_op jit(solution)/shard_map/ppermute | solution.py:32
  42.1 0.9 %collective-permute-done.1 = bf16[3,32,256]{2,1,0:T(8,128)(2,1)S(1)} collective-permute-done((bf16[3,32,256]{2,1,0:T(8,128)(2,1)S(1)}, bf16[3,32,256]{2,1,0:T(8,128)(2,1)S(1)}, u32[]{:S(2)}, u32[]{:S(2)}) %collective-permute-start.1) | collective-permute-done | bytes 49184 | tf_op jit(solution)/shard_map/ppermute | solution.py:32
  43.0 0.1 multiply_reduce_fusion
  43.1 0.1 reduce_sum.103
  43.2 0.1 copy.147
  43.3 0.1 copy.152
  43.5 0.1 copy.151
  43.6 0.7 copy-done.9
  44.3 0.2 convolution_convert_fusion.1
  44.5 0.8 %maximum_bitcast_fusion = bf16[16,3,2,640]{3,2,1,0:T(2,128)(2,1)} fusion(bf16[3,16,2,1]{3,2,0,1:T(2,128)(2,1)S(1)} %copy.152, bf16[3,16,2,1]{3,2,0,1:T(2,128)(2,1)S(1)} %copy.151, bf16[640]{0:T(1024)(128)(2,1)S(1)} %pad.3.clone, bf16[3,16,2,512]{3,2,1,0:T(2,128)(2,1)S(1)} %concatenate.14), kind=kLoop, calls=%fused_computation.36 | loop fusion | flops 491520 | bytes 222848 | tf_op jit(solution)/shard_map/transpose | solution.py:53
  45.3 3.5 %all-to-all-start.2 = ((bf16[16,3,2,640]{3,2,1,0:T(2,128)(2,1)}), bf16[16,3,2,640]{3,2,1,0:T(2,128)(2,1)S(1)}, u32[]{:S(2)}, u32[]{:S(2)}) async-start(bf16[16,3,2,640]{3,2,1,0:T(2,128)(2,1)} %maximum_bitcast_fusion), calls=%async_computation.2 | async-start | bytes 245760 | tf_op jit(solution)/shard_map/all_to_all | solution.py:54
  48.9 6.7 %all-to-all-done.2 = bf16[16,3,2,640]{3,2,1,0:T(2,128)(2,1)S(1)} async-done(((bf16[16,3,2,640]{3,2,1,0:T(2,128)(2,1)}), bf16[16,3,2,640]{3,2,1,0:T(2,128)(2,1)S(1)}, u32[]{:S(2)}, u32[]{:S(2)}) %all-to-all-start.2) | async-done | bytes 122912 | tf_op jit(solution)/shard_map/all_to_all | solution.py:54
  55.8 0.1 copy.173
  55.9 0.1 copy.174
  56.0 0.1 copy.158
  56.1 0.1 fusion.30
  56.2 0.2 convert_reduce_fusion.2
  56.4 0.1 fusion.4
  56.6 9.9 %all_to_all.20 = bf16[16,3,2,512]{3,2,1,0:T(2,128)(2,1)S(1)} all-to-all(bf16[16,3,2,512]{3,2,1,0:T(2,128)(2,1)S(1)} %broadcast_in_dim.128), channel_id=1, replica_groups=mesh['enc'=16,'dp'=2,'tensor'=4] {'enc'}, dimensions={0} | all-to-all | bytes 196608 | tf_op jit(solution)/shard_map/all_to_all | solution.py:24
  66.6 0.2 convolution_convert_fusion.2
  66.8 3.5 %collective-permute-start.6 = (bf16[3,32,256]{2,1,0:T(8,128)(2,1)S(1)}, bf16[3,32,256]{2,1,0:T(8,128)(2,1)S(1)}, u32[]{:S(2)}, u32[]{:S(2)}) collective-permute-start(bf16[3,32,256]{2,1,0:T(8,128)(2,1)S(1)} %convolution_convert_fusion.2), channel_id=1, source_target_pairs={{0,3},{1,2},{2,1},{3,0},{4,7},{5,6},{6,5},{7,4},{8,11},{9,10},{10,... | collective-permute-start | bytes 147464 | tf_op jit(solution)/shard_map/ppermute | solution.py:32
  70.3 0.6 collective-permute-start.5
  71.0 1.7 %collective-permute-done.6 = bf16[3,32,256]{2,1,0:T(8,128)(2,1)S(1)} collective-permute-done((bf16[3,32,256]{2,1,0:T(8,128)(2,1)S(1)}, bf16[3,32,256]{2,1,0:T(8,128)(2,1)S(1)}, u32[]{:S(2)}, u32[]{:S(2)}) %collective-permute-start.6) | collective-permute-done | bytes 49184 | tf_op jit(solution)/shard_map/ppermute | solution.py:32
  72.6 1.2 %collective-permute-done.5 = bf16[3,32,256]{2,1,0:T(8,128)(2,1)S(1)} collective-permute-done((bf16[3,32,256]{2,1,0:T(8,128)(2,1)S(1)}, bf16[3,32,256]{2,1,0:T(8,128)(2,1)S(1)}, u32[]{:S(2)}, u32[]{:S(2)}) %collective-permute-start.5) | collective-permute-done | bytes 49184 | tf_op jit(solution)/shard_map/ppermute | solution.py:32
  73.9 0.7 add_convert_fusion
  (55 shorter events, 1.0 us)
Async XLA Ops:
  0.0 1.2 %copy-start = (bf16[256,3,512]{2,0,1:T(8,128)(2,1)S(1)}, bf16[256,3,512]{2,0,1:T(8,128)(2,1)}, u32[]{:S(2)}) copy-start(bf16[256,3,512]{2,0,1:T(8,128)(2,1)} %param.19) | copy-start | bytes 2359300
  0.0 1.2 %copy-start.1 = (bf16[3,32,256]{2,1,0:T(8,128)(2,1)S(1)}, bf16[3,32,256]{2,1,0:T(8,128)(2,1)}, u32[]{:S(2)}) copy-start(bf16[3,32,256]{2,1,0:T(8,128)(2,1)} %param.12) | copy-start | bytes 147460
  0.0 1.2 %copy-start.8 = (f32[256]{0:T(256)S(1)}, f32[256]{0:T(256)}, u32[]{:S(2)}) copy-start(f32[256]{0:T(256)} %param.18) | copy-start | bytes 3076
  4.2 17.0 %all-to-all-start = ((bf16[16,3,2,1664]{3,2,1,0:T(2,128)(2,1)}), bf16[16,3,2,1664]{3,2,1,0:T(2,128)(2,1)S(1)}, u32[]{:S(2)}, u32[]{:S(2)}) async-start(bf16[16,3,2,1664]{3,2,1,0:T(2,128)(2,1)} %copy.131), calls=%async_computation | async-start | bytes 638976 | tf_op jit(solution)/shard_map/all_to_all | solution.py:54
  12.8 4.0 %copy-start.5 = (bf16[2,8,2,512]{3,2,1,0:T(2,128)(2,1)S(1)}, bf16[2,8,2,512]{3,2,1,0:T(2,128)(2,1)}, u32[]{:S(2)}) copy-start(bf16[2,8,2,512]{3,2,1,0:T(2,128)(2,1)} %param.13) | copy-start | bytes 98308
  12.8 0.7 copy-start.7
  16.8 0.7 copy-start.10
  17.6 0.7 copy-start.11
  23.3 5.5 %copy-start.6 = (bf16[2,24,2,512]{3,2,1,0:T(2,128)(2,1)S(1)}, bf16[2,24,2,512]{3,2,1,0:T(2,128)(2,1)}, u32[]{:S(2)}) copy-start(bf16[2,24,2,512]{3,2,1,0:T(2,128)(2,1)} %param.14) | copy-start | bytes 294916
  23.3 12.2 %all-to-all-start.1 = ((bf16[16,3,2,512]{3,2,1,0:T(2,128)(2,1)}), bf16[16,3,2,512]{3,2,1,0:T(2,128)(2,1)S(1)}, u32[]{:S(2)}, u32[]{:S(2)}) async-start(bf16[16,3,2,512]{3,2,1,0:T(2,128)(2,1)} %broadcast_in_dim.119), calls=%async_computation.1 | async-start | bytes 196608 | tf_op jit(solution)/shard_map/all_to_all | solution.py:24
  28.8 6.8 %copy-start.3 = (bf16[512,256]{1,0:T(8,128)(2,1)S(1)}, bf16[512,256]{1,0:T(8,128)(2,1)}, u32[]{:S(2)}) copy-start(bf16[512,256]{1,0:T(8,128)(2,1)} %param.20) | copy-start | bytes 786436
  28.8 11.3 %collective-permute-start.3 = (bf16[24,2,512]{2,0,1:T(8,128)(2,1)S(1)}, bf16[24,2,512]{2,0,1:T(8,128)(2,1)S(1)}, u32[]{:S(2)}, u32[]{:S(2)}) collective-permute-start(bf16[24,2,512]{2,0,1:T(8,128)(2,1)S(1)} %get-tuple-element.22), channel_id=1, source_target_pairs={{0,4},{4,0},{1,5},{5,1},{2,6},{6,2},{3,7},{7,3},{8,12},{12,8},{9,1... | collective-permute-start | bytes 147464 | tf_op jit(solution)/shard_map/ppermute | solution.py:82
  35.7 6.3 %collective-permute-start.2 = (bf16[3,32,256]{2,1,0:T(8,128)(2,1)S(1)}, bf16[3,32,256]{2,1,0:T(8,128)(2,1)S(1)}, u32[]{:S(2)}, u32[]{:S(2)}) collective-permute-start(bf16[3,32,256]{2,1,0:T(8,128)(2,1)S(1)} %convolution_convert_fusion.3), channel_id=1, source_target_pairs={{0,3},{1,2},{2,1},{3,0},{4,7},{5,6},{6,5},{7,4},{8,11},{9,10},{10,... | collective-permute-start | bytes 147464 | tf_op jit(solution)/shard_map/ppermute | solution.py:32
  39.6 3.4 %collective-permute-start.1 = (bf16[3,32,256]{2,1,0:T(8,128)(2,1)S(1)}, bf16[3,32,256]{2,1,0:T(8,128)(2,1)S(1)}, u32[]{:S(2)}, u32[]{:S(2)}) collective-permute-start(bf16[3,32,256]{2,1,0:T(8,128)(2,1)S(1)} %convolution_convert_fusion.3), channel_id=1, source_target_pairs={{0,2},{1,3},{2,0},{3,1},{4,6},{5,7},{6,4},{7,5},{8,10},{9,11},{10,... | collective-permute-start | bytes 147464 | tf_op jit(solution)/shard_map/ppermute | solution.py:32
  39.8 3.2 %collective-permute-start = (bf16[3,32,256]{2,1,0:T(8,128)(2,1)S(1)}, bf16[3,32,256]{2,1,0:T(8,128)(2,1)S(1)}, u32[]{:S(2)}, u32[]{:S(2)}) collective-permute-start(bf16[3,32,256]{2,1,0:T(8,128)(2,1)S(1)} %convolution_convert_fusion.3), channel_id=1, source_target_pairs={{0,1},{1,0},{2,3},{3,2},{4,5},{5,4},{6,7},{7,6},{8,9},{9,8},{10,11... | collective-permute-start | bytes 147464 | tf_op jit(solution)/shard_map/ppermute | solution.py:32
  40.2 3.5 %copy-start.2 = (bf16[256,512]{1,0:T(8,128)(2,1)S(1)}, bf16[256,512]{1,0:T(8,128)(2,1)}, u32[]{:S(2)}) copy-start(bf16[256,512]{1,0:T(8,128)(2,1)} %param.22) | copy-start | bytes 786436
  43.6 0.7 copy-start.9
  45.3 10.3 %all-to-all-start.2 = ((bf16[16,3,2,640]{3,2,1,0:T(2,128)(2,1)}), bf16[16,3,2,640]{3,2,1,0:T(2,128)(2,1)S(1)}, u32[]{:S(2)}, u32[]{:S(2)}) async-start(bf16[16,3,2,640]{3,2,1,0:T(2,128)(2,1)} %maximum_bitcast_fusion), calls=%async_computation.2 | async-start | bytes 245760 | tf_op jit(solution)/shard_map/all_to_all | solution.py:54
  56.6 10.0 %copy-start.4 = (bf16[512,256]{1,0:T(8,128)(2,1)S(1)}, bf16[512,256]{1,0:T(8,128)(2,1)}, u32[]{:S(2)}) copy-start(bf16[512,256]{1,0:T(8,128)(2,1)} %param.23) | copy-start | bytes 786436
  66.8 5.8 %collective-permute-start.6 = (bf16[3,32,256]{2,1,0:T(8,128)(2,1)S(1)}, bf16[3,32,256]{2,1,0:T(8,128)(2,1)S(1)}, u32[]{:S(2)}, u32[]{:S(2)}) collective-permute-start(bf16[3,32,256]{2,1,0:T(8,128)(2,1)S(1)} %convolution_convert_fusion.2), channel_id=1, source_target_pairs={{0,3},{1,2},{2,1},{3,0},{4,7},{5,6},{6,5},{7,4},{8,11},{9,10},{10,... | collective-permute-start | bytes 147464 | tf_op jit(solution)/shard_map/ppermute | solution.py:32
  70.3 3.5 %collective-permute-start.5 = (bf16[3,32,256]{2,1,0:T(8,128)(2,1)S(1)}, bf16[3,32,256]{2,1,0:T(8,128)(2,1)S(1)}, u32[]{:S(2)}, u32[]{:S(2)}) collective-permute-start(bf16[3,32,256]{2,1,0:T(8,128)(2,1)S(1)} %convolution_convert_fusion.2), channel_id=1, source_target_pairs={{0,2},{1,3},{2,0},{3,1},{4,6},{5,7},{6,4},{7,5},{8,10},{9,11},{10,... | collective-permute-start | bytes 147464 | tf_op jit(solution)/shard_map/ppermute | solution.py:32
  70.9 2.9 %collective-permute-start.4 = (bf16[3,32,256]{2,1,0:T(8,128)(2,1)S(1)}, bf16[3,32,256]{2,1,0:T(8,128)(2,1)S(1)}, u32[]{:S(2)}, u32[]{:S(2)}) collective-permute-start(bf16[3,32,256]{2,1,0:T(8,128)(2,1)S(1)} %convolution_convert_fusion.2), channel_id=1, source_target_pairs={{0,1},{1,0},{2,3},{3,2},{4,5},{5,4},{6,7},{7,6},{8,9},{9,8},{10,11... | collective-permute-start | bytes 147464 | tf_op jit(solution)/shard_map/ppermute | solution.py:32

commit v8 on v7

--- a/solution.py
+++ b/solution.py
@@ -38,7 +38,13 @@
 
 
 def with_sumsq(partial, rows_in):
-    squares = jnp.sum(rows_in * rows_in, axis=-1, keepdims=True)
+    sq = rows_in * rows_in
+    sq_high = sq.astype(jnp.bfloat16)
+    sq_low = (sq - sq_high.astype(jnp.float32)).astype(jnp.bfloat16)
+    ones = jnp.ones((sq.shape[-1], 1), jnp.bfloat16)
+    squares = jnp.dot(sq_high, ones, preferred_element_type=jnp.float32) + jnp.dot(
+        sq_low, ones, preferred_element_type=jnp.float32
+    )
     high = squares.astype(jnp.bfloat16)
     low = jnp.where(
         jnp.isfinite(squares), squares - high.astype(jnp.float32), 0.0

time: 75.1 us -> 76.1 us (1.013)
  matrix products: 1.76 us -> 3.23 us
  other arithmetic: 4.11 us -> 3.08 us
    dot_general x0 -> x4, matrix products: none -> 1.45 us  [the longest x2 1.15 us: with_sumsq(): jnp.dot(sq_low, ones, preferred_element_type=jnp.float32)]
    concatenate x5 -> x11, local copies, waits for them, and re-layouts: 0.98 us -> 2.24 us  [with_sumsq(): jnp.concatenate([partial.astype(jnp.bfloat16), high, low, pad], axis=-1)]
    reduce_sum x2 -> x0, other arithmetic: 1.08 us -> none  [with_sumsq(): squares = jnp.sum(rows_in * rows_in, axis=-1, keepdims=True)]
where the time goes in v8:
time: 76.1 us; the launch traced here: 75.5 us
  starting transfers between devices  29 us (38%)
  waiting for transfers between devices  17.4 us (23%)
  blocking collectives  9.89 us (13%)
  local copies, waits for them, and re-layouts  8.52 us (11%)
  between operations  4.37 us (6%)
  matrix products  3.23 us (4%)
  other arithmetic  3.08 us (4%)
    all_to_all x2, starting transfers between devices, rows_reduce_scatter(): got = lax.all_to_all(send, 'enc', 0, 0, tiled=True)  12.1 us
    all_to_all x1, blocking collectives, rows_gather(): got = lax.all_to_all(send, 'enc', 0, 0, tiled=True)  9.89 us
    ppermute x6, starting transfers between devices, tensor_sum(): lax.ppermute(value, 'tensor', [(i, i ^ k) for i in range(n_t)])  8.44 us
    all_to_all x2, waiting for transfers between devices, rows_reduce_scatter(): got = lax.all_to_all(send, 'enc', 0, 0, tiled=True)  7.85 us
    ppermute x6, waiting for transfers between devices, tensor_sum(): lax.ppermute(value, 'tensor', [(i, i ^ k) for i in range(n_t)])  5.77 us
    all_to_all x1, starting transfers between devices, rows_gather(): got = lax.all_to_all(send, 'enc', 0, 0, tiled=True)  5.64 us
    all_to_all x1, waiting for transfers between devices, rows_gather(): got = lax.all_to_all(send, 'enc', 0, 0, tiled=True)  3.77 us
    unnamed x28, local copies, waits for them, and re-layouts  3.09 us
  transfers between devices with their start and end apart: 10, of which 7 were waited for; matrix products, arithmetic and copies ran while one was open for 2% of the time, Pallas kernels for 0%

profile of v8, /device:TPU:1, one launch (start us, length us, event | category | flops | bytes accessed | tf_op | source)
XLA Modules:
  0.0 75.5 jit_solution(3256266651029907642)
XLA Ops:
  0.0 1.0 %fusion.32 = f32[1,3,32]{2,0,1:T(1,128)S(1)} fusion(bf16[3,32,256]{2,1,0:T(8,128)(2,1)} %param.12), kind=kOutput, calls=%fused_computation.54 | convolution fusion | flops 196608 | bytes 49536 | tf_op jit(solution)/shard_map/dot_general | solution.py:45
  1.0 0.2 fusion.36
  1.2 0.6 copy-done.8
  1.8 0.3 convolution_convert_fusion
  2.0 0.3 copy.113
  2.3 0.3 convert_element_type.148
  2.6 0.1 concatenate.28
  2.7 0.1 concatenate.29
  2.8 0.8 %concatenate.23 = bf16[3,16,2,1664]{3,2,1,0:T(2,128)(2,1)S(1)} concatenate(bf16[3,16,2,1536]{3,2,1,0:T(2,128)(2,1)S(1)} %convert_element_type.148, bf16[3,16,2,1]{3,2,1,0:T(2,128)(2,1)S(1)} %concatenate.28, bf16[3,16,2,1]{3,2,1,0:T(2,128)(2,1)S(1)} %concatenate.29, bf16[3,16,2,126]{3,2,1,0:T(2,128)(2,1)S(1)} %concatenate.22), dimensions={3} | concatenate | bytes 638976 | tf_op jit(solution)/shard_map/concatenate | solution.py:53
  3.7 0.9 %copy.116 = bf16[16,3,2,1664]{3,2,1,0:T(2,128)(2,1)} copy(bf16[16,3,2,1664]{3,2,0,1:T(2,128)(2,1)S(1)} %bitcast.119) | data formatting | bytes 638976 | tf_op jit(solution)/shard_map/transpose | solution.py:59
  4.6 8.6 %all-to-all-start = ((bf16[16,3,2,1664]{3,2,1,0:T(2,128)(2,1)}), bf16[16,3,2,1664]{3,2,1,0:T(2,128)(2,1)S(1)}, u32[]{:S(2)}, u32[]{:S(2)}) async-start(bf16[16,3,2,1664]{3,2,1,0:T(2,128)(2,1)} %copy.116), calls=%async_computation | async-start | bytes 638976 | tf_op jit(solution)/shard_map/all_to_all | solution.py:60
  13.3 0.6 copy-done.7
  13.9 0.8 %fusion.49 = (s32[]{:T(128)}, s32[2]{0:T(128)S(1)}, s32[2]{0:T(128)S(1)}, s32[]{:T(128)}) fusion(s32[]{:T(128)S(6)} %add.104, s32[64]{0:T(128)S(1)} %copy-done.7, s32[]{:T(128)S(6)} %select_n.86, s32[]{:T(128)S(6)} %select_n.94), kind=kLoop, calls=%fused_computation.100 | loop fusion | flops 86 | bytes 52 | tf_op jit(solution)/shard_map/reduce_sum | solution.py:85
  17.4 0.1 slice_reduce_fusion
  17.5 0.5 copy-done.10
  18.1 0.1 iota_compare_fusion.2
  18.2 0.7 copy-done.11
  18.8 0.2 fusion.41
  19.1 0.1 pad.3.clone
  20.5 1.1 %all-to-all-done = bf16[16,3,2,1664]{3,2,1,0:T(2,128)(2,1)S(1)} async-done(((bf16[16,3,2,1664]{3,2,1,0:T(2,128)(2,1)}), bf16[16,3,2,1664]{3,2,1,0:T(2,128)(2,1)S(1)}, u32[]{:S(2)}, u32[]{:S(2)}) %all-to-all-start) | async-done | bytes 319520 | tf_op jit(solution)/shard_map/all_to_all | solution.py:60
  21.6 0.1 convert_reduce_fusion
  21.8 0.1 copy.154
  21.9 0.1 copy.155
  22.0 0.1 copy.121
  22.1 0.1 fusion.38
  22.3 0.2 convert_reduce_fusion.4
  22.5 0.1 convolution_bitcast_fusion.2
  22.6 0.1 convert_reduce_fusion.3
  22.8 0.2 fusion.3
  23.0 0.7 broadcast_in_dim.117
  23.7 5.6 %all-to-all-start.1 = ((bf16[16,3,2,512]{3,2,1,0:T(2,128)(2,1)}), bf16[16,3,2,512]{3,2,1,0:T(2,128)(2,1)S(1)}, u32[]{:S(2)}, u32[]{:S(2)}) async-start(bf16[16,3,2,512]{3,2,1,0:T(2,128)(2,1)} %broadcast_in_dim.117), calls=%async_computation.1 | async-start | bytes 196608 | tf_op jit(solution)/shard_map/all_to_all | solution.py:24
  29.4 2.8 %collective-permute-start.3 = (bf16[24,2,512]{2,0,1:T(8,128)(2,1)S(1)}, bf16[24,2,512]{2,0,1:T(8,128)(2,1)S(1)}, u32[]{:S(2)}, u32[]{:S(2)}) collective-permute-start(bf16[24,2,512]{2,0,1:T(8,128)(2,1)S(1)} %get-tuple-element.16), channel_id=1, source_target_pairs={{0,4},{4,0},{1,5},{5,1},{2,6},{6,2},{3,7},{7,3},{8,12},{12,8},{9,1... | collective-permute-start | bytes 147464 | tf_op jit(solution)/shard_map/ppermute | solution.py:88
  32.2 3.8 %all-to-all-done.1 = bf16[16,3,2,512]{3,2,1,0:T(2,128)(2,1)S(1)} async-done(((bf16[16,3,2,512]{3,2,1,0:T(2,128)(2,1)}), bf16[16,3,2,512]{3,2,1,0:T(2,128)(2,1)S(1)}, u32[]{:S(2)}, u32[]{:S(2)}) %all-to-all-start.1) | async-done | bytes 98336 | tf_op jit(solution)/shard_map/all_to_all | solution.py:24
  36.1 0.2 convolution_convert_fusion.3
  36.3 3.8 %collective-permute-start.2 = (bf16[3,32,256]{2,1,0:T(8,128)(2,1)S(1)}, bf16[3,32,256]{2,1,0:T(8,128)(2,1)S(1)}, u32[]{:S(2)}, u32[]{:S(2)}) collective-permute-start(bf16[3,32,256]{2,1,0:T(8,128)(2,1)S(1)} %convolution_convert_fusion.3), channel_id=1, source_target_pairs={{0,3},{1,2},{2,1},{3,0},{4,7},{5,6},{6,5},{7,4},{8,11},{9,10},{10,... | collective-permute-start | bytes 147464 | tf_op jit(solution)/shard_map/ppermute | solution.py:32
  40.2 0.3 collective-permute-start.1
  40.4 0.2 collective-permute-start
  40.7 0.1 broadcast_select_fusion
  40.7 1.9 %collective-permute-done.2 = bf16[3,32,256]{2,1,0:T(8,128)(2,1)S(1)} collective-permute-done((bf16[3,32,256]{2,1,0:T(8,128)(2,1)S(1)}, bf16[3,32,256]{2,1,0:T(8,128)(2,1)S(1)}, u32[]{:S(2)}, u32[]{:S(2)}) %collective-permute-start.2) | collective-permute-done | bytes 49184 | tf_op jit(solution)/shard_map/ppermute | solution.py:32
  42.7 0.9 %collective-permute-done.1 = bf16[3,32,256]{2,1,0:T(8,128)(2,1)S(1)} collective-permute-done((bf16[3,32,256]{2,1,0:T(8,128)(2,1)S(1)}, bf16[3,32,256]{2,1,0:T(8,128)(2,1)S(1)}, u32[]{:S(2)}, u32[]{:S(2)}) %collective-permute-start.1) | collective-permute-done | bytes 49184 | tf_op jit(solution)/shard_map/ppermute | solution.py:32
  43.6 0.1 fusion.34
  43.8 0.2 fusion.25
  43.9 0.1 concatenate.26
  44.1 0.4 copy.134
  44.5 0.1 concatenate.25
  44.6 0.4 copy.133
  45.0 0.3 copy-done.9
  45.3 0.2 convolution_convert_fusion.1
  45.5 0.8 %maximum_bitcast_fusion = bf16[16,3,2,640]{3,2,1,0:T(2,128)(2,1)} fusion(bf16[3,16,2,1]{3,2,0,1:T(2,128)(2,1)S(1)} %copy.134, bf16[3,16,2,1]{3,2,0,1:T(2,128)(2,1)S(1)} %copy.133, bf16[640]{0:T(1024)(128)(2,1)S(1)} %pad.3.clone, bf16[3,16,2,512]{3,2,1,0:T(2,128)(2,1)S(1)} %concatenate.24), kind=kLoop, calls=%fused_computation.36 | loop fusion | flops 491520 | bytes 222848 | tf_op jit(solution)/shard_map/transpose | solution.py:59
  46.3 3.5 %all-to-all-start.2 = ((bf16[16,3,2,640]{3,2,1,0:T(2,128)(2,1)}), bf16[16,3,2,640]{3,2,1,0:T(2,128)(2,1)S(1)}, u32[]{:S(2)}, u32[]{:S(2)}) async-start(bf16[16,3,2,640]{3,2,1,0:T(2,128)(2,1)} %maximum_bitcast_fusion), calls=%async_computation.2 | async-start | bytes 245760 | tf_op jit(solution)/shard_map/all_to_all | solution.py:60
  49.9 6.7 %all-to-all-done.2 = bf16[16,3,2,640]{3,2,1,0:T(2,128)(2,1)S(1)} async-done(((bf16[16,3,2,640]{3,2,1,0:T(2,128)(2,1)}), bf16[16,3,2,640]{3,2,1,0:T(2,128)(2,1)S(1)}, u32[]{:S(2)}, u32[]{:S(2)}) %all-to-all-start.2) | async-done | bytes 122912 | tf_op jit(solution)/shard_map/all_to_all | solution.py:60
  56.7 0.1 copy.159
  56.8 0.1 copy.160
  56.9 0.1 copy.140
  57.0 0.1 fusion.39
  57.1 0.2 convert_reduce_fusion.2
  57.4 0.1 fusion.4
  57.6 9.9 %all_to_all.20 = bf16[16,3,2,512]{3,2,1,0:T(2,128)(2,1)S(1)} all-to-all(bf16[16,3,2,512]{3,2,1,0:T(2,128)(2,1)S(1)} %broadcast_in_dim.126), channel_id=1, replica_groups=mesh['enc'=16,'dp'=2,'tensor'=4] {'enc'}, dimensions={0} | all-to-all | bytes 196608 | tf_op jit(solution)/shard_map/all_to_all | solution.py:24
  67.6 0.2 convolution_convert_fusion.2
  67.8 3.5 %collective-permute-start.6 = (bf16[3,32,256]{2,1,0:T(8,128)(2,1)S(1)}, bf16[3,32,256]{2,1,0:T(8,128)(2,1)S(1)}, u32[]{:S(2)}, u32[]{:S(2)}) collective-permute-start(bf16[3,32,256]{2,1,0:T(8,128)(2,1)S(1)} %convolution_convert_fusion.2), channel_id=1, source_target_pairs={{0,3},{1,2},{2,1},{3,0},{4,7},{5,6},{6,5},{7,4},{8,11},{9,10},{10,... | collective-permute-start | bytes 147464 | tf_op jit(solution)/shard_map/ppermute | solution.py:32
  71.3 0.6 collective-permute-start.5
  71.9 1.6 %collective-permute-done.6 = bf16[3,32,256]{2,1,0:T(8,128)(2,1)S(1)} collective-permute-done((bf16[3,32,256]{2,1,0:T(8,128)(2,1)S(1)}, bf16[3,32,256]{2,1,0:T(8,128)(2,1)S(1)}, u32[]{:S(2)}, u32[]{:S(2)}) %collective-permute-start.6) | collective-permute-done | bytes 49184 | tf_op jit(solution)/shard_map/ppermute | solution.py:32
  73.6 1.3 %collective-permute-done.5 = bf16[3,32,256]{2,1,0:T(8,128)(2,1)S(1)} collective-permute-done((bf16[3,32,256]{2,1,0:T(8,128)(2,1)S(1)}, bf16[3,32,256]{2,1,0:T(8,128)(2,1)S(1)}, u32[]{:S(2)}, u32[]{:S(2)}) %collective-permute-start.5) | collective-permute-done | bytes 49184 | tf_op jit(solution)/shard_map/ppermute | solution.py:32
  74.8 0.7 add_convert_fusion
  (56 shorter events, 1.1 us)
Async XLA Ops:
  0.0 1.2 %copy-start = (bf16[256,3,512]{2,0,1:T(8,128)(2,1)S(1)}, bf16[256,3,512]{2,0,1:T(8,128)(2,1)}, u32[]{:S(2)}) copy-start(bf16[256,3,512]{2,0,1:T(8,128)(2,1)} %param.19) | copy-start | bytes 2359300
  0.0 1.0 %copy-start.4 = (bf16[3,32,256]{2,1,0:T(8,128)(2,1)S(1)}, bf16[3,32,256]{2,1,0:T(8,128)(2,1)}, u32[]{:S(2)}) copy-start(bf16[3,32,256]{2,1,0:T(8,128)(2,1)} %param.12) | copy-start | bytes 147460
  1.0 0.7 copy-start.8
  4.6 17.0 %all-to-all-start = ((bf16[16,3,2,1664]{3,2,1,0:T(2,128)(2,1)}), bf16[16,3,2,1664]{3,2,1,0:T(2,128)(2,1)S(1)}, u32[]{:S(2)}, u32[]{:S(2)}) async-start(bf16[16,3,2,1664]{3,2,1,0:T(2,128)(2,1)} %copy.116), calls=%async_computation | async-start | bytes 638976 | tf_op jit(solution)/shard_map/all_to_all | solution.py:60
  13.2 4.1 %copy-start.5 = (bf16[2,8,2,512]{3,2,1,0:T(2,128)(2,1)S(1)}, bf16[2,8,2,512]{3,2,1,0:T(2,128)(2,1)}, u32[]{:S(2)}) copy-start(bf16[2,8,2,512]{3,2,1,0:T(2,128)(2,1)} %param.13) | copy-start | bytes 98308
  13.3 0.7 copy-start.7
  17.3 0.7 copy-start.10
  18.2 0.7 copy-start.11
  23.7 5.7 %copy-start.6 = (bf16[2,24,2,512]{3,2,1,0:T(2,128)(2,1)S(1)}, bf16[2,24,2,512]{3,2,1,0:T(2,128)(2,1)}, u32[]{:S(2)}) copy-start(bf16[2,24,2,512]{3,2,1,0:T(2,128)(2,1)} %param.14) | copy-start | bytes 294916
  23.7 12.3 %all-to-all-start.1 = ((bf16[16,3,2,512]{3,2,1,0:T(2,128)(2,1)}), bf16[16,3,2,512]{3,2,1,0:T(2,128)(2,1)S(1)}, u32[]{:S(2)}, u32[]{:S(2)}) async-start(bf16[16,3,2,512]{3,2,1,0:T(2,128)(2,1)} %broadcast_in_dim.117), calls=%async_computation.1 | async-start | bytes 196608 | tf_op jit(solution)/shard_map/all_to_all | solution.py:24
  29.4 6.8 %copy-start.2 = (bf16[512,256]{1,0:T(8,128)(2,1)S(1)}, bf16[512,256]{1,0:T(8,128)(2,1)}, u32[]{:S(2)}) copy-start(bf16[512,256]{1,0:T(8,128)(2,1)} %param.20) | copy-start | bytes 786436
  29.4 11.2 %collective-permute-start.3 = (bf16[24,2,512]{2,0,1:T(8,128)(2,1)S(1)}, bf16[24,2,512]{2,0,1:T(8,128)(2,1)S(1)}, u32[]{:S(2)}, u32[]{:S(2)}) collective-permute-start(bf16[24,2,512]{2,0,1:T(8,128)(2,1)S(1)} %get-tuple-element.16), channel_id=1, source_target_pairs={{0,4},{4,0},{1,5},{5,1},{2,6},{6,2},{3,7},{7,3},{8,12},{12,8},{9,1... | collective-permute-start | bytes 147464 | tf_op jit(solution)/shard_map/ppermute | solution.py:88
  36.3 6.3 %collective-permute-start.2 = (bf16[3,32,256]{2,1,0:T(8,128)(2,1)S(1)}, bf16[3,32,256]{2,1,0:T(8,128)(2,1)S(1)}, u32[]{:S(2)}, u32[]{:S(2)}) collective-permute-start(bf16[3,32,256]{2,1,0:T(8,128)(2,1)S(1)} %convolution_convert_fusion.3), channel_id=1, source_target_pairs={{0,3},{1,2},{2,1},{3,0},{4,7},{5,6},{6,5},{7,4},{8,11},{9,10},{10,... | collective-permute-start | bytes 147464 | tf_op jit(solution)/shard_map/ppermute | solution.py:32
  40.2 3.4 %collective-permute-start.1 = (bf16[3,32,256]{2,1,0:T(8,128)(2,1)S(1)}, bf16[3,32,256]{2,1,0:T(8,128)(2,1)S(1)}, u32[]{:S(2)}, u32[]{:S(2)}) collective-permute-start(bf16[3,32,256]{2,1,0:T(8,128)(2,1)S(1)} %convolution_convert_fusion.3), channel_id=1, source_target_pairs={{0,2},{1,3},{2,0},{3,1},{4,6},{5,7},{6,4},{7,5},{8,10},{9,11},{10,... | collective-permute-start | bytes 147464 | tf_op jit(solution)/shard_map/ppermute | solution.py:32
  40.4 3.2 %collective-permute-start = (bf16[3,32,256]{2,1,0:T(8,128)(2,1)S(1)}, bf16[3,32,256]{2,1,0:T(8,128)(2,1)S(1)}, u32[]{:S(2)}, u32[]{:S(2)}) collective-permute-start(bf16[3,32,256]{2,1,0:T(8,128)(2,1)S(1)} %convolution_convert_fusion.3), channel_id=1, source_target_pairs={{0,1},{1,0},{2,3},{3,2},{4,5},{5,4},{6,7},{7,6},{8,9},{9,8},{10,11... | collective-permute-start | bytes 147464 | tf_op jit(solution)/shard_map/ppermute | solution.py:32
  40.7 4.3 %copy-start.1 = (bf16[256,512]{1,0:T(8,128)(2,1)S(1)}, bf16[256,512]{1,0:T(8,128)(2,1)}, u32[]{:S(2)}) copy-start(bf16[256,512]{1,0:T(8,128)(2,1)} %param.22) | copy-start | bytes 786436
  44.6 0.7 copy-start.9
  46.3 10.3 %all-to-all-start.2 = ((bf16[16,3,2,640]{3,2,1,0:T(2,128)(2,1)}), bf16[16,3,2,640]{3,2,1,0:T(2,128)(2,1)S(1)}, u32[]{:S(2)}, u32[]{:S(2)}) async-start(bf16[16,3,2,640]{3,2,1,0:T(2,128)(2,1)} %maximum_bitcast_fusion), calls=%async_computation.2 | async-start | bytes 245760 | tf_op jit(solution)/shard_map/all_to_all | solution.py:60
  57.6 10.0 %copy-start.3 = (bf16[512,256]{1,0:T(8,128)(2,1)S(1)}, bf16[512,256]{1,0:T(8,128)(2,1)}, u32[]{:S(2)}) copy-start(bf16[512,256]{1,0:T(8,128)(2,1)} %param.23) | copy-start | bytes 786436
  67.8 5.8 %collective-permute-start.6 = (bf16[3,32,256]{2,1,0:T(8,128)(2,1)S(1)}, bf16[3,32,256]{2,1,0:T(8,128)(2,1)S(1)}, u32[]{:S(2)}, u32[]{:S(2)}) collective-permute-start(bf16[3,32,256]{2,1,0:T(8,128)(2,1)S(1)} %convolution_convert_fusion.2), channel_id=1, source_target_pairs={{0,3},{1,2},{2,1},{3,0},{4,7},{5,6},{6,5},{7,4},{8,11},{9,10},{10,... | collective-permute-start | bytes 147464 | tf_op jit(solution)/shard_map/ppermute | solution.py:32
  71.3 3.5 %collective-permute-start.5 = (bf16[3,32,256]{2,1,0:T(8,128)(2,1)S(1)}, bf16[3,32,256]{2,1,0:T(8,128)(2,1)S(1)}, u32[]{:S(2)}, u32[]{:S(2)}) collective-permute-start(bf16[3,32,256]{2,1,0:T(8,128)(2,1)S(1)} %convolution_convert_fusion.2), channel_id=1, source_target_pairs={{0,2},{1,3},{2,0},{3,1},{4,6},{5,7},{6,4},{7,5},{8,10},{9,11},{10,... | collective-permute-start | bytes 147464 | tf_op jit(solution)/shard_map/ppermute | solution.py:32
  71.9 2.9 %collective-permute-start.4 = (bf16[3,32,256]{2,1,0:T(8,128)(2,1)S(1)}, bf16[3,32,256]{2,1,0:T(8,128)(2,1)S(1)}, u32[]{:S(2)}, u32[]{:S(2)}) collective-permute-start(bf16[3,32,256]{2,1,0:T(8,128)(2,1)S(1)} %convolution_convert_fusion.2), channel_id=1, source_target_pairs={{0,1},{1,0},{2,3},{3,2},{4,5},{5,4},{6,7},{7,6},{8,9},{9,8},{10,11... | collective-permute-start | bytes 147464 | tf_op jit(solution)/shard_map/ppermute | solution.py:32

commit v9 on v7

--- a/solution.py
+++ b/solution.py
@@ -27,14 +27,14 @@
 
 def tensor_sum(value):
     n_t = lax.axis_size("tensor")
-    value = value.astype(jnp.bfloat16)
-    terms = [value] + [
-        lax.ppermute(value, "tensor", [(i, i ^ k) for i in range(n_t)]) for k in range(1, n_t)
-    ]
-    terms = [term.astype(jnp.float32) for term in terms]
-    while len(terms) > 1:
-        terms = [terms[k] + terms[k + 1] for k in range(0, len(terms), 2)]
-    return terms[0]
+    value = value.astype(jnp.bfloat16).astype(jnp.float32)
+    bit = 1
+    while bit < n_t:
+        sent = value.astype(jnp.bfloat16) if bit == 1 else value
+        other = lax.ppermute(sent, "tensor", [(i, i ^ bit) for i in range(n_t)])
+        value = value + other.astype(jnp.float32)
+        bit *= 2
+    return value
 
 
 def with_sumsq(partial, rows_in):

time: 75.1 us -> 77.9 us (1.037)
  waiting for transfers between devices: 17.6 us -> 21.6 us
  starting transfers between devices: 28.8 us -> 27 us
  local copies, waits for them, and re-layouts: 8.11 us -> 8.97 us
    all_to_all x2, waiting for transfers between devices: 8.01 us -> 11.2 us  [rows_reduce_scatter(): got = lax.all_to_all(send, 'enc', 0, 0, tiled=True)]
    all_to_all x1, starting transfers between devices: 5.48 us -> 3.64 us  [rows_gather(): got = lax.all_to_all(send, 'enc', 0, 0, tiled=True)]
    ppermute x1, waiting for transfers between devices: 0.01 us -> 1.61 us  [exchange_sources(): lax.ppermute(piece, 'dp', [(i, (i + shift) % dp_count) for i in range(dp_...]
    all_to_all x1, waiting for transfers between devices: 3.77 us -> 2.86 us  [rows_gather(): got = lax.all_to_all(send, 'enc', 0, 0, tiled=True)]
    unnamed x28, local copies, waits for them, and re-layouts: 3.08 us -> 3.95 us
    ppermute x6 -> x4, waiting for transfers between devices: 5.78 us -> 5.96 us  [tensor_sum(): other = lax.ppermute(sent, 'tensor', [(i, i ^ bit) for i in range(n_t)])]
    ppermute x6 -> x4, starting transfers between devices: 8.44 us -> 8.28 us  [tensor_sum(): other = lax.ppermute(sent, 'tensor', [(i, i ^ bit) for i in range(n_t)])]
  transfers between devices with their start and end apart: 10 -> 8, of which waited for: 7 -> 7; matrix products, arithmetic and copies ran while one was open for 2% -> 2% of each run, Pallas kernels for 0% -> 0%
where the time goes in v9:
time: 77.9 us; the launch traced here: 77.3 us
  starting transfers between devices  27 us (35%)
  waiting for transfers between devices  21.6 us (28%)
  blocking collectives  9.9 us (13%)
  local copies, waits for them, and re-layouts  8.97 us (12%)
  other arithmetic  4.08 us (5%)
  between operations  4.01 us (5%)
  matrix products  1.77 us (2%)
    all_to_all x2, starting transfers between devices, rows_reduce_scatter(): got = lax.all_to_all(send, 'enc', 0, 0, tiled=True)  12.2 us
    all_to_all x2, waiting for transfers between devices, rows_reduce_scatter(): got = lax.all_to_all(send, 'enc', 0, 0, tiled=True)  11.2 us
    all_to_all x1, blocking collectives, rows_gather(): got = lax.all_to_all(send, 'enc', 0, 0, tiled=True)  9.9 us
    ppermute x4, starting transfers between devices, tensor_sum(): other = lax.ppermute(sent, 'tensor', [(i, i ^ bit) for i in range(n_t)])  8.28 us
    ppermute x4, waiting for transfers between devices, tensor_sum(): other = lax.ppermute(sent, 'tensor', [(i, i ^ bit) for i in range(n_t)])  5.96 us
    unnamed x28, local copies, waits for them, and re-layouts  3.95 us
    all_to_all x1, starting transfers between devices, rows_gather(): got = lax.all_to_all(send, 'enc', 0, 0, tiled=True)  3.64 us
    all_to_all x1, waiting for transfers between devices, rows_gather(): got = lax.all_to_all(send, 'enc', 0, 0, tiled=True)  2.86 us
  transfers between devices with their start and end apart: 8, of which 7 were waited for; matrix products, arithmetic and copies ran while one was open for 2% of the time, Pallas kernels for 0%

profile of v9, /device:TPU:1, one launch (start us, length us, event | category | flops | bytes accessed | tf_op | source)
XLA Modules:
  0.0 77.3 jit_solution(11564864223519937544)
XLA Ops:
  0.0 1.0 %fusion.22 = f32[3,32]{1,0:T(4,128)S(1)} fusion(bf16[3,32,256]{2,1,0:T(8,128)(2,1)} %param.12), kind=kLoop, calls=%fused_computation.38 | loop fusion | flops 73632 | bytes 49536 | tf_op jit(solution)/shard_map/reduce_sum | solution.py:41
  1.0 0.2 copy-done
  1.2 0.3 convolution_convert_fusion
  1.4 0.3 copy.125
  1.7 0.3 convert_element_type.178
  1.9 0.1 reduce_sum.95
  2.0 0.1 copy.126
  2.1 0.1 copy.129
  2.3 0.1 copy.130
  2.4 0.8 %concatenate.13 = bf16[3,16,2,1664]{3,2,1,0:T(2,128)(2,1)S(1)} concatenate(bf16[3,16,2,1536]{3,2,1,0:T(2,128)(2,1)S(1)} %convert_element_type.178, bf16[3,16,2,1]{3,2,1,0:T(2,128)(2,1)S(1)} %copy.129, bf16[3,16,2,1]{3,2,1,0:T(2,128)(2,1)S(1)} %copy.130, bf16[3,16,2,126]{3,2,1,0:T(2,128)(2,1)S(1)} %concatenate.12), dimensions={3} | concatenate | bytes 638976 | tf_op jit(solution)/shard_map/concatenate | solution.py:47
  3.3 0.9 %copy.131 = bf16[16,3,2,1664]{3,2,1,0:T(2,128)(2,1)} copy(bf16[16,3,2,1664]{3,2,0,1:T(2,128)(2,1)S(1)} %bitcast.87) | data formatting | bytes 638976 | tf_op jit(solution)/shard_map/transpose | solution.py:53
  4.2 8.6 %all-to-all-start = ((bf16[16,3,2,1664]{3,2,1,0:T(2,128)(2,1)}), bf16[16,3,2,1664]{3,2,1,0:T(2,128)(2,1)S(1)}, u32[]{:S(2)}, u32[]{:S(2)}) async-start(bf16[16,3,2,1664]{3,2,1,0:T(2,128)(2,1)} %copy.131), calls=%async_computation | async-start | bytes 638976 | tf_op jit(solution)/shard_map/all_to_all | solution.py:54
  12.8 0.7 copy-done.5
  13.6 0.1 slice_reduce_fusion
  13.7 0.6 copy-done.10
  14.4 0.1 iota_compare_fusion.2
  14.5 0.7 copy-done.7
  15.2 0.7 fusion.36
  15.9 0.7 copy-done.11
  16.5 0.2 fusion.34
  16.8 4.4 %all-to-all-done = bf16[16,3,2,1664]{3,2,1,0:T(2,128)(2,1)S(1)} async-done(((bf16[16,3,2,1664]{3,2,1,0:T(2,128)(2,1)}), bf16[16,3,2,1664]{3,2,1,0:T(2,128)(2,1)S(1)}, u32[]{:S(2)}, u32[]{:S(2)}) %all-to-all-start) | async-done | bytes 319520 | tf_op jit(solution)/shard_map/all_to_all | solution.py:54
  21.2 0.1 convert_reduce_fusion
  21.4 0.1 copy.168
  21.5 0.1 copy.169
  21.6 0.1 copy.136
  21.7 0.1 fusion.29
  21.9 0.2 convert_reduce_fusion.4
  22.1 0.1 convolution_bitcast_fusion.2
  22.2 0.1 convert_reduce_fusion.3
  22.4 0.2 fusion.3
  22.6 0.7 broadcast_in_dim.119
  23.3 3.6 %all-to-all-start.1 = ((bf16[16,3,2,512]{3,2,1,0:T(2,128)(2,1)}), bf16[16,3,2,512]{3,2,1,0:T(2,128)(2,1)S(1)}, u32[]{:S(2)}, u32[]{:S(2)}) async-start(bf16[16,3,2,512]{3,2,1,0:T(2,128)(2,1)} %broadcast_in_dim.119), calls=%async_computation.1 | async-start | bytes 196608 | tf_op jit(solution)/shard_map/all_to_all | solution.py:24
  29.4 0.1 pad.3.clone
  30.7 2.9 %all-to-all-done.1 = bf16[16,3,2,512]{3,2,1,0:T(2,128)(2,1)S(1)} async-done(((bf16[16,3,2,512]{3,2,1,0:T(2,128)(2,1)}), bf16[16,3,2,512]{3,2,1,0:T(2,128)(2,1)S(1)}, u32[]{:S(2)}, u32[]{:S(2)}) %all-to-all-start.1) | async-done | bytes 98336 | tf_op jit(solution)/shard_map/all_to_all | solution.py:24
  33.7 0.2 convolution_convert_fusion.3
  33.9 3.0 %collective-permute-start = (bf16[3,32,256]{2,1,0:T(8,128)(2,1)S(1)}, bf16[3,32,256]{2,1,0:T(8,128)(2,1)S(1)}, u32[]{:S(2)}, u32[]{:S(2)}) collective-permute-start(bf16[3,32,256]{2,1,0:T(8,128)(2,1)S(1)} %convolution_convert_fusion.3), channel_id=1, source_target_pairs={{0,1},{1,0},{2,3},{3,2},{4,5},{5,4},{6,7},{7,6},{8,9},{9,8},{10,11... | collective-permute-start | bytes 147464 | tf_op jit(solution)/shard_map/ppermute | solution.py:34
  36.9 2.8 %collective-permute-start.2 = (bf16[24,2,512]{2,0,1:T(8,128)(2,1)S(1)}, bf16[24,2,512]{2,0,1:T(8,128)(2,1)S(1)}, u32[]{:S(2)}, u32[]{:S(2)}) collective-permute-start(bf16[24,2,512]{2,0,1:T(8,128)(2,1)S(1)} %get-tuple-element.22), channel_id=1, source_target_pairs={{0,4},{4,0},{1,5},{5,1},{2,6},{6,2},{3,7},{7,3},{8,12},{12,8},{9,1... | collective-permute-start | bytes 147464 | tf_op jit(solution)/shard_map/ppermute | solution.py:82
  39.8 0.4 collective-permute-start.1
  40.1 1.6 %collective-permute-done.2 = bf16[24,2,512]{2,0,1:T(8,128)(2,1)S(1)} collective-permute-done((bf16[24,2,512]{2,0,1:T(8,128)(2,1)S(1)}, bf16[24,2,512]{2,0,1:T(8,128)(2,1)S(1)}, u32[]{:S(2)}, u32[]{:S(2)}) %collective-permute-start.2) | collective-permute-done | bytes 49184 | tf_op jit(solution)/shard_map/ppermute | solution.py:82
  41.8 0.1 broadcast_select_fusion
  41.8 2.0 %collective-permute-done.1 = f32[3,32,256]{2,1,0:T(8,128)S(1)} collective-permute-done((f32[3,32,256]{2,1,0:T(8,128)S(1)}, f32[3,32,256]{2,1,0:T(8,128)S(1)}, u32[]{:S(2)}, u32[]{:S(2)}) %collective-permute-start.1) | collective-permute-done | bytes 98336 | tf_op jit(solution)/shard_map/ppermute | solution.py:34
  43.9 0.1 multiply_reduce_fusion
  44.0 0.1 reduce_sum.103
  44.1 0.1 copy.147
  44.2 0.1 copy.152
  44.3 0.1 copy.151
  44.5 0.7 copy-done.9
  45.1 0.2 convolution_convert_fusion.1
  45.4 0.8 %maximum_bitcast_fusion = bf16[16,3,2,640]{3,2,1,0:T(2,128)(2,1)} fusion(bf16[3,16,2,1]{3,2,0,1:T(2,128)(2,1)S(1)} %copy.152, bf16[3,16,2,1]{3,2,0,1:T(2,128)(2,1)S(1)} %copy.151, bf16[640]{0:T(1024)(128)(2,1)S(1)} %pad.3.clone, bf16[3,16,2,512]{3,2,1,0:T(2,128)(2,1)S(1)} %concatenate.14), kind=kLoop, calls=%fused_computation.36 | loop fusion | flops 491520 | bytes 222848 | tf_op jit(solution)/shard_map/transpose | solution.py:53
  46.2 3.7 %all-to-all-start.2 = ((bf16[16,3,2,640]{3,2,1,0:T(2,128)(2,1)}), bf16[16,3,2,640]{3,2,1,0:T(2,128)(2,1)S(1)}, u32[]{:S(2)}, u32[]{:S(2)}) async-start(bf16[16,3,2,640]{3,2,1,0:T(2,128)(2,1)} %maximum_bitcast_fusion), calls=%async_computation.2 | async-start | bytes 245760 | tf_op jit(solution)/shard_map/all_to_all | solution.py:54
  49.9 6.7 %all-to-all-done.2 = bf16[16,3,2,640]{3,2,1,0:T(2,128)(2,1)S(1)} async-done(((bf16[16,3,2,640]{3,2,1,0:T(2,128)(2,1)}), bf16[16,3,2,640]{3,2,1,0:T(2,128)(2,1)S(1)}, u32[]{:S(2)}, u32[]{:S(2)}) %all-to-all-start.2) | async-done | bytes 122912 | tf_op jit(solution)/shard_map/all_to_all | solution.py:54
  56.8 0.1 copy.173
  56.9 0.1 copy.174
  57.0 0.1 copy.158
  57.1 0.1 fusion.30
  57.2 0.2 convert_reduce_fusion.2
  57.4 0.1 fusion.4
  57.6 9.9 %all_to_all.20 = bf16[16,3,2,512]{3,2,1,0:T(2,128)(2,1)S(1)} all-to-all(bf16[16,3,2,512]{3,2,1,0:T(2,128)(2,1)S(1)} %broadcast_in_dim.128), channel_id=1, replica_groups=mesh['enc'=16,'dp'=2,'tensor'=4] {'enc'}, dimensions={0} | all-to-all | bytes 196608 | tf_op jit(solution)/shard_map/all_to_all | solution.py:24
  67.7 0.2 convolution_convert_fusion.2
  67.8 3.8 %collective-permute-start.3 = (bf16[3,32,256]{2,1,0:T(8,128)(2,1)S(1)}, bf16[3,32,256]{2,1,0:T(8,128)(2,1)S(1)}, u32[]{:S(2)}, u32[]{:S(2)}) collective-permute-start(bf16[3,32,256]{2,1,0:T(8,128)(2,1)S(1)} %convolution_convert_fusion.2), channel_id=1, source_target_pairs={{0,1},{1,0},{2,3},{3,2},{4,5},{5,4},{6,7},{7,6},{8,9},{9,8},{10,11... | collective-permute-start | bytes 147464 | tf_op jit(solution)/shard_map/ppermute | solution.py:34
  71.7 0.9 %collective-permute-done.3 = bf16[3,32,256]{2,1,0:T(8,128)(2,1)S(1)} collective-permute-done((bf16[3,32,256]{2,1,0:T(8,128)(2,1)S(1)}, bf16[3,32,256]{2,1,0:T(8,128)(2,1)S(1)}, u32[]{:S(2)}, u32[]{:S(2)}) %collective-permute-start.3) | collective-permute-done | bytes 49184 | tf_op jit(solution)/shard_map/ppermute | solution.py:34
  72.6 1.0 %collective-permute-start.4 = (f32[3,32,256]{2,1,0:T(8,128)S(1)}, f32[3,32,256]{2,1,0:T(8,128)S(1)}, u32[]{:S(2)}, u32[]{:S(2)}) collective-permute-start(f32[3,32,256]{2,1,0:T(8,128)S(1)} %convert_add_fusion.1), channel_id=1, source_target_pairs={{0,2},{1,3},{2,0},{3,1},{4,6},{5,7},{6,4},{7,5},{8,10},{9,11},{10,... | collective-permute-start | bytes 294920 | tf_op jit(solution)/shard_map/ppermute | solution.py:34
  73.6 3.1 %collective-permute-done.4 = f32[3,32,256]{2,1,0:T(8,128)S(1)} collective-permute-done((f32[3,32,256]{2,1,0:T(8,128)S(1)}, f32[3,32,256]{2,1,0:T(8,128)S(1)}, u32[]{:S(2)}, u32[]{:S(2)}) %collective-permute-start.4) | collective-permute-done | bytes 98336 | tf_op jit(solution)/shard_map/ppermute | solution.py:34
  76.6 0.6 add_convert_fusion
  (53 shorter events, 1.0 us)
Async XLA Ops:
  0.0 1.2 %copy-start = (bf16[256,3,512]{2,0,1:T(8,128)(2,1)S(1)}, bf16[256,3,512]{2,0,1:T(8,128)(2,1)}, u32[]{:S(2)}) copy-start(bf16[256,3,512]{2,0,1:T(8,128)(2,1)} %param.19) | copy-start | bytes 2359300
  0.0 1.2 %copy-start.1 = (bf16[3,32,256]{2,1,0:T(8,128)(2,1)S(1)}, bf16[3,32,256]{2,1,0:T(8,128)(2,1)}, u32[]{:S(2)}) copy-start(bf16[3,32,256]{2,1,0:T(8,128)(2,1)} %param.12) | copy-start | bytes 147460
  0.0 1.2 %copy-start.8 = (f32[256]{0:T(256)S(1)}, f32[256]{0:T(256)}, u32[]{:S(2)}) copy-start(f32[256]{0:T(256)} %param.18) | copy-start | bytes 3076
  4.2 17.0 %all-to-all-start = ((bf16[16,3,2,1664]{3,2,1,0:T(2,128)(2,1)}), bf16[16,3,2,1664]{3,2,1,0:T(2,128)(2,1)S(1)}, u32[]{:S(2)}, u32[]{:S(2)}) async-start(bf16[16,3,2,1664]{3,2,1,0:T(2,128)(2,1)} %copy.131), calls=%async_computation | async-start | bytes 638976 | tf_op jit(solution)/shard_map/all_to_all | solution.py:54
  12.8 0.8 copy-start.5
  13.7 0.7 copy-start.10
  14.5 0.7 copy-start.7
  15.9 0.7 copy-start.11
  23.3 7.4 %copy-start.6 = (bf16[2,24,2,512]{3,2,1,0:T(2,128)(2,1)S(1)}, bf16[2,24,2,512]{3,2,1,0:T(2,128)(2,1)}, u32[]{:S(2)}) copy-start(bf16[2,24,2,512]{3,2,1,0:T(2,128)(2,1)} %param.14) | copy-start | bytes 294916
  23.3 10.3 %all-to-all-start.1 = ((bf16[16,3,2,512]{3,2,1,0:T(2,128)(2,1)}), bf16[16,3,2,512]{3,2,1,0:T(2,128)(2,1)S(1)}, u32[]{:S(2)}, u32[]{:S(2)}) async-start(bf16[16,3,2,512]{3,2,1,0:T(2,128)(2,1)} %broadcast_in_dim.119), calls=%async_computation.1 | async-start | bytes 196608 | tf_op jit(solution)/shard_map/all_to_all | solution.py:24
  30.7 3.0 %copy-start.3 = (bf16[512,256]{1,0:T(8,128)(2,1)S(1)}, bf16[512,256]{1,0:T(8,128)(2,1)}, u32[]{:S(2)}) copy-start(bf16[512,256]{1,0:T(8,128)(2,1)} %param.20) | copy-start | bytes 786436
  33.9 5.9 %collective-permute-start = (bf16[3,32,256]{2,1,0:T(8,128)(2,1)S(1)}, bf16[3,32,256]{2,1,0:T(8,128)(2,1)S(1)}, u32[]{:S(2)}, u32[]{:S(2)}) collective-permute-start(bf16[3,32,256]{2,1,0:T(8,128)(2,1)S(1)} %convolution_convert_fusion.3), channel_id=1, source_target_pairs={{0,1},{1,0},{2,3},{3,2},{4,5},{5,4},{6,7},{7,6},{8,9},{9,8},{10,11... | collective-permute-start | bytes 147464 | tf_op jit(solution)/shard_map/ppermute | solution.py:34
  36.9 4.8 %collective-permute-start.2 = (bf16[24,2,512]{2,0,1:T(8,128)(2,1)S(1)}, bf16[24,2,512]{2,0,1:T(8,128)(2,1)S(1)}, u32[]{:S(2)}, u32[]{:S(2)}) collective-permute-start(bf16[24,2,512]{2,0,1:T(8,128)(2,1)S(1)} %get-tuple-element.22), channel_id=1, source_target_pairs={{0,4},{4,0},{1,5},{5,1},{2,6},{6,2},{3,7},{7,3},{8,12},{12,8},{9,1... | collective-permute-start | bytes 147464 | tf_op jit(solution)/shard_map/ppermute | solution.py:82
  39.8 4.1 %collective-permute-start.1 = (f32[3,32,256]{2,1,0:T(8,128)S(1)}, f32[3,32,256]{2,1,0:T(8,128)S(1)}, u32[]{:S(2)}, u32[]{:S(2)}) collective-permute-start(f32[3,32,256]{2,1,0:T(8,128)S(1)} %convert_add_fusion.2), channel_id=1, source_target_pairs={{0,2},{1,3},{2,0},{3,1},{4,6},{5,7},{6,4},{7,5},{8,10},{9,11},{10,... | collective-permute-start | bytes 294920 | tf_op jit(solution)/shard_map/ppermute | solution.py:34
  41.8 2.6 %copy-start.2 = (bf16[256,512]{1,0:T(8,128)(2,1)S(1)}, bf16[256,512]{1,0:T(8,128)(2,1)}, u32[]{:S(2)}) copy-start(bf16[256,512]{1,0:T(8,128)(2,1)} %param.22) | copy-start | bytes 786436
  44.4 0.7 copy-start.9
  46.2 10.5 %all-to-all-start.2 = ((bf16[16,3,2,640]{3,2,1,0:T(2,128)(2,1)}), bf16[16,3,2,640]{3,2,1,0:T(2,128)(2,1)S(1)}, u32[]{:S(2)}, u32[]{:S(2)}) async-start(bf16[16,3,2,640]{3,2,1,0:T(2,128)(2,1)} %maximum_bitcast_fusion), calls=%async_computation.2 | async-start | bytes 245760 | tf_op jit(solution)/shard_map/all_to_all | solution.py:54
  57.6 10.0 %copy-start.4 = (bf16[512,256]{1,0:T(8,128)(2,1)S(1)}, bf16[512,256]{1,0:T(8,128)(2,1)}, u32[]{:S(2)}) copy-start(bf16[512,256]{1,0:T(8,128)(2,1)} %param.23) | copy-start | bytes 786436
  67.8 4.7 %collective-permute-start.3 = (bf16[3,32,256]{2,1,0:T(8,128)(2,1)S(1)}, bf16[3,32,256]{2,1,0:T(8,128)(2,1)S(1)}, u32[]{:S(2)}, u32[]{:S(2)}) collective-permute-start(bf16[3,32,256]{2,1,0:T(8,128)(2,1)S(1)} %convolution_convert_fusion.2), channel_id=1, source_target_pairs={{0,1},{1,0},{2,3},{3,2},{4,5},{5,4},{6,7},{7,6},{8,9},{9,8},{10,11... | collective-permute-start | bytes 147464 | tf_op jit(solution)/shard_map/ppermute | solution.py:34
  72.6 4.1 %collective-permute-start.4 = (f32[3,32,256]{2,1,0:T(8,128)S(1)}, f32[3,32,256]{2,1,0:T(8,128)S(1)}, u32[]{:S(2)}, u32[]{:S(2)}) collective-permute-start(f32[3,32,256]{2,1,0:T(8,128)S(1)} %convert_add_fusion.1), channel_id=1, source_target_pairs={{0,2},{1,3},{2,0},{3,1},{4,6},{5,7},{6,4},{7,5},{8,10},{9,11},{10,... | collective-permute-start | bytes 294920 | tf_op jit(solution)/shard_map/ppermute | solution.py:34

commit v10 on v7

--- a/solution.py
+++ b/solution.py
@@ -138,8 +138,13 @@
 
     current = hidden_in.astype(jnp.float32)
     scaled = (current * gain_self[None, None, :]).astype(jnp.bfloat16)
-    proj = jnp.einsum("tsd,dcw->tscw", scaled, w_qkv, preferred_element_type=jnp.float32)
-    proj = proj.reshape(steps, current.shape[1], 3 * width)
+    proj = jnp.concatenate(
+        [
+            jnp.einsum("tsd,dw->tsw", scaled, w_qkv[:, part], preferred_element_type=jnp.float32)
+            for part in range(3)
+        ],
+        axis=-1,
+    )
     own = rows_reduce_scatter(with_sumsq(proj, current), seq_dev)
     qkv = split_norm(own, 3 * width).reshape(steps, seq_dev, 3, head_count, DK)
     query = qkv[:, :, 0]

time: 75.1 us -> 78.3 us (1.043)
  matrix products: 1.76 us -> 4.89 us
    dot_general x1 -> x3, matrix products: 0.26 us -> 3.38 us  [on_device(): jnp.einsum('tsd,dw->tsw', scaled, w_qkv[:, part], preferred_element_type=...]
    unnamed x28 -> x24, local copies, waits for them, and re-layouts: 3.08 us -> 3.68 us
where the time goes in v10:
time: 78.3 us; the launch traced here: 77.6 us
  starting transfers between devices  29.3 us (37%)
  waiting for transfers between devices  17.7 us (23%)
  blocking collectives  9.9 us (13%)
  local copies, waits for them, and re-layouts  7.5 us (10%)
  matrix products  4.89 us (6%)
  between operations  4.22 us (5%)
  other arithmetic  4.06 us (5%)
    all_to_all x2, starting transfers between devices, rows_reduce_scatter(): got = lax.all_to_all(send, 'enc', 0, 0, tiled=True)  12.1 us
    all_to_all x1, blocking collectives, rows_gather(): got = lax.all_to_all(send, 'enc', 0, 0, tiled=True)  9.9 us
    ppermute x6, starting transfers between devices, tensor_sum(): lax.ppermute(value, 'tensor', [(i, i ^ k) for i in range(n_t)])  8.93 us
    all_to_all x2, waiting for transfers between devices, rows_reduce_scatter(): got = lax.all_to_all(send, 'enc', 0, 0, tiled=True)  7.91 us
    ppermute x6, waiting for transfers between devices, tensor_sum(): lax.ppermute(value, 'tensor', [(i, i ^ k) for i in range(n_t)])  6.02 us
    all_to_all x1, starting transfers between devices, rows_gather(): got = lax.all_to_all(send, 'enc', 0, 0, tiled=True)  5.45 us
    all_to_all x1, waiting for transfers between devices, rows_gather(): got = lax.all_to_all(send, 'enc', 0, 0, tiled=True)  3.8 us
    unnamed x24, local copies, waits for them, and re-layouts  3.68 us
  transfers between devices with their start and end apart: 10, of which 7 were waited for; matrix products, arithmetic and copies ran while one was open for 2% of the time, Pallas kernels for 0%

profile of v10, /device:TPU:1, one launch (start us, length us, event | category | flops | bytes accessed | tf_op | source)
XLA Modules:
  0.0 77.6 jit_solution(10160979245779432579)
XLA Ops:
  0.0 0.9 %fusion.27 = (f32[3,32]{1,0:T(4,128)S(1)}, bf16[3,32,256]{2,1,0:T(8,128)(2,1)S(1)}) fusion(bf16[3,32,256]{2,1,0:T(8,128)(2,1)} %param.12, f32[256]{0:T(256)} %param.18), kind=kLoop, calls=%fused_computation.45 | loop fusion | flops 122784 | bytes 99712 | tf_op jit(solution)/shard_map/reduce_sum | solution.py:41
  1.0 1.1 %convolution_convert_fusion.1 = bf16[3,16,2,512]{3,1,2,0:T(8,128)(2,1)S(1)} fusion(bf16[256,3,512]{2,0,1:T(8,128)(2,1)} %param.19, bf16[3,16,2,256]{3,2,1,0:T(2,128)(2,1)S(1)} %dot_general.38), kind=kOutput, calls=%fused_computation.1 | convolution fusion | flops 25214976 | bytes 409600 | tf_op jit(solution)/shard_map/tsd,dw->tsw/dot_general | solution.py:143
  2.1 1.1 %convolution_convert_fusion.2 = bf16[3,16,2,512]{3,1,2,0:T(8,128)(2,1)S(1)} fusion(bf16[256,3,512]{2,0,1:T(8,128)(2,1)} %param.19, bf16[3,16,2,256]{3,2,1,0:T(2,128)(2,1)S(1)} %dot_general.38), kind=kOutput, calls=%fused_computation.2 | convolution fusion | flops 25214976 | bytes 409600 | tf_op jit(solution)/shard_map/tsd,dw->tsw/dot_general | solution.py:143
  3.2 1.1 %convolution_convert_fusion.3 = bf16[3,16,2,512]{3,1,2,0:T(8,128)(2,1)S(1)} fusion(bf16[256,3,512]{2,0,1:T(8,128)(2,1)} %param.19, bf16[3,16,2,256]{3,2,1,0:T(2,128)(2,1)S(1)} %dot_general.38), kind=kOutput, calls=%fused_computation.3 | convolution fusion | flops 25214976 | bytes 409600 | tf_op jit(solution)/shard_map/tsd,dw->tsw/dot_general | solution.py:143
  4.4 0.1 reduce_sum.95
  4.5 0.1 copy.150
  4.6 0.1 copy.153
  4.7 0.1 copy.154
  4.8 0.1 concatenate.17
  4.9 1.0 %copy.155 = bf16[16,3,2,1664]{3,2,1,0:T(2,128)(2,1)} copy(bf16[16,3,2,1664]{3,0,2,1:T(8,128)(2,1)S(1)} %bitcast.100) | data formatting | bytes 638976 | tf_op jit(solution)/shard_map/transpose | solution.py:53
  5.9 8.6 %all-to-all-start = ((bf16[16,3,2,1664]{3,2,1,0:T(2,128)(2,1)}), bf16[16,3,2,1664]{3,2,1,0:T(2,128)(2,1)S(1)}, u32[]{:S(2)}, u32[]{:S(2)}) async-start(bf16[16,3,2,1664]{3,2,1,0:T(2,128)(2,1)} %copy.155), calls=%async_computation | async-start | bytes 638976 | tf_op jit(solution)/shard_map/all_to_all | solution.py:54
  14.6 0.6 copy-done.6
  15.2 0.7 fusion.41
  18.5 0.6 copy-done.8
  19.3 0.1 slice_reduce_fusion
  19.4 0.6 copy-done.9
  20.1 0.2 fusion.39
  20.3 0.1 iota_compare_fusion.1
  21.7 1.2 %all-to-all-done = bf16[16,3,2,1664]{3,2,1,0:T(2,128)(2,1)S(1)} async-done(((bf16[16,3,2,1664]{3,2,1,0:T(2,128)(2,1)}), bf16[16,3,2,1664]{3,2,1,0:T(2,128)(2,1)S(1)}, u32[]{:S(2)}, u32[]{:S(2)}) %all-to-all-start) | async-done | bytes 319520 | tf_op jit(solution)/shard_map/all_to_all | solution.py:54
  22.9 0.1 convert_reduce_fusion
  23.1 0.1 copy.192
  23.2 0.1 copy.193
  23.3 0.1 copy.159
  23.4 0.1 fusion.34
  23.6 0.1 convert_reduce_fusion.3
  23.7 0.2 convert_reduce_fusion.4
  23.9 0.1 convolution_bitcast_fusion.2
  24.1 0.2 fusion.3
  24.3 0.7 copy-done.5
  25.0 0.7 broadcast_in_dim.119
  25.7 5.4 %all-to-all-start.1 = ((bf16[16,3,2,512]{3,2,1,0:T(2,128)(2,1)}), bf16[16,3,2,512]{3,2,1,0:T(2,128)(2,1)S(1)}, u32[]{:S(2)}, u32[]{:S(2)}) async-start(bf16[16,3,2,512]{3,2,1,0:T(2,128)(2,1)} %broadcast_in_dim.119), calls=%async_computation.1 | async-start | bytes 196608 | tf_op jit(solution)/shard_map/all_to_all | solution.py:24
  31.1 2.8 %collective-permute-start.3 = (bf16[24,2,512]{2,0,1:T(8,128)(2,1)S(1)}, bf16[24,2,512]{2,0,1:T(8,128)(2,1)S(1)}, u32[]{:S(2)}, u32[]{:S(2)}) collective-permute-start(bf16[24,2,512]{2,0,1:T(8,128)(2,1)S(1)} %get-tuple-element.22), channel_id=1, source_target_pairs={{0,4},{4,0},{1,5},{5,1},{2,6},{6,2},{3,7},{7,3},{8,12},{12,8},{9,1... | collective-permute-start | bytes 147464 | tf_op jit(solution)/shard_map/ppermute | solution.py:82
  34.0 3.8 %all-to-all-done.1 = bf16[16,3,2,512]{3,2,1,0:T(2,128)(2,1)S(1)} async-done(((bf16[16,3,2,512]{3,2,1,0:T(2,128)(2,1)}), bf16[16,3,2,512]{3,2,1,0:T(2,128)(2,1)S(1)}, u32[]{:S(2)}, u32[]{:S(2)}) %all-to-all-start.1) | async-done | bytes 98336 | tf_op jit(solution)/shard_map/all_to_all | solution.py:24
  37.9 0.2 convolution_convert_fusion.5
  38.1 2.7 %collective-permute-start = (bf16[3,32,256]{2,1,0:T(8,128)(2,1)S(1)}, bf16[3,32,256]{2,1,0:T(8,128)(2,1)S(1)}, u32[]{:S(2)}, u32[]{:S(2)}) collective-permute-start(bf16[3,32,256]{2,1,0:T(8,128)(2,1)S(1)} %convolution_convert_fusion.5), channel_id=1, source_target_pairs={{0,1},{1,0},{2,3},{3,2},{4,5},{5,4},{6,7},{7,6},{8,9},{9,8},{10,11... | collective-permute-start | bytes 147464 | tf_op jit(solution)/shard_map/ppermute | solution.py:32
  40.8 1.2 %collective-permute-start.1 = (bf16[3,32,256]{2,1,0:T(8,128)(2,1)S(1)}, bf16[3,32,256]{2,1,0:T(8,128)(2,1)S(1)}, u32[]{:S(2)}, u32[]{:S(2)}) collective-permute-start(bf16[3,32,256]{2,1,0:T(8,128)(2,1)S(1)} %convolution_convert_fusion.5), channel_id=1, source_target_pairs={{0,2},{1,3},{2,0},{3,1},{4,6},{5,7},{6,4},{7,5},{8,10},{9,11},{10,... | collective-permute-start | bytes 147464 | tf_op jit(solution)/shard_map/ppermute | solution.py:32
  42.1 0.5 collective-permute-start.2
  42.6 0.1 broadcast_select_fusion
  42.7 1.1 %collective-permute-done.1 = bf16[3,32,256]{2,1,0:T(8,128)(2,1)S(1)} collective-permute-done((bf16[3,32,256]{2,1,0:T(8,128)(2,1)S(1)}, bf16[3,32,256]{2,1,0:T(8,128)(2,1)S(1)}, u32[]{:S(2)}, u32[]{:S(2)}) %collective-permute-start.1) | collective-permute-done | bytes 49184 | tf_op jit(solution)/shard_map/ppermute | solution.py:32
  43.8 2.0 %collective-permute-done.2 = bf16[3,32,256]{2,1,0:T(8,128)(2,1)S(1)} collective-permute-done((bf16[3,32,256]{2,1,0:T(8,128)(2,1)S(1)}, bf16[3,32,256]{2,1,0:T(8,128)(2,1)S(1)}, u32[]{:S(2)}, u32[]{:S(2)}) %collective-permute-start.2) | collective-permute-done | bytes 49184 | tf_op jit(solution)/shard_map/ppermute | solution.py:32
  45.8 0.1 multiply_reduce_fusion
  45.9 0.7 copy-done.7
  46.6 0.2 convolution_convert_fusion
  46.8 0.1 reduce_sum.103
  46.9 0.1 copy.170
  47.0 0.1 copy.174
  47.1 0.1 copy.175
  47.3 0.8 %maximum_bitcast_fusion = bf16[16,3,2,640]{3,2,1,0:T(2,128)(2,1)} fusion(bf16[3,16,2,1]{3,2,0,1:T(2,128)(2,1)S(1)} %copy.175, bf16[3,16,2,1]{3,2,0,1:T(2,128)(2,1)S(1)} %copy.174, bf16[640]{0:T(1024)(128)(2,1)S(1)} %pad.3.clone, bf16[3,16,2,512]{3,2,1,0:T(2,128)(2,1)S(1)} %concatenate.18), kind=kLoop, calls=%fused_computation.43 | loop fusion | flops 491520 | bytes 222848 | tf_op jit(solution)/shard_map/transpose | solution.py:53
  48.1 3.5 %all-to-all-start.2 = ((bf16[16,3,2,640]{3,2,1,0:T(2,128)(2,1)}), bf16[16,3,2,640]{3,2,1,0:T(2,128)(2,1)S(1)}, u32[]{:S(2)}, u32[]{:S(2)}) async-start(bf16[16,3,2,640]{3,2,1,0:T(2,128)(2,1)} %maximum_bitcast_fusion), calls=%async_computation.2 | async-start | bytes 245760 | tf_op jit(solution)/shard_map/all_to_all | solution.py:54
  51.7 6.7 %all-to-all-done.2 = bf16[16,3,2,640]{3,2,1,0:T(2,128)(2,1)S(1)} async-done(((bf16[16,3,2,640]{3,2,1,0:T(2,128)(2,1)}), bf16[16,3,2,640]{3,2,1,0:T(2,128)(2,1)S(1)}, u32[]{:S(2)}, u32[]{:S(2)}) %all-to-all-start.2) | async-done | bytes 122912 | tf_op jit(solution)/shard_map/all_to_all | solution.py:54
  58.5 0.1 copy.197
  58.6 0.1 copy.198
  58.7 0.1 copy.181
  58.8 0.1 fusion.35
  58.9 0.2 convert_reduce_fusion.2
  59.1 0.1 fusion.4
  59.4 9.9 %all_to_all.20 = bf16[16,3,2,512]{3,2,1,0:T(2,128)(2,1)S(1)} all-to-all(bf16[16,3,2,512]{3,2,1,0:T(2,128)(2,1)S(1)} %broadcast_in_dim.128), channel_id=1, replica_groups=mesh['enc'=16,'dp'=2,'tensor'=4] {'enc'}, dimensions={0} | all-to-all | bytes 196608 | tf_op jit(solution)/shard_map/all_to_all | solution.py:24
  69.4 0.2 convolution_convert_fusion.4
  69.6 2.7 %collective-permute-start.4 = (bf16[3,32,256]{2,1,0:T(8,128)(2,1)S(1)}, bf16[3,32,256]{2,1,0:T(8,128)(2,1)S(1)}, u32[]{:S(2)}, u32[]{:S(2)}) collective-permute-start(bf16[3,32,256]{2,1,0:T(8,128)(2,1)S(1)} %convolution_convert_fusion.4), channel_id=1, source_target_pairs={{0,1},{1,0},{2,3},{3,2},{4,5},{5,4},{6,7},{7,6},{8,9},{9,8},{10,11... | collective-permute-start | bytes 147464 | tf_op jit(solution)/shard_map/ppermute | solution.py:32
  72.3 0.6 collective-permute-start.5
  72.9 1.1 %collective-permute-start.6 = (bf16[3,32,256]{2,1,0:T(8,128)(2,1)S(1)}, bf16[3,32,256]{2,1,0:T(8,128)(2,1)S(1)}, u32[]{:S(2)}, u32[]{:S(2)}) collective-permute-start(bf16[3,32,256]{2,1,0:T(8,128)(2,1)S(1)} %convolution_convert_fusion.4), channel_id=1, source_target_pairs={{0,3},{1,2},{2,1},{3,0},{4,7},{5,6},{6,5},{7,4},{8,11},{9,10},{10,... | collective-permute-start | bytes 147464 | tf_op jit(solution)/shard_map/ppermute | solution.py:32
  74.0 1.2 %collective-permute-done.5 = bf16[3,32,256]{2,1,0:T(8,128)(2,1)S(1)} collective-permute-done((bf16[3,32,256]{2,1,0:T(8,128)(2,1)S(1)}, bf16[3,32,256]{2,1,0:T(8,128)(2,1)S(1)}, u32[]{:S(2)}, u32[]{:S(2)}) %collective-permute-start.5) | collective-permute-done | bytes 49184 | tf_op jit(solution)/shard_map/ppermute | solution.py:32
  75.3 1.7 %collective-permute-done.6 = bf16[3,32,256]{2,1,0:T(8,128)(2,1)S(1)} collective-permute-done((bf16[3,32,256]{2,1,0:T(8,128)(2,1)S(1)}, bf16[3,32,256]{2,1,0:T(8,128)(2,1)S(1)}, u32[]{:S(2)}, u32[]{:S(2)}) %collective-permute-start.6) | collective-permute-done | bytes 49184 | tf_op jit(solution)/shard_map/ppermute | solution.py:32
  76.9 0.7 add_convert_fusion
  (52 shorter events, 1.1 us)
Async XLA Ops:
  0.0 45.9 %copy-start = (bf16[256,512]{1,0:T(8,128)(2,1)S(1)}, bf16[256,512]{1,0:T(8,128)(2,1)}, u32[]{:S(2)}) copy-start(bf16[256,512]{1,0:T(8,128)(2,1)} %param.22) | copy-start | bytes 786436
  5.9 17.0 %all-to-all-start = ((bf16[16,3,2,1664]{3,2,1,0:T(2,128)(2,1)}), bf16[16,3,2,1664]{3,2,1,0:T(2,128)(2,1)S(1)}, u32[]{:S(2)}, u32[]{:S(2)}) async-start(bf16[16,3,2,1664]{3,2,1,0:T(2,128)(2,1)} %copy.155), calls=%async_computation | async-start | bytes 638976 | tf_op jit(solution)/shard_map/all_to_all | solution.py:54
  14.5 0.7 copy-start.6
  14.5 4.7 %copy-start.4 = (bf16[2,8,2,512]{3,2,1,0:T(2,128)(2,1)S(1)}, bf16[2,8,2,512]{3,2,1,0:T(2,128)(2,1)}, u32[]{:S(2)}) copy-start(bf16[2,8,2,512]{3,2,1,0:T(2,128)(2,1)} %param.13) | copy-start | bytes 98308
  18.5 0.7 copy-start.8
  19.4 0.7 copy-start.9
  24.1 0.9 %copy-start.5 = (bf16[2,24,2,512]{3,2,1,0:T(2,128)(2,1)S(1)}, bf16[2,24,2,512]{3,2,1,0:T(2,128)(2,1)}, u32[]{:S(2)}) copy-start(bf16[2,24,2,512]{3,2,1,0:T(2,128)(2,1)} %param.14) | copy-start | bytes 294916
  25.7 12.1 %all-to-all-start.1 = ((bf16[16,3,2,512]{3,2,1,0:T(2,128)(2,1)}), bf16[16,3,2,512]{3,2,1,0:T(2,128)(2,1)S(1)}, u32[]{:S(2)}, u32[]{:S(2)}) async-start(bf16[16,3,2,512]{3,2,1,0:T(2,128)(2,1)} %broadcast_in_dim.119), calls=%async_computation.1 | async-start | bytes 196608 | tf_op jit(solution)/shard_map/all_to_all | solution.py:24
  31.1 6.8 %copy-start.1 = (bf16[512,256]{1,0:T(8,128)(2,1)S(1)}, bf16[512,256]{1,0:T(8,128)(2,1)}, u32[]{:S(2)}) copy-start(bf16[512,256]{1,0:T(8,128)(2,1)} %param.20) | copy-start | bytes 786436
  31.1 11.4 %collective-permute-start.3 = (bf16[24,2,512]{2,0,1:T(8,128)(2,1)S(1)}, bf16[24,2,512]{2,0,1:T(8,128)(2,1)S(1)}, u32[]{:S(2)}, u32[]{:S(2)}) collective-permute-start(bf16[24,2,512]{2,0,1:T(8,128)(2,1)S(1)} %get-tuple-element.22), channel_id=1, source_target_pairs={{0,4},{4,0},{1,5},{5,1},{2,6},{6,2},{3,7},{7,3},{8,12},{12,8},{9,1... | collective-permute-start | bytes 147464 | tf_op jit(solution)/shard_map/ppermute | solution.py:82
  38.1 4.6 %collective-permute-start = (bf16[3,32,256]{2,1,0:T(8,128)(2,1)S(1)}, bf16[3,32,256]{2,1,0:T(8,128)(2,1)S(1)}, u32[]{:S(2)}, u32[]{:S(2)}) collective-permute-start(bf16[3,32,256]{2,1,0:T(8,128)(2,1)S(1)} %convolution_convert_fusion.5), channel_id=1, source_target_pairs={{0,1},{1,0},{2,3},{3,2},{4,5},{5,4},{6,7},{7,6},{8,9},{9,8},{10,11... | collective-permute-start | bytes 147464 | tf_op jit(solution)/shard_map/ppermute | solution.py:32
  40.8 2.9 %collective-permute-start.1 = (bf16[3,32,256]{2,1,0:T(8,128)(2,1)S(1)}, bf16[3,32,256]{2,1,0:T(8,128)(2,1)S(1)}, u32[]{:S(2)}, u32[]{:S(2)}) collective-permute-start(bf16[3,32,256]{2,1,0:T(8,128)(2,1)S(1)} %convolution_convert_fusion.5), channel_id=1, source_target_pairs={{0,2},{1,3},{2,0},{3,1},{4,6},{5,7},{6,4},{7,5},{8,10},{9,11},{10,... | collective-permute-start | bytes 147464 | tf_op jit(solution)/shard_map/ppermute | solution.py:32
  42.1 3.7 %collective-permute-start.2 = (bf16[3,32,256]{2,1,0:T(8,128)(2,1)S(1)}, bf16[3,32,256]{2,1,0:T(8,128)(2,1)S(1)}, u32[]{:S(2)}, u32[]{:S(2)}) collective-permute-start(bf16[3,32,256]{2,1,0:T(8,128)(2,1)S(1)} %convolution_convert_fusion.5), channel_id=1, source_target_pairs={{0,3},{1,2},{2,1},{3,0},{4,7},{5,6},{6,5},{7,4},{8,11},{9,10},{10,... | collective-permute-start | bytes 147464 | tf_op jit(solution)/shard_map/ppermute | solution.py:32
  42.6 3.2 %copy-start.3 = (bf16[3,32,256]{2,1,0:T(8,128)(2,1)S(1)}, bf16[3,32,256]{2,1,0:T(8,128)(2,1)}, u32[]{:S(2)}) copy-start(bf16[3,32,256]{2,1,0:T(8,128)(2,1)} %param.12) | copy-start | bytes 147460
  45.9 0.7 copy-start.7
  48.1 10.3 %all-to-all-start.2 = ((bf16[16,3,2,640]{3,2,1,0:T(2,128)(2,1)}), bf16[16,3,2,640]{3,2,1,0:T(2,128)(2,1)S(1)}, u32[]{:S(2)}, u32[]{:S(2)}) async-start(bf16[16,3,2,640]{3,2,1,0:T(2,128)(2,1)} %maximum_bitcast_fusion), calls=%async_computation.2 | async-start | bytes 245760 | tf_op jit(solution)/shard_map/all_to_all | solution.py:54
  59.3 10.0 %copy-start.2 = (bf16[512,256]{1,0:T(8,128)(2,1)S(1)}, bf16[512,256]{1,0:T(8,128)(2,1)}, u32[]{:S(2)}) copy-start(bf16[512,256]{1,0:T(8,128)(2,1)} %param.23) | copy-start | bytes 786436
  69.6 4.5 %collective-permute-start.4 = (bf16[3,32,256]{2,1,0:T(8,128)(2,1)S(1)}, bf16[3,32,256]{2,1,0:T(8,128)(2,1)S(1)}, u32[]{:S(2)}, u32[]{:S(2)}) collective-permute-start(bf16[3,32,256]{2,1,0:T(8,128)(2,1)S(1)} %convolution_convert_fusion.4), channel_id=1, source_target_pairs={{0,1},{1,0},{2,3},{3,2},{4,5},{5,4},{6,7},{7,6},{8,9},{9,8},{10,11... | collective-permute-start | bytes 147464 | tf_op jit(solution)/shard_map/ppermute | solution.py:32
  72.3 2.9 %collective-permute-start.5 = (bf16[3,32,256]{2,1,0:T(8,128)(2,1)S(1)}, bf16[3,32,256]{2,1,0:T(8,128)(2,1)S(1)}, u32[]{:S(2)}, u32[]{:S(2)}) collective-permute-start(bf16[3,32,256]{2,1,0:T(8,128)(2,1)S(1)} %convolution_convert_fusion.4), channel_id=1, source_target_pairs={{0,2},{1,3},{2,0},{3,1},{4,6},{5,7},{6,4},{7,5},{8,10},{9,11},{10,... | collective-permute-start | bytes 147464 | tf_op jit(solution)/shard_map/ppermute | solution.py:32
  72.9 4.0 %collective-permute-start.6 = (bf16[3,32,256]{2,1,0:T(8,128)(2,1)S(1)}, bf16[3,32,256]{2,1,0:T(8,128)(2,1)S(1)}, u32[]{:S(2)}, u32[]{:S(2)}) collective-permute-start(bf16[3,32,256]{2,1,0:T(8,128)(2,1)S(1)} %convolution_convert_fusion.4), channel_id=1, source_target_pairs={{0,3},{1,2},{2,1},{3,0},{4,7},{5,6},{6,5},{7,4},{8,11},{9,10},{10,... | collective-permute-start | bytes 147464 | tf_op jit(solution)/shard_map/ppermute | solution.py:32

commit v11 on v7

--- a/solution.py
+++ b/solution.py
@@ -138,8 +138,12 @@
 
     current = hidden_in.astype(jnp.float32)
     scaled = (current * gain_self[None, None, :]).astype(jnp.bfloat16)
-    proj = jnp.einsum("tsd,dcw->tscw", scaled, w_qkv, preferred_element_type=jnp.float32)
-    proj = proj.reshape(steps, current.shape[1], 3 * width)
+    proj = jnp.einsum(
+        "tsd,dw->tsw",
+        scaled,
+        w_qkv.reshape(w_qkv.shape[0], 3 * width),
+        preferred_element_type=jnp.float32,
+    )
     own = rows_reduce_scatter(with_sumsq(proj, current), seq_dev)
     qkv = split_norm(own, 3 * width).reshape(steps, seq_dev, 3, head_count, DK)
     query = qkv[:, :, 0]

time: 75.1 us -> 76.1 us (1.013)
  local copies, waits for them, and re-layouts: 8.11 us -> 9.81 us
  other arithmetic: 4.11 us -> 3.22 us
    unnamed x28 -> x27, local copies, waits for them, and re-layouts: 3.08 us -> 5.03 us
    concatenate x5, local copies, waits for them, and re-layouts: 0.98 us -> 2.19 us  [with_sumsq(): jnp.concatenate([partial.astype(jnp.bfloat16), high, low, pad], axis=-1)]
    transpose x1 -> x0, local copies, waits for them, and re-layouts: 0.93 us -> none  [rows_reduce_scatter(): send = partial.reshape(steps, n_enc, owned, cols).transpose(1, 0, 2, 3)]
    reduce_sum x2, other arithmetic: 1.08 us -> 0.21 us  [with_sumsq(): squares = jnp.sum(rows_in * rows_in, axis=-1, keepdims=True)]
where the time goes in v11:
time: 76.1 us; the launch traced here: 75.5 us
  starting transfers between devices  28.7 us (38%)
  waiting for transfers between devices  17.7 us (23%)
  blocking collectives  9.89 us (13%)
  local copies, waits for them, and re-layouts  9.81 us (13%)
  between operations  4.24 us (6%)
  other arithmetic  3.22 us (4%)
  matrix products  1.88 us (2%)
    all_to_all x2, starting transfers between devices, rows_reduce_scatter(): got = lax.all_to_all(send, 'enc', 0, 0, tiled=True)  12.1 us
    all_to_all x1, blocking collectives, rows_gather(): got = lax.all_to_all(send, 'enc', 0, 0, tiled=True)  9.89 us
    ppermute x6, starting transfers between devices, tensor_sum(): lax.ppermute(value, 'tensor', [(i, i ^ k) for i in range(n_t)])  8.44 us
    all_to_all x2, waiting for transfers between devices, rows_reduce_scatter(): got = lax.all_to_all(send, 'enc', 0, 0, tiled=True)  8.12 us
    ppermute x6, waiting for transfers between devices, tensor_sum(): lax.ppermute(value, 'tensor', [(i, i ^ k) for i in range(n_t)])  5.78 us
    all_to_all x1, starting transfers between devices, rows_gather(): got = lax.all_to_all(send, 'enc', 0, 0, tiled=True)  5.37 us
    unnamed x27, local copies, waits for them, and re-layouts  5.03 us
    all_to_all x1, waiting for transfers between devices, rows_gather(): got = lax.all_to_all(send, 'enc', 0, 0, tiled=True)  3.77 us
  transfers between devices with their start and end apart: 10, of which 7 were waited for; matrix products, arithmetic and copies ran while one was open for 2% of the time, Pallas kernels for 0%

profile of v11, /device:TPU:1, one launch (start us, length us, event | category | flops | bytes accessed | tf_op | source)
XLA Modules:
  0.0 75.5 jit_solution(12612327517403662072)
XLA Ops:
  0.0 1.5 %copy.115 = bf16[256,3,512]{0,2,1:T(8,128)(2,1)S(1)} copy(bf16[256,3,512]{2,0,1:T(8,128)(2,1)} %param.19) | data formatting | bytes 1572864 | tf_op args[7]
  1.5 0.1 fusion.21
  1.6 0.7 copy-done.7
  2.3 0.4 convolution_convert_fusion
  2.6 0.1 concatenate.14
  2.7 0.2 copy.120
  3.0 0.1 reduce_sum.95
  3.1 0.1 copy.117
  3.2 0.1 copy.121
  3.3 0.1 copy.122
  3.4 1.8 %concatenate.16 = bf16[3,16,2,1664]{3,2,0,1:T(2,128)(2,1)} concatenate(bf16[3,16,2,1536]{3,2,0,1:T(2,128)(2,1)S(1)} %copy.120, bf16[3,16,2,1]{3,2,0,1:T(2,128)(2,1)S(1)} %copy.121, bf16[3,16,2,1]{3,2,0,1:T(2,128)(2,1)S(1)} %copy.122, bf16[3,16,2,126]{3,2,0,1:T(2,128)(2,1)S(1)} %concatenate.15), dimensions={3} | concatenate | bytes 638976 | tf_op jit(solution)/shard_map/concatenate | solution.py:47
  5.2 8.6 %all-to-all-start = ((bf16[16,3,2,1664]{3,2,1,0:T(2,128)(2,1)}), bf16[16,3,2,1664]{3,2,1,0:T(2,128)(2,1)S(1)}, u32[]{:S(2)}, u32[]{:S(2)}) async-start(bf16[16,3,2,1664]{3,2,1,0:T(2,128)(2,1)} %bitcast.2), calls=%async_computation | async-start | bytes 638976 | tf_op jit(solution)/shard_map/all_to_all | solution.py:54
  13.9 0.6 copy-done.6
  14.5 0.7 fusion.34
  17.8 0.1 slice_reduce_fusion
  18.0 0.5 copy-done.9
  18.6 0.1 iota_compare_fusion.2
  18.6 0.7 copy-done.10
  19.3 0.2 fusion.32
  19.5 0.1 iota_compare_fusion.1
  20.9 1.4 %all-to-all-done = bf16[16,3,2,1664]{3,2,1,0:T(2,128)(2,1)S(1)} async-done(((bf16[16,3,2,1664]{3,2,1,0:T(2,128)(2,1)}), bf16[16,3,2,1664]{3,2,1,0:T(2,128)(2,1)S(1)}, u32[]{:S(2)}, u32[]{:S(2)}) %all-to-all-start) | async-done | bytes 319520 | tf_op jit(solution)/shard_map/all_to_all | solution.py:54
  22.3 0.1 convert_reduce_fusion
  22.5 0.1 copy.159
  22.6 0.1 copy.160
  22.7 0.1 copy.127
  22.8 0.1 fusion.27
  22.9 0.2 convert_reduce_fusion.4
  23.1 0.1 convolution_bitcast_fusion.2
  23.2 0.1 convert_reduce_fusion.3
  23.4 0.2 fusion.3
  23.6 0.7 broadcast_in_dim.119
  24.3 5.4 %all-to-all-start.1 = ((bf16[16,3,2,512]{3,2,1,0:T(2,128)(2,1)}), bf16[16,3,2,512]{3,2,1,0:T(2,128)(2,1)S(1)}, u32[]{:S(2)}, u32[]{:S(2)}) async-start(bf16[16,3,2,512]{3,2,1,0:T(2,128)(2,1)} %broadcast_in_dim.119), calls=%async_computation.1 | async-start | bytes 196608 | tf_op jit(solution)/shard_map/all_to_all | solution.py:24
  29.8 2.8 %collective-permute-start.3 = (bf16[24,2,512]{2,0,1:T(8,128)(2,1)S(1)}, bf16[24,2,512]{2,0,1:T(8,128)(2,1)S(1)}, u32[]{:S(2)}, u32[]{:S(2)}) collective-permute-start(bf16[24,2,512]{2,0,1:T(8,128)(2,1)S(1)} %get-tuple-element.22), channel_id=1, source_target_pairs={{0,4},{4,0},{1,5},{5,1},{2,6},{6,2},{3,7},{7,3},{8,12},{12,8},{9,1... | collective-permute-start | bytes 147464 | tf_op jit(solution)/shard_map/ppermute | solution.py:82
  32.6 3.8 %all-to-all-done.1 = bf16[16,3,2,512]{3,2,1,0:T(2,128)(2,1)S(1)} async-done(((bf16[16,3,2,512]{3,2,1,0:T(2,128)(2,1)}), bf16[16,3,2,512]{3,2,1,0:T(2,128)(2,1)S(1)}, u32[]{:S(2)}, u32[]{:S(2)}) %all-to-all-start.1) | async-done | bytes 98336 | tf_op jit(solution)/shard_map/all_to_all | solution.py:24
  36.5 0.2 convolution_convert_fusion.3
  36.7 3.8 %collective-permute-start.2 = (bf16[3,32,256]{2,1,0:T(8,128)(2,1)S(1)}, bf16[3,32,256]{2,1,0:T(8,128)(2,1)S(1)}, u32[]{:S(2)}, u32[]{:S(2)}) collective-permute-start(bf16[3,32,256]{2,1,0:T(8,128)(2,1)S(1)} %convolution_convert_fusion.3), channel_id=1, source_target_pairs={{0,3},{1,2},{2,1},{3,0},{4,7},{5,6},{6,5},{7,4},{8,11},{9,10},{10,... | collective-permute-start | bytes 147464 | tf_op jit(solution)/shard_map/ppermute | solution.py:32
  40.5 0.3 collective-permute-start.1
  40.8 0.2 collective-permute-start
  41.0 0.1 broadcast_select_fusion
  41.1 1.9 %collective-permute-done.2 = bf16[3,32,256]{2,1,0:T(8,128)(2,1)S(1)} collective-permute-done((bf16[3,32,256]{2,1,0:T(8,128)(2,1)S(1)}, bf16[3,32,256]{2,1,0:T(8,128)(2,1)S(1)}, u32[]{:S(2)}, u32[]{:S(2)}) %collective-permute-start.2) | collective-permute-done | bytes 49184 | tf_op jit(solution)/shard_map/ppermute | solution.py:32
  43.0 0.9 %collective-permute-done.1 = bf16[3,32,256]{2,1,0:T(8,128)(2,1)S(1)} collective-permute-done((bf16[3,32,256]{2,1,0:T(8,128)(2,1)S(1)}, bf16[3,32,256]{2,1,0:T(8,128)(2,1)S(1)}, u32[]{:S(2)}, u32[]{:S(2)}) %collective-permute-start.1) | collective-permute-done | bytes 49184 | tf_op jit(solution)/shard_map/ppermute | solution.py:32
  44.0 0.1 multiply_reduce_fusion
  44.1 0.1 reduce_sum.103
  44.2 0.1 copy.138
  44.3 0.1 copy.143
  44.4 0.1 copy.142
  44.5 0.7 copy-done.8
  45.2 0.2 convolution_convert_fusion.1
  45.4 0.8 %maximum_bitcast_fusion = bf16[16,3,2,640]{3,2,1,0:T(2,128)(2,1)} fusion(bf16[3,16,2,126]{3,2,0,1:T(2,128)(2,1)S(1)} %concatenate.15, bf16[3,16,2,1]{3,2,0,1:T(2,128)(2,1)S(1)} %copy.143, bf16[3,16,2,1]{3,2,0,1:T(2,128)(2,1)S(1)} %copy.142, bf16[3,16,2,512]{3,2,1,0:T(2,128)(2,1)S(1)} %concatenate.17), kind=kLoop, calls=%fused_computation.35 | loop fusion | flops 491520 | bytes 245760 | tf_op jit(solution)/shard_map/transpose | solution.py:53
  46.3 3.5 %all-to-all-start.2 = ((bf16[16,3,2,640]{3,2,1,0:T(2,128)(2,1)}), bf16[16,3,2,640]{3,2,1,0:T(2,128)(2,1)S(1)}, u32[]{:S(2)}, u32[]{:S(2)}) async-start(bf16[16,3,2,640]{3,2,1,0:T(2,128)(2,1)} %maximum_bitcast_fusion), calls=%async_computation.2 | async-start | bytes 245760 | tf_op jit(solution)/shard_map/all_to_all | solution.py:54
  49.9 6.7 %all-to-all-done.2 = bf16[16,3,2,640]{3,2,1,0:T(2,128)(2,1)S(1)} async-done(((bf16[16,3,2,640]{3,2,1,0:T(2,128)(2,1)}), bf16[16,3,2,640]{3,2,1,0:T(2,128)(2,1)S(1)}, u32[]{:S(2)}, u32[]{:S(2)}) %all-to-all-start.2) | async-done | bytes 122912 | tf_op jit(solution)/shard_map/all_to_all | solution.py:54
  56.7 0.1 copy.164
  56.8 0.1 copy.165
  56.9 0.1 copy.148
  57.0 0.1 fusion.28
  57.1 0.2 convert_reduce_fusion.2
  57.3 0.1 fusion.4
  57.6 9.9 %all_to_all.20 = bf16[16,3,2,512]{3,2,1,0:T(2,128)(2,1)S(1)} all-to-all(bf16[16,3,2,512]{3,2,1,0:T(2,128)(2,1)S(1)} %broadcast_in_dim.128), channel_id=1, replica_groups=mesh['enc'=16,'dp'=2,'tensor'=4] {'enc'}, dimensions={0} | all-to-all | bytes 196608 | tf_op jit(solution)/shard_map/all_to_all | solution.py:24
  67.6 0.2 convolution_convert_fusion.2
  67.8 3.5 %collective-permute-start.6 = (bf16[3,32,256]{2,1,0:T(8,128)(2,1)S(1)}, bf16[3,32,256]{2,1,0:T(8,128)(2,1)S(1)}, u32[]{:S(2)}, u32[]{:S(2)}) collective-permute-start(bf16[3,32,256]{2,1,0:T(8,128)(2,1)S(1)} %convolution_convert_fusion.2), channel_id=1, source_target_pairs={{0,3},{1,2},{2,1},{3,0},{4,7},{5,6},{6,5},{7,4},{8,11},{9,10},{10,... | collective-permute-start | bytes 147464 | tf_op jit(solution)/shard_map/ppermute | solution.py:32
  71.3 0.6 collective-permute-start.5
  71.9 1.7 %collective-permute-done.6 = bf16[3,32,256]{2,1,0:T(8,128)(2,1)S(1)} collective-permute-done((bf16[3,32,256]{2,1,0:T(8,128)(2,1)S(1)}, bf16[3,32,256]{2,1,0:T(8,128)(2,1)S(1)}, u32[]{:S(2)}, u32[]{:S(2)}) %collective-permute-start.6) | collective-permute-done | bytes 49184 | tf_op jit(solution)/shard_map/ppermute | solution.py:32
  73.5 1.3 %collective-permute-done.5 = bf16[3,32,256]{2,1,0:T(8,128)(2,1)S(1)} collective-permute-done((bf16[3,32,256]{2,1,0:T(8,128)(2,1)S(1)}, bf16[3,32,256]{2,1,0:T(8,128)(2,1)S(1)}, u32[]{:S(2)}, u32[]{:S(2)}) %collective-permute-start.5) | collective-permute-done | bytes 49184 | tf_op jit(solution)/shard_map/ppermute | solution.py:32
  74.8 0.7 add_convert_fusion
  (51 shorter events, 0.9 us)
Async XLA Ops:
  0.0 44.5 %copy-start = (bf16[256,512]{1,0:T(8,128)(2,1)S(1)}, bf16[256,512]{1,0:T(8,128)(2,1)}, u32[]{:S(2)}) copy-start(bf16[256,512]{1,0:T(8,128)(2,1)} %param.22) | copy-start | bytes 786436
  0.0 1.5 %copy-start.1 = (bf16[3,32,256]{2,1,0:T(8,128)(2,1)S(1)}, bf16[3,32,256]{2,1,0:T(8,128)(2,1)}, u32[]{:S(2)}) copy-start(bf16[3,32,256]{2,1,0:T(8,128)(2,1)} %param.12) | copy-start | bytes 147460
  1.6 0.7 copy-start.7
  5.2 17.0 %all-to-all-start = ((bf16[16,3,2,1664]{3,2,1,0:T(2,128)(2,1)}), bf16[16,3,2,1664]{3,2,1,0:T(2,128)(2,1)S(1)}, u32[]{:S(2)}, u32[]{:S(2)}) async-start(bf16[16,3,2,1664]{3,2,1,0:T(2,128)(2,1)} %bitcast.2), calls=%async_computation | async-start | bytes 638976 | tf_op jit(solution)/shard_map/all_to_all | solution.py:54
  13.8 4.0 %copy-start.4 = (bf16[2,8,2,512]{3,2,1,0:T(2,128)(2,1)S(1)}, bf16[2,8,2,512]{3,2,1,0:T(2,128)(2,1)}, u32[]{:S(2)}) copy-start(bf16[2,8,2,512]{3,2,1,0:T(2,128)(2,1)} %param.13) | copy-start | bytes 98308
  13.9 0.7 copy-start.6
  17.8 0.7 copy-start.9
  18.6 0.7 copy-start.10
  24.3 5.4 %copy-start.5 = (bf16[2,24,2,512]{3,2,1,0:T(2,128)(2,1)S(1)}, bf16[2,24,2,512]{3,2,1,0:T(2,128)(2,1)}, u32[]{:S(2)}) copy-start(bf16[2,24,2,512]{3,2,1,0:T(2,128)(2,1)} %param.14) | copy-start | bytes 294916
  24.3 12.0 %all-to-all-start.1 = ((bf16[16,3,2,512]{3,2,1,0:T(2,128)(2,1)}), bf16[16,3,2,512]{3,2,1,0:T(2,128)(2,1)S(1)}, u32[]{:S(2)}, u32[]{:S(2)}) async-start(bf16[16,3,2,512]{3,2,1,0:T(2,128)(2,1)} %broadcast_in_dim.119), calls=%async_computation.1 | async-start | bytes 196608 | tf_op jit(solution)/shard_map/all_to_all | solution.py:24
  29.7 6.8 %copy-start.2 = (bf16[512,256]{1,0:T(8,128)(2,1)S(1)}, bf16[512,256]{1,0:T(8,128)(2,1)}, u32[]{:S(2)}) copy-start(bf16[512,256]{1,0:T(8,128)(2,1)} %param.20) | copy-start | bytes 786436
  29.8 11.2 %collective-permute-start.3 = (bf16[24,2,512]{2,0,1:T(8,128)(2,1)S(1)}, bf16[24,2,512]{2,0,1:T(8,128)(2,1)S(1)}, u32[]{:S(2)}, u32[]{:S(2)}) collective-permute-start(bf16[24,2,512]{2,0,1:T(8,128)(2,1)S(1)} %get-tuple-element.22), channel_id=1, source_target_pairs={{0,4},{4,0},{1,5},{5,1},{2,6},{6,2},{3,7},{7,3},{8,12},{12,8},{9,1... | collective-permute-start | bytes 147464 | tf_op jit(solution)/shard_map/ppermute | solution.py:82
  36.7 6.3 %collective-permute-start.2 = (bf16[3,32,256]{2,1,0:T(8,128)(2,1)S(1)}, bf16[3,32,256]{2,1,0:T(8,128)(2,1)S(1)}, u32[]{:S(2)}, u32[]{:S(2)}) collective-permute-start(bf16[3,32,256]{2,1,0:T(8,128)(2,1)S(1)} %convolution_convert_fusion.3), channel_id=1, source_target_pairs={{0,3},{1,2},{2,1},{3,0},{4,7},{5,6},{6,5},{7,4},{8,11},{9,10},{10,... | collective-permute-start | bytes 147464 | tf_op jit(solution)/shard_map/ppermute | solution.py:32
  40.5 3.4 %collective-permute-start.1 = (bf16[3,32,256]{2,1,0:T(8,128)(2,1)S(1)}, bf16[3,32,256]{2,1,0:T(8,128)(2,1)S(1)}, u32[]{:S(2)}, u32[]{:S(2)}) collective-permute-start(bf16[3,32,256]{2,1,0:T(8,128)(2,1)S(1)} %convolution_convert_fusion.3), channel_id=1, source_target_pairs={{0,2},{1,3},{2,0},{3,1},{4,6},{5,7},{6,4},{7,5},{8,10},{9,11},{10,... | collective-permute-start | bytes 147464 | tf_op jit(solution)/shard_map/ppermute | solution.py:32
  40.8 3.2 %collective-permute-start = (bf16[3,32,256]{2,1,0:T(8,128)(2,1)S(1)}, bf16[3,32,256]{2,1,0:T(8,128)(2,1)S(1)}, u32[]{:S(2)}, u32[]{:S(2)}) collective-permute-start(bf16[3,32,256]{2,1,0:T(8,128)(2,1)S(1)} %convolution_convert_fusion.3), channel_id=1, source_target_pairs={{0,1},{1,0},{2,3},{3,2},{4,5},{5,4},{6,7},{7,6},{8,9},{9,8},{10,11... | collective-permute-start | bytes 147464 | tf_op jit(solution)/shard_map/ppermute | solution.py:32
  44.5 0.7 copy-start.8
  46.3 10.3 %all-to-all-start.2 = ((bf16[16,3,2,640]{3,2,1,0:T(2,128)(2,1)}), bf16[16,3,2,640]{3,2,1,0:T(2,128)(2,1)S(1)}, u32[]{:S(2)}, u32[]{:S(2)}) async-start(bf16[16,3,2,640]{3,2,1,0:T(2,128)(2,1)} %maximum_bitcast_fusion), calls=%async_computation.2 | async-start | bytes 245760 | tf_op jit(solution)/shard_map/all_to_all | solution.py:54
  57.5 10.0 %copy-start.3 = (bf16[512,256]{1,0:T(8,128)(2,1)S(1)}, bf16[512,256]{1,0:T(8,128)(2,1)}, u32[]{:S(2)}) copy-start(bf16[512,256]{1,0:T(8,128)(2,1)} %param.23) | copy-start | bytes 786436
  67.8 5.8 %collective-permute-start.6 = (bf16[3,32,256]{2,1,0:T(8,128)(2,1)S(1)}, bf16[3,32,256]{2,1,0:T(8,128)(2,1)S(1)}, u32[]{:S(2)}, u32[]{:S(2)}) collective-permute-start(bf16[3,32,256]{2,1,0:T(8,128)(2,1)S(1)} %convolution_convert_fusion.2), channel_id=1, source_target_pairs={{0,3},{1,2},{2,1},{3,0},{4,7},{5,6},{6,5},{7,4},{8,11},{9,10},{10,... | collective-permute-start | bytes 147464 | tf_op jit(solution)/shard_map/ppermute | solution.py:32
  71.3 3.5 %collective-permute-start.5 = (bf16[3,32,256]{2,1,0:T(8,128)(2,1)S(1)}, bf16[3,32,256]{2,1,0:T(8,128)(2,1)S(1)}, u32[]{:S(2)}, u32[]{:S(2)}) collective-permute-start(bf16[3,32,256]{2,1,0:T(8,128)(2,1)S(1)} %convolution_convert_fusion.2), channel_id=1, source_target_pairs={{0,2},{1,3},{2,0},{3,1},{4,6},{5,7},{6,4},{7,5},{8,10},{9,11},{10,... | collective-permute-start | bytes 147464 | tf_op jit(solution)/shard_map/ppermute | solution.py:32
  71.9 2.9 %collective-permute-start.4 = (bf16[3,32,256]{2,1,0:T(8,128)(2,1)S(1)}, bf16[3,32,256]{2,1,0:T(8,128)(2,1)S(1)}, u32[]{:S(2)}, u32[]{:S(2)}) collective-permute-start(bf16[3,32,256]{2,1,0:T(8,128)(2,1)S(1)} %convolution_convert_fusion.2), channel_id=1, source_target_pairs={{0,1},{1,0},{2,3},{3,2},{4,5},{5,4},{6,7},{7,6},{8,9},{9,8},{10,11... | collective-permute-start | bytes 147464 | tf_op jit(solution)/shard_map/ppermute | solution.py:32

commit v12 on v7

--- a/solution.py
+++ b/solution.py
@@ -170,14 +170,15 @@
         w_new.astype(jnp.float32), axis=-1
     )
     context = (weighted / totals[..., None]).reshape(steps, seq_dev, width).astype(jnp.bfloat16)
-    context, src_late = lax.optimization_barrier((context, src_pool))
+    context_all = rows_gather(context)
+    partial_out = jnp.einsum(
+        "tsw,wf->tsf", context_all, w_out_self, preferred_element_type=jnp.float32
+    )
+    partial_out, src_late = lax.optimization_barrier((partial_out, src_pool))
     cross_kv = exchange_sources(
         src_late, assign, my_sources, block_at, enc_at, dp_at, dp_count, enc_count, seq_dev
     )
-    context_all = rows_gather(context)
-    residual = current + tensor_sum(
-        jnp.einsum("tsw,wf->tsf", context_all, w_out_self, preferred_element_type=jnp.float32)
-    )
+    residual = current + tensor_sum(partial_out)
 
     scaled = (residual * gain_cross[None, None, :]).astype(jnp.bfloat16)
     cq = jnp.einsum("tsd,dw->tsw", scaled, w_q_cross, preferred_element_type=jnp.float32)

time: 75.1 us -> 73.6 us (0.980)
  starting transfers between devices: 28.8 us -> 27.2 us
  local copies, waits for them, and re-layouts: 8.11 us -> 8.98 us
    all_to_all x2, waiting for transfers between devices: 8.01 us -> 11 us  [rows_reduce_scatter(): got = lax.all_to_all(send, 'enc', 0, 0, tiled=True)]
    ppermute x6, waiting for transfers between devices: 5.78 us -> 3.18 us  [tensor_sum(): lax.ppermute(value, 'tensor', [(i, i ^ k) for i in range(n_t)])]
    all_to_all x1, starting transfers between devices: 5.48 us -> 3.64 us  [rows_gather(): got = lax.all_to_all(send, 'enc', 0, 0, tiled=True)]
    all_to_all x1, waiting for transfers between devices: 3.77 us -> 2.69 us  [rows_gather(): got = lax.all_to_all(send, 'enc', 0, 0, tiled=True)]
    unnamed x28, local copies, waits for them, and re-layouts: 3.08 us -> 3.96 us
  transfers between devices with their start and end apart: 10 -> 10, of which waited for: 7 -> 6; matrix products, arithmetic and copies ran while one was open for 2% -> 4% of each run, Pallas kernels for 0% -> 0%
where the time goes in v12:
time: 73.6 us; the launch traced here: 73 us
  starting transfers between devices  27.2 us (37%)
  waiting for transfers between devices  16.9 us (23%)
  blocking collectives  9.9 us (13%)
  local copies, waits for them, and re-layouts  8.98 us (12%)
  between operations  4.22 us (6%)
  other arithmetic  4.11 us (6%)
  matrix products  1.76 us (2%)
    all_to_all x2, starting transfers between devices, rows_reduce_scatter(): got = lax.all_to_all(send, 'enc', 0, 0, tiled=True)  12.1 us
    all_to_all x2, waiting for transfers between devices, rows_reduce_scatter(): got = lax.all_to_all(send, 'enc', 0, 0, tiled=True)  11 us
    all_to_all x1, blocking collectives, rows_gather(): got = lax.all_to_all(send, 'enc', 0, 0, tiled=True)  9.9 us
    ppermute x6, starting transfers between devices, tensor_sum(): lax.ppermute(value, 'tensor', [(i, i ^ k) for i in range(n_t)])  8.84 us
    unnamed x28, local copies, waits for them, and re-layouts  3.96 us
    all_to_all x1, starting transfers between devices, rows_gather(): got = lax.all_to_all(send, 'enc', 0, 0, tiled=True)  3.64 us
    ppermute x6, waiting for transfers between devices, tensor_sum(): lax.ppermute(value, 'tensor', [(i, i ^ k) for i in range(n_t)])  3.18 us
    all_to_all x1, waiting for transfers between devices, rows_gather(): got = lax.all_to_all(send, 'enc', 0, 0, tiled=True)  2.69 us
  transfers between devices with their start and end apart: 10, of which 6 were waited for; matrix products, arithmetic and copies ran while one was open for 4% of the time, Pallas kernels for 0%

profile of v12, /device:TPU:1, one launch (start us, length us, event | category | flops | bytes accessed | tf_op | source)
XLA Modules:
  0.0 73.0 jit_solution(7702069447641893862)
XLA Ops:
  0.0 1.0 %fusion.23 = f32[3,32]{1,0:T(4,128)S(1)} fusion(bf16[3,32,256]{2,1,0:T(8,128)(2,1)} %param.12), kind=kLoop, calls=%fused_computation.38 | loop fusion | flops 73632 | bytes 49536 | tf_op jit(solution)/shard_map/reduce_sum | solution.py:41
  1.0 0.2 copy-done
  1.2 0.3 convolution_convert_fusion
  1.4 0.3 copy.125
  1.7 0.3 convert_element_type.192
  1.9 0.1 reduce_sum.95
  2.0 0.1 copy.126
  2.1 0.1 copy.129
  2.3 0.1 copy.130
  2.4 0.8 %concatenate.13 = bf16[3,16,2,1664]{3,2,1,0:T(2,128)(2,1)S(1)} concatenate(bf16[3,16,2,1536]{3,2,1,0:T(2,128)(2,1)S(1)} %convert_element_type.192, bf16[3,16,2,1]{3,2,1,0:T(2,128)(2,1)S(1)} %copy.129, bf16[3,16,2,1]{3,2,1,0:T(2,128)(2,1)S(1)} %copy.130, bf16[3,16,2,126]{3,2,1,0:T(2,128)(2,1)S(1)} %concatenate.12), dimensions={3} | concatenate | bytes 638976 | tf_op jit(solution)/shard_map/concatenate | solution.py:47
  3.3 0.9 %copy.131 = bf16[16,3,2,1664]{3,2,1,0:T(2,128)(2,1)} copy(bf16[16,3,2,1664]{3,2,0,1:T(2,128)(2,1)S(1)} %bitcast.87) | data formatting | bytes 638976 | tf_op jit(solution)/shard_map/transpose | solution.py:53
  4.2 8.6 %all-to-all-start = ((bf16[16,3,2,1664]{3,2,1,0:T(2,128)(2,1)}), bf16[16,3,2,1664]{3,2,1,0:T(2,128)(2,1)S(1)}, u32[]{:S(2)}, u32[]{:S(2)}) async-start(bf16[16,3,2,1664]{3,2,1,0:T(2,128)(2,1)} %copy.131), calls=%async_computation | async-start | bytes 638976 | tf_op jit(solution)/shard_map/all_to_all | solution.py:54
  12.8 0.7 copy-done.5
  13.6 0.1 slice_reduce_fusion
  13.7 0.6 copy-done.10
  14.4 0.1 iota_compare_fusion.2
  14.5 0.7 copy-done.7
  15.2 0.7 %fusion.37 = (s32[]{:T(128)}, s32[2]{0:T(128)S(1)}, s32[2]{0:T(128)S(1)}, s32[]{:T(128)}) fusion(s32[]{:T(128)S(6)} %add.96, s32[64]{0:T(128)S(1)} %copy-done.7, s32[]{:T(128)S(6)} %select_n.102, s32[]{:T(128)S(6)} %select_n.110), kind=kLoop, calls=%fused_computation.87 | loop fusion | flops 86 | bytes 52 | tf_op jit(solution)/shard_map/reduce_sum | solution.py:79
  15.9 0.7 copy-done.11
  16.6 0.2 fusion.35
  16.8 4.4 %all-to-all-done = bf16[16,3,2,1664]{3,2,1,0:T(2,128)(2,1)S(1)} async-done(((bf16[16,3,2,1664]{3,2,1,0:T(2,128)(2,1)}), bf16[16,3,2,1664]{3,2,1,0:T(2,128)(2,1)S(1)}, u32[]{:S(2)}, u32[]{:S(2)}) %all-to-all-start) | async-done | bytes 319520 | tf_op jit(solution)/shard_map/all_to_all | solution.py:54
  21.2 0.1 convert_reduce_fusion
  21.4 0.1 copy.168
  21.5 0.1 copy.169
  21.6 0.1 copy.136
  21.7 0.1 fusion.30
  21.9 0.2 convert_reduce_fusion.4
  22.1 0.1 convolution_bitcast_fusion.2
  22.2 0.1 convert_reduce_fusion.3
  22.4 0.2 fusion.3
  22.6 0.7 broadcast_in_dim.119
  23.3 3.6 %all-to-all-start.1 = ((bf16[16,3,2,512]{3,2,1,0:T(2,128)(2,1)}), bf16[16,3,2,512]{3,2,1,0:T(2,128)(2,1)S(1)}, u32[]{:S(2)}, u32[]{:S(2)}) async-start(bf16[16,3,2,512]{3,2,1,0:T(2,128)(2,1)} %broadcast_in_dim.119), calls=%async_computation.1 | async-start | bytes 196608 | tf_op jit(solution)/shard_map/all_to_all | solution.py:24
  29.5 0.1 pad.3.clone
  30.9 2.7 %all-to-all-done.1 = bf16[16,3,2,512]{3,2,1,0:T(2,128)(2,1)S(1)} async-done(((bf16[16,3,2,512]{3,2,1,0:T(2,128)(2,1)}), bf16[16,3,2,512]{3,2,1,0:T(2,128)(2,1)S(1)}, u32[]{:S(2)}, u32[]{:S(2)}) %all-to-all-start.1) | async-done | bytes 98336 | tf_op jit(solution)/shard_map/all_to_all | solution.py:24
  33.7 0.2 fusion.20
  33.9 4.1 %collective-permute-start.2 = (bf16[3,32,256]{2,1,0:T(8,128)(2,1)S(1)}, bf16[3,32,256]{2,1,0:T(8,128)(2,1)S(1)}, u32[]{:S(2)}, u32[]{:S(2)}) collective-permute-start(bf16[3,32,256]{2,1,0:T(8,128)(2,1)S(1)} %fusion.20), channel_id=1, source_target_pairs={{0,3},{1,2},{2,1},{3,0},{4,7},{5,6},{6,5},{7,4},{8,11},{9,10},{10,... | collective-permute-start | bytes 147464 | tf_op jit(solution)/shard_map/ppermute | solution.py:32
  38.0 0.3 collective-permute-start.1
  38.3 0.2 collective-permute-start
  38.6 2.6 %collective-permute-start.3 = (bf16[24,2,512]{2,0,1:T(8,128)(2,1)S(1)}, bf16[24,2,512]{2,0,1:T(8,128)(2,1)S(1)}, u32[]{:S(2)}, u32[]{:S(2)}) collective-permute-start(bf16[24,2,512]{2,0,1:T(8,128)(2,1)S(1)} %get-tuple-element.22), channel_id=1, source_target_pairs={{0,4},{4,0},{1,5},{5,1},{2,6},{6,2},{3,7},{7,3},{8,12},{12,8},{9,1... | collective-permute-start | bytes 147464 | tf_op jit(solution)/shard_map/ppermute | solution.py:82
  41.2 0.3 collective-permute-done.1
  41.5 0.1 multiply_reduce_fusion
  41.6 0.1 reduce_sum.103
  41.7 0.1 copy.147
  41.8 0.1 copy.152
  41.9 0.1 copy.151
  42.1 0.7 copy-done.9
  42.7 0.2 convolution_convert_fusion.1
  42.9 0.8 %maximum_bitcast_fusion = bf16[16,3,2,640]{3,2,1,0:T(2,128)(2,1)} fusion(bf16[3,16,2,1]{3,2,0,1:T(2,128)(2,1)S(1)} %copy.152, bf16[3,16,2,1]{3,2,0,1:T(2,128)(2,1)S(1)} %copy.151, bf16[640]{0:T(1024)(128)(2,1)S(1)} %pad.3.clone, bf16[3,16,2,512]{3,2,1,0:T(2,128)(2,1)S(1)} %concatenate.14), kind=kLoop, calls=%fused_computation.36 | loop fusion | flops 491520 | bytes 222848 | tf_op jit(solution)/shard_map/transpose | solution.py:53
  43.8 3.5 %all-to-all-start.2 = ((bf16[16,3,2,640]{3,2,1,0:T(2,128)(2,1)}), bf16[16,3,2,640]{3,2,1,0:T(2,128)(2,1)S(1)}, u32[]{:S(2)}, u32[]{:S(2)}) async-start(bf16[16,3,2,640]{3,2,1,0:T(2,128)(2,1)} %maximum_bitcast_fusion), calls=%async_computation.2 | async-start | bytes 245760 | tf_op jit(solution)/shard_map/all_to_all | solution.py:54
  47.3 0.1 broadcast_select_fusion
  47.4 6.6 %all-to-all-done.2 = bf16[16,3,2,640]{3,2,1,0:T(2,128)(2,1)S(1)} async-done(((bf16[16,3,2,640]{3,2,1,0:T(2,128)(2,1)}), bf16[16,3,2,640]{3,2,1,0:T(2,128)(2,1)S(1)}, u32[]{:S(2)}, u32[]{:S(2)}) %all-to-all-start.2) | async-done | bytes 122912 | tf_op jit(solution)/shard_map/all_to_all | solution.py:54
  54.2 0.1 copy.173
  54.3 0.1 copy.174
  54.4 0.1 copy.158
  54.5 0.1 fusion.31
  54.6 0.2 convert_reduce_fusion.2
  54.8 0.1 fusion.4
  55.0 9.9 %all_to_all.20 = bf16[16,3,2,512]{3,2,1,0:T(2,128)(2,1)S(1)} all-to-all(bf16[16,3,2,512]{3,2,1,0:T(2,128)(2,1)S(1)} %broadcast_in_dim.128), channel_id=1, replica_groups=mesh['enc'=16,'dp'=2,'tensor'=4] {'enc'}, dimensions={0} | all-to-all | bytes 196608 | tf_op jit(solution)/shard_map/all_to_all | solution.py:24
  65.1 0.2 convolution_convert_fusion.2
  65.3 3.5 %collective-permute-start.6 = (bf16[3,32,256]{2,1,0:T(8,128)(2,1)S(1)}, bf16[3,32,256]{2,1,0:T(8,128)(2,1)S(1)}, u32[]{:S(2)}, u32[]{:S(2)}) collective-permute-start(bf16[3,32,256]{2,1,0:T(8,128)(2,1)S(1)} %convolution_convert_fusion.2), channel_id=1, source_target_pairs={{0,3},{1,2},{2,1},{3,0},{4,7},{5,6},{6,5},{7,4},{8,11},{9,10},{10,... | collective-permute-start | bytes 147464 | tf_op jit(solution)/shard_map/ppermute | solution.py:32
  68.8 0.7 collective-permute-start.5
  69.5 1.4 %collective-permute-done.6 = bf16[3,32,256]{2,1,0:T(8,128)(2,1)S(1)} collective-permute-done((bf16[3,32,256]{2,1,0:T(8,128)(2,1)S(1)}, bf16[3,32,256]{2,1,0:T(8,128)(2,1)S(1)}, u32[]{:S(2)}, u32[]{:S(2)}) %collective-permute-start.6) | collective-permute-done | bytes 49184 | tf_op jit(solution)/shard_map/ppermute | solution.py:32
  70.9 1.4 %collective-permute-done.5 = bf16[3,32,256]{2,1,0:T(8,128)(2,1)S(1)} collective-permute-done((bf16[3,32,256]{2,1,0:T(8,128)(2,1)S(1)}, bf16[3,32,256]{2,1,0:T(8,128)(2,1)S(1)}, u32[]{:S(2)}, u32[]{:S(2)}) %collective-permute-start.5) | collective-permute-done | bytes 49184 | tf_op jit(solution)/shard_map/ppermute | solution.py:32
  72.4 0.7 add_convert_fusion
  (55 shorter events, 1.0 us)
Async XLA Ops:
  0.0 1.2 %copy-start = (bf16[256,3,512]{2,0,1:T(8,128)(2,1)S(1)}, bf16[256,3,512]{2,0,1:T(8,128)(2,1)}, u32[]{:S(2)}) copy-start(bf16[256,3,512]{2,0,1:T(8,128)(2,1)} %param.19) | copy-start | bytes 2359300
  0.0 1.2 %copy-start.1 = (bf16[3,32,256]{2,1,0:T(8,128)(2,1)S(1)}, bf16[3,32,256]{2,1,0:T(8,128)(2,1)}, u32[]{:S(2)}) copy-start(bf16[3,32,256]{2,1,0:T(8,128)(2,1)} %param.12) | copy-start | bytes 147460
  0.0 1.2 %copy-start.8 = (f32[256]{0:T(256)S(1)}, f32[256]{0:T(256)}, u32[]{:S(2)}) copy-start(f32[256]{0:T(256)} %param.18) | copy-start | bytes 3076
  4.2 17.0 %all-to-all-start = ((bf16[16,3,2,1664]{3,2,1,0:T(2,128)(2,1)}), bf16[16,3,2,1664]{3,2,1,0:T(2,128)(2,1)S(1)}, u32[]{:S(2)}, u32[]{:S(2)}) async-start(bf16[16,3,2,1664]{3,2,1,0:T(2,128)(2,1)} %copy.131), calls=%async_computation | async-start | bytes 638976 | tf_op jit(solution)/shard_map/all_to_all | solution.py:54
  12.8 0.8 %copy-start.5 = (bf16[2,8,2,512]{3,2,1,0:T(2,128)(2,1)S(1)}, bf16[2,8,2,512]{3,2,1,0:T(2,128)(2,1)}, u32[]{:S(2)}) copy-start(bf16[2,8,2,512]{3,2,1,0:T(2,128)(2,1)} %param.13) | copy-start | bytes 98308
  13.7 0.7 copy-start.10
  14.5 0.7 copy-start.7
  15.9 0.7 copy-start.11
  23.3 10.4 %copy-start.3 = (bf16[512,256]{1,0:T(8,128)(2,1)S(1)}, bf16[512,256]{1,0:T(8,128)(2,1)}, u32[]{:S(2)}) copy-start(bf16[512,256]{1,0:T(8,128)(2,1)} %param.20) | copy-start | bytes 786436
  23.3 10.3 %all-to-all-start.1 = ((bf16[16,3,2,512]{3,2,1,0:T(2,128)(2,1)}), bf16[16,3,2,512]{3,2,1,0:T(2,128)(2,1)S(1)}, u32[]{:S(2)}, u32[]{:S(2)}) async-start(bf16[16,3,2,512]{3,2,1,0:T(2,128)(2,1)} %broadcast_in_dim.119), calls=%async_computation.1 | async-start | bytes 196608 | tf_op jit(solution)/shard_map/all_to_all | solution.py:24
  33.7 4.8 %copy-start.6 = (bf16[2,24,2,512]{3,2,1,0:T(2,128)(2,1)S(1)}, bf16[2,24,2,512]{3,2,1,0:T(2,128)(2,1)}, u32[]{:S(2)}) copy-start(bf16[2,24,2,512]{3,2,1,0:T(2,128)(2,1)} %param.14) | copy-start | bytes 294916
  33.9 7.3 %collective-permute-start.2 = (bf16[3,32,256]{2,1,0:T(8,128)(2,1)S(1)}, bf16[3,32,256]{2,1,0:T(8,128)(2,1)S(1)}, u32[]{:S(2)}, u32[]{:S(2)}) collective-permute-start(bf16[3,32,256]{2,1,0:T(8,128)(2,1)S(1)} %fusion.20), channel_id=1, source_target_pairs={{0,3},{1,2},{2,1},{3,0},{4,7},{5,6},{6,5},{7,4},{8,11},{9,10},{10,... | collective-permute-start | bytes 147464 | tf_op jit(solution)/shard_map/ppermute | solution.py:32
  38.0 3.4 %collective-permute-start.1 = (bf16[3,32,256]{2,1,0:T(8,128)(2,1)S(1)}, bf16[3,32,256]{2,1,0:T(8,128)(2,1)S(1)}, u32[]{:S(2)}, u32[]{:S(2)}) collective-permute-start(bf16[3,32,256]{2,1,0:T(8,128)(2,1)S(1)} %fusion.20), channel_id=1, source_target_pairs={{0,2},{1,3},{2,0},{3,1},{4,6},{5,7},{6,4},{7,5},{8,10},{9,11},{10,... | collective-permute-start | bytes 147464 | tf_op jit(solution)/shard_map/ppermute | solution.py:32
  38.3 3.2 %collective-permute-start = (bf16[3,32,256]{2,1,0:T(8,128)(2,1)S(1)}, bf16[3,32,256]{2,1,0:T(8,128)(2,1)S(1)}, u32[]{:S(2)}, u32[]{:S(2)}) collective-permute-start(bf16[3,32,256]{2,1,0:T(8,128)(2,1)S(1)} %fusion.20), channel_id=1, source_target_pairs={{0,1},{1,0},{2,3},{3,2},{4,5},{5,4},{6,7},{7,6},{8,9},{9,8},{10,11... | collective-permute-start | bytes 147464 | tf_op jit(solution)/shard_map/ppermute | solution.py:32
  38.5 3.5 %copy-start.2 = (bf16[256,512]{1,0:T(8,128)(2,1)S(1)}, bf16[256,512]{1,0:T(8,128)(2,1)}, u32[]{:S(2)}) copy-start(bf16[256,512]{1,0:T(8,128)(2,1)} %param.22) | copy-start | bytes 786436
  38.6 8.7 %collective-permute-start.3 = (bf16[24,2,512]{2,0,1:T(8,128)(2,1)S(1)}, bf16[24,2,512]{2,0,1:T(8,128)(2,1)S(1)}, u32[]{:S(2)}, u32[]{:S(2)}) collective-permute-start(bf16[24,2,512]{2,0,1:T(8,128)(2,1)S(1)} %get-tuple-element.22), channel_id=1, source_target_pairs={{0,4},{4,0},{1,5},{5,1},{2,6},{6,2},{3,7},{7,3},{8,12},{12,8},{9,1... | collective-permute-start | bytes 147464 | tf_op jit(solution)/shard_map/ppermute | solution.py:82
  42.0 0.7 copy-start.9
  43.8 10.3 %all-to-all-start.2 = ((bf16[16,3,2,640]{3,2,1,0:T(2,128)(2,1)}), bf16[16,3,2,640]{3,2,1,0:T(2,128)(2,1)S(1)}, u32[]{:S(2)}, u32[]{:S(2)}) async-start(bf16[16,3,2,640]{3,2,1,0:T(2,128)(2,1)} %maximum_bitcast_fusion), calls=%async_computation.2 | async-start | bytes 245760 | tf_op jit(solution)/shard_map/all_to_all | solution.py:54
  55.0 10.0 %copy-start.4 = (bf16[512,256]{1,0:T(8,128)(2,1)S(1)}, bf16[512,256]{1,0:T(8,128)(2,1)}, u32[]{:S(2)}) copy-start(bf16[512,256]{1,0:T(8,128)(2,1)} %param.23) | copy-start | bytes 786436
  65.3 5.7 %collective-permute-start.6 = (bf16[3,32,256]{2,1,0:T(8,128)(2,1)S(1)}, bf16[3,32,256]{2,1,0:T(8,128)(2,1)S(1)}, u32[]{:S(2)}, u32[]{:S(2)}) collective-permute-start(bf16[3,32,256]{2,1,0:T(8,128)(2,1)S(1)} %convolution_convert_fusion.2), channel_id=1, source_target_pairs={{0,3},{1,2},{2,1},{3,0},{4,7},{5,6},{6,5},{7,4},{8,11},{9,10},{10,... | collective-permute-start | bytes 147464 | tf_op jit(solution)/shard_map/ppermute | solution.py:32
  68.8 3.6 %collective-permute-start.5 = (bf16[3,32,256]{2,1,0:T(8,128)(2,1)S(1)}, bf16[3,32,256]{2,1,0:T(8,128)(2,1)S(1)}, u32[]{:S(2)}, u32[]{:S(2)}) collective-permute-start(bf16[3,32,256]{2,1,0:T(8,128)(2,1)S(1)} %convolution_convert_fusion.2), channel_id=1, source_target_pairs={{0,2},{1,3},{2,0},{3,1},{4,6},{5,7},{6,4},{7,5},{8,10},{9,11},{10,... | collective-permute-start | bytes 147464 | tf_op jit(solution)/shard_map/ppermute | solution.py:32
  69.5 2.9 %collective-permute-start.4 = (bf16[3,32,256]{2,1,0:T(8,128)(2,1)S(1)}, bf16[3,32,256]{2,1,0:T(8,128)(2,1)S(1)}, u32[]{:S(2)}, u32[]{:S(2)}) collective-permute-start(bf16[3,32,256]{2,1,0:T(8,128)(2,1)S(1)} %convolution_convert_fusion.2), channel_id=1, source_target_pairs={{0,1},{1,0},{2,3},{3,2},{4,5},{5,4},{6,7},{7,6},{8,9},{9,8},{10,11... | collective-permute-start | bytes 147464 | tf_op jit(solution)/shard_map/ppermute | solution.py:32

commit v13 on v12

--- a/solution.py
+++ b/solution.py
@@ -136,6 +136,8 @@
     )
     cross_usable = token_at[None, :] < my_len[:, None]
 
+    w_q_gained = (gain_cross[:, None] * w_q_cross.astype(jnp.float32)).astype(jnp.bfloat16)
+
     current = hidden_in.astype(jnp.float32)
     scaled = (current * gain_self[None, None, :]).astype(jnp.bfloat16)
     proj = jnp.einsum("tsd,dcw->tscw", scaled, w_qkv, preferred_element_type=jnp.float32)
@@ -174,14 +176,17 @@
     partial_out = jnp.einsum(
         "tsw,wf->tsf", context_all, w_out_self, preferred_element_type=jnp.float32
     )
-    partial_out, src_late = lax.optimization_barrier((partial_out, src_pool))
+    partial_out, src_late, w_q_gained = lax.optimization_barrier(
+        (partial_out, src_pool, w_q_gained)
+    )
     cross_kv = exchange_sources(
         src_late, assign, my_sources, block_at, enc_at, dp_at, dp_count, enc_count, seq_dev
     )
     residual = current + tensor_sum(partial_out)
 
-    scaled = (residual * gain_cross[None, None, :]).astype(jnp.bfloat16)
-    cq = jnp.einsum("tsd,dw->tsw", scaled, w_q_cross, preferred_element_type=jnp.float32)
+    cq = jnp.einsum(
+        "tsd,dw->tsw", residual.astype(jnp.bfloat16), w_q_gained, preferred_element_type=jnp.float32
+    )
     own = rows_reduce_scatter(with_sumsq(cq, residual), seq_dev)
     cross_query = split_norm(own, width).reshape(steps, seq_dev, head_count, DK)
     cross_keys = cross_kv[:, :, 0].reshape(seq_dev, source_len, head_count, DK)

time: 73.6 us -> 73 us (level)
  waiting for transfers between devices: 16.9 us -> 16.1 us
    all_to_all x2, waiting for transfers between devices: 11 us -> 10.2 us  [rows_reduce_scatter(): got = lax.all_to_all(send, 'enc', 0, 0, tiled=True)]
  transfers between devices with their start and end apart: 10 -> 10, of which waited for: 6 -> 6; matrix products, arithmetic and copies ran while one was open for 4% -> 5% of each run, Pallas kernels for 0% -> 0%
where the time goes in v13:
time: 73 us; the launch traced here: 72.5 us
  starting transfers between devices  27.3 us (37%)
  waiting for transfers between devices  16.1 us (22%)
  blocking collectives  9.9 us (14%)
  local copies, waits for them, and re-layouts  8.97 us (12%)
  other arithmetic  4.21 us (6%)
  between operations  4.21 us (6%)
  matrix products  1.77 us (2%)
    all_to_all x2, starting transfers between devices, rows_reduce_scatter(): got = lax.all_to_all(send, 'enc', 0, 0, tiled=True)  12.2 us
    all_to_all x2, waiting for transfers between devices, rows_reduce_scatter(): got = lax.all_to_all(send, 'enc', 0, 0, tiled=True)  10.2 us
    all_to_all x1, blocking collectives, rows_gather(): got = lax.all_to_all(send, 'enc', 0, 0, tiled=True)  9.9 us
    ppermute x6, starting transfers between devices, tensor_sum(): lax.ppermute(value, 'tensor', [(i, i ^ k) for i in range(n_t)])  8.82 us
    unnamed x28, local copies, waits for them, and re-layouts  3.95 us
    all_to_all x1, starting transfers between devices, rows_gather(): got = lax.all_to_all(send, 'enc', 0, 0, tiled=True)  3.64 us
    ppermute x6, waiting for transfers between devices, tensor_sum(): lax.ppermute(value, 'tensor', [(i, i ^ k) for i in range(n_t)])  3.19 us
    all_to_all x1, waiting for transfers between devices, rows_gather(): got = lax.all_to_all(send, 'enc', 0, 0, tiled=True)  2.69 us
  transfers between devices with their start and end apart: 10, of which 6 were waited for; matrix products, arithmetic and copies ran while one was open for 5% of the time, Pallas kernels for 0%

profile of v13, /device:TPU:1, one launch (start us, length us, event | category | flops | bytes accessed | tf_op | source)
XLA Modules:
  0.0 72.5 jit_solution(11261446083267265441)
XLA Ops:
  0.0 1.0 %fusion.23 = f32[3,32]{1,0:T(4,128)S(1)} fusion(bf16[3,32,256]{2,1,0:T(8,128)(2,1)} %param.12), kind=kLoop, calls=%fused_computation.39 | loop fusion | flops 73632 | bytes 49536 | tf_op jit(solution)/shard_map/reduce_sum | solution.py:41
  1.0 0.2 copy-done
  1.2 0.3 convolution_convert_fusion
  1.4 0.3 copy.125
  1.7 0.3 convert_element_type.198
  1.9 0.1 reduce_sum.95
  2.0 0.1 copy.126
  2.1 0.1 copy.129
  2.3 0.1 copy.130
  2.4 0.8 %concatenate.13 = bf16[3,16,2,1664]{3,2,1,0:T(2,128)(2,1)S(1)} concatenate(bf16[3,16,2,1536]{3,2,1,0:T(2,128)(2,1)S(1)} %convert_element_type.198, bf16[3,16,2,1]{3,2,1,0:T(2,128)(2,1)S(1)} %copy.129, bf16[3,16,2,1]{3,2,1,0:T(2,128)(2,1)S(1)} %copy.130, bf16[3,16,2,126]{3,2,1,0:T(2,128)(2,1)S(1)} %concatenate.12), dimensions={3} | concatenate | bytes 638976 | tf_op jit(solution)/shard_map/concatenate | solution.py:47
  3.3 0.9 %copy.131 = bf16[16,3,2,1664]{3,2,1,0:T(2,128)(2,1)} copy(bf16[16,3,2,1664]{3,2,0,1:T(2,128)(2,1)S(1)} %bitcast.87) | data formatting | bytes 638976 | tf_op jit(solution)/shard_map/transpose | solution.py:53
  4.2 8.7 %all-to-all-start = ((bf16[16,3,2,1664]{3,2,1,0:T(2,128)(2,1)}), bf16[16,3,2,1664]{3,2,1,0:T(2,128)(2,1)S(1)}, u32[]{:S(2)}, u32[]{:S(2)}) async-start(bf16[16,3,2,1664]{3,2,1,0:T(2,128)(2,1)} %copy.131), calls=%async_computation | async-start | bytes 638976 | tf_op jit(solution)/shard_map/all_to_all | solution.py:54
  13.0 0.7 copy-done.5
  13.7 0.1 slice_reduce_fusion
  13.8 0.6 copy-done.10
  14.6 0.1 iota_compare_fusion.2
  14.6 0.7 copy-done.7
  15.3 0.7 %fusion.37 = (s32[]{:T(128)}, s32[2]{0:T(128)S(1)}, s32[2]{0:T(128)S(1)}, s32[]{:T(128)}) fusion(s32[]{:T(128)S(6)} %add.96, s32[64]{0:T(128)S(1)} %copy-done.7, s32[]{:T(128)S(6)} %select_n.102, s32[]{:T(128)S(6)} %select_n.110), kind=kLoop, calls=%fused_computation.87 | loop fusion | flops 86 | bytes 52 | tf_op jit(solution)/shard_map/reduce_sum | solution.py:79
  16.0 0.7 copy-done.11
  16.7 0.2 fusion.35
  17.0 0.7 copy-done.9
  17.6 0.1 multiply_convert_fusion
  17.8 3.6 %all-to-all-done = bf16[16,3,2,1664]{3,2,1,0:T(2,128)(2,1)S(1)} async-done(((bf16[16,3,2,1664]{3,2,1,0:T(2,128)(2,1)}), bf16[16,3,2,1664]{3,2,1,0:T(2,128)(2,1)S(1)}, u32[]{:S(2)}, u32[]{:S(2)}) %all-to-all-start) | async-done | bytes 319520 | tf_op jit(solution)/shard_map/all_to_all | solution.py:54
  21.4 0.1 convert_reduce_fusion
  21.6 0.1 copy.168
  21.7 0.1 copy.169
  21.8 0.1 copy.136
  21.9 0.1 fusion.30
  22.0 0.2 convert_reduce_fusion.4
  22.2 0.1 convolution_bitcast_fusion.2
  22.3 0.1 convert_reduce_fusion.3
  22.5 0.2 fusion.3
  22.7 0.7 broadcast_in_dim.119
  23.4 3.6 %all-to-all-start.1 = ((bf16[16,3,2,512]{3,2,1,0:T(2,128)(2,1)}), bf16[16,3,2,512]{3,2,1,0:T(2,128)(2,1)S(1)}, u32[]{:S(2)}, u32[]{:S(2)}) async-start(bf16[16,3,2,512]{3,2,1,0:T(2,128)(2,1)} %broadcast_in_dim.119), calls=%async_computation.1 | async-start | bytes 196608 | tf_op jit(solution)/shard_map/all_to_all | solution.py:24
  31.0 2.7 %all-to-all-done.1 = bf16[16,3,2,512]{3,2,1,0:T(2,128)(2,1)S(1)} async-done(((bf16[16,3,2,512]{3,2,1,0:T(2,128)(2,1)}), bf16[16,3,2,512]{3,2,1,0:T(2,128)(2,1)S(1)}, u32[]{:S(2)}, u32[]{:S(2)}) %all-to-all-start.1) | async-done | bytes 98336 | tf_op jit(solution)/shard_map/all_to_all | solution.py:24
  33.8 0.2 fusion.20
  34.0 4.1 %collective-permute-start.2 = (bf16[3,32,256]{2,1,0:T(8,128)(2,1)S(1)}, bf16[3,32,256]{2,1,0:T(8,128)(2,1)S(1)}, u32[]{:S(2)}, u32[]{:S(2)}) collective-permute-start(bf16[3,32,256]{2,1,0:T(8,128)(2,1)S(1)} %fusion.20), channel_id=1, source_target_pairs={{0,3},{1,2},{2,1},{3,0},{4,7},{5,6},{6,5},{7,4},{8,11},{9,10},{10,... | collective-permute-start | bytes 147464 | tf_op jit(solution)/shard_map/ppermute | solution.py:32
  38.1 0.3 collective-permute-start.1
  38.4 0.2 collective-permute-start
  38.7 2.6 %collective-permute-start.3 = (bf16[24,2,512]{2,0,1:T(8,128)(2,1)S(1)}, bf16[24,2,512]{2,0,1:T(8,128)(2,1)S(1)}, u32[]{:S(2)}, u32[]{:S(2)}) collective-permute-start(bf16[24,2,512]{2,0,1:T(8,128)(2,1)S(1)} %get-tuple-element.24), channel_id=1, source_target_pairs={{0,4},{4,0},{1,5},{5,1},{2,6},{6,2},{3,7},{7,3},{8,12},{12,8},{9,1... | collective-permute-start | bytes 147464 | tf_op jit(solution)/shard_map/ppermute | solution.py:82
  41.3 0.3 collective-permute-done.1
  41.6 0.1 multiply_reduce_fusion
  41.7 0.1 reduce_sum.103
  41.8 0.1 copy.147
  41.9 0.1 copy.152
  42.0 0.1 copy.151
  42.2 0.2 convolution_convert_fusion.1
  42.4 0.8 %maximum_bitcast_fusion = bf16[16,3,2,640]{3,2,1,0:T(2,128)(2,1)} fusion(bf16[3,16,2,1]{3,2,0,1:T(2,128)(2,1)S(1)} %copy.152, bf16[3,16,2,1]{3,2,0,1:T(2,128)(2,1)S(1)} %copy.151, bf16[640]{0:T(1024)(128)(2,1)S(1)} %pad.3.clone, bf16[3,16,2,512]{3,2,1,0:T(2,128)(2,1)S(1)} %concatenate.14), kind=kLoop, calls=%fused_computation.37 | loop fusion | flops 491520 | bytes 222848 | tf_op jit(solution)/shard_map/transpose | solution.py:53
  43.2 3.5 %all-to-all-start.2 = ((bf16[16,3,2,640]{3,2,1,0:T(2,128)(2,1)}), bf16[16,3,2,640]{3,2,1,0:T(2,128)(2,1)S(1)}, u32[]{:S(2)}, u32[]{:S(2)}) async-start(bf16[16,3,2,640]{3,2,1,0:T(2,128)(2,1)} %maximum_bitcast_fusion), calls=%async_computation.2 | async-start | bytes 245760 | tf_op jit(solution)/shard_map/all_to_all | solution.py:54
  46.8 0.1 broadcast_select_fusion
  46.9 6.6 %all-to-all-done.2 = bf16[16,3,2,640]{3,2,1,0:T(2,128)(2,1)S(1)} async-done(((bf16[16,3,2,640]{3,2,1,0:T(2,128)(2,1)}), bf16[16,3,2,640]{3,2,1,0:T(2,128)(2,1)S(1)}, u32[]{:S(2)}, u32[]{:S(2)}) %all-to-all-start.2) | async-done | bytes 122912 | tf_op jit(solution)/shard_map/all_to_all | solution.py:54
  53.6 0.1 copy.173
  53.7 0.1 copy.174
  53.8 0.1 copy.158
  53.9 0.1 fusion.31
  54.0 0.2 convert_reduce_fusion.2
  54.3 0.1 fusion.4
  54.5 9.9 %all_to_all.20 = bf16[16,3,2,512]{3,2,1,0:T(2,128)(2,1)S(1)} all-to-all(bf16[16,3,2,512]{3,2,1,0:T(2,128)(2,1)S(1)} %broadcast_in_dim.128), channel_id=1, replica_groups=mesh['enc'=16,'dp'=2,'tensor'=4] {'enc'}, dimensions={0} | all-to-all | bytes 196608 | tf_op jit(solution)/shard_map/all_to_all | solution.py:24
  64.5 0.2 convolution_convert_fusion.2
  64.7 3.5 %collective-permute-start.6 = (bf16[3,32,256]{2,1,0:T(8,128)(2,1)S(1)}, bf16[3,32,256]{2,1,0:T(8,128)(2,1)S(1)}, u32[]{:S(2)}, u32[]{:S(2)}) collective-permute-start(bf16[3,32,256]{2,1,0:T(8,128)(2,1)S(1)} %convolution_convert_fusion.2), channel_id=1, source_target_pairs={{0,3},{1,2},{2,1},{3,0},{4,7},{5,6},{6,5},{7,4},{8,11},{9,10},{10,... | collective-permute-start | bytes 147464 | tf_op jit(solution)/shard_map/ppermute | solution.py:32
  68.2 0.7 collective-permute-start.5
  68.9 1.5 %collective-permute-done.6 = bf16[3,32,256]{2,1,0:T(8,128)(2,1)S(1)} collective-permute-done((bf16[3,32,256]{2,1,0:T(8,128)(2,1)S(1)}, bf16[3,32,256]{2,1,0:T(8,128)(2,1)S(1)}, u32[]{:S(2)}, u32[]{:S(2)}) %collective-permute-start.6) | collective-permute-done | bytes 49184 | tf_op jit(solution)/shard_map/ppermute | solution.py:32
  70.4 1.4 %collective-permute-done.5 = bf16[3,32,256]{2,1,0:T(8,128)(2,1)S(1)} collective-permute-done((bf16[3,32,256]{2,1,0:T(8,128)(2,1)S(1)}, bf16[3,32,256]{2,1,0:T(8,128)(2,1)S(1)}, u32[]{:S(2)}, u32[]{:S(2)}) %collective-permute-start.5) | collective-permute-done | bytes 49184 | tf_op jit(solution)/shard_map/ppermute | solution.py:32
  71.8 0.7 add_convert_fusion
  (56 shorter events, 1.1 us)
Async XLA Ops:
  0.0 1.2 %copy-start = (bf16[256,3,512]{2,0,1:T(8,128)(2,1)S(1)}, bf16[256,3,512]{2,0,1:T(8,128)(2,1)}, u32[]{:S(2)}) copy-start(bf16[256,3,512]{2,0,1:T(8,128)(2,1)} %param.19) | copy-start | bytes 2359300
  0.0 1.2 %copy-start.1 = (bf16[3,32,256]{2,1,0:T(8,128)(2,1)S(1)}, bf16[3,32,256]{2,1,0:T(8,128)(2,1)}, u32[]{:S(2)}) copy-start(bf16[3,32,256]{2,1,0:T(8,128)(2,1)} %param.12) | copy-start | bytes 147460
  0.0 1.2 %copy-start.8 = (f32[256]{0:T(256)S(1)}, f32[256]{0:T(256)}, u32[]{:S(2)}) copy-start(f32[256]{0:T(256)} %param.18) | copy-start | bytes 3076
  4.2 12.8 %copy-start.2 = (bf16[256,512]{1,0:T(8,128)(2,1)S(1)}, bf16[256,512]{1,0:T(8,128)(2,1)}, u32[]{:S(2)}) copy-start(bf16[256,512]{1,0:T(8,128)(2,1)} %param.22) | copy-start | bytes 786436
  4.2 17.2 %all-to-all-start = ((bf16[16,3,2,1664]{3,2,1,0:T(2,128)(2,1)}), bf16[16,3,2,1664]{3,2,1,0:T(2,128)(2,1)S(1)}, u32[]{:S(2)}, u32[]{:S(2)}) async-start(bf16[16,3,2,1664]{3,2,1,0:T(2,128)(2,1)} %copy.131), calls=%async_computation | async-start | bytes 638976 | tf_op jit(solution)/shard_map/all_to_all | solution.py:54
  12.9 0.8 %copy-start.5 = (bf16[2,8,2,512]{3,2,1,0:T(2,128)(2,1)S(1)}, bf16[2,8,2,512]{3,2,1,0:T(2,128)(2,1)}, u32[]{:S(2)}) copy-start(bf16[2,8,2,512]{3,2,1,0:T(2,128)(2,1)} %param.13) | copy-start | bytes 98308
  13.8 0.7 copy-start.10
  14.6 0.7 copy-start.7
  16.0 0.7 copy-start.11
  17.0 0.7 copy-start.9
  23.4 10.4 %copy-start.3 = (bf16[512,256]{1,0:T(8,128)(2,1)S(1)}, bf16[512,256]{1,0:T(8,128)(2,1)}, u32[]{:S(2)}) copy-start(bf16[512,256]{1,0:T(8,128)(2,1)} %param.20) | copy-start | bytes 786436
  23.4 10.3 %all-to-all-start.1 = ((bf16[16,3,2,512]{3,2,1,0:T(2,128)(2,1)}), bf16[16,3,2,512]{3,2,1,0:T(2,128)(2,1)S(1)}, u32[]{:S(2)}, u32[]{:S(2)}) async-start(bf16[16,3,2,512]{3,2,1,0:T(2,128)(2,1)} %broadcast_in_dim.119), calls=%async_computation.1 | async-start | bytes 196608 | tf_op jit(solution)/shard_map/all_to_all | solution.py:24
  33.8 4.8 %copy-start.6 = (bf16[2,24,2,512]{3,2,1,0:T(2,128)(2,1)S(1)}, bf16[2,24,2,512]{3,2,1,0:T(2,128)(2,1)}, u32[]{:S(2)}) copy-start(bf16[2,24,2,512]{3,2,1,0:T(2,128)(2,1)} %param.14) | copy-start | bytes 294916
  34.0 7.3 %collective-permute-start.2 = (bf16[3,32,256]{2,1,0:T(8,128)(2,1)S(1)}, bf16[3,32,256]{2,1,0:T(8,128)(2,1)S(1)}, u32[]{:S(2)}, u32[]{:S(2)}) collective-permute-start(bf16[3,32,256]{2,1,0:T(8,128)(2,1)S(1)} %fusion.20), channel_id=1, source_target_pairs={{0,3},{1,2},{2,1},{3,0},{4,7},{5,6},{6,5},{7,4},{8,11},{9,10},{10,... | collective-permute-start | bytes 147464 | tf_op jit(solution)/shard_map/ppermute | solution.py:32
  38.1 3.4 %collective-permute-start.1 = (bf16[3,32,256]{2,1,0:T(8,128)(2,1)S(1)}, bf16[3,32,256]{2,1,0:T(8,128)(2,1)S(1)}, u32[]{:S(2)}, u32[]{:S(2)}) collective-permute-start(bf16[3,32,256]{2,1,0:T(8,128)(2,1)S(1)} %fusion.20), channel_id=1, source_target_pairs={{0,2},{1,3},{2,0},{3,1},{4,6},{5,7},{6,4},{7,5},{8,10},{9,11},{10,... | collective-permute-start | bytes 147464 | tf_op jit(solution)/shard_map/ppermute | solution.py:32
  38.4 3.2 %collective-permute-start = (bf16[3,32,256]{2,1,0:T(8,128)(2,1)S(1)}, bf16[3,32,256]{2,1,0:T(8,128)(2,1)S(1)}, u32[]{:S(2)}, u32[]{:S(2)}) collective-permute-start(bf16[3,32,256]{2,1,0:T(8,128)(2,1)S(1)} %fusion.20), channel_id=1, source_target_pairs={{0,1},{1,0},{2,3},{3,2},{4,5},{5,4},{6,7},{7,6},{8,9},{9,8},{10,11... | collective-permute-start | bytes 147464 | tf_op jit(solution)/shard_map/ppermute | solution.py:32
  38.7 8.1 %collective-permute-start.3 = (bf16[24,2,512]{2,0,1:T(8,128)(2,1)S(1)}, bf16[24,2,512]{2,0,1:T(8,128)(2,1)S(1)}, u32[]{:S(2)}, u32[]{:S(2)}) collective-permute-start(bf16[24,2,512]{2,0,1:T(8,128)(2,1)S(1)} %get-tuple-element.24), channel_id=1, source_target_pairs={{0,4},{4,0},{1,5},{5,1},{2,6},{6,2},{3,7},{7,3},{8,12},{12,8},{9,1... | collective-permute-start | bytes 147464 | tf_op jit(solution)/shard_map/ppermute | solution.py:82
  43.2 10.3 %all-to-all-start.2 = ((bf16[16,3,2,640]{3,2,1,0:T(2,128)(2,1)}), bf16[16,3,2,640]{3,2,1,0:T(2,128)(2,1)S(1)}, u32[]{:S(2)}, u32[]{:S(2)}) async-start(bf16[16,3,2,640]{3,2,1,0:T(2,128)(2,1)} %maximum_bitcast_fusion), calls=%async_computation.2 | async-start | bytes 245760 | tf_op jit(solution)/shard_map/all_to_all | solution.py:54
  54.5 10.0 %copy-start.4 = (bf16[512,256]{1,0:T(8,128)(2,1)S(1)}, bf16[512,256]{1,0:T(8,128)(2,1)}, u32[]{:S(2)}) copy-start(bf16[512,256]{1,0:T(8,128)(2,1)} %param.23) | copy-start | bytes 786436
  64.7 5.7 %collective-permute-start.6 = (bf16[3,32,256]{2,1,0:T(8,128)(2,1)S(1)}, bf16[3,32,256]{2,1,0:T(8,128)(2,1)S(1)}, u32[]{:S(2)}, u32[]{:S(2)}) collective-permute-start(bf16[3,32,256]{2,1,0:T(8,128)(2,1)S(1)} %convolution_convert_fusion.2), channel_id=1, source_target_pairs={{0,3},{1,2},{2,1},{3,0},{4,7},{5,6},{6,5},{7,4},{8,11},{9,10},{10,... | collective-permute-start | bytes 147464 | tf_op jit(solution)/shard_map/ppermute | solution.py:32
  68.2 3.6 %collective-permute-start.5 = (bf16[3,32,256]{2,1,0:T(8,128)(2,1)S(1)}, bf16[3,32,256]{2,1,0:T(8,128)(2,1)S(1)}, u32[]{:S(2)}, u32[]{:S(2)}) collective-permute-start(bf16[3,32,256]{2,1,0:T(8,128)(2,1)S(1)} %convolution_convert_fusion.2), channel_id=1, source_target_pairs={{0,2},{1,3},{2,0},{3,1},{4,6},{5,7},{6,4},{7,5},{8,10},{9,11},{10,... | collective-permute-start | bytes 147464 | tf_op jit(solution)/shard_map/ppermute | solution.py:32
  68.9 2.9 %collective-permute-start.4 = (bf16[3,32,256]{2,1,0:T(8,128)(2,1)S(1)}, bf16[3,32,256]{2,1,0:T(8,128)(2,1)S(1)}, u32[]{:S(2)}, u32[]{:S(2)}) collective-permute-start(bf16[3,32,256]{2,1,0:T(8,128)(2,1)S(1)} %convolution_convert_fusion.2), channel_id=1, source_target_pairs={{0,1},{1,0},{2,3},{3,2},{4,5},{5,4},{6,7},{7,6},{8,9},{9,8},{10,11... | collective-permute-start | bytes 147464 | tf_op jit(solution)/shard_map/ppermute | solution.py:32

commit v14 on v13

--- a/solution.py
+++ b/solution.py
@@ -176,9 +176,8 @@
     partial_out = jnp.einsum(
         "tsw,wf->tsf", context_all, w_out_self, preferred_element_type=jnp.float32
     )
-    partial_out, src_late, w_q_gained = lax.optimization_barrier(
-        (partial_out, src_pool, w_q_gained)
-    )
+    partial_out, w_q_gained = lax.optimization_barrier((partial_out, w_q_gained))
+    src_late = src_pool
     cross_kv = exchange_sources(
         src_late, assign, my_sources, block_at, enc_at, dp_at, dp_count, enc_count, seq_dev
     )

time: 73 us -> 77.3 us (1.059)
  starting transfers between devices: 27.3 us -> 30.3 us
  waiting for transfers between devices: 16.1 us -> 18.7 us
  local copies, waits for them, and re-layouts: 8.97 us -> 7.53 us
    all_to_all x1, waiting for transfers between devices: 2.69 us -> 6.53 us  [rows_gather(): got = lax.all_to_all(send, 'enc', 0, 0, tiled=True)]
    all_to_all x2, waiting for transfers between devices: 10.2 us -> 6.7 us  [rows_reduce_scatter(): got = lax.all_to_all(send, 'enc', 0, 0, tiled=True)]
    all_to_all x1, starting transfers between devices: 3.64 us -> 6.65 us  [rows_gather(): got = lax.all_to_all(send, 'enc', 0, 0, tiled=True)]
    ppermute x6, waiting for transfers between devices: 3.19 us -> 5.51 us  [tensor_sum(): lax.ppermute(value, 'tensor', [(i, i ^ k) for i in range(n_t)])]
    unnamed x28 -> x30, local copies, waits for them, and re-layouts: 3.95 us -> 2.46 us
where the time goes in v14:
time: 77.3 us; the launch traced here: 76.7 us
  starting transfers between devices  30.3 us (39%)
  waiting for transfers between devices  18.7 us (24%)
  blocking collectives  9.9 us (13%)
  local copies, waits for them, and re-layouts  7.53 us (10%)
  other arithmetic  4.22 us (5%)
  between operations  4.22 us (5%)
  matrix products  1.78 us (2%)
    all_to_all x2, starting transfers between devices, rows_reduce_scatter(): got = lax.all_to_all(send, 'enc', 0, 0, tiled=True)  12.2 us
    all_to_all x1, blocking collectives, rows_gather(): got = lax.all_to_all(send, 'enc', 0, 0, tiled=True)  9.9 us
    ppermute x6, starting transfers between devices, tensor_sum(): lax.ppermute(value, 'tensor', [(i, i ^ k) for i in range(n_t)])  8.63 us
    all_to_all x2, waiting for transfers between devices, rows_reduce_scatter(): got = lax.all_to_all(send, 'enc', 0, 0, tiled=True)  6.7 us
    all_to_all x1, starting transfers between devices, rows_gather(): got = lax.all_to_all(send, 'enc', 0, 0, tiled=True)  6.65 us
    all_to_all x1, waiting for transfers between devices, rows_gather(): got = lax.all_to_all(send, 'enc', 0, 0, tiled=True)  6.53 us
    ppermute x6, waiting for transfers between devices, tensor_sum(): lax.ppermute(value, 'tensor', [(i, i ^ k) for i in range(n_t)])  5.51 us
    ppermute x1, starting transfers between devices, exchange_sources(): lax.ppermute(piece, 'dp', [(i, (i + shift) % dp_count) for i in range(dp_...  2.82 us
  transfers between devices with their start and end apart: 10, of which 6 were waited for; matrix products, arithmetic and copies ran while one was open for 5% of the time, Pallas kernels for 0%

profile of v14, /device:TPU:1, one launch (start us, length us, event | category | flops | bytes accessed | tf_op | source)
XLA Modules:
  0.0 76.7 jit_solution(1231789435564835321)
XLA Ops:
  0.0 1.0 %fusion.23 = f32[3,32]{1,0:T(4,128)S(1)} fusion(bf16[3,32,256]{2,1,0:T(8,128)(2,1)} %param.12), kind=kLoop, calls=%fused_computation.39 | loop fusion | flops 73632 | bytes 49536 | tf_op jit(solution)/shard_map/reduce_sum | solution.py:41
  1.0 0.2 copy-done
  1.2 0.3 convolution_convert_fusion
  1.4 0.3 copy.125
  1.7 0.3 convert_element_type.198
  1.9 0.1 reduce_sum.95
  2.0 0.1 copy.126
  2.1 0.1 copy.129
  2.3 0.1 copy.130
  2.4 0.8 %concatenate.13 = bf16[3,16,2,1664]{3,2,1,0:T(2,128)(2,1)S(1)} concatenate(bf16[3,16,2,1536]{3,2,1,0:T(2,128)(2,1)S(1)} %convert_element_type.198, bf16[3,16,2,1]{3,2,1,0:T(2,128)(2,1)S(1)} %copy.129, bf16[3,16,2,1]{3,2,1,0:T(2,128)(2,1)S(1)} %copy.130, bf16[3,16,2,126]{3,2,1,0:T(2,128)(2,1)S(1)} %concatenate.12), dimensions={3} | concatenate | bytes 638976 | tf_op jit(solution)/shard_map/concatenate | solution.py:47
  3.3 0.9 %copy.131 = bf16[16,3,2,1664]{3,2,1,0:T(2,128)(2,1)} copy(bf16[16,3,2,1664]{3,2,0,1:T(2,128)(2,1)S(1)} %bitcast.89) | data formatting | bytes 638976 | tf_op jit(solution)/shard_map/transpose | solution.py:53
  4.2 8.7 %all-to-all-start = ((bf16[16,3,2,1664]{3,2,1,0:T(2,128)(2,1)}), bf16[16,3,2,1664]{3,2,1,0:T(2,128)(2,1)S(1)}, u32[]{:S(2)}, u32[]{:S(2)}) async-start(bf16[16,3,2,1664]{3,2,1,0:T(2,128)(2,1)} %copy.131), calls=%async_computation | async-start | bytes 638976 | tf_op jit(solution)/shard_map/all_to_all | solution.py:54
  13.0 0.8 fusion.37
  17.6 0.1 constant_dynamic-slice_fusion.1
  17.7 2.8 %collective-permute-start.3 = (bf16[24,2,512]{2,0,1:T(8,128)(2,1)S(1)}, bf16[24,2,512]{2,0,1:T(8,128)(2,1)S(1)}, u32[]{:S(2)}, u32[]{:S(2)}) collective-permute-start(bf16[24,2,512]{2,0,1:T(8,128)(2,1)S(1)} %bitcast.94), channel_id=1, source_target_pairs={{0,4},{4,0},{1,5},{5,1},{2,6},{6,2},{3,7},{7,3},{8,12},{12,8},{9,1... | collective-permute-start | bytes 147464 | tf_op jit(solution)/shard_map/ppermute | solution.py:82
  20.5 0.1 slice_reduce_fusion
  20.7 0.5 copy-done.10
  21.2 0.1 iota_compare_fusion.2
  21.3 0.7 copy-done.11
  22.0 0.2 fusion.35
  22.2 0.1 iota_compare_fusion.1
  22.2 0.7 copy-done.9
  22.9 0.1 multiply_convert_fusion
  23.0 0.1 convert_reduce_fusion
  23.2 0.1 copy.168
  23.3 0.1 copy.169
  23.4 0.1 copy.136
  23.5 0.1 fusion.30
  23.7 0.2 convert_reduce_fusion.4
  23.9 0.1 convolution_bitcast_fusion.2
  24.0 0.1 convert_reduce_fusion.3
  24.2 0.2 fusion.3
  24.4 0.7 broadcast_in_dim.119
  25.1 6.7 %all-to-all-start.1 = ((bf16[16,3,2,512]{3,2,1,0:T(2,128)(2,1)}), bf16[16,3,2,512]{3,2,1,0:T(2,128)(2,1)S(1)}, u32[]{:S(2)}, u32[]{:S(2)}) async-start(bf16[16,3,2,512]{3,2,1,0:T(2,128)(2,1)} %broadcast_in_dim.119), calls=%async_computation.1 | async-start | bytes 196608 | tf_op jit(solution)/shard_map/all_to_all | solution.py:24
  31.8 0.1 pad.3.clone
  31.9 6.5 %all-to-all-done.1 = bf16[16,3,2,512]{3,2,1,0:T(2,128)(2,1)S(1)} async-done(((bf16[16,3,2,512]{3,2,1,0:T(2,128)(2,1)}), bf16[16,3,2,512]{3,2,1,0:T(2,128)(2,1)S(1)}, u32[]{:S(2)}, u32[]{:S(2)}) %all-to-all-start.1) | async-done | bytes 98336 | tf_op jit(solution)/shard_map/all_to_all | solution.py:24
  38.5 0.2 fusion.20
  38.7 3.2 %collective-permute-start.2 = (bf16[3,32,256]{2,1,0:T(8,128)(2,1)S(1)}, bf16[3,32,256]{2,1,0:T(8,128)(2,1)S(1)}, u32[]{:S(2)}, u32[]{:S(2)}) collective-permute-start(bf16[3,32,256]{2,1,0:T(8,128)(2,1)S(1)} %fusion.20), channel_id=1, source_target_pairs={{0,3},{1,2},{2,1},{3,0},{4,7},{5,6},{6,5},{7,4},{8,11},{9,10},{10,... | collective-permute-start | bytes 147464 | tf_op jit(solution)/shard_map/ppermute | solution.py:32
  41.9 1.2 %collective-permute-start.1 = (bf16[3,32,256]{2,1,0:T(8,128)(2,1)S(1)}, bf16[3,32,256]{2,1,0:T(8,128)(2,1)S(1)}, u32[]{:S(2)}, u32[]{:S(2)}) collective-permute-start(bf16[3,32,256]{2,1,0:T(8,128)(2,1)S(1)} %fusion.20), channel_id=1, source_target_pairs={{0,2},{1,3},{2,0},{3,1},{4,6},{5,7},{6,4},{7,5},{8,10},{9,11},{10,... | collective-permute-start | bytes 147464 | tf_op jit(solution)/shard_map/ppermute | solution.py:32
  43.1 0.1 broadcast_select_fusion
  43.2 0.5 collective-permute-done.2
  43.7 2.1 %collective-permute-done.1 = bf16[3,32,256]{2,1,0:T(8,128)(2,1)S(1)} collective-permute-done((bf16[3,32,256]{2,1,0:T(8,128)(2,1)S(1)}, bf16[3,32,256]{2,1,0:T(8,128)(2,1)S(1)}, u32[]{:S(2)}, u32[]{:S(2)}) %collective-permute-start.1) | collective-permute-done | bytes 49184 | tf_op jit(solution)/shard_map/ppermute | solution.py:32
  45.8 0.1 multiply_reduce_fusion
  45.9 0.1 reduce_sum.103
  46.0 0.1 copy.147
  46.1 0.1 copy.152
  46.2 0.1 copy.151
  46.4 0.2 convolution_convert_fusion.1
  46.6 0.8 %maximum_bitcast_fusion = bf16[16,3,2,640]{3,2,1,0:T(2,128)(2,1)} fusion(bf16[3,16,2,1]{3,2,0,1:T(2,128)(2,1)S(1)} %copy.152, bf16[3,16,2,1]{3,2,0,1:T(2,128)(2,1)S(1)} %copy.151, bf16[640]{0:T(1024)(128)(2,1)S(1)} %pad.3.clone, bf16[3,16,2,512]{3,2,1,0:T(2,128)(2,1)S(1)} %concatenate.14), kind=kLoop, calls=%fused_computation.37 | loop fusion | flops 491520 | bytes 222848 | tf_op jit(solution)/shard_map/transpose | solution.py:53
  47.4 3.5 %all-to-all-start.2 = ((bf16[16,3,2,640]{3,2,1,0:T(2,128)(2,1)}), bf16[16,3,2,640]{3,2,1,0:T(2,128)(2,1)S(1)}, u32[]{:S(2)}, u32[]{:S(2)}) async-start(bf16[16,3,2,640]{3,2,1,0:T(2,128)(2,1)} %maximum_bitcast_fusion), calls=%async_computation.2 | async-start | bytes 245760 | tf_op jit(solution)/shard_map/all_to_all | solution.py:54
  51.0 6.7 %all-to-all-done.2 = bf16[16,3,2,640]{3,2,1,0:T(2,128)(2,1)S(1)} async-done(((bf16[16,3,2,640]{3,2,1,0:T(2,128)(2,1)}), bf16[16,3,2,640]{3,2,1,0:T(2,128)(2,1)S(1)}, u32[]{:S(2)}, u32[]{:S(2)}) %all-to-all-start.2) | async-done | bytes 122912 | tf_op jit(solution)/shard_map/all_to_all | solution.py:54
  57.8 0.1 copy.175
  57.9 0.1 copy.176
  58.0 0.1 copy.158
  58.1 0.1 fusion.31
  58.2 0.2 convert_reduce_fusion.2
  58.4 0.1 fusion.4
  58.7 9.9 %all_to_all.20 = bf16[16,3,2,512]{3,2,1,0:T(2,128)(2,1)S(1)} all-to-all(bf16[16,3,2,512]{3,2,1,0:T(2,128)(2,1)S(1)} %broadcast_in_dim.128), channel_id=1, replica_groups=mesh['enc'=16,'dp'=2,'tensor'=4] {'enc'}, dimensions={0} | all-to-all | bytes 196608 | tf_op jit(solution)/shard_map/all_to_all | solution.py:24
  68.7 0.2 convolution_convert_fusion.2
  68.9 3.5 %collective-permute-start.6 = (bf16[3,32,256]{2,1,0:T(8,128)(2,1)S(1)}, bf16[3,32,256]{2,1,0:T(8,128)(2,1)S(1)}, u32[]{:S(2)}, u32[]{:S(2)}) collective-permute-start(bf16[3,32,256]{2,1,0:T(8,128)(2,1)S(1)} %convolution_convert_fusion.2), channel_id=1, source_target_pairs={{0,3},{1,2},{2,1},{3,0},{4,7},{5,6},{6,5},{7,4},{8,11},{9,10},{10,... | collective-permute-start | bytes 147464 | tf_op jit(solution)/shard_map/ppermute | solution.py:32
  72.4 0.8 collective-permute-start.5
  73.2 1.4 %collective-permute-done.6 = bf16[3,32,256]{2,1,0:T(8,128)(2,1)S(1)} collective-permute-done((bf16[3,32,256]{2,1,0:T(8,128)(2,1)S(1)}, bf16[3,32,256]{2,1,0:T(8,128)(2,1)S(1)}, u32[]{:S(2)}, u32[]{:S(2)}) %collective-permute-start.6) | collective-permute-done | bytes 49184 | tf_op jit(solution)/shard_map/ppermute | solution.py:32
  74.6 1.5 %collective-permute-done.5 = bf16[3,32,256]{2,1,0:T(8,128)(2,1)S(1)} collective-permute-done((bf16[3,32,256]{2,1,0:T(8,128)(2,1)S(1)}, bf16[3,32,256]{2,1,0:T(8,128)(2,1)S(1)}, u32[]{:S(2)}, u32[]{:S(2)}) %collective-permute-start.5) | collective-permute-done | bytes 49184 | tf_op jit(solution)/shard_map/ppermute | solution.py:32
  76.1 0.7 add_convert_fusion
  (57 shorter events, 0.9 us)
Async XLA Ops:
  0.0 1.2 %copy-start = (bf16[256,3,512]{2,0,1:T(8,128)(2,1)S(1)}, bf16[256,3,512]{2,0,1:T(8,128)(2,1)}, u32[]{:S(2)}) copy-start(bf16[256,3,512]{2,0,1:T(8,128)(2,1)} %param.19) | copy-start | bytes 2359300
  0.0 1.2 %copy-start.1 = (bf16[3,32,256]{2,1,0:T(8,128)(2,1)S(1)}, bf16[3,32,256]{2,1,0:T(8,128)(2,1)}, u32[]{:S(2)}) copy-start(bf16[3,32,256]{2,1,0:T(8,128)(2,1)} %param.12) | copy-start | bytes 147460
  0.0 1.2 %copy-start.8 = (f32[256]{0:T(256)S(1)}, f32[256]{0:T(256)}, u32[]{:S(2)}) copy-start(f32[256]{0:T(256)} %param.18) | copy-start | bytes 3076
  4.2 8.8 %copy-start.7 = (s32[64]{0:T(128)S(1)}, s32[64]{0:T(128)}, u32[]{:S(2)}) copy-start(s32[64]{0:T(128)} %param.15) | copy-start | bytes 772
  4.2 13.4 %copy-start.6 = (bf16[2,24,2,512]{3,2,1,0:T(2,128)(2,1)S(1)}, bf16[2,24,2,512]{3,2,1,0:T(2,128)(2,1)}, u32[]{:S(2)}) copy-start(bf16[2,24,2,512]{3,2,1,0:T(2,128)(2,1)} %param.14) | copy-start | bytes 294916
  4.2 18.8 %all-to-all-start = ((bf16[16,3,2,1664]{3,2,1,0:T(2,128)(2,1)}), bf16[16,3,2,1664]{3,2,1,0:T(2,128)(2,1)S(1)}, u32[]{:S(2)}, u32[]{:S(2)}) async-start(bf16[16,3,2,1664]{3,2,1,0:T(2,128)(2,1)} %copy.131), calls=%async_computation | async-start | bytes 638976 | tf_op jit(solution)/shard_map/all_to_all | solution.py:54
  12.9 9.3 %copy-start.2 = (bf16[256,512]{1,0:T(8,128)(2,1)S(1)}, bf16[256,512]{1,0:T(8,128)(2,1)}, u32[]{:S(2)}) copy-start(bf16[256,512]{1,0:T(8,128)(2,1)} %param.22) | copy-start | bytes 786436
  17.7 2.9 %copy-start.5 = (bf16[2,8,2,512]{3,2,1,0:T(2,128)(2,1)S(1)}, bf16[2,8,2,512]{3,2,1,0:T(2,128)(2,1)}, u32[]{:S(2)}) copy-start(bf16[2,8,2,512]{3,2,1,0:T(2,128)(2,1)} %param.13) | copy-start | bytes 98308
  17.7 25.4 %collective-permute-start.3 = (bf16[24,2,512]{2,0,1:T(8,128)(2,1)S(1)}, bf16[24,2,512]{2,0,1:T(8,128)(2,1)S(1)}, u32[]{:S(2)}, u32[]{:S(2)}) collective-permute-start(bf16[24,2,512]{2,0,1:T(8,128)(2,1)S(1)} %bitcast.94), channel_id=1, source_target_pairs={{0,4},{4,0},{1,5},{5,1},{2,6},{6,2},{3,7},{7,3},{8,12},{12,8},{9,1... | collective-permute-start | bytes 147464 | tf_op jit(solution)/shard_map/ppermute | solution.py:82
  20.5 0.7 copy-start.10
  21.3 0.7 copy-start.11
  22.2 0.7 copy-start.9
  25.1 13.3 %all-to-all-start.1 = ((bf16[16,3,2,512]{3,2,1,0:T(2,128)(2,1)}), bf16[16,3,2,512]{3,2,1,0:T(2,128)(2,1)S(1)}, u32[]{:S(2)}, u32[]{:S(2)}) async-start(bf16[16,3,2,512]{3,2,1,0:T(2,128)(2,1)} %broadcast_in_dim.119), calls=%async_computation.1 | async-start | bytes 196608 | tf_op jit(solution)/shard_map/all_to_all | solution.py:24
  31.7 6.8 %copy-start.3 = (bf16[512,256]{1,0:T(8,128)(2,1)S(1)}, bf16[512,256]{1,0:T(8,128)(2,1)}, u32[]{:S(2)}) copy-start(bf16[512,256]{1,0:T(8,128)(2,1)} %param.20) | copy-start | bytes 786436
  38.7 5.0 %collective-permute-start.2 = (bf16[3,32,256]{2,1,0:T(8,128)(2,1)S(1)}, bf16[3,32,256]{2,1,0:T(8,128)(2,1)S(1)}, u32[]{:S(2)}, u32[]{:S(2)}) collective-permute-start(bf16[3,32,256]{2,1,0:T(8,128)(2,1)S(1)} %fusion.20), channel_id=1, source_target_pairs={{0,3},{1,2},{2,1},{3,0},{4,7},{5,6},{6,5},{7,4},{8,11},{9,10},{10,... | collective-permute-start | bytes 147464 | tf_op jit(solution)/shard_map/ppermute | solution.py:32
  41.9 3.8 %collective-permute-start.1 = (bf16[3,32,256]{2,1,0:T(8,128)(2,1)S(1)}, bf16[3,32,256]{2,1,0:T(8,128)(2,1)S(1)}, u32[]{:S(2)}, u32[]{:S(2)}) collective-permute-start(bf16[3,32,256]{2,1,0:T(8,128)(2,1)S(1)} %fusion.20), channel_id=1, source_target_pairs={{0,2},{1,3},{2,0},{3,1},{4,6},{5,7},{6,4},{7,5},{8,10},{9,11},{10,... | collective-permute-start | bytes 147464 | tf_op jit(solution)/shard_map/ppermute | solution.py:32
  43.1 2.7 %collective-permute-start = (bf16[3,32,256]{2,1,0:T(8,128)(2,1)S(1)}, bf16[3,32,256]{2,1,0:T(8,128)(2,1)S(1)}, u32[]{:S(2)}, u32[]{:S(2)}) collective-permute-start(bf16[3,32,256]{2,1,0:T(8,128)(2,1)S(1)} %fusion.20), channel_id=1, source_target_pairs={{0,1},{1,0},{2,3},{3,2},{4,5},{5,4},{6,7},{7,6},{8,9},{9,8},{10,11... | collective-permute-start | bytes 147464 | tf_op jit(solution)/shard_map/ppermute | solution.py:32
  47.4 10.3 %all-to-all-start.2 = ((bf16[16,3,2,640]{3,2,1,0:T(2,128)(2,1)}), bf16[16,3,2,640]{3,2,1,0:T(2,128)(2,1)S(1)}, u32[]{:S(2)}, u32[]{:S(2)}) async-start(bf16[16,3,2,640]{3,2,1,0:T(2,128)(2,1)} %maximum_bitcast_fusion), calls=%async_computation.2 | async-start | bytes 245760 | tf_op jit(solution)/shard_map/all_to_all | solution.py:54
  58.7 10.0 %copy-start.4 = (bf16[512,256]{1,0:T(8,128)(2,1)S(1)}, bf16[512,256]{1,0:T(8,128)(2,1)}, u32[]{:S(2)}) copy-start(bf16[512,256]{1,0:T(8,128)(2,1)} %param.23) | copy-start | bytes 786436
  68.9 5.6 %collective-permute-start.6 = (bf16[3,32,256]{2,1,0:T(8,128)(2,1)S(1)}, bf16[3,32,256]{2,1,0:T(8,128)(2,1)S(1)}, u32[]{:S(2)}, u32[]{:S(2)}) collective-permute-start(bf16[3,32,256]{2,1,0:T(8,128)(2,1)S(1)} %convolution_convert_fusion.2), channel_id=1, source_target_pairs={{0,3},{1,2},{2,1},{3,0},{4,7},{5,6},{6,5},{7,4},{8,11},{9,10},{10,... | collective-permute-start | bytes 147464 | tf_op jit(solution)/shard_map/ppermute | solution.py:32
  72.4 3.7 %collective-permute-start.5 = (bf16[3,32,256]{2,1,0:T(8,128)(2,1)S(1)}, bf16[3,32,256]{2,1,0:T(8,128)(2,1)S(1)}, u32[]{:S(2)}, u32[]{:S(2)}) collective-permute-start(bf16[3,32,256]{2,1,0:T(8,128)(2,1)S(1)} %convolution_convert_fusion.2), channel_id=1, source_target_pairs={{0,2},{1,3},{2,0},{3,1},{4,6},{5,7},{6,4},{7,5},{8,10},{9,11},{10,... | collective-permute-start | bytes 147464 | tf_op jit(solution)/shard_map/ppermute | solution.py:32
  73.2 2.9 %collective-permute-start.4 = (bf16[3,32,256]{2,1,0:T(8,128)(2,1)S(1)}, bf16[3,32,256]{2,1,0:T(8,128)(2,1)S(1)}, u32[]{:S(2)}, u32[]{:S(2)}) collective-permute-start(bf16[3,32,256]{2,1,0:T(8,128)(2,1)S(1)} %convolution_convert_fusion.2), channel_id=1, source_target_pairs={{0,1},{1,0},{2,3},{3,2},{4,5},{5,4},{6,7},{7,6},{8,9},{9,8},{10,11... | collective-permute-start | bytes 147464 | tf_op jit(solution)/shard_map/ppermute | solution.py:32

commit v15 on v14

--- a/solution.py
+++ b/solution.py
@@ -138,6 +138,11 @@
 
     w_q_gained = (gain_cross[:, None] * w_q_cross.astype(jnp.float32)).astype(jnp.bfloat16)
 
+    cross_kv = exchange_sources(
+        src_pool, assign, my_sources, block_at, enc_at, dp_at, dp_count, enc_count, seq_dev
+    )
+    cross_kv, hidden_in = lax.optimization_barrier((cross_kv, hidden_in))
+
     current = hidden_in.astype(jnp.float32)
     scaled = (current * gain_self[None, None, :]).astype(jnp.bfloat16)
     proj = jnp.einsum("tsd,dcw->tscw", scaled, w_qkv, preferred_element_type=jnp.float32)
@@ -177,10 +182,6 @@
         "tsw,wf->tsf", context_all, w_out_self, preferred_element_type=jnp.float32
     )
     partial_out, w_q_gained = lax.optimization_barrier((partial_out, w_q_gained))
-    src_late = src_pool
-    cross_kv = exchange_sources(
-        src_late, assign, my_sources, block_at, enc_at, dp_at, dp_count, enc_count, seq_dev
-    )
     residual = current + tensor_sum(partial_out)
 
     cq = jnp.einsum(

time: 77.3 us -> 85.7 us (1.11)
  waiting for transfers between devices: 18.7 us -> 27.3 us
  local copies, waits for them, and re-layouts: 7.53 us -> 9.01 us
  other arithmetic: 4.22 us -> 3.33 us
    all_to_all x2, waiting for transfers between devices: 6.7 us -> 13.8 us  [rows_reduce_scatter(): got = lax.all_to_all(send, 'enc', 0, 0, tiled=True)]
    all_to_all x1, starting transfers between devices: 6.65 us -> 3.64 us  [rows_gather(): got = lax.all_to_all(send, 'enc', 0, 0, tiled=True)]
    ppermute x6, starting transfers between devices: 8.63 us -> 10.7 us  [tensor_sum(): lax.ppermute(value, 'tensor', [(i, i ^ k) for i in range(n_t)])]
    ppermute x1, waiting for transfers between devices: 0.01 us -> 1.15 us  [exchange_sources(): lax.ppermute(piece, 'dp', [(i, (i + shift) % dp_count) for i in range(dp_...]
    reduce_sum x2, other arithmetic: 1.08 us -> 0.21 us  [with_sumsq(): squares = jnp.sum(rows_in * rows_in, axis=-1, keepdims=True)]
    unnamed x30 -> x28, local copies, waits for them, and re-layouts: 2.46 us -> 3.12 us
  transfers between devices with their start and end apart: 10 -> 10, of which waited for: 6 -> 8; matrix products, arithmetic and copies ran while one was open for 5% -> 1% of each run, Pallas kernels for 0% -> 0%
where the time goes in v15:
time: 85.7 us; the launch traced here: 85.1 us
  starting transfers between devices  29.6 us (35%)
  waiting for transfers between devices  27.3 us (32%)
  blocking collectives  9.89 us (12%)
  local copies, waits for them, and re-layouts  9.01 us (11%)
  between operations  4.19 us (5%)
  other arithmetic  3.33 us (4%)
  matrix products  1.78 us (2%)
    all_to_all x2, waiting for transfers between devices, rows_reduce_scatter(): got = lax.all_to_all(send, 'enc', 0, 0, tiled=True)  13.8 us
    all_to_all x2, starting transfers between devices, rows_reduce_scatter(): got = lax.all_to_all(send, 'enc', 0, 0, tiled=True)  11.6 us
    ppermute x6, starting transfers between devices, tensor_sum(): lax.ppermute(value, 'tensor', [(i, i ^ k) for i in range(n_t)])  10.7 us
    all_to_all x1, blocking collectives, rows_gather(): got = lax.all_to_all(send, 'enc', 0, 0, tiled=True)  9.89 us
    all_to_all x1, waiting for transfers between devices, rows_gather(): got = lax.all_to_all(send, 'enc', 0, 0, tiled=True)  6.43 us
    ppermute x6, waiting for transfers between devices, tensor_sum(): lax.ppermute(value, 'tensor', [(i, i ^ k) for i in range(n_t)])  5.97 us
    ppermute x1, starting transfers between devices, exchange_sources(): lax.ppermute(piece, 'dp', [(i, (i + shift) % dp_count) for i in range(dp_...  3.64 us
    all_to_all x1, starting transfers between devices, rows_gather(): got = lax.all_to_all(send, 'enc', 0, 0, tiled=True)  3.64 us
  transfers between devices with their start and end apart: 10, of which 8 were waited for; matrix products, arithmetic and copies ran while one was open for 1% of the time, Pallas kernels for 0%

profile of v15, /device:TPU:1, one launch (start us, length us, event | category | flops | bytes accessed | tf_op | source)
XLA Modules:
  0.0 85.1 jit_solution(9804381720893239708)
XLA Ops:
  0.0 0.7 copy-done.6
  0.7 0.7 fusion.37
  5.3 0.9 %constant_dynamic-slice_fusion.1 = (bf16[1,24,2,512]{3,2,1,0:T(2,128)(2,1)S(1)}, bf16[1,24,2,512]{3,2,1,0:T(2,128)(2,1)S(1)}) fusion(bf16[2,24,2,512]{3,2,1,0:T(2,128)(2,1)} %param.14, s32[]{:T(128)S(6)} %select_n.110, s32[]{:T(128)S(6)} %select_n.113), kind=kLoop, calls=%fused_computation.88 | loop fusion | bytes 196616 | tf_op jit(solution)/shard_map/jit(dynamic_index_in_dim)/dynamic_slice | solution.py:80
  6.3 3.6 %collective-permute-start = (bf16[24,2,512]{2,0,1:T(8,128)(2,1)S(1)}, bf16[24,2,512]{2,0,1:T(8,128)(2,1)S(1)}, u32[]{:S(2)}, u32[]{:S(2)}) collective-permute-start(bf16[24,2,512]{2,0,1:T(8,128)(2,1)S(1)} %bitcast.94), channel_id=1, source_target_pairs={{0,4},{4,0},{1,5},{5,1},{2,6},{6,2},{3,7},{7,3},{8,12},{12,8},{9,1... | collective-permute-start | bytes 147464 | tf_op jit(solution)/shard_map/ppermute | solution.py:82
  10.1 0.1 slice_reduce_fusion
  10.2 1.2 %collective-permute-done = bf16[24,2,512]{2,0,1:T(8,128)(2,1)S(1)} collective-permute-done((bf16[24,2,512]{2,0,1:T(8,128)(2,1)S(1)}, bf16[24,2,512]{2,0,1:T(8,128)(2,1)S(1)}, u32[]{:S(2)}, u32[]{:S(2)}) %collective-permute-start) | collective-permute-done | bytes 49184 | tf_op jit(solution)/shard_map/ppermute | solution.py:82
  11.4 0.1 broadcast_select_fusion
  11.5 0.7 copy-done.1
  12.2 0.1 fusion.23
  12.3 0.6 copy-done.7
  12.9 0.3 convolution_convert_fusion
  13.1 0.3 copy.127
  13.4 0.3 convert_element_type.198
  13.6 0.1 reduce_sum.97
  13.7 0.1 copy.128
  13.8 0.1 copy.131
  14.0 0.1 copy.132
  14.1 0.8 concatenate.13
  15.0 0.9 %copy.133 = bf16[16,3,2,1664]{3,2,1,0:T(2,128)(2,1)} copy(bf16[16,3,2,1664]{3,2,0,1:T(2,128)(2,1)S(1)} %bitcast.89) | data formatting | bytes 638976 | tf_op jit(solution)/shard_map/transpose | solution.py:53
  15.9 8.1 %all-to-all-start = ((bf16[16,3,2,1664]{3,2,1,0:T(2,128)(2,1)}), bf16[16,3,2,1664]{3,2,1,0:T(2,128)(2,1)S(1)}, u32[]{:S(2)}, u32[]{:S(2)}) async-start(bf16[16,3,2,1664]{3,2,1,0:T(2,128)(2,1)} %copy.133), calls=%async_computation | async-start | bytes 638976 | tf_op jit(solution)/shard_map/all_to_all | solution.py:54
  24.1 0.6 copy-done.8
  24.7 0.1 multiply_convert_fusion
  24.8 7.1 %all-to-all-done = bf16[16,3,2,1664]{3,2,1,0:T(2,128)(2,1)S(1)} async-done(((bf16[16,3,2,1664]{3,2,1,0:T(2,128)(2,1)}), bf16[16,3,2,1664]{3,2,1,0:T(2,128)(2,1)S(1)}, u32[]{:S(2)}, u32[]{:S(2)}) %all-to-all-start) | async-done | bytes 319520 | tf_op jit(solution)/shard_map/all_to_all | solution.py:54
  31.9 0.1 convert_reduce_fusion
  32.1 0.1 copy.170
  32.2 0.1 copy.171
  32.3 0.1 copy.138
  32.4 0.1 fusion.30
  32.5 0.1 convert_reduce_fusion.3
  32.7 0.2 convert_reduce_fusion.4
  32.9 0.1 convolution_bitcast_fusion.2
  33.0 0.2 fusion.3
  33.2 0.7 broadcast_in_dim.123
  33.9 3.6 %all-to-all-start.1 = ((bf16[16,3,2,512]{3,2,1,0:T(2,128)(2,1)}), bf16[16,3,2,512]{3,2,1,0:T(2,128)(2,1)S(1)}, u32[]{:S(2)}, u32[]{:S(2)}) async-start(bf16[16,3,2,512]{3,2,1,0:T(2,128)(2,1)} %broadcast_in_dim.123), calls=%async_computation.1 | async-start | bytes 196608 | tf_op jit(solution)/shard_map/all_to_all | solution.py:24
  37.6 0.2 fusion.35
  37.8 6.4 %all-to-all-done.1 = bf16[16,3,2,512]{3,2,1,0:T(2,128)(2,1)S(1)} async-done(((bf16[16,3,2,512]{3,2,1,0:T(2,128)(2,1)}), bf16[16,3,2,512]{3,2,1,0:T(2,128)(2,1)S(1)}, u32[]{:S(2)}, u32[]{:S(2)}) %all-to-all-start.1) | async-done | bytes 98336 | tf_op jit(solution)/shard_map/all_to_all | solution.py:24
  44.3 0.2 fusion.20
  44.5 4.5 %collective-permute-start.1 = (bf16[3,32,256]{2,1,0:T(8,128)(2,1)S(1)}, bf16[3,32,256]{2,1,0:T(8,128)(2,1)S(1)}, u32[]{:S(2)}, u32[]{:S(2)}) collective-permute-start(bf16[3,32,256]{2,1,0:T(8,128)(2,1)S(1)} %fusion.20), channel_id=1, source_target_pairs={{0,1},{1,0},{2,3},{3,2},{4,5},{5,4},{6,7},{7,6},{8,9},{9,8},{10,11... | collective-permute-start | bytes 147464 | tf_op jit(solution)/shard_map/ppermute | solution.py:32
  49.0 1.2 %collective-permute-start.2 = (bf16[3,32,256]{2,1,0:T(8,128)(2,1)S(1)}, bf16[3,32,256]{2,1,0:T(8,128)(2,1)S(1)}, u32[]{:S(2)}, u32[]{:S(2)}) collective-permute-start(bf16[3,32,256]{2,1,0:T(8,128)(2,1)S(1)} %fusion.20), channel_id=1, source_target_pairs={{0,2},{1,3},{2,0},{3,1},{4,6},{5,7},{6,4},{7,5},{8,10},{9,11},{10,... | collective-permute-start | bytes 147464 | tf_op jit(solution)/shard_map/ppermute | solution.py:32
  50.2 0.5 collective-permute-start.3
  50.9 1.1 %collective-permute-done.2 = bf16[3,32,256]{2,1,0:T(8,128)(2,1)S(1)} collective-permute-done((bf16[3,32,256]{2,1,0:T(8,128)(2,1)S(1)}, bf16[3,32,256]{2,1,0:T(8,128)(2,1)S(1)}, u32[]{:S(2)}, u32[]{:S(2)}) %collective-permute-start.2) | collective-permute-done | bytes 49184 | tf_op jit(solution)/shard_map/ppermute | solution.py:32
  51.9 2.0 %collective-permute-done.3 = bf16[3,32,256]{2,1,0:T(8,128)(2,1)S(1)} collective-permute-done((bf16[3,32,256]{2,1,0:T(8,128)(2,1)S(1)}, bf16[3,32,256]{2,1,0:T(8,128)(2,1)S(1)}, u32[]{:S(2)}, u32[]{:S(2)}) %collective-permute-start.3) | collective-permute-done | bytes 49184 | tf_op jit(solution)/shard_map/ppermute | solution.py:32
  53.9 0.1 multiply_reduce_fusion
  54.1 0.2 convolution_convert_fusion.1
  54.3 0.1 reduce_sum.103
  54.4 0.1 copy.147
  54.5 0.1 copy.151
  54.6 0.1 copy.152
  54.7 0.8 maximum_bitcast_fusion
  55.6 3.5 %all-to-all-start.2 = ((bf16[16,3,2,640]{3,2,1,0:T(2,128)(2,1)}), bf16[16,3,2,640]{3,2,1,0:T(2,128)(2,1)S(1)}, u32[]{:S(2)}, u32[]{:S(2)}) async-start(bf16[16,3,2,640]{3,2,1,0:T(2,128)(2,1)} %maximum_bitcast_fusion), calls=%async_computation.2 | async-start | bytes 245760 | tf_op jit(solution)/shard_map/all_to_all | solution.py:54
  59.1 6.7 %all-to-all-done.2 = bf16[16,3,2,640]{3,2,1,0:T(2,128)(2,1)S(1)} async-done(((bf16[16,3,2,640]{3,2,1,0:T(2,128)(2,1)}), bf16[16,3,2,640]{3,2,1,0:T(2,128)(2,1)S(1)}, u32[]{:S(2)}, u32[]{:S(2)}) %all-to-all-start.2) | async-done | bytes 122912 | tf_op jit(solution)/shard_map/all_to_all | solution.py:54
  66.0 0.1 copy.175
  66.1 0.1 copy.176
  66.2 0.1 copy.158
  66.4 0.2 convert_reduce_fusion.2
  66.6 0.1 fusion.4
  66.8 9.9 %all_to_all.20 = bf16[16,3,2,512]{3,2,1,0:T(2,128)(2,1)S(1)} all-to-all(bf16[16,3,2,512]{3,2,1,0:T(2,128)(2,1)S(1)} %broadcast_in_dim.128), channel_id=1, replica_groups=mesh['enc'=16,'dp'=2,'tensor'=4] {'enc'}, dimensions={0} | all-to-all | bytes 196608 | tf_op jit(solution)/shard_map/all_to_all | solution.py:24
  76.9 0.2 convolution_convert_fusion.2
  77.1 2.7 %collective-permute-start.4 = (bf16[3,32,256]{2,1,0:T(8,128)(2,1)S(1)}, bf16[3,32,256]{2,1,0:T(8,128)(2,1)S(1)}, u32[]{:S(2)}, u32[]{:S(2)}) collective-permute-start(bf16[3,32,256]{2,1,0:T(8,128)(2,1)S(1)} %convolution_convert_fusion.2), channel_id=1, source_target_pairs={{0,1},{1,0},{2,3},{3,2},{4,5},{5,4},{6,7},{7,6},{8,9},{9,8},{10,11... | collective-permute-start | bytes 147464 | tf_op jit(solution)/shard_map/ppermute | solution.py:32
  79.8 0.6 collective-permute-start.5
  80.4 1.1 %collective-permute-start.6 = (bf16[3,32,256]{2,1,0:T(8,128)(2,1)S(1)}, bf16[3,32,256]{2,1,0:T(8,128)(2,1)S(1)}, u32[]{:S(2)}, u32[]{:S(2)}) collective-permute-start(bf16[3,32,256]{2,1,0:T(8,128)(2,1)S(1)} %convolution_convert_fusion.2), channel_id=1, source_target_pairs={{0,3},{1,2},{2,1},{3,0},{4,7},{5,6},{6,5},{7,4},{8,11},{9,10},{10,... | collective-permute-start | bytes 147464 | tf_op jit(solution)/shard_map/ppermute | solution.py:32
  81.5 1.2 %collective-permute-done.5 = bf16[3,32,256]{2,1,0:T(8,128)(2,1)S(1)} collective-permute-done((bf16[3,32,256]{2,1,0:T(8,128)(2,1)S(1)}, bf16[3,32,256]{2,1,0:T(8,128)(2,1)S(1)}, u32[]{:S(2)}, u32[]{:S(2)}) %collective-permute-start.5) | collective-permute-done | bytes 49184 | tf_op jit(solution)/shard_map/ppermute | solution.py:32
  82.7 1.7 %collective-permute-done.6 = bf16[3,32,256]{2,1,0:T(8,128)(2,1)S(1)} collective-permute-done((bf16[3,32,256]{2,1,0:T(8,128)(2,1)S(1)}, bf16[3,32,256]{2,1,0:T(8,128)(2,1)S(1)}, u32[]{:S(2)}, u32[]{:S(2)}) %collective-permute-start.6) | collective-permute-done | bytes 49184 | tf_op jit(solution)/shard_map/ppermute | solution.py:32
  84.4 0.7 add_convert_fusion
  (55 shorter events, 1.2 us)
Async XLA Ops:
  0.0 12.3 %copy-start = (bf16[256,3,512]{2,0,1:T(8,128)(2,1)S(1)}, bf16[256,3,512]{2,0,1:T(8,128)(2,1)}, u32[]{:S(2)}) copy-start(bf16[256,3,512]{2,0,1:T(8,128)(2,1)} %param.19) | copy-start | bytes 2359300
  0.0 0.7 copy-start.6
  6.2 3.7 %copy-start.9 = (s32[64]{0:T(128)S(1)}, s32[64]{0:T(128)}, u32[]{:S(2)}) copy-start(s32[64]{0:T(128)} %param.17) | copy-start | bytes 772
  6.2 3.8 %copy-start.5 = (bf16[2,8,2,512]{3,2,1,0:T(2,128)(2,1)S(1)}, bf16[2,8,2,512]{3,2,1,0:T(2,128)(2,1)}, u32[]{:S(2)}) copy-start(bf16[2,8,2,512]{3,2,1,0:T(2,128)(2,1)} %param.13) | copy-start | bytes 98308
  6.3 5.1 %collective-permute-start = (bf16[24,2,512]{2,0,1:T(8,128)(2,1)S(1)}, bf16[24,2,512]{2,0,1:T(8,128)(2,1)S(1)}, u32[]{:S(2)}, u32[]{:S(2)}) collective-permute-start(bf16[24,2,512]{2,0,1:T(8,128)(2,1)S(1)} %bitcast.94), channel_id=1, source_target_pairs={{0,4},{4,0},{1,5},{5,1},{2,6},{6,2},{3,7},{7,3},{8,12},{12,8},{9,1... | collective-permute-start | bytes 147464 | tf_op jit(solution)/shard_map/ppermute | solution.py:82
  11.4 0.8 copy-start.1
  12.2 0.7 copy-start.7
  15.9 8.2 %copy-start.2 = (bf16[256,512]{1,0:T(8,128)(2,1)S(1)}, bf16[256,512]{1,0:T(8,128)(2,1)}, u32[]{:S(2)}) copy-start(bf16[256,512]{1,0:T(8,128)(2,1)} %param.22) | copy-start | bytes 786436
  15.9 16.0 %all-to-all-start = ((bf16[16,3,2,1664]{3,2,1,0:T(2,128)(2,1)}), bf16[16,3,2,1664]{3,2,1,0:T(2,128)(2,1)S(1)}, u32[]{:S(2)}, u32[]{:S(2)}) async-start(bf16[16,3,2,1664]{3,2,1,0:T(2,128)(2,1)} %copy.133), calls=%async_computation | async-start | bytes 638976 | tf_op jit(solution)/shard_map/all_to_all | solution.py:54
  24.0 0.7 copy-start.8
  33.2 4.3 %copy-start.10 = (s32[64]{0:T(128)S(1)}, s32[64]{0:T(128)}, u32[]{:S(2)}) copy-start(s32[64]{0:T(128)} %param.16) | copy-start | bytes 772
  33.9 10.4 %copy-start.3 = (bf16[512,256]{1,0:T(8,128)(2,1)S(1)}, bf16[512,256]{1,0:T(8,128)(2,1)}, u32[]{:S(2)}) copy-start(bf16[512,256]{1,0:T(8,128)(2,1)} %param.20) | copy-start | bytes 786436
  33.9 10.3 %all-to-all-start.1 = ((bf16[16,3,2,512]{3,2,1,0:T(2,128)(2,1)}), bf16[16,3,2,512]{3,2,1,0:T(2,128)(2,1)S(1)}, u32[]{:S(2)}, u32[]{:S(2)}) async-start(bf16[16,3,2,512]{3,2,1,0:T(2,128)(2,1)} %broadcast_in_dim.123), calls=%async_computation.1 | async-start | bytes 196608 | tf_op jit(solution)/shard_map/all_to_all | solution.py:24
  44.5 6.4 %collective-permute-start.1 = (bf16[3,32,256]{2,1,0:T(8,128)(2,1)S(1)}, bf16[3,32,256]{2,1,0:T(8,128)(2,1)S(1)}, u32[]{:S(2)}, u32[]{:S(2)}) collective-permute-start(bf16[3,32,256]{2,1,0:T(8,128)(2,1)S(1)} %fusion.20), channel_id=1, source_target_pairs={{0,1},{1,0},{2,3},{3,2},{4,5},{5,4},{6,7},{7,6},{8,9},{9,8},{10,11... | collective-permute-start | bytes 147464 | tf_op jit(solution)/shard_map/ppermute | solution.py:32
  49.0 2.9 %collective-permute-start.2 = (bf16[3,32,256]{2,1,0:T(8,128)(2,1)S(1)}, bf16[3,32,256]{2,1,0:T(8,128)(2,1)S(1)}, u32[]{:S(2)}, u32[]{:S(2)}) collective-permute-start(bf16[3,32,256]{2,1,0:T(8,128)(2,1)S(1)} %fusion.20), channel_id=1, source_target_pairs={{0,2},{1,3},{2,0},{3,1},{4,6},{5,7},{6,4},{7,5},{8,10},{9,11},{10,... | collective-permute-start | bytes 147464 | tf_op jit(solution)/shard_map/ppermute | solution.py:32
  50.2 3.7 %collective-permute-start.3 = (bf16[3,32,256]{2,1,0:T(8,128)(2,1)S(1)}, bf16[3,32,256]{2,1,0:T(8,128)(2,1)S(1)}, u32[]{:S(2)}, u32[]{:S(2)}) collective-permute-start(bf16[3,32,256]{2,1,0:T(8,128)(2,1)S(1)} %fusion.20), channel_id=1, source_target_pairs={{0,3},{1,2},{2,1},{3,0},{4,7},{5,6},{6,5},{7,4},{8,11},{9,10},{10,... | collective-permute-start | bytes 147464 | tf_op jit(solution)/shard_map/ppermute | solution.py:32
  55.6 10.3 %all-to-all-start.2 = ((bf16[16,3,2,640]{3,2,1,0:T(2,128)(2,1)}), bf16[16,3,2,640]{3,2,1,0:T(2,128)(2,1)S(1)}, u32[]{:S(2)}, u32[]{:S(2)}) async-start(bf16[16,3,2,640]{3,2,1,0:T(2,128)(2,1)} %maximum_bitcast_fusion), calls=%async_computation.2 | async-start | bytes 245760 | tf_op jit(solution)/shard_map/all_to_all | solution.py:54
  66.8 10.0 %copy-start.4 = (bf16[512,256]{1,0:T(8,128)(2,1)S(1)}, bf16[512,256]{1,0:T(8,128)(2,1)}, u32[]{:S(2)}) copy-start(bf16[512,256]{1,0:T(8,128)(2,1)} %param.23) | copy-start | bytes 786436
  77.1 4.5 %collective-permute-start.4 = (bf16[3,32,256]{2,1,0:T(8,128)(2,1)S(1)}, bf16[3,32,256]{2,1,0:T(8,128)(2,1)S(1)}, u32[]{:S(2)}, u32[]{:S(2)}) collective-permute-start(bf16[3,32,256]{2,1,0:T(8,128)(2,1)S(1)} %convolution_convert_fusion.2), channel_id=1, source_target_pairs={{0,1},{1,0},{2,3},{3,2},{4,5},{5,4},{6,7},{7,6},{8,9},{9,8},{10,11... | collective-permute-start | bytes 147464 | tf_op jit(solution)/shard_map/ppermute | solution.py:32
  79.8 2.9 %collective-permute-start.5 = (bf16[3,32,256]{2,1,0:T(8,128)(2,1)S(1)}, bf16[3,32,256]{2,1,0:T(8,128)(2,1)S(1)}, u32[]{:S(2)}, u32[]{:S(2)}) collective-permute-start(bf16[3,32,256]{2,1,0:T(8,128)(2,1)S(1)} %convolution_convert_fusion.2), channel_id=1, source_target_pairs={{0,2},{1,3},{2,0},{3,1},{4,6},{5,7},{6,4},{7,5},{8,10},{9,11},{10,... | collective-permute-start | bytes 147464 | tf_op jit(solution)/shard_map/ppermute | solution.py:32
  80.4 4.0 %collective-permute-start.6 = (bf16[3,32,256]{2,1,0:T(8,128)(2,1)S(1)}, bf16[3,32,256]{2,1,0:T(8,128)(2,1)S(1)}, u32[]{:S(2)}, u32[]{:S(2)}) collective-permute-start(bf16[3,32,256]{2,1,0:T(8,128)(2,1)S(1)} %convolution_convert_fusion.2), channel_id=1, source_target_pairs={{0,3},{1,2},{2,1},{3,0},{4,7},{5,6},{6,5},{7,4},{8,11},{9,10},{10,... | collective-permute-start | bytes 147464 | tf_op jit(solution)/shard_map/ppermute | solution.py:32

commit v16 on v13

--- a/solution.py
+++ b/solution.py
@@ -187,8 +187,28 @@
     cq = jnp.einsum(
         "tsd,dw->tsw", residual.astype(jnp.bfloat16), w_q_gained, preferred_element_type=jnp.float32
     )
-    own = rows_reduce_scatter(with_sumsq(cq, residual), seq_dev)
-    cross_query = split_norm(own, width).reshape(steps, seq_dev, head_count, DK)
+    n_enc = enc_count
+    blocks = cq.reshape(steps, n_enc, seq_dev, width).transpose(1, 0, 2, 3)
+    squares = jnp.sum(residual * residual, axis=-1).reshape(steps, n_enc, seq_dev)
+    squares = squares.transpose(1, 0, 2).reshape(n_enc, steps * seq_dev)
+    high = squares.astype(jnp.bfloat16)
+    low = jnp.where(
+        jnp.isfinite(squares), squares - high.astype(jnp.float32), 0.0
+    ).astype(jnp.bfloat16)
+    tail = jnp.concatenate(
+        [high, low, jnp.zeros((n_enc, LANE - 2 * steps * seq_dev), jnp.bfloat16)], axis=-1
+    )
+    send = jnp.concatenate(
+        [blocks.astype(jnp.bfloat16).reshape(n_enc, steps * seq_dev * width), tail], axis=-1
+    )
+    got = jnp.sum(lax.all_to_all(send, "enc", 0, 0, tiled=True).astype(jnp.float32), axis=0)
+    body = got[: steps * seq_dev * width].reshape(steps, seq_dev, width)
+    cut = steps * seq_dev * width
+    sums = got[cut : cut + steps * seq_dev] + got[cut + steps * seq_dev : cut + 2 * steps * seq_dev]
+    scale = lax.rsqrt(sums.reshape(steps, seq_dev) / D + EPSILON)
+    cross_query = (body * scale[..., None]).astype(jnp.bfloat16).reshape(
+        steps, seq_dev, head_count, DK
+    )
     cross_keys = cross_kv[:, :, 0].reshape(seq_dev, source_len, head_count, DK)
     cross_values = cross_kv[:, :, 1].reshape(seq_dev, source_len, head_count, DK)
     s_cross = jnp.einsum(

time: 73 us -> 74.2 us (1.016)
  local copies, waits for them, and re-layouts: 8.97 us -> 9.81 us
    all_to_all x2 -> x1, waiting for transfers between devices: 10.2 us -> 3.57 us  [rows_reduce_scatter(): got = lax.all_to_all(send, 'enc', 0, 0, tiled=True)]
    all_to_all x0 -> x1, waiting for transfers between devices: none -> 6.52 us  [on_device(): lax.all_to_all(send, 'enc', 0, 0, tiled=True).astype(jnp.float32)]
    all_to_all x2 -> x1, starting transfers between devices: 12.2 us -> 8.72 us  [rows_reduce_scatter(): got = lax.all_to_all(send, 'enc', 0, 0, tiled=True)]
    all_to_all x0 -> x1, starting transfers between devices: none -> 3.51 us  [on_device(): lax.all_to_all(send, 'enc', 0, 0, tiled=True).astype(jnp.float32)]
    transpose x1 -> x0, other arithmetic: 0.83 us -> none  [rows_reduce_scatter(): send = partial.reshape(steps, n_enc, owned, cols).transpose(1, 0, 2, 3)]
    unnamed x28, local copies, waits for them, and re-layouts: 3.95 us -> 4.71 us
  transfers between devices with their start and end apart: 10 -> 10, of which waited for: 6 -> 6; matrix products, arithmetic and copies ran while one was open for 5% -> 6% of each run, Pallas kernels for 0% -> 0%
where the time goes in v16:
time: 74.2 us; the launch traced here: 73.6 us
  starting transfers between devices  27.3 us (37%)
  waiting for transfers between devices  15.9 us (21%)
  blocking collectives  9.92 us (13%)
  local copies, waits for them, and re-layouts  9.81 us (13%)
  other arithmetic  4.48 us (6%)
  between operations  4.44 us (6%)
  matrix products  1.77 us (2%)
    all_to_all x1, blocking collectives, rows_gather(): got = lax.all_to_all(send, 'enc', 0, 0, tiled=True)  9.92 us
    ppermute x6, starting transfers between devices, tensor_sum(): lax.ppermute(value, 'tensor', [(i, i ^ k) for i in range(n_t)])  8.82 us
    all_to_all x1, starting transfers between devices, rows_reduce_scatter(): got = lax.all_to_all(send, 'enc', 0, 0, tiled=True)  8.72 us
    all_to_all x1, waiting for transfers between devices, on_device(): lax.all_to_all(send, 'enc', 0, 0, tiled=True).astype(jnp.float32)  6.52 us
    unnamed x28, local copies, waits for them, and re-layouts  4.71 us
    all_to_all x1, starting transfers between devices, rows_gather(): got = lax.all_to_all(send, 'enc', 0, 0, tiled=True)  3.64 us
    all_to_all x1, waiting for transfers between devices, rows_reduce_scatter(): got = lax.all_to_all(send, 'enc', 0, 0, tiled=True)  3.57 us
    all_to_all x1, starting transfers between devices, on_device(): lax.all_to_all(send, 'enc', 0, 0, tiled=True).astype(jnp.float32)  3.51 us
  transfers between devices with their start and end apart: 10, of which 6 were waited for; matrix products, arithmetic and copies ran while one was open for 6% of the time, Pallas kernels for 0%

profile of v16, /device:TPU:1, one launch (start us, length us, event | category | flops | bytes accessed | tf_op | source)
XLA Modules:
  0.0 73.6 jit_solution(9762315560549435783)
XLA Ops:
  0.0 1.0 %fusion.23 = f32[3,32]{1,0:T(4,128)S(1)} fusion(bf16[3,32,256]{2,1,0:T(8,128)(2,1)} %param.12), kind=kLoop, calls=%fused_computation.38 | loop fusion | flops 73632 | bytes 49536 | tf_op jit(solution)/shard_map/reduce_sum | solution.py:41
  1.0 0.2 copy-done
  1.2 0.3 convolution_convert_fusion
  1.4 0.3 copy.149
  1.7 0.3 convert_element_type.174
  1.9 0.1 reduce_sum.103
  2.1 0.8 %concatenate.7 = bf16[3,16,2,1664]{3,2,1,0:T(2,128)(2,1)S(1)} concatenate(bf16[3,16,2,1536]{3,2,1,0:T(2,128)(2,1)S(1)} %convert_element_type.174, bf16[3,16,2,1]{3,2,1,0:T(2,128)(2,1)S(1)} %get-tuple-element.21, bf16[3,16,2,1]{3,2,1,0:T(2,128)(2,1)S(1)} %get-tuple-element.20, bf16[3,16,2,126]{3,2,1,0:T(2,128)(2,1)S(1)} %broadcast_in_dim.124), dimensions={3} | concatenate | bytes 638976 | tf_op jit(solution)/shard_map/concatenate | solution.py:47
  3.0 0.9 %copy.153 = bf16[16,3,2,1664]{3,2,1,0:T(2,128)(2,1)} copy(bf16[16,3,2,1664]{3,2,0,1:T(2,128)(2,1)S(1)} %bitcast.90) | data formatting | bytes 638976 | tf_op jit(solution)/shard_map/transpose | solution.py:53
  3.9 8.7 %all-to-all-start = ((bf16[16,3,2,1664]{3,2,1,0:T(2,128)(2,1)}), bf16[16,3,2,1664]{3,2,1,0:T(2,128)(2,1)S(1)}, u32[]{:S(2)}, u32[]{:S(2)}) async-start(bf16[16,3,2,1664]{3,2,1,0:T(2,128)(2,1)} %copy.153), calls=%async_computation | async-start | bytes 638976 | tf_op jit(solution)/shard_map/all_to_all | solution.py:54
  12.7 0.7 copy-done.5
  13.4 0.1 slice_reduce_fusion
  13.6 0.6 copy-done.10
  14.3 0.1 iota_compare_fusion.2
  14.4 0.7 copy-done.7
  15.0 0.8 %fusion.36 = (s32[]{:T(128)}, s32[2]{0:T(128)S(1)}, s32[2]{0:T(128)S(1)}, s32[]{:T(128)}) fusion(s32[]{:T(128)S(6)} %add.97, s32[64]{0:T(128)S(1)} %copy-done.7, s32[]{:T(128)S(6)} %select_n.94, s32[]{:T(128)S(6)} %select_n.102), kind=kLoop, calls=%fused_computation.87 | loop fusion | flops 86 | bytes 52 | tf_op jit(solution)/shard_map/reduce_sum | solution.py:79
  15.8 0.7 copy-done.11
  16.5 0.2 fusion.33
  16.7 0.7 copy-done.9
  17.4 0.1 multiply_convert_fusion
  17.5 3.6 %all-to-all-done = bf16[16,3,2,1664]{3,2,1,0:T(2,128)(2,1)S(1)} async-done(((bf16[16,3,2,1664]{3,2,1,0:T(2,128)(2,1)}), bf16[16,3,2,1664]{3,2,1,0:T(2,128)(2,1)S(1)}, u32[]{:S(2)}, u32[]{:S(2)}) %all-to-all-start) | async-done | bytes 319520 | tf_op jit(solution)/shard_map/all_to_all | solution.py:54
  21.1 0.3 convert_reduce_fusion
  21.4 0.1 copy.180
  21.5 0.1 copy.181
  21.6 0.1 copy.156
  21.7 0.1 fusion.31
  21.9 0.2 convert_reduce_fusion.4
  22.1 0.1 convolution_bitcast_fusion.2
  22.2 0.1 convert_reduce_fusion.3
  22.4 0.2 fusion.3
  22.6 0.7 broadcast_in_dim.128
  23.3 3.6 %all-to-all-start.1 = ((bf16[16,3,2,512]{3,2,1,0:T(2,128)(2,1)}), bf16[16,3,2,512]{3,2,1,0:T(2,128)(2,1)S(1)}, u32[]{:S(2)}, u32[]{:S(2)}) async-start(bf16[16,3,2,512]{3,2,1,0:T(2,128)(2,1)} %broadcast_in_dim.128), calls=%async_computation.1 | async-start | bytes 196608 | tf_op jit(solution)/shard_map/all_to_all | solution.py:24
  30.9 2.6 %all-to-all-done.1 = bf16[16,3,2,512]{3,2,1,0:T(2,128)(2,1)S(1)} async-done(((bf16[16,3,2,512]{3,2,1,0:T(2,128)(2,1)}), bf16[16,3,2,512]{3,2,1,0:T(2,128)(2,1)S(1)}, u32[]{:S(2)}, u32[]{:S(2)}) %all-to-all-start.1) | async-done | bytes 98336 | tf_op jit(solution)/shard_map/all_to_all | solution.py:24
  33.7 0.2 fusion.20
  33.9 4.1 %collective-permute-start.2 = (bf16[3,32,256]{2,1,0:T(8,128)(2,1)S(1)}, bf16[3,32,256]{2,1,0:T(8,128)(2,1)S(1)}, u32[]{:S(2)}, u32[]{:S(2)}) collective-permute-start(bf16[3,32,256]{2,1,0:T(8,128)(2,1)S(1)} %fusion.20), channel_id=1, source_target_pairs={{0,3},{1,2},{2,1},{3,0},{4,7},{5,6},{6,5},{7,4},{8,11},{9,10},{10,... | collective-permute-start | bytes 147464 | tf_op jit(solution)/shard_map/ppermute | solution.py:32
  38.0 0.3 collective-permute-start.1
  38.3 0.2 collective-permute-start
  38.5 2.6 %collective-permute-start.3 = (bf16[24,2,512]{2,0,1:T(8,128)(2,1)S(1)}, bf16[24,2,512]{2,0,1:T(8,128)(2,1)S(1)}, u32[]{:S(2)}, u32[]{:S(2)}) collective-permute-start(bf16[24,2,512]{2,0,1:T(8,128)(2,1)S(1)} %get-tuple-element.24), channel_id=1, source_target_pairs={{0,4},{4,0},{1,5},{5,1},{2,6},{6,2},{3,7},{7,3},{8,12},{12,8},{9,1... | collective-permute-start | bytes 147464 | tf_op jit(solution)/shard_map/ppermute | solution.py:82
  41.1 0.3 collective-permute-done.1
  41.5 0.1 multiply_reduce_fusion
  41.6 0.1 reshape.185
  41.7 0.1 copy.168
  41.8 0.1 copy.169
  41.9 0.2 convolution_convert_fusion.1
  42.3 0.1 concatenate.8
  42.4 0.5 broadcast.133
  42.9 0.7 reduce.5
  43.5 0.8 %reshape.196 = bf16[16,2,1600]{2,1,0:T(2,128)(2,1)} reshape(bf16[16,3200]{1,0:T(8,128)(2,1)S(1)} %reduce.5) | data formatting | bytes 204800
  44.3 3.5 %all-to-all-start.2 = ((bf16[16,2,1600]{2,1,0:T(2,128)(2,1)}), bf16[16,2,1600]{2,1,0:T(2,128)(2,1)S(1)}, u32[]{:S(2)}, u32[]{:S(2)}) async-start(bf16[16,2,1600]{2,1,0:T(2,128)(2,1)} %reshape.196), calls=%async_computation.2 | async-start | bytes 212992 | tf_op jit(solution)/shard_map/all_to_all | solution.py:204
  47.9 0.1 broadcast_select_fusion
  48.0 6.5 %all-to-all-done.2 = bf16[16,2,1600]{2,1,0:T(2,128)(2,1)S(1)} async-done(((bf16[16,2,1600]{2,1,0:T(2,128)(2,1)}), bf16[16,2,1600]{2,1,0:T(2,128)(2,1)S(1)}, u32[]{:S(2)}, u32[]{:S(2)}) %all-to-all-start.2) | async-done | bytes 102432 | tf_op jit(solution)/shard_map/all_to_all | solution.py:204
  54.5 0.2 reshape.197
  54.7 0.2 convert_reduce_fusion.1
  54.9 0.1 add_rsqrt_fusion
  55.0 0.1 rsqrt.12
  55.1 0.1 multiply_convert_fusion.1
  55.2 0.2 convert_reduce_fusion.2
  55.4 0.1 fusion.4
  55.6 9.9 %all_to_all.24 = bf16[16,3,2,512]{3,2,1,0:T(2,128)(2,1)S(1)} all-to-all(bf16[16,3,2,512]{3,2,1,0:T(2,128)(2,1)S(1)} %broadcast_in_dim.139), channel_id=1, replica_groups=mesh['enc'=16,'dp'=2,'tensor'=4] {'enc'}, dimensions={0} | all-to-all | bytes 196608 | tf_op jit(solution)/shard_map/all_to_all | solution.py:24
  65.7 0.2 convolution_convert_fusion.2
  65.9 3.5 %collective-permute-start.6 = (bf16[3,32,256]{2,1,0:T(8,128)(2,1)S(1)}, bf16[3,32,256]{2,1,0:T(8,128)(2,1)S(1)}, u32[]{:S(2)}, u32[]{:S(2)}) collective-permute-start(bf16[3,32,256]{2,1,0:T(8,128)(2,1)S(1)} %convolution_convert_fusion.2), channel_id=1, source_target_pairs={{0,3},{1,2},{2,1},{3,0},{4,7},{5,6},{6,5},{7,4},{8,11},{9,10},{10,... | collective-permute-start | bytes 147464 | tf_op jit(solution)/shard_map/ppermute | solution.py:32
  69.3 0.7 collective-permute-start.5
  70.1 1.5 %collective-permute-done.6 = bf16[3,32,256]{2,1,0:T(8,128)(2,1)S(1)} collective-permute-done((bf16[3,32,256]{2,1,0:T(8,128)(2,1)S(1)}, bf16[3,32,256]{2,1,0:T(8,128)(2,1)S(1)}, u32[]{:S(2)}, u32[]{:S(2)}) %collective-permute-start.6) | collective-permute-done | bytes 49184 | tf_op jit(solution)/shard_map/ppermute | solution.py:32
  71.5 1.4 %collective-permute-done.5 = bf16[3,32,256]{2,1,0:T(8,128)(2,1)S(1)} collective-permute-done((bf16[3,32,256]{2,1,0:T(8,128)(2,1)S(1)}, bf16[3,32,256]{2,1,0:T(8,128)(2,1)S(1)}, u32[]{:S(2)}, u32[]{:S(2)}) %collective-permute-start.5) | collective-permute-done | bytes 49184 | tf_op jit(solution)/shard_map/ppermute | solution.py:32
  72.9 0.7 add_convert_fusion
  (56 shorter events, 1.0 us)
Async XLA Ops:
  0.0 1.2 %copy-start = (bf16[256,3,512]{2,0,1:T(8,128)(2,1)S(1)}, bf16[256,3,512]{2,0,1:T(8,128)(2,1)}, u32[]{:S(2)}) copy-start(bf16[256,3,512]{2,0,1:T(8,128)(2,1)} %param.19) | copy-start | bytes 2359300
  0.0 1.2 %copy-start.1 = (bf16[3,32,256]{2,1,0:T(8,128)(2,1)S(1)}, bf16[3,32,256]{2,1,0:T(8,128)(2,1)}, u32[]{:S(2)}) copy-start(bf16[3,32,256]{2,1,0:T(8,128)(2,1)} %param.12) | copy-start | bytes 147460
  0.0 1.2 %copy-start.8 = (f32[256]{0:T(256)S(1)}, f32[256]{0:T(256)}, u32[]{:S(2)}) copy-start(f32[256]{0:T(256)} %param.18) | copy-start | bytes 3076
  3.9 12.8 %copy-start.2 = (bf16[256,512]{1,0:T(8,128)(2,1)S(1)}, bf16[256,512]{1,0:T(8,128)(2,1)}, u32[]{:S(2)}) copy-start(bf16[256,512]{1,0:T(8,128)(2,1)} %param.22) | copy-start | bytes 786436
  3.9 17.2 %all-to-all-start = ((bf16[16,3,2,1664]{3,2,1,0:T(2,128)(2,1)}), bf16[16,3,2,1664]{3,2,1,0:T(2,128)(2,1)S(1)}, u32[]{:S(2)}, u32[]{:S(2)}) async-start(bf16[16,3,2,1664]{3,2,1,0:T(2,128)(2,1)} %copy.153), calls=%async_computation | async-start | bytes 638976 | tf_op jit(solution)/shard_map/all_to_all | solution.py:54
  12.6 0.8 %copy-start.5 = (bf16[2,8,2,512]{3,2,1,0:T(2,128)(2,1)S(1)}, bf16[2,8,2,512]{3,2,1,0:T(2,128)(2,1)}, u32[]{:S(2)}) copy-start(bf16[2,8,2,512]{3,2,1,0:T(2,128)(2,1)} %param.13) | copy-start | bytes 98308
  13.6 0.7 copy-start.10
  14.4 0.7 copy-start.7
  15.8 0.7 copy-start.11
  16.7 0.7 copy-start.9
  23.3 10.4 %copy-start.3 = (bf16[512,256]{1,0:T(8,128)(2,1)S(1)}, bf16[512,256]{1,0:T(8,128)(2,1)}, u32[]{:S(2)}) copy-start(bf16[512,256]{1,0:T(8,128)(2,1)} %param.20) | copy-start | bytes 786436
  23.3 10.3 %all-to-all-start.1 = ((bf16[16,3,2,512]{3,2,1,0:T(2,128)(2,1)}), bf16[16,3,2,512]{3,2,1,0:T(2,128)(2,1)S(1)}, u32[]{:S(2)}, u32[]{:S(2)}) async-start(bf16[16,3,2,512]{3,2,1,0:T(2,128)(2,1)} %broadcast_in_dim.128), calls=%async_computation.1 | async-start | bytes 196608 | tf_op jit(solution)/shard_map/all_to_all | solution.py:24
  33.7 4.8 %copy-start.6 = (bf16[2,24,2,512]{3,2,1,0:T(2,128)(2,1)S(1)}, bf16[2,24,2,512]{3,2,1,0:T(2,128)(2,1)}, u32[]{:S(2)}) copy-start(bf16[2,24,2,512]{3,2,1,0:T(2,128)(2,1)} %param.14) | copy-start | bytes 294916
  33.9 7.3 %collective-permute-start.2 = (bf16[3,32,256]{2,1,0:T(8,128)(2,1)S(1)}, bf16[3,32,256]{2,1,0:T(8,128)(2,1)S(1)}, u32[]{:S(2)}, u32[]{:S(2)}) collective-permute-start(bf16[3,32,256]{2,1,0:T(8,128)(2,1)S(1)} %fusion.20), channel_id=1, source_target_pairs={{0,3},{1,2},{2,1},{3,0},{4,7},{5,6},{6,5},{7,4},{8,11},{9,10},{10,... | collective-permute-start | bytes 147464 | tf_op jit(solution)/shard_map/ppermute | solution.py:32
  38.0 3.4 %collective-permute-start.1 = (bf16[3,32,256]{2,1,0:T(8,128)(2,1)S(1)}, bf16[3,32,256]{2,1,0:T(8,128)(2,1)S(1)}, u32[]{:S(2)}, u32[]{:S(2)}) collective-permute-start(bf16[3,32,256]{2,1,0:T(8,128)(2,1)S(1)} %fusion.20), channel_id=1, source_target_pairs={{0,2},{1,3},{2,0},{3,1},{4,6},{5,7},{6,4},{7,5},{8,10},{9,11},{10,... | collective-permute-start | bytes 147464 | tf_op jit(solution)/shard_map/ppermute | solution.py:32
  38.3 3.2 %collective-permute-start = (bf16[3,32,256]{2,1,0:T(8,128)(2,1)S(1)}, bf16[3,32,256]{2,1,0:T(8,128)(2,1)S(1)}, u32[]{:S(2)}, u32[]{:S(2)}) collective-permute-start(bf16[3,32,256]{2,1,0:T(8,128)(2,1)S(1)} %fusion.20), channel_id=1, source_target_pairs={{0,1},{1,0},{2,3},{3,2},{4,5},{5,4},{6,7},{7,6},{8,9},{9,8},{10,11... | collective-permute-start | bytes 147464 | tf_op jit(solution)/shard_map/ppermute | solution.py:32
  38.5 9.3 %collective-permute-start.3 = (bf16[24,2,512]{2,0,1:T(8,128)(2,1)S(1)}, bf16[24,2,512]{2,0,1:T(8,128)(2,1)S(1)}, u32[]{:S(2)}, u32[]{:S(2)}) collective-permute-start(bf16[24,2,512]{2,0,1:T(8,128)(2,1)S(1)} %get-tuple-element.24), channel_id=1, source_target_pairs={{0,4},{4,0},{1,5},{5,1},{2,6},{6,2},{3,7},{7,3},{8,12},{12,8},{9,1... | collective-permute-start | bytes 147464 | tf_op jit(solution)/shard_map/ppermute | solution.py:82
  44.3 10.2 %all-to-all-start.2 = ((bf16[16,2,1600]{2,1,0:T(2,128)(2,1)}), bf16[16,2,1600]{2,1,0:T(2,128)(2,1)S(1)}, u32[]{:S(2)}, u32[]{:S(2)}) async-start(bf16[16,2,1600]{2,1,0:T(2,128)(2,1)} %reshape.196), calls=%async_computation.2 | async-start | bytes 212992 | tf_op jit(solution)/shard_map/all_to_all | solution.py:204
  55.6 10.1 %copy-start.4 = (bf16[512,256]{1,0:T(8,128)(2,1)S(1)}, bf16[512,256]{1,0:T(8,128)(2,1)}, u32[]{:S(2)}) copy-start(bf16[512,256]{1,0:T(8,128)(2,1)} %param.23) | copy-start | bytes 786436
  65.9 5.7 %collective-permute-start.6 = (bf16[3,32,256]{2,1,0:T(8,128)(2,1)S(1)}, bf16[3,32,256]{2,1,0:T(8,128)(2,1)S(1)}, u32[]{:S(2)}, u32[]{:S(2)}) collective-permute-start(bf16[3,32,256]{2,1,0:T(8,128)(2,1)S(1)} %convolution_convert_fusion.2), channel_id=1, source_target_pairs={{0,3},{1,2},{2,1},{3,0},{4,7},{5,6},{6,5},{7,4},{8,11},{9,10},{10,... | collective-permute-start | bytes 147464 | tf_op jit(solution)/shard_map/ppermute | solution.py:32
  69.3 3.6 %collective-permute-start.5 = (bf16[3,32,256]{2,1,0:T(8,128)(2,1)S(1)}, bf16[3,32,256]{2,1,0:T(8,128)(2,1)S(1)}, u32[]{:S(2)}, u32[]{:S(2)}) collective-permute-start(bf16[3,32,256]{2,1,0:T(8,128)(2,1)S(1)} %convolution_convert_fusion.2), channel_id=1, source_target_pairs={{0,2},{1,3},{2,0},{3,1},{4,6},{5,7},{6,4},{7,5},{8,10},{9,11},{10,... | collective-permute-start | bytes 147464 | tf_op jit(solution)/shard_map/ppermute | solution.py:32
  70.1 2.9 %collective-permute-start.4 = (bf16[3,32,256]{2,1,0:T(8,128)(2,1)S(1)}, bf16[3,32,256]{2,1,0:T(8,128)(2,1)S(1)}, u32[]{:S(2)}, u32[]{:S(2)}) collective-permute-start(bf16[3,32,256]{2,1,0:T(8,128)(2,1)S(1)} %convolution_convert_fusion.2), channel_id=1, source_target_pairs={{0,1},{1,0},{2,3},{3,2},{4,5},{5,4},{6,7},{7,6},{8,9},{9,8},{10,11... | collective-permute-start | bytes 147464 | tf_op jit(solution)/shard_map/ppermute | solution.py:32

commit v17 on v13

--- a/solution.py
+++ b/solution.py
@@ -21,8 +21,7 @@
     n_enc = lax.axis_size("enc")
     steps, owned, width = chunk.shape
     send = jnp.broadcast_to(chunk[None], (n_enc, steps, owned, width))
-    got = lax.all_to_all(send, "enc", 0, 0, tiled=True)
-    return got.transpose(1, 0, 2, 3).reshape(steps, n_enc * owned, width)
+    return lax.all_to_all(send, "enc", 0, 0, tiled=True)
 
 
 def tensor_sum(value):
@@ -173,8 +172,9 @@
     )
     context = (weighted / totals[..., None]).reshape(steps, seq_dev, width).astype(jnp.bfloat16)
     context_all = rows_gather(context)
+    current_blocks = current.reshape(steps, enc_count, seq_dev, -1).transpose(1, 0, 2, 3)
     partial_out = jnp.einsum(
-        "tsw,wf->tsf", context_all, w_out_self, preferred_element_type=jnp.float32
+        "jtsw,wf->jtsf", context_all, w_out_self, preferred_element_type=jnp.float32
     )
     partial_out, src_late, w_q_gained = lax.optimization_barrier(
         (partial_out, src_pool, w_q_gained)
@@ -182,12 +182,13 @@
     cross_kv = exchange_sources(
         src_late, assign, my_sources, block_at, enc_at, dp_at, dp_count, enc_count, seq_dev
     )
-    residual = current + tensor_sum(partial_out)
+    residual = current_blocks + tensor_sum(partial_out)
 
     cq = jnp.einsum(
-        "tsd,dw->tsw", residual.astype(jnp.bfloat16), w_q_gained, preferred_element_type=jnp.float32
-    )
-    own = rows_reduce_scatter(with_sumsq(cq, residual), seq_dev)
+        "jtsd,dw->jtsw", residual.astype(jnp.bfloat16), w_q_gained, preferred_element_type=jnp.float32
+    )
+    got = lax.all_to_all(with_sumsq(cq, residual), "enc", 0, 0, tiled=True)
+    own = jnp.sum(got.astype(jnp.float32), axis=0)
     cross_query = split_norm(own, width).reshape(steps, seq_dev, head_count, DK)
     cross_keys = cross_kv[:, :, 0].reshape(seq_dev, source_len, head_count, DK)
     cross_values = cross_kv[:, :, 1].reshape(seq_dev, source_len, head_count, DK)
@@ -204,9 +205,10 @@
     context = (weighted / totals[..., None]).reshape(steps, seq_dev, width).astype(jnp.bfloat16)
     context_all = rows_gather(context)
     output_rows = residual + tensor_sum(
-        jnp.einsum("tsw,wf->tsf", context_all, w_out_cross, preferred_element_type=jnp.float32)
-    )
-    return output_rows.astype(jnp.bfloat16)
+        jnp.einsum("jtsw,wf->jtsf", context_all, w_out_cross, preferred_element_type=jnp.float32)
+    )
+    output_rows = output_rows.astype(jnp.bfloat16).transpose(1, 0, 2, 3)
+    return output_rows.reshape(steps, enc_count * seq_dev, -1)
 
 
 def solution(mesh):

time: 73 us -> 71.9 us (0.985)
  other arithmetic: 4.21 us -> 2.89 us
    all_to_all x2 -> x1, waiting for transfers between devices: 10.2 us -> 3.61 us  [rows_reduce_scatter(): got = lax.all_to_all(send, 'enc', 0, 0, tiled=True)]
    all_to_all x1 -> x2, waiting for transfers between devices: 2.69 us -> 9.23 us  [the longest x1 6.61 us: on_device(): got = lax.all_to_all(with_sumsq(cq, residual), 'enc', 0, 0, tiled=True)]
    all_to_all x2 -> x1, starting transfers between devices: 12.2 us -> 8.72 us  [rows_reduce_scatter(): got = lax.all_to_all(send, 'enc', 0, 0, tiled=True)]
    all_to_all x1 -> x2, starting transfers between devices: 3.64 us -> 7.02 us  [the longest x1 3.51 us: on_device(): got = lax.all_to_all(with_sumsq(cq, residual), 'enc', 0, 0, tiled=True)]
    transpose x1, other arithmetic: 0.83 us -> 0.03 us  [on_device(): output_rows = output_rows.astype(jnp.bfloat16).transpose(1, 0, 2, 3)]
    concatenate x5 -> x3, local copies, waits for them, and re-layouts: 0.98 us -> 1.65 us  [with_sumsq(): jnp.concatenate([partial.astype(jnp.bfloat16), high, low, pad], axis=-1)]
  transfers between devices with their start and end apart: 10 -> 10, of which waited for: 6 -> 6; matrix products, arithmetic and copies ran while one was open for 5% -> 4% of each run, Pallas kernels for 0% -> 0%
where the time goes in v17:
time: 71.9 us; the launch traced here: 71.3 us
  starting transfers between devices  27.1 us (38%)
  waiting for transfers between devices  16 us (22%)
  blocking collectives  9.77 us (14%)
  local copies, waits for them, and re-layouts  9.53 us (13%)
  between operations  4.19 us (6%)
  other arithmetic  2.89 us (4%)
  matrix products  1.76 us (2%)
    all_to_all x1, blocking collectives, rows_gather(): return lax.all_to_all(send, 'enc', 0, 0, tiled=True)  9.77 us
    ppermute x6, starting transfers between devices, tensor_sum(): lax.ppermute(value, 'tensor', [(i, i ^ k) for i in range(n_t)])  8.81 us
    all_to_all x1, starting transfers between devices, rows_reduce_scatter(): got = lax.all_to_all(send, 'enc', 0, 0, tiled=True)  8.72 us
    all_to_all x1, waiting for transfers between devices, on_device(): got = lax.all_to_all(with_sumsq(cq, residual), 'enc', 0, 0, tiled=True)  6.61 us
    unnamed x28, local copies, waits for them, and re-layouts  3.94 us
    all_to_all x1, waiting for transfers between devices, rows_reduce_scatter(): got = lax.all_to_all(send, 'enc', 0, 0, tiled=True)  3.61 us
    all_to_all x1, starting transfers between devices, on_device(): got = lax.all_to_all(with_sumsq(cq, residual), 'enc', 0, 0, tiled=True)  3.51 us
    all_to_all x1, starting transfers between devices, rows_gather(): return lax.all_to_all(send, 'enc', 0, 0, tiled=True)  3.51 us
  transfers between devices with their start and end apart: 10, of which 6 were waited for; matrix products, arithmetic and copies ran while one was open for 4% of the time, Pallas kernels for 0%

profile of v17, /device:TPU:1, one launch (start us, length us, event | category | flops | bytes accessed | tf_op | source)
XLA Modules:
  0.0 71.3 jit_solution(15803541560246235629)
XLA Ops:
  0.0 1.0 %multiply_reduce_fusion.1 = f32[3,32]{1,0:T(4,128)S(1)} fusion(bf16[3,32,256]{2,1,0:T(8,128)(2,1)} %param.12), kind=kLoop, calls=%fused_computation.40 | loop fusion | flops 73632 | bytes 49536 | tf_op jit(solution)/shard_map/reduce_sum | solution.py:40
  1.0 0.2 copy-done
  1.2 0.3 convolution_convert_fusion
  1.4 0.3 copy.129
  1.7 0.3 convert_element_type.194
  1.9 0.1 reduce_sum.106
  2.1 0.8 %concatenate.7 = bf16[3,16,2,1664]{3,2,1,0:T(2,128)(2,1)S(1)} concatenate(bf16[3,16,2,1536]{3,2,1,0:T(2,128)(2,1)S(1)} %convert_element_type.194, bf16[3,16,2,1]{3,2,1,0:T(2,128)(2,1)S(1)} %get-tuple-element.21, bf16[3,16,2,1]{3,2,1,0:T(2,128)(2,1)S(1)} %get-tuple-element.20, bf16[3,16,2,126]{3,2,1,0:T(2,128)(2,1)S(1)} %broadcast_in_dim.125), dimensions={3} | concatenate | bytes 638976 | tf_op jit(solution)/shard_map/concatenate | solution.py:46
  3.0 0.9 %copy.133 = bf16[16,3,2,1664]{3,2,1,0:T(2,128)(2,1)} copy(bf16[16,3,2,1664]{3,2,0,1:T(2,128)(2,1)S(1)} %bitcast.93) | data formatting | bytes 638976 | tf_op jit(solution)/shard_map/transpose | solution.py:52
  3.9 8.7 %all-to-all-start = ((bf16[16,3,2,1664]{3,2,1,0:T(2,128)(2,1)}), bf16[16,3,2,1664]{3,2,1,0:T(2,128)(2,1)S(1)}, u32[]{:S(2)}, u32[]{:S(2)}) async-start(bf16[16,3,2,1664]{3,2,1,0:T(2,128)(2,1)} %copy.133), calls=%async_computation | async-start | bytes 638976 | tf_op jit(solution)/shard_map/all_to_all | solution.py:53
  12.7 0.7 %copy-done.5 = bf16[2,8,2,512]{3,2,1,0:T(2,128)(2,1)S(1)} copy-done((bf16[2,8,2,512]{3,2,1,0:T(2,128)(2,1)S(1)}, bf16[2,8,2,512]{3,2,1,0:T(2,128)(2,1)}, u32[]{:S(2)}) %copy-start.5) | copy-done | bytes 32792
  13.4 0.1 slice_reduce_fusion
  13.6 0.6 copy-done.10
  14.2 0.1 dynamic_slice.16
  14.3 0.1 iota_compare_fusion.2
  14.4 0.7 copy-done.7
  15.0 0.7 %fusion.38 = (s32[]{:T(128)}, s32[2]{0:T(128)S(1)}, s32[2]{0:T(128)S(1)}, s32[]{:T(128)}) fusion(s32[]{:T(128)S(6)} %add.96, s32[64]{0:T(128)S(1)} %copy-done.7, s32[]{:T(128)S(6)} %select_n.102, s32[]{:T(128)S(6)} %select_n.110), kind=kLoop, calls=%fused_computation.88 | loop fusion | flops 86 | bytes 52 | tf_op jit(solution)/shard_map/reduce_sum | solution.py:78
  15.8 0.7 copy-done.11
  16.4 0.2 fusion.36
  16.6 0.1 iota_compare_fusion.1
  16.7 0.7 copy-done.9
  17.4 0.1 multiply_convert_fusion
  17.5 3.6 %all-to-all-done = bf16[16,3,2,1664]{3,2,1,0:T(2,128)(2,1)S(1)} async-done(((bf16[16,3,2,1664]{3,2,1,0:T(2,128)(2,1)}), bf16[16,3,2,1664]{3,2,1,0:T(2,128)(2,1)S(1)}, u32[]{:S(2)}, u32[]{:S(2)}) %all-to-all-start) | async-done | bytes 319520 | tf_op jit(solution)/shard_map/all_to_all | solution.py:53
  21.1 0.1 convert_reduce_fusion
  21.2 0.1 fusion.40
  21.3 0.1 copy.169
  21.4 0.1 copy.170
  21.5 0.1 copy.138
  21.6 0.1 fusion.33
  21.7 0.2 convert_reduce_fusion.4
  21.9 0.1 convolution_bitcast_fusion.2
  22.1 0.1 convert_reduce_fusion.3
  22.2 0.2 fusion.3
  22.4 0.7 broadcast_in_dim.129
  23.1 3.5 %all-to-all-start.1 = ((bf16[16,3,2,512]{3,2,1,0:T(2,128)(2,1)}), bf16[16,3,2,512]{3,2,1,0:T(2,128)(2,1)S(1)}, u32[]{:S(2)}, u32[]{:S(2)}) async-start(bf16[16,3,2,512]{3,2,1,0:T(2,128)(2,1)} %broadcast_in_dim.129), calls=%async_computation.1 | async-start | bytes 196608 | tf_op jit(solution)/shard_map/all_to_all | solution.py:24
  29.3 0.1 pad.3.clone
  30.6 2.6 %all-to-all-done.1 = bf16[16,3,2,512]{3,2,1,0:T(2,128)(2,1)S(1)} async-done(((bf16[16,3,2,512]{3,2,1,0:T(2,128)(2,1)}), bf16[16,3,2,512]{3,2,1,0:T(2,128)(2,1)S(1)}, u32[]{:S(2)}, u32[]{:S(2)}) %all-to-all-start.1) | async-done | bytes 98336 | tf_op jit(solution)/shard_map/all_to_all | solution.py:24
  33.3 0.2 fusion.20
  33.5 4.1 %collective-permute-start.2 = (bf16[16,3,2,256]{3,0,2,1:T(8,128)(2,1)S(1)}, bf16[16,3,2,256]{3,0,2,1:T(8,128)(2,1)S(1)}, u32[]{:S(2)}, u32[]{:S(2)}) collective-permute-start(bf16[16,3,2,256]{3,0,2,1:T(8,128)(2,1)S(1)} %fusion.20), channel_id=1, source_target_pairs={{0,3},{1,2},{2,1},{3,0},{4,7},{5,6},{6,5},{7,4},{8,11},{9,10},{10,... | collective-permute-start | bytes 147464 | tf_op jit(solution)/shard_map/ppermute | solution.py:31
  37.6 0.3 collective-permute-start.1
  37.9 0.2 collective-permute-start
  38.1 2.6 %collective-permute-start.3 = (bf16[24,2,512]{2,0,1:T(8,128)(2,1)S(1)}, bf16[24,2,512]{2,0,1:T(8,128)(2,1)S(1)}, u32[]{:S(2)}, u32[]{:S(2)}) collective-permute-start(bf16[24,2,512]{2,0,1:T(8,128)(2,1)S(1)} %get-tuple-element.24), channel_id=1, source_target_pairs={{0,4},{4,0},{1,5},{5,1},{2,6},{6,2},{3,7},{7,3},{8,12},{12,8},{9,1... | collective-permute-start | bytes 147464 | tf_op jit(solution)/shard_map/ppermute | solution.py:81
  40.7 0.3 collective-permute-done.1
  41.0 0.1 multiply_reduce_fusion
  41.2 0.1 copy.149
  41.3 0.2 convolution_convert_fusion.1
  41.5 0.1 maximum_maximum_fusion
  41.6 0.7 %copy.152 = bf16[16,3,2,640]{3,2,1,0:T(2,128)(2,1)} copy(bf16[16,3,2,640]{3,0,2,1:T(8,128)(2,1)S(1)} %maximum_maximum_fusion) | data formatting | bytes 245760 | tf_op jit(solution)/shard_map/concatenate | solution.py:46
  42.3 3.5 %all-to-all-start.2 = ((bf16[16,3,2,640]{3,2,1,0:T(2,128)(2,1)}), bf16[16,3,2,640]{3,2,1,0:T(2,128)(2,1)S(1)}, u32[]{:S(2)}, u32[]{:S(2)}) async-start(bf16[16,3,2,640]{3,2,1,0:T(2,128)(2,1)} %copy.152), calls=%async_computation.2 | async-start | bytes 245760 | tf_op jit(solution)/shard_map/all_to_all | solution.py:190
  45.8 0.1 broadcast_select_fusion
  46.0 6.6 %all-to-all-done.2 = bf16[16,3,2,640]{3,2,1,0:T(2,128)(2,1)S(1)} async-done(((bf16[16,3,2,640]{3,2,1,0:T(2,128)(2,1)}), bf16[16,3,2,640]{3,2,1,0:T(2,128)(2,1)S(1)}, u32[]{:S(2)}, u32[]{:S(2)}) %all-to-all-start.2) | async-done | bytes 122912 | tf_op jit(solution)/shard_map/all_to_all | solution.py:190
  52.6 0.1 fusion.42
  52.7 0.1 copy.174
  52.8 0.1 copy.175
  52.9 0.1 copy.156
  53.0 0.1 fusion.34
  53.1 0.2 convert_reduce_fusion.2
  53.3 0.1 fusion.4
  53.6 9.8 %all_to_all.20 = bf16[16,3,2,512]{3,2,1,0:T(2,128)(2,1)S(1)} all-to-all(bf16[16,3,2,512]{3,2,1,0:T(2,128)(2,1)S(1)} %broadcast_in_dim.140), channel_id=1, replica_groups=mesh['enc'=16,'dp'=2,'tensor'=4] {'enc'}, dimensions={0} | all-to-all | bytes 196608 | tf_op jit(solution)/shard_map/all_to_all | solution.py:24
  63.3 0.2 convolution_convert_fusion.2
  63.5 3.5 %collective-permute-start.6 = (bf16[16,3,2,256]{3,0,2,1:T(8,128)(2,1)S(1)}, bf16[16,3,2,256]{3,0,2,1:T(8,128)(2,1)S(1)}, u32[]{:S(2)}, u32[]{:S(2)}) collective-permute-start(bf16[16,3,2,256]{3,0,2,1:T(8,128)(2,1)S(1)} %convolution_convert_fusion.2), channel_id=1, source_target_pairs={{0,3},{1,2},{2,1},{3,0},{4,7},{5,6},{6,5},{7,4},{8,11},{9,10},{10,... | collective-permute-start | bytes 147464 | tf_op jit(solution)/shard_map/ppermute | solution.py:31
  67.0 0.7 collective-permute-start.5
  67.7 1.5 %collective-permute-done.6 = bf16[16,3,2,256]{3,0,2,1:T(8,128)(2,1)S(1)} collective-permute-done((bf16[16,3,2,256]{3,0,2,1:T(8,128)(2,1)S(1)}, bf16[16,3,2,256]{3,0,2,1:T(8,128)(2,1)S(1)}, u32[]{:S(2)}, u32[]{:S(2)}) %collective-permute-start.6) | collective-permute-done | bytes 49184 | tf_op jit(solution)/shard_map/ppermute | solution.py:31
  69.2 1.4 %collective-permute-done.5 = bf16[16,3,2,256]{3,0,2,1:T(8,128)(2,1)S(1)} collective-permute-done((bf16[16,3,2,256]{3,0,2,1:T(8,128)(2,1)S(1)}, bf16[16,3,2,256]{3,0,2,1:T(8,128)(2,1)S(1)}, u32[]{:S(2)}, u32[]{:S(2)}) %collective-permute-start.5) | collective-permute-done | bytes 49184 | tf_op jit(solution)/shard_map/ppermute | solution.py:31
  70.7 0.6 reshape.177
  (49 shorter events, 0.6 us)
Async XLA Ops:
  0.0 1.2 %copy-start = (bf16[256,3,512]{2,0,1:T(8,128)(2,1)S(1)}, bf16[256,3,512]{2,0,1:T(8,128)(2,1)}, u32[]{:S(2)}) copy-start(bf16[256,3,512]{2,0,1:T(8,128)(2,1)} %param.19) | copy-start | bytes 2359300
  0.0 1.2 %copy-start.1 = (bf16[3,32,256]{2,1,0:T(8,128)(2,1)S(1)}, bf16[3,32,256]{2,1,0:T(8,128)(2,1)}, u32[]{:S(2)}) copy-start(bf16[3,32,256]{2,1,0:T(8,128)(2,1)} %param.12) | copy-start | bytes 147460
  0.0 1.2 %copy-start.8 = (f32[256]{0:T(256)S(1)}, f32[256]{0:T(256)}, u32[]{:S(2)}) copy-start(f32[256]{0:T(256)} %param.18) | copy-start | bytes 3076
  3.9 12.8 %copy-start.2 = (bf16[256,512]{1,0:T(8,128)(2,1)S(1)}, bf16[256,512]{1,0:T(8,128)(2,1)}, u32[]{:S(2)}) copy-start(bf16[256,512]{1,0:T(8,128)(2,1)} %param.22) | copy-start | bytes 786436
  3.9 17.2 %all-to-all-start = ((bf16[16,3,2,1664]{3,2,1,0:T(2,128)(2,1)}), bf16[16,3,2,1664]{3,2,1,0:T(2,128)(2,1)S(1)}, u32[]{:S(2)}, u32[]{:S(2)}) async-start(bf16[16,3,2,1664]{3,2,1,0:T(2,128)(2,1)} %copy.133), calls=%async_computation | async-start | bytes 638976 | tf_op jit(solution)/shard_map/all_to_all | solution.py:53
  12.7 0.8 %copy-start.5 = (bf16[2,8,2,512]{3,2,1,0:T(2,128)(2,1)S(1)}, bf16[2,8,2,512]{3,2,1,0:T(2,128)(2,1)}, u32[]{:S(2)}) copy-start(bf16[2,8,2,512]{3,2,1,0:T(2,128)(2,1)} %param.13) | copy-start | bytes 98308
  13.6 0.7 copy-start.10
  14.4 0.7 copy-start.7
  15.8 0.7 copy-start.11
  16.7 0.7 copy-start.9
  22.4 10.9 %copy-start.3 = (bf16[512,256]{1,0:T(8,128)(2,1)S(1)}, bf16[512,256]{1,0:T(8,128)(2,1)}, u32[]{:S(2)}) copy-start(bf16[512,256]{1,0:T(8,128)(2,1)} %param.20) | copy-start | bytes 786436
  23.1 10.1 %all-to-all-start.1 = ((bf16[16,3,2,512]{3,2,1,0:T(2,128)(2,1)}), bf16[16,3,2,512]{3,2,1,0:T(2,128)(2,1)S(1)}, u32[]{:S(2)}, u32[]{:S(2)}) async-start(bf16[16,3,2,512]{3,2,1,0:T(2,128)(2,1)} %broadcast_in_dim.129), calls=%async_computation.1 | async-start | bytes 196608 | tf_op jit(solution)/shard_map/all_to_all | solution.py:24
  30.6 7.4 %copy-start.6 = (bf16[2,24,2,512]{3,2,1,0:T(2,128)(2,1)S(1)}, bf16[2,24,2,512]{3,2,1,0:T(2,128)(2,1)}, u32[]{:S(2)}) copy-start(bf16[2,24,2,512]{3,2,1,0:T(2,128)(2,1)} %param.14) | copy-start | bytes 294916
  33.5 7.3 %collective-permute-start.2 = (bf16[16,3,2,256]{3,0,2,1:T(8,128)(2,1)S(1)}, bf16[16,3,2,256]{3,0,2,1:T(8,128)(2,1)S(1)}, u32[]{:S(2)}, u32[]{:S(2)}) collective-permute-start(bf16[16,3,2,256]{3,0,2,1:T(8,128)(2,1)S(1)} %fusion.20), channel_id=1, source_target_pairs={{0,3},{1,2},{2,1},{3,0},{4,7},{5,6},{6,5},{7,4},{8,11},{9,10},{10,... | collective-permute-start | bytes 147464 | tf_op jit(solution)/shard_map/ppermute | solution.py:31
  37.6 3.4 %collective-permute-start.1 = (bf16[16,3,2,256]{3,0,2,1:T(8,128)(2,1)S(1)}, bf16[16,3,2,256]{3,0,2,1:T(8,128)(2,1)S(1)}, u32[]{:S(2)}, u32[]{:S(2)}) collective-permute-start(bf16[16,3,2,256]{3,0,2,1:T(8,128)(2,1)S(1)} %fusion.20), channel_id=1, source_target_pairs={{0,2},{1,3},{2,0},{3,1},{4,6},{5,7},{6,4},{7,5},{8,10},{9,11},{10,... | collective-permute-start | bytes 147464 | tf_op jit(solution)/shard_map/ppermute | solution.py:31
  37.9 3.2 %collective-permute-start = (bf16[16,3,2,256]{3,0,2,1:T(8,128)(2,1)S(1)}, bf16[16,3,2,256]{3,0,2,1:T(8,128)(2,1)S(1)}, u32[]{:S(2)}, u32[]{:S(2)}) collective-permute-start(bf16[16,3,2,256]{3,0,2,1:T(8,128)(2,1)S(1)} %fusion.20), channel_id=1, source_target_pairs={{0,1},{1,0},{2,3},{3,2},{4,5},{5,4},{6,7},{7,6},{8,9},{9,8},{10,11... | collective-permute-start | bytes 147464 | tf_op jit(solution)/shard_map/ppermute | solution.py:31
  38.1 7.7 %collective-permute-start.3 = (bf16[24,2,512]{2,0,1:T(8,128)(2,1)S(1)}, bf16[24,2,512]{2,0,1:T(8,128)(2,1)S(1)}, u32[]{:S(2)}, u32[]{:S(2)}) collective-permute-start(bf16[24,2,512]{2,0,1:T(8,128)(2,1)S(1)} %get-tuple-element.24), channel_id=1, source_target_pairs={{0,4},{4,0},{1,5},{5,1},{2,6},{6,2},{3,7},{7,3},{8,12},{12,8},{9,1... | collective-permute-start | bytes 147464 | tf_op jit(solution)/shard_map/ppermute | solution.py:81
  42.3 10.3 %all-to-all-start.2 = ((bf16[16,3,2,640]{3,2,1,0:T(2,128)(2,1)}), bf16[16,3,2,640]{3,2,1,0:T(2,128)(2,1)S(1)}, u32[]{:S(2)}, u32[]{:S(2)}) async-start(bf16[16,3,2,640]{3,2,1,0:T(2,128)(2,1)} %copy.152), calls=%async_computation.2 | async-start | bytes 245760 | tf_op jit(solution)/shard_map/all_to_all | solution.py:190
  53.3 10.0 %copy-start.4 = (bf16[512,256]{1,0:T(8,128)(2,1)S(1)}, bf16[512,256]{1,0:T(8,128)(2,1)}, u32[]{:S(2)}) copy-start(bf16[512,256]{1,0:T(8,128)(2,1)} %param.23) | copy-start | bytes 786436
  63.5 5.7 %collective-permute-start.6 = (bf16[16,3,2,256]{3,0,2,1:T(8,128)(2,1)S(1)}, bf16[16,3,2,256]{3,0,2,1:T(8,128)(2,1)S(1)}, u32[]{:S(2)}, u32[]{:S(2)}) collective-permute-start(bf16[16,3,2,256]{3,0,2,1:T(8,128)(2,1)S(1)} %convolution_convert_fusion.2), channel_id=1, source_target_pairs={{0,3},{1,2},{2,1},{3,0},{4,7},{5,6},{6,5},{7,4},{8,11},{9,10},{10,... | collective-permute-start | bytes 147464 | tf_op jit(solution)/shard_map/ppermute | solution.py:31
  67.0 3.6 %collective-permute-start.5 = (bf16[16,3,2,256]{3,0,2,1:T(8,128)(2,1)S(1)}, bf16[16,3,2,256]{3,0,2,1:T(8,128)(2,1)S(1)}, u32[]{:S(2)}, u32[]{:S(2)}) collective-permute-start(bf16[16,3,2,256]{3,0,2,1:T(8,128)(2,1)S(1)} %convolution_convert_fusion.2), channel_id=1, source_target_pairs={{0,2},{1,3},{2,0},{3,1},{4,6},{5,7},{6,4},{7,5},{8,10},{9,11},{10,... | collective-permute-start | bytes 147464 | tf_op jit(solution)/shard_map/ppermute | solution.py:31
  67.7 2.9 %collective-permute-start.4 = (bf16[16,3,2,256]{3,0,2,1:T(8,128)(2,1)S(1)}, bf16[16,3,2,256]{3,0,2,1:T(8,128)(2,1)S(1)}, u32[]{:S(2)}, u32[]{:S(2)}) collective-permute-start(bf16[16,3,2,256]{3,0,2,1:T(8,128)(2,1)S(1)} %convolution_convert_fusion.2), channel_id=1, source_target_pairs={{0,1},{1,0},{2,3},{3,2},{4,5},{5,4},{6,7},{7,6},{8,9},{9,8},{10,11... | collective-permute-start | bytes 147464 | tf_op jit(solution)/shard_map/ppermute | solution.py:31
